TPU v7x, 32 devices: a whole 2x2x4 slice. The times are simulated.
32 devices in a mesh: grp: 2 (over y), gx: 16 (over z, x, core).
Axes of the slice: x: 2, y: 2, z: 4, core: 2. Of those that a mesh axis runs over, the one named last changes fastest.
Arguments:
- adjoint_state: float32 [16, 512, 1024], P(None, ('grp', 'gx')), parts along dimension 1, may hold values from -6 to 6
- speed_x: float32 [16, 512, 1024], P(None, ('grp', 'gx')), parts along dimension 1, may hold values from 0.2 to 2
- speed_y: float32 [16, 512, 1024], P(None, ('grp', 'gx')), parts along dimension 1, may hold values from 0.2 to 2
- speed_z: float32 [16, 512, 1024], P(None, ('grp', 'gx')), parts along dimension 1, may hold values from 0.2 to 2
- dispersion: float32 [16, 512, 1024], P(None, ('grp', 'gx')), parts along dimension 1, may hold values from 0.05 to 0.5
- face_flags: int32 [16, 512, 1024], P(None, ('grp', 'gx')), parts along dimension 1, may hold values from 0 to 7
- layer_weight: float32 [16], replicated, may hold values from 0.1 to 1
- cov_x: bfloat16 [256, 4, 128], P('gx'), may hold values from -0.25 to 0.25
- offsets_x: int32 [2, 4], replicated, may hold values from 0 to 1, as said below
- cov_y: float32 [1024, 4, 128], replicated, may hold values from -0.25 to 0.25
- offsets_y: int32 [8, 4], replicated, may hold values from 0 to 7, as said below
Outputs:
- recharge: float32 [512, 1024], P(('grp', 'gx')), parts along dimension 0
- prior: float32 [512, 1024], P(('grp', 'gx')), parts along dimension 0
There are 2 independent parts, one for each index of `grp`. A program takes and returns all parts, laid end to end along the dimension named above; an argument that names none is the same for every part. Nothing has to cross between parts.
Inputs may be any that keep to these rules, and one draw needn't show every extreme that they name: `offsets_x`: in every row, column 0 is 0, column 1 is 1 and column 2 is 1; the others are arbitrary. `offsets_y`: in every row, column 0 is 0, column 1 is 7 and column 2 is 4; the others are arbitrary.
All inputs are finite; a program needn't handle non-finite values.
Results may differ from a plain program's by a relative error of at most 0.00035.
Values may be sent and summed in bfloat16 or wider, within the bound.
No kernel may reach another device: no remote copies, remote signals or barrier semaphores. Data moves between devices by JAX's collectives and lax.ppermute only.
A program may use at most 128 MiB of HBM per device.

v0:
```python
import jax
import jax.numpy as jnp
from jax import lax
from jax.sharding import PartitionSpec as P

BLK = 128


precise = lax.Precision.HIGHEST


def passed_along(value, axis, steps):
    count = lax.axis_size(axis)
    first, last = (max(0, -steps), min(count, count - steps))
    return lax.ppermute(value, axis, [(source, source + steps) for source in range(first, last)])


def step_back(field, axis_number):
    length = field.shape[axis_number]
    leading = jnp.zeros_like(lax.slice_in_dim(field, 0, 1, axis=axis_number))
    return jnp.concatenate(
        [leading, lax.slice_in_dim(field, 0, length - 1, axis=axis_number)], axis=axis_number
    )


def step_ahead(field, axis_number):
    length = field.shape[axis_number]
    trailing = jnp.zeros_like(lax.slice_in_dim(field, 0, 1, axis=axis_number))
    return jnp.concatenate(
        [lax.slice_in_dim(field, 1, length, axis=axis_number), trailing], axis=axis_number
    )


def face_term(field, speed, upwind, spread, axis_number):
    lower_coef = speed * upwind + spread
    upper_coef = speed * (1.0 - upwind) + spread
    jump = field - step_back(field, axis_number)
    return upper_coef * jump + step_ahead(-lower_coef * jump, axis_number)


def band_rows(values, offsets, row_block):
    blocks = offsets.shape[0]
    block_ids = jnp.arange(blocks)
    owner = (row_block[:, None] == block_ids[None, :]).astype(jnp.int32)
    row_offsets = jnp.sum(owner[:, :, None] * offsets[None, :, :], axis=1)
    target = (row_block[:, None] + row_offsets) % blocks
    picks = (target[:, :, None] == block_ids[None, None, :]).astype(jnp.float32)
    dense = jnp.einsum("rkb,rkc->rbc", picks, values.astype(jnp.float32), precision=precise)
    return dense.reshape(values.shape[0], blocks * BLK)


def body(
    adjoint_state,
    speed_x,
    speed_y,
    speed_z,
    dispersion,
    face_flags,
    layer_weight,
    cov_x,
    offsets_x,
    cov_y,
    offsets_y,
):
    upwind_x = (face_flags % 2).astype(jnp.float32)
    upwind_y = (face_flags // 2 % 2).astype(jnp.float32)
    upwind_z = (face_flags // 4 % 2).astype(jnp.float32)
    lower_x = speed_x * upwind_x + dispersion
    upper_x = speed_x * (1.0 - upwind_x) + dispersion
    last_layer = adjoint_state[:, -1:, :]
    below = passed_along(last_layer, "gx", 1)
    behind = jnp.concatenate([below, adjoint_state[:, :-1, :]], axis=1)
    jump = adjoint_state - behind
    outgoing = -lower_x * jump
    above = passed_along(outgoing[:, :1, :], "gx", -1)
    ahead = jnp.concatenate([outgoing[:, 1:, :], above], axis=1)
    image = upper_x * jump + ahead
    image = image + face_term(adjoint_state, speed_y, upwind_y, dispersion, 2)
    image = image + face_term(adjoint_state, speed_z, upwind_z, dispersion, 0)
    recharge = jnp.einsum("z,zxy->xy", layer_weight, image, precision=precise)
    y_rows = jnp.arange(cov_y.shape[0]) // BLK
    dense_y = band_rows(cov_y, offsets_y, y_rows)
    smoothed = jnp.einsum("xc,rc->xr", recharge, dense_y, precision=precise)
    local_rows = recharge.shape[0]
    first_row = lax.axis_index("gx") * local_rows
    global_rows = first_row + jnp.arange(local_rows)
    slab = band_rows(cov_x, offsets_x, global_rows // BLK)
    prior = jnp.dot(
        slab,
        lax.all_gather(smoothed, "gx", axis=0, tiled=True),
        precision=precise,
        preferred_element_type=jnp.float32,
    )
    return (recharge, prior)


def solution(mesh):
    return jax.shard_map(
        body,
        mesh=mesh,
        in_specs=(
            P(None, ("grp", "gx"), None),
            P(None, ("grp", "gx"), None),
            P(None, ("grp", "gx"), None),
            P(None, ("grp", "gx"), None),
            P(None, ("grp", "gx"), None),
            P(None, ("grp", "gx"), None),
            P(),
            P("gx", None, None),
            P(),
            P(),
            P(),
        ),
        out_specs=(P(("grp", "gx"), None), P(("grp", "gx"), None)),
        check_vma=False,
    )
```

profile of v0, /device:TPU:0, one launch (start us, length us, event | category | flops | bytes accessed | tf_op | source)
XLA Modules:
  0.0 90.3 jit_solution(11556844308033964221)
XLA Ops:
  7.2 0.0 copy-start
  7.2 0.0 all-gather.2.cloned.1.call-start
  7.2 1.2 %slice.24 = f32[16,1,1024]{2,1,0:T(1,128)S(1)} slice(f32[16,16,1024]{2,1,0:T(8,128)} %param.11), slice={[0:16], [15:16], [0:1024]} | slice | bytes 131072 | tf_op jit(solution)/shard_map/slice | solution.py:70
  8.5 2.4 %collective-permute-start = (f32[16,1,1024]{2,1,0:T(1,128)S(1)}, f32[16,1,1024]{2,1,0:T(1,128)S(1)}, u32[]{:S(2)}, u32[]{:S(2)}) collective-permute-start(f32[16,1,1024]{2,1,0:T(1,128)S(1)} %slice.24), channel_id=1, source_target_pairs={{0,1},{1,2},{2,3},{3,4},{4,5},{5,6},{6,7},{7,8},{8,9},{9,10},{10,1... | collective-permute-start | bytes 196616 | tf_op jit(solution)/shard_map/ppermute | solution.py:15
  10.8 4.5 %fusion.6 = (f32[16,16,1024]{2,1,0:T(8,128)}, f32[16,16,1024]{2,1,0:T(8,128)}) fusion(s32[16,16,1024]{2,1,0:T(8,128)} %param.16), kind=kLoop, calls=%fused_computation.21 | loop fusion | flops 12845056 | bytes 3145728 | tf_op jit(solution)/shard_map/convert_element_type | solution.py:66
  15.3 0.8 multiply_reduce_fusion
  16.1 0.0 copy-start.1
  16.1 1.0 %copy.15 = s32[1024,4]{1,0:T(8,128)} copy(s32[1024,4]{0,1:T(4,128)S(1)} %add_select_fusion.5) | data formatting | bytes 32768 | tf_op jit(solution)/shard_map/jit(remainder)/select_n | solution.py:46
  17.2 6.5 %fusion.3 = f32[1024,8,128]{2,1,0:T(8,128)S(1)} fusion(f32[1024,4,128]{2,1,0:T(4,128)S(1)} %copy-done, s32[1024,4]{1,0:T(8,128)} %copy.15), kind=kOutput, calls=%fused_computation.4 | convolution fusion | flops 50364416 | bytes 6307840 | tf_op jit(solution)/shard_map/rkb,rkc->rbc/dot_general | solution.py:48
  23.7 0.1 slice.30
  23.7 0.0 collective-permute-done
  23.8 0.0 copy-start.6
  23.8 1.0 %pad_subtract_fusion.1 = (f32[16,16,1024]{2,1,0:T(8,128)S(1)}, f32[16,16,1024]{2,1,0:T(8,128)S(1)}, f32[16,16,1024]{2,1,0:T(8,128)S(1)}) fusion(f32[16,16,1024]{2,1,0:T(8,128)S(1)} %copy-done.1, f32[16,16,1023]{2,1,0:T(8,128)S(1)} %bitcast.20, f32[16,15,1024]{2,1,0:T(8,128)S(1)} %bitcast.21, f32[16,1,1024]{2,1,0:T(1,128)S(1)} %collective-permute-done, ...), kind=kLoop, calls=%fused_computation.37 | loop fusion | flops 5242880 | bytes 10419200 | tf_op jit(solution)/shard_map/sub | solution.py:37
  24.8 0.0 copy-start.8
  24.9 1.6 %collective-permute-start.1 = (f32[16,1,1024]{2,1,0:T(1,128)S(1)}, f32[16,1,1024]{2,1,0:T(1,128)S(1)}, u32[]{:S(2)}, u32[]{:S(2)}) collective-permute-start(f32[16,1,1024]{2,1,0:T(1,128)S(1)} %slice.33), channel_id=1, source_target_pairs={{1,0},{2,1},{3,2},{4,3},{5,4},{6,5},{7,6},{8,7},{9,8},{10,9},{11,1... | collective-permute-start | bytes 196616 | tf_op jit(solution)/shard_map/ppermute | solution.py:15
  26.5 1.1 %slice_multiply_fusion = f32[16,16,1023]{2,1,0:T(8,128)S(1)} fusion(f32[16,16,1024]{2,1,0:T(8,128)S(1)} %get-tuple-element.4, f32[16,16,1024]{2,1,0:T(8,128)S(1)} %copy-done.2, f32[16,16,1024]{2,1,0:T(8,128)S(1)} %copy-done.4, f32[16,16,1024]{2,1,0:T(8,128)S(1)} %copy-done.6), kind=kLoop, calls=%fused_computation.25 | loop fusion | flops 1047552 | bytes 5237760 | tf_op jit(solution)/shard_map/mul | solution.py:38
  27.7 0.4 slice_multiply_fusion.2
  28.1 0.1 slice.32
  28.2 0.0 copy-start.11
  28.2 2.0 %collective-permute-done.1 = f32[16,1,1024]{2,1,0:T(1,128)S(1)} collective-permute-done((f32[16,1,1024]{2,1,0:T(1,128)S(1)}, f32[16,1,1024]{2,1,0:T(1,128)S(1)}, u32[]{:S(2)}, u32[]{:S(2)}) %collective-permute-start.1) | collective-permute-done | bytes 65568 | tf_op jit(solution)/shard_map/ppermute | solution.py:15
  30.2 3.1 %fusion.12 = f32[16,16,1024]{2,1,0:T(8,128)S(1)} fusion(f32[16,1,1024]{2,1,0:T(1,128)S(1)} %collective-permute-done.1, f32[16,15,1024]{2,1,0:T(8,128)S(1)} %slice.32, f32[15,16,1024]{2,1,0:T(8,128)S(1)} %slice_multiply_fusion.2, f32[16,16,1024]{2,1,0:T(8,128)S(1)} %copy-done.2, f32[16,16,1024]{2,1,0:T(8,128)S(1)} %copy-done.8, ...), kind=kLoop, calls=%fused_computation.32 | loop fusion | flops 19922944 | bytes 13498368 | tf_op jit(solution)/shard_map/add | solution.py:79
  33.4 0.0 copy-start.10
  33.4 0.0 copy-start.12
  33.4 1.3 %fusion.13 = f32[1,16,1024]{2,0,1:T(1,128)S(1)} fusion(f32[16,16,1024]{2,1,0:T(8,128)S(1)} %fusion.12, f32[16]{0:T(128)S(1)} %copy-done.11), kind=kOutput, calls=%fused_computation.33 | convolution fusion | flops 3145728 | bytes 1114176 | tf_op jit(solution)/shard_map/z,zxy->xy/dot_general | solution.py:80
  34.7 0.0 copy-start.9
  34.7 4.4 %fusion = f32[16,1024]{1,0:T(8,128)} fusion(f32[16,1024]{1,0:T(8,128)S(1)} %bitcast.25, f32[128,8,8,128]{3,2,1,0:T(8,128)S(1)} %bitcast.24), kind=kOutput, calls=%fused_computation | convolution fusion | flops 201326592 | bytes 4325376 | tf_op jit(solution)/shard_map/xc,rc->xr/dot_general | solution.py:83
  39.1 0.0 all-gather.2.cloned.1.call-update
  39.2 0.1 multiply_reduce_fusion.1
  39.3 0.1 copy.14
  39.4 0.1 fusion.20
  39.5 41.5 %all-gather.2.cloned.1.call-done = f32[256,1024]{1,0:T(8,128)} async-done(((f32[16,1024]{1,0:T(8,128)}), f32[256,1024]{1,0:T(8,128)}) %all-gather.2.cloned.1.call-update) | async-done | bytes 1048592 | tf_op jit(solution)/shard_map/all_gather | solution.py:90
  81.0 2.5 %fusion.23 = f32[16,1024]{1,0:T(8,128)} fusion(f32[256,1024]{1,0:T(8,128)} %all-gather.2.cloned.1.call-done, f32[2,8,2,128]{3,2,1,0:T(2,128)S(1)} %bitcast.27), kind=kOutput, calls=%fused_computation.56 | convolution fusion | flops 50331648 | bytes 1130496 | tf_op jit(solution)/shard_map/dot_general | solution.py:88
  (26 shorter events, 0.1 us)
Async XLA Ops:
  7.2 10.0 %copy-start = (f32[1024,4,128]{2,1,0:T(4,128)S(1)}, f32[1024,4,128]{2,1,0:T(4,128)}, u32[]{:S(2)}) copy-start(f32[1024,4,128]{2,1,0:T(4,128)} %param.20) | copy-start | bytes 6291460
  7.2 73.8 %all-gather.2.cloned.1.call-start = ((), (), s32[]{:S(2)}) async-start(), calls=%async_computation | async-start | bytes 1114112 | tf_op jit(solution)/shard_map/all_gather | solution.py:90
  8.5 15.3 %collective-permute-start = (f32[16,1,1024]{2,1,0:T(1,128)S(1)}, f32[16,1,1024]{2,1,0:T(1,128)S(1)}, u32[]{:S(2)}, u32[]{:S(2)}) collective-permute-start(f32[16,1,1024]{2,1,0:T(1,128)S(1)} %slice.24), channel_id=1, source_target_pairs={{0,1},{1,2},{2,3},{3,4},{4,5},{5,6},{6,7},{7,8},{8,9},{9,10},{10,1... | collective-permute-start | bytes 196616 | tf_op jit(solution)/shard_map/ppermute | solution.py:15
  16.1 7.5 %copy-start.1 = (f32[16,16,1024]{2,1,0:T(8,128)S(1)}, f32[16,16,1024]{2,1,0:T(8,128)}, u32[]{:S(2)}) copy-start(f32[16,16,1024]{2,1,0:T(8,128)} %param.11) | copy-start | bytes 3145732
  17.2 6.6 %copy-start.2 = (f32[16,16,1024]{2,1,0:T(8,128)S(1)}, f32[16,16,1024]{2,1,0:T(8,128)}, u32[]{:S(2)}) copy-start(f32[16,16,1024]{2,1,0:T(8,128)} %param.15) | copy-start | bytes 3145732
  17.2 6.6 %copy-start.3 = (s32[16,16,1024]{2,1,0:T(8,128)S(1)}, s32[16,16,1024]{2,1,0:T(8,128)}, u32[]{:S(2)}) copy-start(s32[16,16,1024]{2,1,0:T(8,128)} %param.16) | copy-start | bytes 3145732
  17.2 6.6 %copy-start.5 = (f32[16,16,1024]{2,1,0:T(8,128)S(1)}, f32[16,16,1024]{2,1,0:T(8,128)}, u32[]{:S(2)}) copy-start(f32[16,16,1024]{2,1,0:T(8,128)} %param.12) | copy-start | bytes 3145732
  23.8 2.7 %copy-start.4 = (f32[16,16,1024]{2,1,0:T(8,128)S(1)}, f32[16,16,1024]{2,1,0:T(8,128)}, u32[]{:S(2)}) copy-start(f32[16,16,1024]{2,1,0:T(8,128)} %get-tuple-element.2) | copy-start | bytes 3145732
  23.8 2.7 %copy-start.6 = (f32[16,16,1024]{2,1,0:T(8,128)S(1)}, f32[16,16,1024]{2,1,0:T(8,128)}, u32[]{:S(2)}) copy-start(f32[16,16,1024]{2,1,0:T(8,128)} %param.13) | copy-start | bytes 3145732
  24.8 2.9 %copy-start.7 = (f32[16,16,1024]{2,1,0:T(8,128)S(1)}, f32[16,16,1024]{2,1,0:T(8,128)}, u32[]{:S(2)}) copy-start(f32[16,16,1024]{2,1,0:T(8,128)} %get-tuple-element.3) | copy-start | bytes 3145732
  24.8 2.9 %copy-start.8 = (f32[16,16,1024]{2,1,0:T(8,128)S(1)}, f32[16,16,1024]{2,1,0:T(8,128)}, u32[]{:S(2)}) copy-start(f32[16,16,1024]{2,1,0:T(8,128)} %param.14) | copy-start | bytes 3145732
  24.9 5.4 %collective-permute-start.1 = (f32[16,1,1024]{2,1,0:T(1,128)S(1)}, f32[16,1,1024]{2,1,0:T(1,128)S(1)}, u32[]{:S(2)}, u32[]{:S(2)}) collective-permute-start(f32[16,1,1024]{2,1,0:T(1,128)S(1)} %slice.33), channel_id=1, source_target_pairs={{1,0},{2,1},{3,2},{4,3},{5,4},{6,5},{7,6},{8,7},{9,8},{10,9},{11,1... | collective-permute-start | bytes 196616 | tf_op jit(solution)/shard_map/ppermute | solution.py:15
  28.2 5.2 %copy-start.11 = (f32[16]{0:T(128)S(1)}, f32[16]{0:T(128)}, u32[]{:S(2)}) copy-start(f32[16]{0:T(128)} %param.17) | copy-start | bytes 196
  33.4 5.8 %copy-start.10 = (s32[2,4]{1,0:T(2,128)S(1)}, s32[2,4]{1,0:T(2,128)}, u32[]{:S(2)}) copy-start(s32[2,4]{1,0:T(2,128)} %param.19) | copy-start | bytes 100
  33.4 6.0 %copy-start.12 = (bf16[16,4,128]{2,1,0:T(4,128)(2,1)S(1)}, bf16[16,4,128]{2,1,0:T(4,128)(2,1)}, u32[]{:S(2)}) copy-start(bf16[16,4,128]{2,1,0:T(4,128)(2,1)} %param.18) | copy-start | bytes 49156
  34.7 48.8 %copy-start.9 = (f32[1,16,1024]{2,1,0:T(8,128)}, f32[1,16,1024]{2,1,0:T(8,128)S(1)}, u32[]{:S(2)}) copy-start(f32[1,16,1024]{2,1,0:T(8,128)S(1)} %copy.31) | copy-start | bytes 196612
Sparse Core Ops, SparseCore 0:
  39.3 41.7 all-gather.1
where the time goes:
time: 90.6 us; the launch traced here: 90.3 us
  waiting for transfers between devices  43.5 us (48%)
  matrix products  14.7 us (16%)
  between operations  14.3 us (16%)
  other arithmetic  11.1 us (12%)
  starting transfers between devices  4 us (4%)
  local copies, waits for them, and re-layouts  2.67 us (3%)
    all_gather x1, waiting for transfers between devices, body(): lax.all_gather(smoothed, 'gx', axis=0, tiled=True)  41.5 us
    dot_general x2, matrix products, band_rows(): jnp.einsum('rkb,rkc->rbc', picks, values.astype(jnp.float32), precision=p...  6.6 us
    convert_element_type x1, other arithmetic, body(): upwind_y = (face_flags // 2 % 2).astype(jnp.float32)  4.46 us
    dot_general x1, matrix products, body(): smoothed = jnp.einsum('xc,rc->xr', recharge, dense_y, precision=precise)  4.4 us
    ppermute x2, starting transfers between devices, passed_along(): lax.ppermute(value, axis, [(source, source + steps) for source in range(f...  3.96 us
    add x1, other arithmetic, body(): image = image + face_term(adjoint_state, speed_z, upwind_z, dispersion, 0)  3.15 us
    dot_general x1, matrix products, body(): jnp.dot(slab, lax.all_gather(smoothed, 'gx', axis=0, tiled=True), precisi...  2.46 us
    ppermute x2, waiting for transfers between devices, passed_along(): lax.ppermute(value, axis, [(source, source + steps) for source in range(f...  2.02 us
  transfers between devices with their start and end apart: 3, of which 2 were waited for; matrix products, arithmetic and copies ran while one was open for 16% of the time, Pallas kernels for 0%

commit v1 on v0

v1 whole, which is shorter than its diff:
```python
import jax
import jax.numpy as jnp
from jax import lax
from jax.experimental import pallas as pl
from jax.experimental.pallas import tpu as pltpu
from jax.sharding import PartitionSpec as P

BLK = 128
Z_CHUNK = 4

precise = lax.Precision.HIGHEST


def passed_along(value, axis, steps):
    count = lax.axis_size(axis)
    first, last = (max(0, -steps), min(count, count - steps))
    return lax.ppermute(value, axis, [(source, source + steps) for source in range(first, last)])


def coefs(flags, bit, speed, spread):
    on = (flags & bit) != 0
    lower = spread + jnp.where(on, speed, 0.0)
    upper = spread + jnp.where(on, 0.0, speed)
    return lower, upper


def stencil_kernel(w_ref, s_ref, sprev_ref, f_ref, vx_ref, vy_ref, vz_ref, d_ref, out_ref):
    c = pl.program_id(0)
    rows, cols = out_ref.shape
    sub = lax.broadcasted_iota(jnp.int32, (rows, cols), 0)
    lane = lax.broadcasted_iota(jnp.int32, (rows, cols), 1)

    @pl.when(c == 0)
    def _():
        out_ref[...] = jnp.zeros_like(out_ref)

    prev = jnp.where(c > 0, sprev_ref[0], 0.0)
    acc = jnp.zeros((rows, cols), jnp.float32)
    for j in range(s_ref.shape[0]):
        z = c * s_ref.shape[0] + j
        s = s_ref[j]
        f = f_ref[j]
        d = d_ref[j]
        lo_x, up_x = coefs(f, 1, vx_ref[j], d)
        lo_y, up_y = coefs(f, 2, vy_ref[j], d)
        lo_z, up_z = coefs(f, 4, vz_ref[j], d)
        s_xm = jnp.where(sub == 0, 0.0, pltpu.roll(s, 1, 0))
        jx = s - s_xm
        ax = -lo_x * jx
        ax_next = jnp.where(sub == rows - 1, 0.0, pltpu.roll(ax, rows - 1, 0))
        img = up_x * jx + ax_next
        s_ym = jnp.where(lane == 0, 0.0, pltpu.roll(s, 1, 1))
        jy = s - s_ym
        ay = -lo_y * jy
        ay_next = jnp.where(lane == cols - 1, 0.0, pltpu.roll(ay, cols - 1, 1))
        img = img + (up_y * jy + ay_next)
        jz = s - prev
        img = img + up_z * jz
        acc = acc + w_ref[z] * img
        w_before = jnp.where(z > 0, w_ref[jnp.maximum(z - 1, 0)], 0.0)
        acc = acc + w_before * (-lo_z * jz)
        prev = s
    out_ref[...] += acc


def stencil(layer_weight, s, f, vx, vy, vz, d):
    depth, rows, cols = s.shape
    zc = Z_CHUNK if depth % Z_CHUNK == 0 else depth
    block = pl.BlockSpec((zc, rows, cols), lambda c: (c, 0, 0))
    prev_block = pl.BlockSpec((1, rows, cols), lambda c: (jnp.maximum(c * zc - 1, 0), 0, 0))
    return pl.pallas_call(
        stencil_kernel,
        grid=(depth // zc,),
        in_specs=[
            pl.BlockSpec(memory_space=pltpu.SMEM),
            block,
            prev_block,
            block,
            block,
            block,
            block,
            block,
        ],
        out_specs=pl.BlockSpec((rows, cols), lambda c: (0, 0)),
        out_shape=jax.ShapeDtypeStruct((rows, cols), jnp.float32),
        compiler_params=pltpu.CompilerParams(dimension_semantics=("arbitrary",)),
    )(layer_weight, s, s, f, vx, vy, vz, d)


def bit_reversed(count):
    bits = count.bit_length() - 1
    return [int(format(p, f"0{bits}b")[::-1], 2) if bits else 0 for p in range(count)]


def gather_rows(local, axis):
    count = lax.axis_size(axis)
    buf = local[None]
    bit = count // 2
    while bit >= 1:
        other = lax.ppermute(buf, axis, [(i, i ^ bit) for i in range(count)])
        buf = jnp.concatenate([buf, other], axis=0)
        bit //= 2
    return buf


def body(
    adjoint_state,
    speed_x,
    speed_y,
    speed_z,
    dispersion,
    face_flags,
    layer_weight,
    cov_x,
    offsets_x,
    cov_y,
    offsets_y,
):
    count = lax.axis_size("gx")
    me = lax.axis_index("gx")
    depth, rows, cols = adjoint_state.shape

    first_s = adjoint_state[:, 0, :]
    lo_x0, up_x0 = coefs(face_flags[:, 0, :], 1, speed_x[:, 0, :], dispersion[:, 0, :])
    last_s = adjoint_state[:, rows - 1, :]
    from_next = passed_along(jnp.stack([first_s, lo_x0]), "gx", -1)
    from_prev = passed_along(last_s, "gx", 1)

    partial = stencil(layer_weight, adjoint_state, face_flags, speed_x, speed_y, speed_z, dispersion)

    corr_first = jnp.sum(layer_weight[:, None] * (-up_x0 * from_prev), axis=0)
    ax_next = -from_next[1] * (from_next[0] - last_s)
    corr_last = jnp.sum(layer_weight[:, None] * ax_next, axis=0)
    recharge = partial.at[0].add(corr_first).at[rows - 1].add(corr_last)

    gathered = gather_rows(recharge, "gx")
    order = me ^ jnp.array(bit_reversed(count), jnp.int32)

    nxb = offsets_x.shape[0]
    global_rows = me * rows + jnp.arange(rows)
    row_block = global_rows // BLK
    target = (row_block[:, None] + offsets_x[row_block]) % nxb
    blocks = jnp.arange(nxb)
    hit = target[:, :, None, None] == blocks[None, None, :, None]
    slab = jnp.sum(jnp.where(hit, cov_x.astype(jnp.float32)[:, :, None, :], 0.0), axis=1)
    slab = slab.reshape(rows, count, rows)
    slab = jnp.take(slab, order, axis=1).reshape(rows, count * rows)
    mixed = jnp.dot(slab, gathered.reshape(count * rows, cols), precision=precise, preferred_element_type=jnp.float32)

    nyb = offsets_y.shape[0]
    col_block = (jnp.arange(nyb)[:, None] + offsets_y) % nyb
    picked = jnp.take(mixed.reshape(rows, nyb, BLK), col_block, axis=1)
    prior = jnp.einsum(
        "xrkc,rikc->xri",
        picked,
        cov_y.reshape(nyb, BLK, cov_y.shape[1], BLK),
        precision=precise,
        preferred_element_type=jnp.float32,
    ).reshape(rows, cols)
    return (recharge, prior)


def solution(mesh):
    return jax.shard_map(
        body,
        mesh=mesh,
        in_specs=(
            P(None, ("grp", "gx"), None),
            P(None, ("grp", "gx"), None),
            P(None, ("grp", "gx"), None),
            P(None, ("grp", "gx"), None),
            P(None, ("grp", "gx"), None),
            P(None, ("grp", "gx"), None),
            P(),
            P("gx", None, None),
            P(),
            P(),
            P(),
        ),
        out_specs=(P(("grp", "gx"), None), P(("grp", "gx"), None)),
        check_vma=False,
    )
```

time: 90.6 us -> 53.5 us (0.59)
  waiting for transfers between devices: 43.5 us -> 17 us
  between operations: 14.3 us -> 0.94 us
  matrix products: 14.7 us -> 2.85 us
  local copies, waits for them, and re-layouts: 2.67 us -> 10.7 us
  starting transfers between devices: 4 us -> 9.85 us
  Pallas kernels: 0 us -> 5 us
  other arithmetic: 11.1 us -> 6.46 us
    all_gather x1 -> x0, waiting for transfers between devices: 41.5 us -> none  [body(): lax.all_gather(smoothed, 'gx', axis=0, tiled=True)]
    ppermute x0 -> x4, waiting for transfers between devices: none -> 17 us  [gather_rows(): other = lax.ppermute(buf, axis, [(i, i ^ bit) for i in range(count)])]
    dot_general x5 -> x2, matrix products: 14.7 us -> 2.85 us  [the longest x1 1.89 us: body(): jnp.einsum('xrkc,rikc->xri', picked, cov_y.reshape(nyb, BLK, cov_y.shape[...]
    ppermute x0 -> x4, starting transfers between devices: none -> 5.53 us  [gather_rows(): other = lax.ppermute(buf, axis, [(i, i ^ bit) for i in range(count)])]
    pallas_call x0 -> x1, Pallas kernels: none -> 5 us  [stencil(): pl.pallas_call(stencil_kernel, grid=(depth // zc,), in_specs=[pl.BlockSpe...]
    convert_element_type x3 -> x0, other arithmetic: 4.47 us -> none  [the longest x1 4.46 us: body(): upwind_y = (face_flags // 2 % 2).astype(jnp.float32)]
    scatter-add x0 -> x2, local copies, waits for them, and re-layouts: none -> 2.78 us  [body(): recharge = partial.at[0].add(corr_first).at[rows - 1].add(corr_last)]
    gather x0 -> x3, local copies, waits for them, and re-layouts: none -> 2.41 us  [the longest x1 1.25 us: body(): target = (row_block[:, None] + offsets_x[row_block]) % nxb]
  transfers between devices with their start and end apart: 3 -> 6, of which waited for: 2 -> 4; matrix products, arithmetic and copies ran while one was open for 16% -> 8% of each run, Pallas kernels for 0% -> 9%
where the time goes in v1:
time: 53.5 us; the launch traced here: 52.8 us
  waiting for transfers between devices  17 us (32%)
  local copies, waits for them, and re-layouts  10.7 us (20%)
  starting transfers between devices  9.85 us (18%)
  other arithmetic  6.46 us (12%)
  Pallas kernels  5 us (9%)
  matrix products  2.85 us (5%)
  between operations  0.94 us (2%)
    ppermute x4, waiting for transfers between devices, gather_rows(): other = lax.ppermute(buf, axis, [(i, i ^ bit) for i in range(count)])  17 us
    ppermute x4, starting transfers between devices, gather_rows(): other = lax.ppermute(buf, axis, [(i, i ^ bit) for i in range(count)])  5.53 us
    pallas_call x1, Pallas kernels, stencil(): pl.pallas_call(stencil_kernel, grid=(depth // zc,), in_specs=[pl.BlockSpe...  5 us
    ppermute x2, starting transfers between devices, passed_along(): lax.ppermute(value, axis, [(source, source + steps) for source in range(f...  4.33 us
    scatter-add x2, local copies, waits for them, and re-layouts, body(): recharge = partial.at[0].add(corr_first).at[rows - 1].add(corr_last)  2.78 us
    dot_general x1, matrix products, body(): jnp.einsum('xrkc,rikc->xri', picked, cov_y.reshape(nyb, BLK, cov_y.shape[...  1.89 us
    concatenate x3, other arithmetic, gather_rows(): buf = jnp.concatenate([buf, other], axis=0)  1.75 us
    dot_general x1, local copies, waits for them, and re-layouts, body(): jnp.dot(slab, gathered.reshape(count * rows, cols), precision=precise, pr...  1.55 us
  transfers between devices with their start and end apart: 6, of which 4 were waited for; matrix products, arithmetic and copies ran while one was open for 8% of the time, Pallas kernels for 9%

profile of v1, /device:TPU:0, one launch (start us, length us, event | category | flops | bytes accessed | tf_op | source)
XLA Modules:
  0.0 52.8 jit_solution(9536458537485231949)
XLA Ops:
  0.6 1.4 %fusion.24 = (f32[16,1,1024]{2,1,0:T(1,128)S(1)}, f32[1,16,1024]{2,0,1:T(1,128)S(1)}) fusion(f32[16,16,1024]{2,1,0:T(8,128)} %sprev_ref.1), kind=kLoop, calls=%fused_computation.69 | loop fusion | bytes 262144 | tf_op jit(solution)/shard_map/slice | solution.py:125
  2.1 1.5 %fusion.23 = (f32[16,1,1024]{2,1,0:T(1,128)S(1)}, f32[1,16,1024]{2,0,1:T(1,128)S(1)}, f32[16,1,1024]{2,1,0:T(1,128)S(1)}) fusion(f32[16,16,1024]{2,1,0:T(8,128)} %d_ref.1, f32[16,16,1024]{2,1,0:T(8,128)} %vx_ref.1, s32[16,16,1024]{2,1,0:T(8,128)} %f_ref.1), kind=kLoop, calls=%fused_computation.68 | loop fusion | flops 65536 | bytes 393216 | tf_op jit(solution)/shard_map/slice | solution.py:124
  3.6 0.1 pad_maximum_fusion.2
  3.7 1.3 %collective-permute-start.1 = (f32[2,16,1024]{2,0,1:T(2,128)S(1)}, f32[2,16,1024]{2,0,1:T(2,128)S(1)}, u32[]{:S(2)}, u32[]{:S(2)}) collective-permute-start(f32[2,16,1024]{2,0,1:T(2,128)S(1)} %pad_maximum_fusion.2), channel_id=1, source_target_pairs={{1,0},{2,1},{3,2},{4,3},{5,4},{6,5},{7,6},{8,7},{9,8},{10,9},{11,1... | collective-permute-start | bytes 393224 | tf_op jit(solution)/shard_map/ppermute | solution.py:17
  5.1 3.0 %collective-permute-start = (f32[16,1024]{1,0:T(8,128)S(1)}, f32[16,1024]{1,0:T(8,128)S(1)}, u32[]{:S(2)}, u32[]{:S(2)}) collective-permute-start(f32[16,1024]{1,0:T(8,128)S(1)} %bitcast.65), channel_id=1, source_target_pairs={{0,1},{1,2},{2,3},{3,4},{4,5},{5,6},{6,7},{7,8},{8,9},{9,10},{10,1... | collective-permute-start | bytes 196616 | tf_op jit(solution)/shard_map/ppermute | solution.py:17
  8.1 1.1 %and_compare_fusion = pred[16,1,1024]{2,1,0:T(4,128)(4,1)S(1)} fusion(s32[16,16,1024]{2,1,0:T(8,128)} %f_ref.1), kind=kLoop, calls=%fused_computation.33 | loop fusion | flops 32768 | bytes 81920 | tf_op jit(solution)/shard_map/ne | solution.py:21
  9.3 1.2 %gather_fusion = s32[16,4]{1,0:T(8,128)S(1)} fusion(s32[2,4]{1,0:T(2,128)} %param.24, s32[1024]{0:T(1024)S(1)} %pad_clamp_fusion.2), kind=kCustom, calls=%fused_computation | custom fusion | bytes 576 | tf_op jit(solution)/shard_map/gather | solution.py:142
  10.7 5.0 %shard_map.131 = f32[16,1024]{1,0:T(8,128)} custom-call(f32[16]{0:T(128)} %w_ref.1, f32[16,16,1024]{2,1,0:T(8,128)} %sprev_ref.1, f32[16,16,1024]{2,1,0:T(8,128)} %sprev_ref.1, s32[16,16,1024]{2,1,0:T(8,128)} %f_ref.1, f32[16,16,1024]{2,1,0:T(8,128)} %vx_ref.1, f32[16,16,1024]{2,1,0:T(8,128)} %vy_ref.1, f32[16,16,1024]{2,1,0:T(8,128)} %vz_ref.1, ...), custom_call_target="tpu_custom_call" | custom-call | tf_op jit(solution)/shard_map/pallas_call | solution.py:71
  15.7 0.1 fusion.25
  15.9 0.1 fusion.12
  16.0 0.8 %slice_add_fusion.1 = f32[1,1024]{1,0:T(1,128)S(1)} fusion(f32[1,1024]{1,0:T(1,128)S(1)} %bitcast.68, f32[16,1024]{1,0:T(8,128)} %shard_map.131), kind=kLoop, calls=%fused_computation.45 | loop fusion | flops 1024 | bytes 12288 | tf_op jit(solution)/shard_map/add | solution.py:134
  16.8 1.4 %scatter-add.6 = f32[16,1024]{1,0:T(8,128)} dynamic-update-slice(f32[16,1024]{1,0:T(8,128)} %shard_map.131, f32[1,1024]{1,0:T(1,128)S(1)} %slice_add_fusion.1, s32[]{:T(128)} %constant.125.clone.1, s32[]{:T(128)} %constant.125.clone.1) | dynamic-update-slice | bytes 8196 | tf_op jit(solution)/shard_map/scatter-add | solution.py:134
  18.1 0.8 %slice_add_fusion = f32[1,1024]{1,0:T(1,128)S(1)} fusion(f32[1,1024]{1,0:T(1,128)S(1)} %bitcast.67, f32[16,1024]{1,0:T(8,128)} %scatter-add.6), kind=kLoop, calls=%fused_computation.44 | loop fusion | flops 1024 | bytes 12288 | tf_op jit(solution)/shard_map/add | solution.py:134
  18.9 1.4 %scatter-add.9 = f32[16,1024]{1,0:T(8,128)} dynamic-update-slice(f32[16,1024]{1,0:T(8,128)} %scatter-add.6, f32[1,1024]{1,0:T(1,128)S(1)} %slice_add_fusion, s32[]{:T(128)} %constant.127.clone.1, s32[]{:T(128)} %constant.125.clone.1) | dynamic-update-slice | bytes 8196 | tf_op jit(solution)/shard_map/scatter-add | solution.py:134
  20.3 4.4 %collective-permute-start.2 = (f32[1,16,1024]{2,1,0:T(8,128)}, f32[1,16,1024]{2,1,0:T(8,128)S(1)}, u32[]{:S(2)}, u32[]{:S(2)}) collective-permute-start(f32[1,16,1024]{2,1,0:T(8,128)} %bitcast.59), channel_id=1, source_target_pairs={{0,8},{1,9},{2,10},{3,11},{4,12},{5,13},{6,14},{7,15},{8,0},{9,1},... | collective-permute-start | bytes 196616 | tf_op jit(solution)/shard_map/ppermute | solution.py:100
  24.7 4.5 %collective-permute-done.2 = f32[1,16,1024]{2,1,0:T(8,128)S(1)} collective-permute-done((f32[1,16,1024]{2,1,0:T(8,128)}, f32[1,16,1024]{2,1,0:T(8,128)S(1)}, u32[]{:S(2)}, u32[]{:S(2)}) %collective-permute-start.2) | collective-permute-done | bytes 65568 | tf_op jit(solution)/shard_map/ppermute | solution.py:100
  29.2 0.8 %pad_maximum_fusion.3 = f32[2,16,1024]{2,1,0:T(8,128)S(1)} fusion(f32[1,16,1024]{2,1,0:T(8,128)S(1)} %collective-permute-done.2, f32[1,16,1024]{2,1,0:T(8,128)} %bitcast.60), kind=kLoop, calls=%fused_computation.11 | loop fusion | flops 32768 | bytes 262144 | tf_op jit(solution)/shard_map/concatenate | solution.py:101
  30.0 1.0 %collective-permute-start.3 = (f32[2,16,1024]{2,1,0:T(8,128)S(1)}, f32[2,16,1024]{2,1,0:T(8,128)S(1)}, u32[]{:S(2)}, u32[]{:S(2)}) collective-permute-start(f32[2,16,1024]{2,1,0:T(8,128)S(1)} %pad_maximum_fusion.3), channel_id=1, source_target_pairs={{0,4},{1,5},{2,6},{3,7},{4,0},{5,1},{6,2},{7,3},{8,12},{9,13},{10,... | collective-permute-start | bytes 393224 | tf_op jit(solution)/shard_map/ppermute | solution.py:100
  31.4 4.3 %collective-permute-done.3 = f32[2,16,1024]{2,1,0:T(8,128)S(1)} collective-permute-done((f32[2,16,1024]{2,1,0:T(8,128)S(1)}, f32[2,16,1024]{2,1,0:T(8,128)S(1)}, u32[]{:S(2)}, u32[]{:S(2)}) %collective-permute-start.3) | collective-permute-done | bytes 131104 | tf_op jit(solution)/shard_map/ppermute | solution.py:100
  35.6 0.9 %pad_maximum_fusion.1 = f32[4,16,1024]{2,1,0:T(8,128)S(1)} fusion(f32[2,16,1024]{2,1,0:T(8,128)S(1)} %collective-permute-done.3, f32[1,16,1024]{2,1,0:T(8,128)S(1)} %collective-permute-done.2, f32[1,16,1024]{2,1,0:T(8,128)} %bitcast.61), kind=kLoop, calls=%fused_computation.7 | loop fusion | flops 131072 | bytes 524288 | tf_op jit(solution)/shard_map/concatenate | solution.py:101
  36.6 0.1 reshape.262
  36.8 0.6 %gather_fusion.1 = f32[16,16,16]{2,1,0:T(8,128)S(1)} fusion(f32[16,16,16]{2,0,1:T(8,128)S(1)} %copy.66, s32[1024]{0:T(1024)S(1)} %get-tuple-element.40), kind=kCustom, calls=%fused_computation.1 | custom fusion | bytes 32832 | tf_op jit(solution)/shard_map/jit(_take)/gather | solution.py:147
  37.5 0.1 reshape.294
  37.6 0.1 copy.62
  37.7 6.4 %collective-permute-done.4 = f32[4,16,1024]{2,1,0:T(8,128)S(1)} collective-permute-done((f32[4,16,1024]{2,1,0:T(8,128)S(1)}, f32[4,16,1024]{2,1,0:T(8,128)S(1)}, u32[]{:S(2)}, u32[]{:S(2)}) %collective-permute-start.4) | collective-permute-done | bytes 262176 | tf_op jit(solution)/shard_map/ppermute | solution.py:100
  44.2 1.8 %collective-permute-done.5 = f32[8,16,1024]{2,1,0:T(8,128)S(1)} collective-permute-done((f32[8,16,1024]{2,1,0:T(8,128)S(1)}, f32[8,16,1024]{2,1,0:T(8,128)S(1)}, u32[]{:S(2)}, u32[]{:S(2)}) %collective-permute-start.5) | collective-permute-done | bytes 524320 | tf_op jit(solution)/shard_map/ppermute | solution.py:100
  46.1 1.0 %copy-done.2 = f32[16,16,1024]{2,1,0:T(8,128)} copy-done((f32[16,16,1024]{2,1,0:T(8,128)}, f32[16,16,1024]{2,1,0:T(8,128)S(1)}, u32[]{:S(2)}) %copy-start.2) | copy-done | bytes 1048600
  47.1 1.6 %copy.68 = f32[1024,256]{1,0:T(8,128)S(1)} copy(f32[1024,256]{0,1:T(8,128)} %bitcast.63) | data formatting | bytes 2097152 | tf_op jit(solution)/shard_map/dot_general | solution.py:148
  48.6 1.0 %fusion.26 = f32[16,8,128]{2,0,1:T(8,128)S(1)} fusion(f32[16,256,1]{1,0,2:T(8,128)S(1)} %reshape.294, f32[8,128,256]{2,1,0:T(8,128)S(1)} %bitcast.58), kind=kOutput, calls=%fused_computation.71 | convolution fusion | flops 50331648 | bytes 1130496 | tf_op jit(solution)/shard_map/dot_general | solution.py:148
  49.6 0.6 %gather_fusion.2 = f32[32,16,128]{2,1,0:T(8,128)S(1)} fusion(f32[16,8,128]{2,0,1:T(8,128)S(1)} %fusion.26, s32[1024]{0:T(1024)S(1)} %get-tuple-element.39), kind=kCustom, calls=%fused_computation.2 | custom fusion | bytes 524416 | tf_op jit(solution)/shard_map/jit(_take)/gather | solution.py:152
  50.2 1.9 %fusion.2 = f32[8,2,8,128]{3,2,1,0:T(8,128)S(1)} fusion(f32[8,128,4,128]{3,2,1,0:T(4,128)S(1)} %bitcast.57, f32[8,4,16,128]{3,2,1,0:T(8,128)S(1)} %bitcast.64, pred[8,4]{1,0:T(8,128)(4,1)S(1)} %copy.62), kind=kOutput, calls=%fused_computation.5 | convolution fusion | flops 100728832 | bytes 2424864 | tf_op jit(solution)/shard_map/xrkc,rikc->xri/dot_general | solution.py:153
  52.1 0.6 %copy.115 = f32[8,2,8,128]{3,2,0,1:T(8,128)} copy(f32[8,2,8,128]{3,2,1,0:T(8,128)S(1)} %fusion.2) | data formatting | bytes 131072 | tf_op jit(solution)/shard_map/reshape | solution.py:159
  (41 shorter events, 1.0 us)
Async XLA Ops:
  0.6 49.6 %copy-start = (f32[1024,4,128]{2,1,0:T(4,128)S(1)}, f32[1024,4,128]{2,1,0:T(4,128)}, u32[]{:S(2)}) copy-start(f32[1024,4,128]{2,1,0:T(4,128)} %param.25) | copy-start | bytes 6291460
  3.7 12.0 %collective-permute-start.1 = (f32[2,16,1024]{2,0,1:T(2,128)S(1)}, f32[2,16,1024]{2,0,1:T(2,128)S(1)}, u32[]{:S(2)}, u32[]{:S(2)}) collective-permute-start(f32[2,16,1024]{2,0,1:T(2,128)S(1)} %pad_maximum_fusion.2), channel_id=1, source_target_pairs={{1,0},{2,1},{3,2},{4,3},{5,4},{6,5},{7,6},{8,7},{9,8},{10,9},{11,1... | collective-permute-start | bytes 393224 | tf_op jit(solution)/shard_map/ppermute | solution.py:17
  5.1 10.8 %collective-permute-start = (f32[16,1024]{1,0:T(8,128)S(1)}, f32[16,1024]{1,0:T(8,128)S(1)}, u32[]{:S(2)}, u32[]{:S(2)}) collective-permute-start(f32[16,1024]{1,0:T(8,128)S(1)} %bitcast.65), channel_id=1, source_target_pairs={{0,1},{1,2},{2,3},{3,4},{4,5},{5,6},{6,7},{7,8},{8,9},{9,10},{10,1... | collective-permute-start | bytes 196616 | tf_op jit(solution)/shard_map/ppermute | solution.py:17
  10.7 5.0 %copy-start.4 = (s32[8,4]{0,1:T(4,128)S(1)}, s32[8,4]{0,1:T(4,128)}, u32[]{:S(2)}) copy-start(s32[8,4]{0,1:T(4,128)} %param.26) | copy-start | bytes 388
  10.7 5.2 %copy-start.5 = (f32[16]{0:T(128)S(1)}, f32[16]{0:T(128)}, u32[]{:S(2)}) copy-start(f32[16]{0:T(128)} %w_ref.1) | copy-start | bytes 196
  10.7 20.4 %copy-start.6 = (s32[16]{0:T(128)S(1)}, s32[16]{0:T(128)}, u32[]{:S(2)}) copy-start(s32[16]{0:T(128)} %constant.136.clone) | copy-start | bytes 196
  10.7 20.4 %copy-start.3 = (bf16[16,4,128]{2,1,0:T(4,128)(2,1)S(1)}, bf16[16,4,128]{2,1,0:T(4,128)(2,1)}, u32[]{:S(2)}) copy-start(bf16[16,4,128]{2,1,0:T(4,128)(2,1)} %param.23) | copy-start | bytes 49156
  20.3 23.7 %copy-start.1 = (f32[16,1024]{1,0:T(8,128)S(1)}, f32[16,1024]{1,0:T(8,128)}, u32[]{:S(2)}) copy-start(f32[16,1024]{1,0:T(8,128)} %scatter-add.9) | copy-start | bytes 196612
  20.3 8.9 %collective-permute-start.2 = (f32[1,16,1024]{2,1,0:T(8,128)}, f32[1,16,1024]{2,1,0:T(8,128)S(1)}, u32[]{:S(2)}, u32[]{:S(2)}) collective-permute-start(f32[1,16,1024]{2,1,0:T(8,128)} %bitcast.59), channel_id=1, source_target_pairs={{0,8},{1,9},{2,10},{3,11},{4,12},{5,13},{6,14},{7,15},{8,0},{9,1},... | collective-permute-start | bytes 196616 | tf_op jit(solution)/shard_map/ppermute | solution.py:100
  30.0 5.6 %collective-permute-start.3 = (f32[2,16,1024]{2,1,0:T(8,128)S(1)}, f32[2,16,1024]{2,1,0:T(8,128)S(1)}, u32[]{:S(2)}, u32[]{:S(2)}) collective-permute-start(f32[2,16,1024]{2,1,0:T(8,128)S(1)} %pad_maximum_fusion.3), channel_id=1, source_target_pairs={{0,4},{1,5},{2,6},{3,7},{4,0},{5,1},{6,2},{7,3},{8,12},{9,13},{10,... | collective-permute-start | bytes 393224 | tf_op jit(solution)/shard_map/ppermute | solution.py:100
  36.5 7.6 %collective-permute-start.4 = (f32[4,16,1024]{2,1,0:T(8,128)S(1)}, f32[4,16,1024]{2,1,0:T(8,128)S(1)}, u32[]{:S(2)}, u32[]{:S(2)}) collective-permute-start(f32[4,16,1024]{2,1,0:T(8,128)S(1)} %pad_maximum_fusion.1), channel_id=1, source_target_pairs={{0,2},{1,3},{2,0},{3,1},{4,6},{5,7},{6,4},{7,5},{8,10},{9,11},{10,... | collective-permute-start | bytes 786440 | tf_op jit(solution)/shard_map/ppermute | solution.py:100
  44.1 2.0 %collective-permute-start.5 = (f32[8,16,1024]{2,1,0:T(8,128)S(1)}, f32[8,16,1024]{2,1,0:T(8,128)S(1)}, u32[]{:S(2)}, u32[]{:S(2)}) collective-permute-start(f32[8,16,1024]{2,1,0:T(8,128)S(1)} %pad_maximum_fusion), channel_id=1, source_target_pairs={{0,1},{1,0},{2,3},{3,2},{4,5},{5,4},{6,7},{7,6},{8,9},{9,8},{10,11... | collective-permute-start | bytes 1572872 | tf_op jit(solution)/shard_map/ppermute | solution.py:100
  46.1 1.0 %copy-start.2 = (f32[16,16,1024]{2,1,0:T(8,128)}, f32[16,16,1024]{2,1,0:T(8,128)S(1)}, u32[]{:S(2)}) copy-start(f32[16,16,1024]{2,1,0:T(8,128)S(1)} %constant_dynamic-update-slice_fusion) | copy-start | bytes 3145732

commit v2 on v1

--- a/solution.py
+++ b/solution.py
@@ -87,20 +87,92 @@
     )(layer_weight, s, s, f, vx, vy, vz, d)
 
 
-def bit_reversed(count):
-    bits = count.bit_length() - 1
-    return [int(format(p, f"0{bits}b")[::-1], 2) if bits else 0 for p in range(count)]
+def gather_rounds(count):
+    bits = []
+    bit = count // 2
+    while bit >= 1:
+        bits.append(bit)
+        bit //= 2
+    if len(bits) < 2:
+        return [bits] if bits else []
+    return [[bits[1], bits[0], bits[0] | bits[1]]] + [[b] for b in bits[2:]]
 
 
 def gather_rows(local, axis):
     count = lax.axis_size(axis)
     buf = local[None]
-    bit = count // 2
-    while bit >= 1:
-        other = lax.ppermute(buf, axis, [(i, i ^ bit) for i in range(count)])
-        buf = jnp.concatenate([buf, other], axis=0)
-        bit //= 2
-    return buf
+    entries = [0]
+    for masks in gather_rounds(count):
+        others = [lax.ppermute(buf, axis, [(i, i ^ m) for i in range(count)]) for m in masks]
+        buf = jnp.concatenate([buf] + others, axis=0)
+        entries = entries + [m ^ q for m in masks for q in entries]
+    return buf, entries
+
+
+def edges_kernel(s_lo_ref, s_hi_ref, f_ref, vx_ref, d_ref, first_ref, last_ref, lo_ref, up_ref):
+    first_ref[...] = s_lo_ref[:, 0, :]
+    last_ref[...] = s_hi_ref[:, s_hi_ref.shape[1] - 1, :]
+    lo, up = coefs(f_ref[:, 0, :], 1, vx_ref[:, 0, :], d_ref[:, 0, :])
+    lo_ref[...] = lo
+    up_ref[...] = up
+
+
+def edges(s, f, vx, d):
+    depth, rows, cols = s.shape
+    part = 8 if rows % 8 == 0 else rows
+    lo_block = pl.BlockSpec((depth, part, cols), lambda i: (0, 0, 0))
+    hi_block = pl.BlockSpec((depth, part, cols), lambda i: (0, rows // part - 1, 0))
+    plane = jax.ShapeDtypeStruct((depth, cols), jnp.float32)
+    whole = pl.BlockSpec((depth, cols), lambda i: (0, 0))
+    return pl.pallas_call(
+        edges_kernel,
+        grid=(1,),
+        in_specs=[lo_block, hi_block, lo_block, lo_block, lo_block],
+        out_specs=[whole] * 4,
+        out_shape=[plane] * 4,
+    )(s, s, f, vx, d)
+
+
+def prior_kernel(cb_ref, slab_ref, buf_ref, cy_ref, out_ref, mixed_ref):
+    rb = pl.program_id(0)
+    kb = cy_ref.shape[1] // BLK
+
+    @pl.when(rb == 0)
+    def _():
+        mixed_ref[...] = jnp.dot(slab_ref[...], buf_ref[...], precision=precise, preferred_element_type=jnp.float32)
+
+    acc = jnp.zeros(out_ref.shape, jnp.float32)
+    for k in range(kb):
+        start = pl.multiple_of(cb_ref[rb * kb + k] * BLK, BLK)
+        picked = mixed_ref[:, pl.ds(start, BLK)]
+        weights = cy_ref[:, k * BLK:(k + 1) * BLK]
+        acc = acc + lax.dot_general(
+            picked, weights, (((1,), (1,)), ((), ())), precision=precise, preferred_element_type=jnp.float32
+        )
+    out_ref[...] = acc
+
+
+def apply_prior(col_block, slab, buf, cy2):
+    rows, inner = slab.shape
+    cols = cy2.shape[0]
+    nyb = cols // BLK
+    grid_spec = pltpu.PrefetchScalarGridSpec(
+        num_scalar_prefetch=1,
+        grid=(nyb,),
+        in_specs=[
+            pl.BlockSpec((rows, inner), lambda r, cb: (0, 0)),
+            pl.BlockSpec((inner, cols), lambda r, cb: (0, 0)),
+            pl.BlockSpec((BLK, cy2.shape[1]), lambda r, cb: (r, 0)),
+        ],
+        out_specs=pl.BlockSpec((rows, BLK), lambda r, cb: (0, r)),
+        scratch_shapes=[pltpu.VMEM((rows, cols), jnp.float32)],
+    )
+    return pl.pallas_call(
+        prior_kernel,
+        grid_spec=grid_spec,
+        out_shape=jax.ShapeDtypeStruct((rows, cols), jnp.float32),
+        compiler_params=pltpu.CompilerParams(dimension_semantics=("arbitrary",)),
+    )(col_block, slab, buf, cy2)
 
 
 def body(
@@ -120,9 +192,7 @@
     me = lax.axis_index("gx")
     depth, rows, cols = adjoint_state.shape
 
-    first_s = adjoint_state[:, 0, :]
-    lo_x0, up_x0 = coefs(face_flags[:, 0, :], 1, speed_x[:, 0, :], dispersion[:, 0, :])
-    last_s = adjoint_state[:, rows - 1, :]
+    first_s, last_s, lo_x0, up_x0 = edges(adjoint_state, face_flags, speed_x, dispersion)
     from_next = passed_along(jnp.stack([first_s, lo_x0]), "gx", -1)
     from_prev = passed_along(last_s, "gx", 1)
 
@@ -131,10 +201,11 @@
     corr_first = jnp.sum(layer_weight[:, None] * (-up_x0 * from_prev), axis=0)
     ax_next = -from_next[1] * (from_next[0] - last_s)
     corr_last = jnp.sum(layer_weight[:, None] * ax_next, axis=0)
-    recharge = partial.at[0].add(corr_first).at[rows - 1].add(corr_last)
-
-    gathered = gather_rows(recharge, "gx")
-    order = me ^ jnp.array(bit_reversed(count), jnp.int32)
+    row = lax.broadcasted_iota(jnp.int32, (rows, cols), 0)
+    recharge = partial + jnp.where(row == 0, corr_first[None, :], 0.0) + jnp.where(row == rows - 1, corr_last[None, :], 0.0)
+
+    gathered, entries = gather_rows(recharge, "gx")
+    order = me ^ jnp.array(entries, jnp.int32)
 
     nxb = offsets_x.shape[0]
     global_rows = me * rows + jnp.arange(rows)
@@ -145,18 +216,11 @@
     slab = jnp.sum(jnp.where(hit, cov_x.astype(jnp.float32)[:, :, None, :], 0.0), axis=1)
     slab = slab.reshape(rows, count, rows)
     slab = jnp.take(slab, order, axis=1).reshape(rows, count * rows)
-    mixed = jnp.dot(slab, gathered.reshape(count * rows, cols), precision=precise, preferred_element_type=jnp.float32)
 
     nyb = offsets_y.shape[0]
-    col_block = (jnp.arange(nyb)[:, None] + offsets_y) % nyb
-    picked = jnp.take(mixed.reshape(rows, nyb, BLK), col_block, axis=1)
-    prior = jnp.einsum(
-        "xrkc,rikc->xri",
-        picked,
-        cov_y.reshape(nyb, BLK, cov_y.shape[1], BLK),
-        precision=precise,
-        preferred_element_type=jnp.float32,
-    ).reshape(rows, cols)
+    col_block = ((jnp.arange(nyb)[:, None] + offsets_y) % nyb).reshape(-1).astype(jnp.int32)
+    cy2 = cov_y.reshape(cov_y.shape[0], cov_y.shape[1] * cov_y.shape[2])
+    prior = apply_prior(col_block, slab, gathered.reshape(count * rows, cols), cy2)
     return (recharge, prior)
 
 

time: 53.5 us -> 52.1 us (0.974)
  Pallas kernels: 5 us -> 16.2 us
  waiting for transfers between devices: 17 us -> 10.8 us
  other arithmetic: 6.46 us -> 3.5 us
  matrix products: 2.85 us -> 0 us
  local copies, waits for them, and re-layouts: 10.7 us -> 8.62 us
  starting transfers between devices: 9.85 us -> 11.5 us
    pallas_call x0 -> x2, Pallas kernels: none -> 11.2 us  [the longest x1 8.79 us: apply_prior(): pl.pallas_call(prior_kernel, grid_spec=grid_spec, out_shape=jax.ShapeDtyp...]
    ppermute x4 -> x5, waiting for transfers between devices: 17 us -> 10.8 us  [gather_rows(): lax.ppermute(buf, axis, [(i, i ^ m) for i in range(count)])]
    unnamed x19 -> x25, local copies, waits for them, and re-layouts: 1.05 us -> 4.43 us
    dot_general x2 -> x0, matrix products: 2.85 us -> none  [the longest x1 1.89 us: body(): jnp.einsum('xrkc,rikc->xri', picked, cov_y.reshape(nyb, BLK, cov_y.shape[...]
    scatter-add x2 -> x0, local copies, waits for them, and re-layouts: 2.78 us -> none  [body(): recharge = partial.at[0].add(corr_first).at[rows - 1].add(corr_last)]
    concatenate x1 -> x2, local copies, waits for them, and re-layouts: 0.04 us -> 1.82 us  [gather_rows(): buf = jnp.concatenate([buf] + others, axis=0)]
    concatenate x3 -> x1, other arithmetic: 1.75 us -> 0.02 us  [gather_rows(): buf = jnp.concatenate([buf] + others, axis=0)]
    unnamed x0 -> x1, other arithmetic: none -> 1.66 us
  transfers between devices with their start and end apart: 6 -> 7, of which waited for: 4 -> 4; matrix products, arithmetic and copies ran while one was open for 8% -> 13% of each run, Pallas kernels for 9% -> 10%
where the time goes in v2:
time: 52.1 us; the launch traced here: 51.5 us
  Pallas kernels  16.2 us (31%)
  starting transfers between devices  11.5 us (22%)
  waiting for transfers between devices  10.8 us (21%)
  local copies, waits for them, and re-layouts  8.62 us (17%)
  other arithmetic  3.5 us (7%)
  between operations  0.89 us (2%)
    ppermute x5, waiting for transfers between devices, gather_rows(): lax.ppermute(buf, axis, [(i, i ^ m) for i in range(count)])  10.8 us
    pallas_call x1, Pallas kernels, apply_prior(): pl.pallas_call(prior_kernel, grid_spec=grid_spec, out_shape=jax.ShapeDtyp...  8.79 us
    ppermute x5, starting transfers between devices, gather_rows(): lax.ppermute(buf, axis, [(i, i ^ m) for i in range(count)])  7.15 us
    pallas_call x1, Pallas kernels, stencil(): pl.pallas_call(stencil_kernel, grid=(depth // zc,), in_specs=[pl.BlockSpe...  5 us
    unnamed x25, local copies, waits for them, and re-layouts  4.43 us
    ppermute x2, starting transfers between devices, passed_along(): lax.ppermute(value, axis, [(source, source + steps) for source in range(f...  4.33 us
    pallas_call x1, Pallas kernels, edges(): pl.pallas_call(edges_kernel, grid=(1,), in_specs=[lo_block, hi_block, lo_...  2.42 us
    concatenate x2, local copies, waits for them, and re-layouts, gather_rows(): buf = jnp.concatenate([buf] + others, axis=0)  1.82 us
  transfers between devices with their start and end apart: 7, of which 4 were waited for; matrix products, arithmetic and copies ran while one was open for 13% of the time, Pallas kernels for 10%

profile of v2, /device:TPU:0, one launch (start us, length us, event | category | flops | bytes accessed | tf_op | source)
XLA Modules:
  0.0 51.5 jit_solution(1377351225579843724)
XLA Ops:
  0.7 2.4 %shard_map.132 = (f32[16,1024]{1,0:T(8,128)}, f32[16,1024]{1,0:T(8,128)}, f32[16,1024]{1,0:T(8,128)}, f32[16,1024]{1,0:T(8,128)}) custom-call(f32[16,16,1024]{2,1,0:T(8,128)} %s_hi_ref.1, f32[16,16,1024]{2,1,0:T(8,128)} %s_hi_ref.1, s32[16,16,1024]{2,1,0:T(8,128)} %f_ref.3, f32[16,16,1024]{2,1,0:T(8,128)} %vx_ref.3, f32[16,16,1024]{2,1,0:T(8,128)} %d_ref.3), custom_call_target="tpu_custom_call" | custom-call | tf_op jit(solution)/shard_map/pallas_call | solution.py:127
  3.1 0.9 %pad_maximum_fusion.1 = f32[2,16,1024]{2,1,0:T(8,128)S(1)} fusion(f32[1,16,1024]{2,1,0:T(8,128)} %bitcast.36, f32[1,16,1024]{2,1,0:T(8,128)} %bitcast.35), kind=kLoop, calls=%fused_computation.4 | loop fusion | flops 32768 | bytes 262144 | tf_op jit(solution)/shard_map/stack | solution.py:196
  4.0 1.3 %collective-permute-start.1 = (f32[2,16,1024]{2,1,0:T(8,128)S(1)}, f32[2,16,1024]{2,1,0:T(8,128)S(1)}, u32[]{:S(2)}, u32[]{:S(2)}) collective-permute-start(f32[2,16,1024]{2,1,0:T(8,128)S(1)} %pad_maximum_fusion.1), channel_id=1, source_target_pairs={{1,0},{2,1},{3,2},{4,3},{5,4},{6,5},{7,6},{8,7},{9,8},{10,9},{11,1... | collective-permute-start | bytes 393224 | tf_op jit(solution)/shard_map/ppermute | solution.py:17
  5.3 3.0 %collective-permute-start = (f32[16,1024]{1,0:T(8,128)}, f32[16,1024]{1,0:T(8,128)S(1)}, u32[]{:S(2)}, u32[]{:S(2)}) collective-permute-start(f32[16,1024]{1,0:T(8,128)} %get-tuple-element.7), channel_id=1, source_target_pairs={{0,1},{1,2},{2,3},{3,4},{4,5},{5,6},{6,7},{7,8},{8,9},{9,10},{10,1... | collective-permute-start | bytes 196616 | tf_op jit(solution)/shard_map/ppermute | solution.py:17
  8.4 0.6 %gather_fusion = s32[16,4]{1,0:T(8,128)S(1)} fusion(s32[2,4]{1,0:T(2,128)S(1)} %copy-done, s32[1024]{0:T(1024)S(1)} %get-tuple-element.27), kind=kCustom, calls=%fused_computation | custom fusion | bytes 576 | tf_op jit(solution)/shard_map/gather | solution.py:213
  9.0 0.1 add_select_fusion
  9.0 0.1 copy.21
  9.2 5.0 %shard_map.131 = f32[16,1024]{1,0:T(8,128)} custom-call(f32[16]{0:T(128)} %w_ref.1, f32[16,16,1024]{2,1,0:T(8,128)} %s_hi_ref.1, f32[16,16,1024]{2,1,0:T(8,128)} %s_hi_ref.1, s32[16,16,1024]{2,1,0:T(8,128)} %f_ref.3, f32[16,16,1024]{2,1,0:T(8,128)} %vx_ref.3, f32[16,16,1024]{2,1,0:T(8,128)} %vy_ref.1, f32[16,16,1024]{2,1,0:T(8,128)} %vz_ref.1, ...), custom_call_target="tpu_custom_call" | custom-call | tf_op jit(solution)/shard_map/pallas_call | solution.py:71
  14.3 0.1 multiply_reduce_fusion
  14.4 1.7 %constant_dynamic-update-slice_fusion.4 = (f32[8,16,1024]{2,1,0:T(8,128)}, f32[16,1024]{1,0:T(8,128)S(1)}) fusion(f32[1024]{0:T(1024)S(1)} %get-tuple-element.11, pred[16]{0:T(512)(128)(4,1)S(1)} %get-tuple-element.24, f32[16,1024]{1,0:T(8,128)} %shard_map.131, f32[1024]{0:T(1024)S(1)} %get-tuple-element.10, pred[16]{0:T(512)(128)(4,1)S(1)} %get-tuple-element.25), kind=kLoop, calls=%fused_computation.19 | loop fusion | flops 65535 | bytes 204832
  16.0 3.3 %collective-permute-start.2 = (f32[1,16,1024]{2,1,0:T(8,128)S(1)}, f32[1,16,1024]{2,1,0:T(8,128)S(1)}, u32[]{:S(2)}, u32[]{:S(2)}) collective-permute-start(f32[1,16,1024]{2,1,0:T(8,128)S(1)} %bitcast.30), channel_id=1, source_target_pairs={{0,4},{1,5},{2,6},{3,7},{4,0},{5,1},{6,2},{7,3},{8,12},{9,13},{10,... | collective-permute-start | bytes 196616 | tf_op jit(solution)/shard_map/ppermute | solution.py:106
  19.4 2.6 %collective-permute-start.3 = (f32[1,16,1024]{2,1,0:T(8,128)S(1)}, f32[1,16,1024]{2,1,0:T(8,128)S(1)}, u32[]{:S(2)}, u32[]{:S(2)}) collective-permute-start(f32[1,16,1024]{2,1,0:T(8,128)S(1)} %bitcast.31), channel_id=1, source_target_pairs={{0,8},{1,9},{2,10},{3,11},{4,12},{5,13},{6,14},{7,15},{8,0},{9,1},... | collective-permute-start | bytes 196616 | tf_op jit(solution)/shard_map/ppermute | solution.py:106
  22.0 4.4 %collective-permute-done.3 = f32[1,16,1024]{2,1,0:T(8,128)S(1)} collective-permute-done((f32[1,16,1024]{2,1,0:T(8,128)S(1)}, f32[1,16,1024]{2,1,0:T(8,128)S(1)}, u32[]{:S(2)}, u32[]{:S(2)}) %collective-permute-start.3) | collective-permute-done | bytes 65568 | tf_op jit(solution)/shard_map/ppermute | solution.py:106
  26.4 1.7 %collective-permute-done.4 = f32[1,16,1024]{2,1,0:T(8,128)S(1)} collective-permute-done((f32[1,16,1024]{2,1,0:T(8,128)S(1)}, f32[1,16,1024]{2,1,0:T(8,128)S(1)}, u32[]{:S(2)}, u32[]{:S(2)}) %collective-permute-start.4) | collective-permute-done | bytes 65568 | tf_op jit(solution)/shard_map/ppermute | solution.py:106
  28.1 1.2 %collective-permute-start.5 = (f32[4,16,1024]{2,1,0:T(8,128)S(1)}, f32[4,16,1024]{2,1,0:T(8,128)S(1)}, u32[]{:S(2)}, u32[]{:S(2)}) collective-permute-start(f32[4,16,1024]{2,1,0:T(8,128)S(1)} %pad_maximum_fusion), channel_id=1, source_target_pairs={{0,2},{1,3},{2,0},{3,1},{4,6},{5,7},{6,4},{7,5},{8,10},{9,11},{10,... | collective-permute-start | bytes 786440 | tf_op jit(solution)/shard_map/ppermute | solution.py:106
  29.3 0.6 %constant_dynamic-update-slice_fusion.3 = (f32[8,16,1024]{2,1,0:T(8,128)}, f32[16,16,1024]{2,1,0:T(8,128)S(1)}) fusion(f32[8,16,1024]{2,1,0:T(8,128)} %get-tuple-element.12, f32[1,16,1024]{2,1,0:T(8,128)S(1)} %collective-permute-done.2, f32[16,16,1024]{2,1,0:T(8,128)S(1)} %constant_dynamic-update-slice_fusion.10), kind=kLoop, calls=%fused_computation.18 | loop fusion | bytes 196608
  29.9 0.6 %constant_dynamic-update-slice_fusion.2 = (f32[8,16,1024]{2,1,0:T(8,128)}, f32[16,16,1024]{2,1,0:T(8,128)S(1)}) fusion(f32[8,16,1024]{2,1,0:T(8,128)} %get-tuple-element.22, f32[1,16,1024]{2,1,0:T(8,128)S(1)} %collective-permute-done.3, f32[16,16,1024]{2,1,0:T(8,128)S(1)} %get-tuple-element.23), kind=kLoop, calls=%fused_computation.17 | loop fusion | bytes 196608
  30.6 0.6 %constant_dynamic-update-slice_fusion.1 = (f32[8,16,1024]{2,1,0:T(8,128)}, f32[16,16,1024]{2,1,0:T(8,128)S(1)}) fusion(f32[8,16,1024]{2,1,0:T(8,128)} %get-tuple-element.20, f32[1,16,1024]{2,1,0:T(8,128)S(1)} %collective-permute-done.4, f32[16,16,1024]{2,1,0:T(8,128)S(1)} %get-tuple-element.21), kind=kLoop, calls=%fused_computation.16 | loop fusion | bytes 196608
  31.2 4.7 %collective-permute-done.5 = f32[4,16,1024]{2,1,0:T(8,128)S(1)} collective-permute-done((f32[4,16,1024]{2,1,0:T(8,128)S(1)}, f32[4,16,1024]{2,1,0:T(8,128)S(1)}, u32[]{:S(2)}, u32[]{:S(2)}) %collective-permute-start.5) | collective-permute-done | bytes 262176 | tf_op jit(solution)/shard_map/ppermute | solution.py:106
  35.9 0.7 %constant_dynamic-update-slice_fusion = (f32[8,16,1024]{2,1,0:T(8,128)}, f32[16,16,1024]{2,1,0:T(8,128)S(1)}) fusion(f32[8,16,1024]{2,1,0:T(8,128)} %get-tuple-element.18, f32[4,16,1024]{2,1,0:T(8,128)S(1)} %collective-permute-done.5, f32[16,16,1024]{2,1,0:T(8,128)S(1)} %get-tuple-element.19), kind=kLoop, calls=%fused_computation.15 | loop fusion | bytes 786432 | tf_op jit(solution)/shard_map/concatenate | solution.py:107
  36.6 0.1 select_reduce_fusion
  36.8 0.1 reshape.128
  36.9 0.6 %gather_fusion.1 = f32[16,16,16]{2,1,0:T(8,128)S(1)} fusion(f32[16,16,16]{2,0,1:T(8,128)S(1)} %copy.24, s32[1024]{0:T(1024)S(1)} %get-tuple-element.26), kind=kCustom, calls=%fused_computation.1 | custom fusion | bytes 32832 | tf_op jit(solution)/shard_map/jit(_take)/gather | solution.py:218
  37.5 0.1 gather.11
  37.7 0.1 broadcast_in_dim.71
  37.8 1.5 %copy.28 = f32[128,8,4,128]{3,1,2,0:T(8,128)} copy(f32[128,8,4,128]{3,2,1,0:T(4,128)S(1)} %bitcast.28) | data formatting | bytes 4194304
  39.4 0.1 copy.20
  39.4 0.6 %reshape.127.cb_ref = s32[32]{0:T(128)} reshape(s32[8,4]{1,0:T(8,128)S(1)} %copy.20) | data formatting | bytes 256 | tf_op jit(solution)/shard_map/reshape | solution.py:221
  40.0 0.6 %broadcast_select_fusion.slab_ref = f32[16,256]{1,0:T(8,128)} fusion(f32[16,256]{1,0:T(8,128)S(1)} %gather.11, pred[256]{0:T(512)(128)(4,1)S(1)} %broadcast_in_dim.71), kind=kLoop, calls=%fused_computation.30 | loop fusion | flops 4096 | bytes 33024 | tf_op jit(solution)/shard_map/jit(_take)/select_n | solution.py:218
  40.7 1.1 %constant_dynamic-update-slice_fusion.5 = f32[16,16,1024]{2,1,0:T(8,128)S(1)} fusion(f32[16,16,1024]{2,1,0:T(8,128)S(1)} %get-tuple-element.17, f32[8,16,1024]{2,1,0:T(8,128)} %collective-permute-done.6), kind=kLoop, calls=%fused_computation.20 | loop fusion | bytes 1048576 | tf_op jit(solution)/shard_map/concatenate | solution.py:107
  41.7 1.0 %copy-done.2 = f32[16,16,1024]{2,1,0:T(8,128)} copy-done((f32[16,16,1024]{2,1,0:T(8,128)}, f32[16,16,1024]{2,1,0:T(8,128)S(1)}, u32[]{:S(2)}) %copy-start.2) | copy-done | bytes 1048600
  42.7 8.8 %shard_map.133 = f32[16,1024]{1,0:T(8,128)} custom-call(s32[32]{0:T(128)} %reshape.127.cb_ref, f32[16,256]{1,0:T(8,128)} %broadcast_select_fusion.slab_ref, f32[256,1024]{1,0:T(8,128)} %bitcast.29, f32[1024,512]{1,0:T(8,128)} %bitcast.27), custom_call_target="tpu_custom_call" | custom-call | tf_op jit(solution)/shard_map/pallas_call | solution.py:170
  (39 shorter events, 0.4 us)
Async XLA Ops:
  0.6 7.8 %copy-start = (s32[2,4]{1,0:T(2,128)S(1)}, s32[2,4]{1,0:T(2,128)}, u32[]{:S(2)}) copy-start(s32[2,4]{1,0:T(2,128)} %param.20) | copy-start | bytes 100
  0.6 7.7 %copy-start.9 = (s32[16]{0:T(128)S(1)}, s32[16]{0:T(128)}, u32[]{:S(2)}) copy-start(s32[16]{0:T(128)} %constant.70.clone) | copy-start | bytes 196
  0.7 8.5 %copy-start.6 = (bf16[16,4,128]{2,1,0:T(4,128)(2,1)S(1)}, bf16[16,4,128]{2,1,0:T(4,128)(2,1)}, u32[]{:S(2)}) copy-start(bf16[16,4,128]{2,1,0:T(4,128)(2,1)} %param.19) | copy-start | bytes 49156
  4.0 10.2 %collective-permute-start.1 = (f32[2,16,1024]{2,1,0:T(8,128)S(1)}, f32[2,16,1024]{2,1,0:T(8,128)S(1)}, u32[]{:S(2)}, u32[]{:S(2)}) collective-permute-start(f32[2,16,1024]{2,1,0:T(8,128)S(1)} %pad_maximum_fusion.1), channel_id=1, source_target_pairs={{1,0},{2,1},{3,2},{4,3},{5,4},{6,5},{7,6},{8,7},{9,8},{10,9},{11,1... | collective-permute-start | bytes 393224 | tf_op jit(solution)/shard_map/ppermute | solution.py:17
  5.3 8.9 %collective-permute-start = (f32[16,1024]{1,0:T(8,128)}, f32[16,1024]{1,0:T(8,128)S(1)}, u32[]{:S(2)}, u32[]{:S(2)}) collective-permute-start(f32[16,1024]{1,0:T(8,128)} %get-tuple-element.7), channel_id=1, source_target_pairs={{0,1},{1,2},{2,3},{3,4},{4,5},{5,6},{6,7},{7,8},{8,9},{9,10},{10,1... | collective-permute-start | bytes 196616 | tf_op jit(solution)/shard_map/ppermute | solution.py:17
  9.2 5.1 %copy-start.4 = (f32[16,1024]{1,0:T(8,128)S(1)}, f32[16,1024]{1,0:T(8,128)}, u32[]{:S(2)}) copy-start(f32[16,1024]{1,0:T(8,128)} %get-tuple-element.7) | copy-start | bytes 196612
  9.2 5.1 %copy-start.5 = (f32[16,1024]{1,0:T(8,128)S(1)}, f32[16,1024]{1,0:T(8,128)}, u32[]{:S(2)}) copy-start(f32[16,1024]{1,0:T(8,128)} %get-tuple-element.6) | copy-start | bytes 196612
  9.2 5.1 %copy-start.8 = (f32[16]{0:T(128)S(1)}, f32[16]{0:T(128)}, u32[]{:S(2)}) copy-start(f32[16]{0:T(128)} %w_ref.1) | copy-start | bytes 196
  14.2 23.6 %copy-start.1 = (f32[1024,4,128]{2,1,0:T(4,128)S(1)}, f32[1024,4,128]{2,1,0:T(4,128)}, u32[]{:S(2)}) copy-start(f32[1024,4,128]{2,1,0:T(4,128)} %param.21) | copy-start | bytes 6291460
  16.0 23.3 %copy-start.3 = (f32[16,1024]{1,0:T(8,128)}, f32[16,1024]{1,0:T(8,128)S(1)}, u32[]{:S(2)}) copy-start(f32[16,1024]{1,0:T(8,128)S(1)} %get-tuple-element.13) | copy-start | bytes 196612
  16.0 6.0 %collective-permute-start.2 = (f32[1,16,1024]{2,1,0:T(8,128)S(1)}, f32[1,16,1024]{2,1,0:T(8,128)S(1)}, u32[]{:S(2)}, u32[]{:S(2)}) collective-permute-start(f32[1,16,1024]{2,1,0:T(8,128)S(1)} %bitcast.30), channel_id=1, source_target_pairs={{0,4},{1,5},{2,6},{3,7},{4,0},{5,1},{6,2},{7,3},{8,12},{9,13},{10,... | collective-permute-start | bytes 196616 | tf_op jit(solution)/shard_map/ppermute | solution.py:106
  19.4 7.1 %collective-permute-start.3 = (f32[1,16,1024]{2,1,0:T(8,128)S(1)}, f32[1,16,1024]{2,1,0:T(8,128)S(1)}, u32[]{:S(2)}, u32[]{:S(2)}) collective-permute-start(f32[1,16,1024]{2,1,0:T(8,128)S(1)} %bitcast.31), channel_id=1, source_target_pairs={{0,8},{1,9},{2,10},{3,11},{4,12},{5,13},{6,14},{7,15},{8,0},{9,1},... | collective-permute-start | bytes 196616 | tf_op jit(solution)/shard_map/ppermute | solution.py:106
  22.0 6.1 %collective-permute-start.4 = (f32[1,16,1024]{2,1,0:T(8,128)S(1)}, f32[1,16,1024]{2,1,0:T(8,128)S(1)}, u32[]{:S(2)}, u32[]{:S(2)}) collective-permute-start(f32[1,16,1024]{2,1,0:T(8,128)S(1)} %bitcast.32), channel_id=1, source_target_pairs={{0,12},{1,13},{2,14},{3,15},{4,8},{5,9},{6,10},{7,11},{8,4},{9,5},... | collective-permute-start | bytes 196616 | tf_op jit(solution)/shard_map/ppermute | solution.py:106
  28.1 7.8 %collective-permute-start.5 = (f32[4,16,1024]{2,1,0:T(8,128)S(1)}, f32[4,16,1024]{2,1,0:T(8,128)S(1)}, u32[]{:S(2)}, u32[]{:S(2)}) collective-permute-start(f32[4,16,1024]{2,1,0:T(8,128)S(1)} %pad_maximum_fusion), channel_id=1, source_target_pairs={{0,2},{1,3},{2,0},{3,1},{4,6},{5,7},{6,4},{7,5},{8,10},{9,11},{10,... | collective-permute-start | bytes 786440 | tf_op jit(solution)/shard_map/ppermute | solution.py:106
  36.6 4.0 %collective-permute-start.6 = (f32[8,16,1024]{2,1,0:T(8,128)}, f32[8,16,1024]{2,1,0:T(8,128)}, u32[]{:S(2)}, u32[]{:S(2)}) collective-permute-start(f32[8,16,1024]{2,1,0:T(8,128)} %get-tuple-element.16), channel_id=1, source_target_pairs={{0,1},{1,0},{2,3},{3,2},{4,5},{5,4},{6,7},{7,6},{8,9},{9,8},{10,11... | collective-permute-start | bytes 1572872 | tf_op jit(solution)/shard_map/ppermute | solution.py:106
  37.8 1.5 %copy-start.7 = (s32[8,4]{0,1:T(4,128)S(1)}, s32[8,4]{0,1:T(4,128)}, u32[]{:S(2)}) copy-start(s32[8,4]{0,1:T(4,128)} %param.22) | copy-start | bytes 388
  41.7 1.0 %copy-start.2 = (f32[16,16,1024]{2,1,0:T(8,128)}, f32[16,16,1024]{2,1,0:T(8,128)S(1)}, u32[]{:S(2)}) copy-start(f32[16,16,1024]{2,1,0:T(8,128)S(1)} %constant_dynamic-update-slice_fusion.5) | copy-start | bytes 3145732

commit v3 on v1

--- a/solution.py
+++ b/solution.py
@@ -87,20 +87,75 @@
     )(layer_weight, s, s, f, vx, vy, vz, d)
 
 
-def bit_reversed(count):
-    bits = count.bit_length() - 1
-    return [int(format(p, f"0{bits}b")[::-1], 2) if bits else 0 for p in range(count)]
-
-
-def gather_rows(local, axis):
+def gather_rounds(count):
+    bits = []
+    bit = count // 2
+    while bit >= 2:
+        bits.append(bit)
+        bit //= 2
+    if len(bits) < 2:
+        return [[b] for b in bits]
+    return [[bits[1], bits[0], bits[0] | bits[1]]] + [[b] for b in bits[2:]]
+
+
+def cx_slab(cov_rows, offsets, device, rows):
+    nxb = offsets.shape[0]
+    global_rows = device * rows + jnp.arange(rows)
+    row_block = global_rows // BLK
+    target = (row_block[:, None] + offsets[row_block]) % nxb
+    blocks = jnp.arange(nxb)
+    hit = target[:, :, None, None] == blocks[None, None, :, None]
+    slab = jnp.sum(jnp.where(hit, cov_rows.astype(jnp.float32)[:, :, None, :], 0.0), axis=1)
+    return slab.reshape(rows, -1)
+
+
+def mixed_rows(local, slab, axis):
     count = lax.axis_size(axis)
+    me = lax.axis_index(axis)
+    rows = local.shape[0]
+    per_device = slab.reshape(slab.shape[0], count, rows)
+
+    def product(piece, masks):
+        cols = jnp.take(per_device, me ^ jnp.array(masks, jnp.int32), axis=1).reshape(slab.shape[0], -1)
+        return jnp.dot(cols, piece.reshape(-1, piece.shape[-1]), precision=precise, preferred_element_type=jnp.float32)
+
     buf = local[None]
-    bit = count // 2
-    while bit >= 1:
-        other = lax.ppermute(buf, axis, [(i, i ^ bit) for i in range(count)])
-        buf = jnp.concatenate([buf, other], axis=0)
-        bit //= 2
-    return buf
+    entries = [0]
+    total = product(buf, entries)
+    for masks in gather_rounds(count):
+        others = [lax.ppermute(buf, axis, [(i, i ^ m) for i in range(count)]) for m in masks]
+        for m, other in zip(masks, others):
+            total = total + product(other, [m ^ q for q in entries])
+        buf = jnp.concatenate([buf] + others, axis=0)
+        entries = entries + [m ^ q for m in masks for q in entries]
+    own, for_partner = total[:rows], total[rows:]
+    if count == 1:
+        return own
+    return own + lax.ppermute(for_partner, axis, [(i, i ^ 1) for i in range(count)])
+
+
+def edges_kernel(s_lo_ref, s_hi_ref, f_ref, vx_ref, d_ref, first_ref, last_ref, lo_ref, up_ref):
+    first_ref[...] = s_lo_ref[:, 0, :]
+    last_ref[...] = s_hi_ref[:, s_hi_ref.shape[1] - 1, :]
+    lo, up = coefs(f_ref[:, 0, :], 1, vx_ref[:, 0, :], d_ref[:, 0, :])
+    lo_ref[...] = lo
+    up_ref[...] = up
+
+
+def edges(s, f, vx, d):
+    depth, rows, cols = s.shape
+    part = 8 if rows % 8 == 0 else rows
+    lo_block = pl.BlockSpec((depth, part, cols), lambda i: (0, 0, 0))
+    hi_block = pl.BlockSpec((depth, part, cols), lambda i: (0, rows // part - 1, 0))
+    plane = jax.ShapeDtypeStruct((depth, cols), jnp.float32)
+    whole = pl.BlockSpec((depth, cols), lambda i: (0, 0))
+    return pl.pallas_call(
+        edges_kernel,
+        grid=(1,),
+        in_specs=[lo_block, hi_block, lo_block, lo_block, lo_block],
+        out_specs=[whole] * 4,
+        out_shape=[plane] * 4,
+    )(s, s, f, vx, d)
 
 
 def body(
@@ -120,9 +175,7 @@
     me = lax.axis_index("gx")
     depth, rows, cols = adjoint_state.shape
 
-    first_s = adjoint_state[:, 0, :]
-    lo_x0, up_x0 = coefs(face_flags[:, 0, :], 1, speed_x[:, 0, :], dispersion[:, 0, :])
-    last_s = adjoint_state[:, rows - 1, :]
+    first_s, last_s, lo_x0, up_x0 = edges(adjoint_state, face_flags, speed_x, dispersion)
     from_next = passed_along(jnp.stack([first_s, lo_x0]), "gx", -1)
     from_prev = passed_along(last_s, "gx", 1)
 
@@ -131,21 +184,14 @@
     corr_first = jnp.sum(layer_weight[:, None] * (-up_x0 * from_prev), axis=0)
     ax_next = -from_next[1] * (from_next[0] - last_s)
     corr_last = jnp.sum(layer_weight[:, None] * ax_next, axis=0)
-    recharge = partial.at[0].add(corr_first).at[rows - 1].add(corr_last)
-
-    gathered = gather_rows(recharge, "gx")
-    order = me ^ jnp.array(bit_reversed(count), jnp.int32)
-
-    nxb = offsets_x.shape[0]
-    global_rows = me * rows + jnp.arange(rows)
-    row_block = global_rows // BLK
-    target = (row_block[:, None] + offsets_x[row_block]) % nxb
-    blocks = jnp.arange(nxb)
-    hit = target[:, :, None, None] == blocks[None, None, :, None]
-    slab = jnp.sum(jnp.where(hit, cov_x.astype(jnp.float32)[:, :, None, :], 0.0), axis=1)
-    slab = slab.reshape(rows, count, rows)
-    slab = jnp.take(slab, order, axis=1).reshape(rows, count * rows)
-    mixed = jnp.dot(slab, gathered.reshape(count * rows, cols), precision=precise, preferred_element_type=jnp.float32)
+    row = lax.broadcasted_iota(jnp.int32, (rows, cols), 0)
+    recharge = partial + jnp.where(row == 0, corr_first[None, :], 0.0) + jnp.where(row == rows - 1, corr_last[None, :], 0.0)
+
+    partner_cov = lax.ppermute(cov_x, "gx", [(i, i ^ 1) for i in range(count)]) if count > 1 else cov_x
+    slab = jnp.concatenate(
+        [cx_slab(cov_x, offsets_x, me, rows), cx_slab(partner_cov, offsets_x, me ^ 1, rows)], axis=0
+    )
+    mixed = mixed_rows(recharge, slab, "gx")
 
     nyb = offsets_y.shape[0]
     col_block = (jnp.arange(nyb)[:, None] + offsets_y) % nyb

time: 53.5 us -> 45.6 us (0.85)
  local copies, waits for them, and re-layouts: 10.7 us -> 3.59 us
  waiting for transfers between devices: 17 us -> 12.8 us
  starting transfers between devices: 9.85 us -> 13 us
  other arithmetic: 6.46 us -> 3.41 us
  Pallas kernels: 5 us -> 7.57 us
  matrix products: 2.85 us -> 3.84 us
    ppermute x4 -> x6, waiting for transfers between devices: 17 us -> 12.8 us  [the longest x4 11.6 us: mixed_rows(): lax.ppermute(buf, axis, [(i, i ^ m) for i in range(count)])]
    ppermute x4 -> x6, starting transfers between devices: 5.53 us -> 9.38 us  [the longest x4 6.02 us: mixed_rows(): lax.ppermute(buf, axis, [(i, i ^ m) for i in range(count)])]
    scatter-add x2 -> x0, local copies, waits for them, and re-layouts: 2.78 us -> none  [body(): recharge = partial.at[0].add(corr_first).at[rows - 1].add(corr_last)]
    pallas_call x0 -> x1, Pallas kernels: none -> 2.56 us  [edges(): pl.pallas_call(edges_kernel, grid=(1,), in_specs=[lo_block, hi_block, lo_...]
    concatenate x3 -> x2, other arithmetic: 1.75 us -> 0.12 us  [the longest x1 0.1 us: body(): jnp.concatenate([cx_slab(cov_x, offsets_x, me, rows), cx_slab(partner_cov...]
    dot_general x1 -> x0, local copies, waits for them, and re-layouts: 1.55 us -> none  [body(): jnp.dot(slab, gathered.reshape(count * rows, cols), precision=precise, pr...]
    slice x2 -> x1, local copies, waits for them, and re-layouts: 1.55 us -> 0.01 us  [mixed_rows(): own, for_partner = (total[:rows], total[rows:])]
    slice x1 -> x0, other arithmetic: 1.51 us -> none  [body(): dispersion[:, 0, :]]
  transfers between devices with their start and end apart: 6 -> 8, of which waited for: 4 -> 4; matrix products, arithmetic and copies ran while one was open for 8% -> 11% of each run, Pallas kernels for 9% -> 11%
where the time goes in v3:
time: 45.6 us; the launch traced here: 45.3 us
  starting transfers between devices  13 us (29%)
  waiting for transfers between devices  12.8 us (28%)
  Pallas kernels  7.57 us (17%)
  matrix products  3.84 us (8%)
  local copies, waits for them, and re-layouts  3.59 us (8%)
  other arithmetic  3.41 us (7%)
  between operations  1.01 us (2%)
    ppermute x4, waiting for transfers between devices, mixed_rows(): lax.ppermute(buf, axis, [(i, i ^ m) for i in range(count)])  11.6 us
    ppermute x4, starting transfers between devices, mixed_rows(): lax.ppermute(buf, axis, [(i, i ^ m) for i in range(count)])  6.02 us
    pallas_call x1, Pallas kernels, stencil(): pl.pallas_call(stencil_kernel, grid=(depth // zc,), in_specs=[pl.BlockSpe...  5 us
    ppermute x2, starting transfers between devices, passed_along(): lax.ppermute(value, axis, [(source, source + steps) for source in range(f...  3.64 us
    ppermute x1, starting transfers between devices, body(): lax.ppermute(cov_x, 'gx', [(i, i ^ 1) for i in range(count)])  3.3 us
    pallas_call x1, Pallas kernels, edges(): pl.pallas_call(edges_kernel, grid=(1,), in_specs=[lo_block, hi_block, lo_...  2.56 us
    dot_general x5, matrix products, product(): jnp.dot(cols, piece.reshape(-1, piece.shape[-1]), precision=precise, pref...  1.95 us
    dot_general x1, matrix products, body(): jnp.einsum('xrkc,rikc->xri', picked, cov_y.reshape(nyb, BLK, cov_y.shape[...  1.89 us
  transfers between devices with their start and end apart: 8, of which 4 were waited for; matrix products, arithmetic and copies ran while one was open for 11% of the time, Pallas kernels for 11%

profile of v3, /device:TPU:0, one launch (start us, length us, event | category | flops | bytes accessed | tf_op | source)
XLA Modules:
  0.0 45.3 jit_solution(9376516638123213936)
XLA Ops:
  0.7 2.6 %shard_map.168 = (f32[16,1024]{1,0:T(8,128)}, f32[16,1024]{1,0:T(8,128)}, f32[16,1024]{1,0:T(8,128)}, f32[16,1024]{1,0:T(8,128)}) custom-call(f32[16,16,1024]{2,1,0:T(8,128)} %s_hi_ref.1, f32[16,16,1024]{2,1,0:T(8,128)} %s_hi_ref.1, s32[16,16,1024]{2,1,0:T(8,128)} %f_ref.3, f32[16,16,1024]{2,1,0:T(8,128)} %vx_ref.3, f32[16,16,1024]{2,1,0:T(8,128)} %d_ref.3), custom_call_target="tpu_custom_call" | custom-call | tf_op jit(solution)/shard_map/pallas_call | solution.py:152
  3.3 2.3 %collective-permute-start = (f32[16,1024]{1,0:T(8,128)}, f32[16,1024]{1,0:T(8,128)S(1)}, u32[]{:S(2)}, u32[]{:S(2)}) collective-permute-start(f32[16,1024]{1,0:T(8,128)} %get-tuple-element.8), channel_id=1, source_target_pairs={{0,1},{1,2},{2,3},{3,4},{4,5},{5,6},{6,7},{7,8},{8,9},{9,10},{10,1... | collective-permute-start | bytes 196616 | tf_op jit(solution)/shard_map/ppermute | solution.py:17
  5.6 0.9 %pad_maximum_fusion.1 = f32[2,16,1024]{2,1,0:T(8,128)S(1)} fusion(f32[1,16,1024]{2,1,0:T(8,128)} %bitcast.94, f32[1,16,1024]{2,1,0:T(8,128)} %bitcast.93), kind=kLoop, calls=%fused_computation.15 | loop fusion | flops 32768 | bytes 262144 | tf_op jit(solution)/shard_map/stack | solution.py:179
  6.5 1.3 %collective-permute-start.1 = (f32[2,16,1024]{2,1,0:T(8,128)S(1)}, f32[2,16,1024]{2,1,0:T(8,128)S(1)}, u32[]{:S(2)}, u32[]{:S(2)}) collective-permute-start(f32[2,16,1024]{2,1,0:T(8,128)S(1)} %pad_maximum_fusion.1), channel_id=1, source_target_pairs={{1,0},{2,1},{3,2},{4,3},{5,4},{6,5},{7,6},{8,7},{9,8},{10,9},{11,1... | collective-permute-start | bytes 393224 | tf_op jit(solution)/shard_map/ppermute | solution.py:17
  7.8 3.3 %collective-permute-start.2 = (bf16[16,4,128]{2,1,0:T(4,128)(2,1)S(1)}, bf16[16,4,128]{2,1,0:T(4,128)(2,1)S(1)}, u32[]{:S(2)}, u32[]{:S(2)}) collective-permute-start(bf16[16,4,128]{2,1,0:T(4,128)(2,1)S(1)} %copy-done.5), channel_id=1, source_target_pairs={{0,1},{1,0},{2,3},{3,2},{4,5},{5,4},{6,7},{7,6},{8,9},{9,8},{10,11... | collective-permute-start | bytes 49160 | tf_op jit(solution)/shard_map/ppermute | solution.py:190
  11.2 0.6 %gather_fusion.1 = s32[16,4]{1,0:T(8,128)S(1)} fusion(s32[2,4]{1,0:T(2,128)S(1)} %copy-done.1, s32[1024]{0:T(1024)S(1)} %pad_clamp_fusion.2), kind=kCustom, calls=%fused_computation.1 | custom fusion | bytes 576 | tf_op jit(solution)/shard_map/gather | solution.py:105
  11.9 0.6 %gather_fusion = s32[16,4]{1,0:T(8,128)S(1)} fusion(s32[2,4]{1,0:T(2,128)S(1)} %copy-done.1, s32[1024]{0:T(1024)S(1)} %pad_clamp_fusion.3), kind=kCustom, calls=%fused_computation | custom fusion | bytes 576 | tf_op jit(solution)/shard_map/gather | solution.py:105
  12.7 0.1 select_reduce_fusion.1
  12.9 0.1 copy.30
  13.1 0.1 copy.27
  13.2 5.0 %shard_map.167 = f32[16,1024]{1,0:T(8,128)} custom-call(f32[16]{0:T(128)} %w_ref.1, f32[16,16,1024]{2,1,0:T(8,128)} %s_hi_ref.1, f32[16,16,1024]{2,1,0:T(8,128)} %s_hi_ref.1, s32[16,16,1024]{2,1,0:T(8,128)} %f_ref.3, f32[16,16,1024]{2,1,0:T(8,128)} %vx_ref.3, f32[16,16,1024]{2,1,0:T(8,128)} %vy_ref.1, f32[16,16,1024]{2,1,0:T(8,128)} %vz_ref.1, ...), custom_call_target="tpu_custom_call" | custom-call | tf_op jit(solution)/shard_map/pallas_call | solution.py:71
  18.3 0.1 copy.33
  18.4 0.1 pad_maximum_fusion.2
  18.5 0.6 %gather_fusion.2 = f32[4,32,16]{1,2,0:T(8,128)S(1)} fusion(f32[32,16,16]{0,2,1:T(8,128)S(1)} %pad_maximum_fusion.2, s32[1024]{0:T(1024)S(1)} %pad_clamp_fusion.1), kind=kCustom, calls=%fused_computation.2 | custom fusion | bytes 16400 | tf_op jit(solution)/shard_map/jit(_take)/gather | solution.py:119
  19.2 0.1 multiply_reduce_fusion
  19.3 0.9 %select_add_fusion = f32[16,1024]{1,0:T(8,128)S(1)} fusion(f32[16,1024]{1,0:T(8,128)} %shard_map.167, f32[1024]{0:T(1024)S(1)} %get-tuple-element.23, f32[1024]{0:T(1024)S(1)} %get-tuple-element.22, pred[16]{0:T(512)(128)(4,1)S(1)} %get-tuple-element.32, pred[16]{0:T(512)(128)(4,1)S(1)} %get-tuple-element.33), kind=kLoop, calls=%fused_computation.44 | loop fusion | flops 65536 | bytes 139296 | tf_op jit(solution)/shard_map/add | solution.py:188
  20.2 0.9 %fusion.71 = f32[1,16,1024]{2,1,0:T(8,128)S(1)} fusion(f32[1024]{0:T(1024)S(1)} %get-tuple-element.23, pred[16]{0:T(512)(128)(4,1)S(1)} %get-tuple-element.32, f32[16,1024]{1,0:T(8,128)} %shard_map.167, f32[1024]{0:T(1024)S(1)} %get-tuple-element.22, pred[16]{0:T(512)(128)(4,1)S(1)} %get-tuple-element.33), kind=kLoop, calls=%fused_computation.129 | loop fusion | flops 65536 | bytes 139296 | tf_op jit(solution)/shard_map/broadcast_in_dim | solution.py:122
  21.1 4.7 %collective-permute-start.5 = (f32[1,16,1024]{2,1,0:T(8,128)S(1)}, f32[1,16,1024]{2,1,0:T(8,128)S(1)}, u32[]{:S(2)}, u32[]{:S(2)}) collective-permute-start(f32[1,16,1024]{2,1,0:T(8,128)S(1)} %fusion.71), channel_id=1, source_target_pairs={{0,12},{1,13},{2,14},{3,15},{4,8},{5,9},{6,10},{7,11},{8,4},{9,5},... | collective-permute-start | bytes 196616 | tf_op jit(solution)/shard_map/ppermute | solution.py:126
  25.9 0.6 %collective-permute-start.3 = (f32[1,16,1024]{2,1,0:T(8,128)S(1)}, f32[1,16,1024]{2,1,0:T(8,128)S(1)}, u32[]{:S(2)}, u32[]{:S(2)}) collective-permute-start(f32[1,16,1024]{2,1,0:T(8,128)S(1)} %fusion.71), channel_id=1, source_target_pairs={{0,4},{1,5},{2,6},{3,7},{4,0},{5,1},{6,2},{7,3},{8,12},{9,13},{10,... | collective-permute-start | bytes 196616 | tf_op jit(solution)/shard_map/ppermute | solution.py:126
  26.5 0.4 fusion.34
  26.9 1.9 %collective-permute-done.5 = f32[1,16,1024]{2,1,0:T(8,128)S(1)} collective-permute-done((f32[1,16,1024]{2,1,0:T(8,128)S(1)}, f32[1,16,1024]{2,1,0:T(8,128)S(1)}, u32[]{:S(2)}, u32[]{:S(2)}) %collective-permute-start.5) | collective-permute-done | bytes 65568 | tf_op jit(solution)/shard_map/ppermute | solution.py:126
  28.8 3.2 %collective-permute-done.4 = f32[1,16,1024]{2,1,0:T(8,128)S(1)} collective-permute-done((f32[1,16,1024]{2,1,0:T(8,128)S(1)}, f32[1,16,1024]{2,1,0:T(8,128)S(1)}, u32[]{:S(2)}, u32[]{:S(2)}) %collective-permute-start.4) | collective-permute-done | bytes 65568 | tf_op jit(solution)/shard_map/ppermute | solution.py:126
  32.0 0.7 %collective-permute-start.6 = (f32[4,16,1024]{2,1,0:T(8,128)S(1)}, f32[4,16,1024]{2,1,0:T(8,128)S(1)}, u32[]{:S(2)}, u32[]{:S(2)}) collective-permute-start(f32[4,16,1024]{2,1,0:T(8,128)S(1)} %pad_maximum_fusion), channel_id=1, source_target_pairs={{0,2},{1,3},{2,0},{3,1},{4,6},{5,7},{6,4},{7,5},{8,10},{9,11},{10,... | collective-permute-start | bytes 786440 | tf_op jit(solution)/shard_map/ppermute | solution.py:126
  32.7 0.4 fusion.17
  33.0 0.4 convolution_add_fusion.1
  33.5 6.5 %collective-permute-done.6 = f32[4,16,1024]{2,1,0:T(8,128)S(1)} collective-permute-done((f32[4,16,1024]{2,1,0:T(8,128)S(1)}, f32[4,16,1024]{2,1,0:T(8,128)S(1)}, u32[]{:S(2)}, u32[]{:S(2)}) %collective-permute-start.6) | collective-permute-done | bytes 262176 | tf_op jit(solution)/shard_map/ppermute | solution.py:126
  40.0 0.4 convolution_bitcast_fusion
  40.4 0.4 fusion.3
  40.9 1.2 %collective-permute-done.7 = f32[16,1024]{1,0:T(8,128)S(1)} collective-permute-done((f32[16,1024]{1,0:T(8,128)S(1)}, f32[16,1024]{1,0:T(8,128)S(1)}, u32[]{:S(2)}, u32[]{:S(2)}) %collective-permute-start.7) | collective-permute-done | bytes 65568 | tf_op jit(solution)/shard_map/ppermute | solution.py:134
  42.1 0.6 %gather_fusion.3 = f32[32,16,128]{2,1,0:T(8,128)S(1)} fusion(f32[16,8,128]{2,0,1:T(8,128)S(1)} %copy_bitcast_fusion.1, s32[1024]{0:T(1024)S(1)} %pad_clamp_fusion), kind=kCustom, calls=%fused_computation.3 | custom fusion | bytes 524416 | tf_op jit(solution)/shard_map/jit(_take)/gather | solution.py:198
  42.7 1.9 %fusion.4 = f32[8,2,8,128]{3,2,1,0:T(8,128)S(1)} fusion(f32[8,128,4,128]{3,2,1,0:T(4,128)S(1)} %bitcast.80, f32[8,4,16,128]{3,2,1,0:T(8,128)S(1)} %bitcast.91, pred[8,4]{1,0:T(8,128)(4,1)S(1)} %copy.27), kind=kOutput, calls=%fused_computation.11 | convolution fusion | flops 100728832 | bytes 2424864 | tf_op jit(solution)/shard_map/xrkc,rikc->xri/dot_general | solution.py:199
  44.6 0.6 %copy.47 = f32[8,2,8,128]{3,2,0,1:T(8,128)} copy(f32[8,2,8,128]{3,2,1,0:T(8,128)S(1)} %fusion.4) | data formatting | bytes 131072 | tf_op jit(solution)/shard_map/reshape | solution.py:205
  (47 shorter events, 0.8 us)
Async XLA Ops:
  0.6 42.1 %copy-start = (f32[1024,4,128]{2,1,0:T(4,128)S(1)}, f32[1024,4,128]{2,1,0:T(4,128)}, u32[]{:S(2)}) copy-start(f32[1024,4,128]{2,1,0:T(4,128)} %param.27) | copy-start | bytes 6291460
  0.6 12.0 %copy-start.8 = (s32[4]{0:T(128)S(1)}, s32[4]{0:T(128)}, u32[]{:S(2)}) copy-start(s32[4]{0:T(128)} %constant.118.clone) | copy-start | bytes 52
  0.7 7.1 %copy-start.5 = (bf16[16,4,128]{2,1,0:T(4,128)(2,1)S(1)}, bf16[16,4,128]{2,1,0:T(4,128)(2,1)}, u32[]{:S(2)}) copy-start(bf16[16,4,128]{2,1,0:T(4,128)(2,1)} %param.25) | copy-start | bytes 49156
  0.7 10.5 %copy-start.1 = (s32[2,4]{1,0:T(2,128)S(1)}, s32[2,4]{1,0:T(2,128)}, u32[]{:S(2)}) copy-start(s32[2,4]{1,0:T(2,128)} %param.26) | copy-start | bytes 100
  0.7 12.0 %copy-start.6 = (s32[8,4]{0,1:T(4,128)S(1)}, s32[8,4]{0,1:T(4,128)}, u32[]{:S(2)}) copy-start(s32[8,4]{0,1:T(4,128)} %param.28) | copy-start | bytes 388
  3.3 15.9 %collective-permute-start = (f32[16,1024]{1,0:T(8,128)}, f32[16,1024]{1,0:T(8,128)S(1)}, u32[]{:S(2)}, u32[]{:S(2)}) collective-permute-start(f32[16,1024]{1,0:T(8,128)} %get-tuple-element.8), channel_id=1, source_target_pairs={{0,1},{1,2},{2,3},{3,4},{4,5},{5,6},{6,7},{7,8},{8,9},{9,10},{10,1... | collective-permute-start | bytes 196616 | tf_op jit(solution)/shard_map/ppermute | solution.py:17
  6.5 12.6 %collective-permute-start.1 = (f32[2,16,1024]{2,1,0:T(8,128)S(1)}, f32[2,16,1024]{2,1,0:T(8,128)S(1)}, u32[]{:S(2)}, u32[]{:S(2)}) collective-permute-start(f32[2,16,1024]{2,1,0:T(8,128)S(1)} %pad_maximum_fusion.1), channel_id=1, source_target_pairs={{1,0},{2,1},{3,2},{4,3},{5,4},{6,5},{7,6},{8,7},{9,8},{10,9},{11,1... | collective-permute-start | bytes 393224 | tf_op jit(solution)/shard_map/ppermute | solution.py:17
  7.8 10.4 %collective-permute-start.2 = (bf16[16,4,128]{2,1,0:T(4,128)(2,1)S(1)}, bf16[16,4,128]{2,1,0:T(4,128)(2,1)S(1)}, u32[]{:S(2)}, u32[]{:S(2)}) collective-permute-start(bf16[16,4,128]{2,1,0:T(4,128)(2,1)S(1)} %copy-done.5), channel_id=1, source_target_pairs={{0,1},{1,0},{2,3},{3,2},{4,5},{5,4},{6,7},{7,6},{8,9},{9,8},{10,11... | collective-permute-start | bytes 49160 | tf_op jit(solution)/shard_map/ppermute | solution.py:190
  13.2 5.9 %copy-start.3 = (f32[16,1024]{1,0:T(8,128)S(1)}, f32[16,1024]{1,0:T(8,128)}, u32[]{:S(2)}) copy-start(f32[16,1024]{1,0:T(8,128)} %get-tuple-element.8) | copy-start | bytes 196612
  13.2 5.9 %copy-start.4 = (f32[16,1024]{1,0:T(8,128)S(1)}, f32[16,1024]{1,0:T(8,128)}, u32[]{:S(2)}) copy-start(f32[16,1024]{1,0:T(8,128)} %get-tuple-element.7) | copy-start | bytes 196612
  13.2 5.9 %copy-start.7 = (f32[16]{0:T(128)S(1)}, f32[16]{0:T(128)}, u32[]{:S(2)}) copy-start(f32[16]{0:T(128)} %w_ref.1) | copy-start | bytes 196
  20.2 22.5 %copy-start.2 = (f32[16,1024]{1,0:T(8,128)}, f32[16,1024]{1,0:T(8,128)S(1)}, u32[]{:S(2)}) copy-start(f32[16,1024]{1,0:T(8,128)S(1)} %select_add_fusion) | copy-start | bytes 196612
  21.1 7.6 %collective-permute-start.5 = (f32[1,16,1024]{2,1,0:T(8,128)S(1)}, f32[1,16,1024]{2,1,0:T(8,128)S(1)}, u32[]{:S(2)}, u32[]{:S(2)}) collective-permute-start(f32[1,16,1024]{2,1,0:T(8,128)S(1)} %fusion.71), channel_id=1, source_target_pairs={{0,12},{1,13},{2,14},{3,15},{4,8},{5,9},{6,10},{7,11},{8,4},{9,5},... | collective-permute-start | bytes 196616 | tf_op jit(solution)/shard_map/ppermute | solution.py:126
  25.9 6.1 %collective-permute-start.4 = (f32[1,16,1024]{2,1,0:T(8,128)S(1)}, f32[1,16,1024]{2,1,0:T(8,128)S(1)}, u32[]{:S(2)}, u32[]{:S(2)}) collective-permute-start(f32[1,16,1024]{2,1,0:T(8,128)S(1)} %fusion.71), channel_id=1, source_target_pairs={{0,8},{1,9},{2,10},{3,11},{4,12},{5,13},{6,14},{7,15},{8,0},{9,1},... | collective-permute-start | bytes 196616 | tf_op jit(solution)/shard_map/ppermute | solution.py:126
  25.9 6.1 %collective-permute-start.3 = (f32[1,16,1024]{2,1,0:T(8,128)S(1)}, f32[1,16,1024]{2,1,0:T(8,128)S(1)}, u32[]{:S(2)}, u32[]{:S(2)}) collective-permute-start(f32[1,16,1024]{2,1,0:T(8,128)S(1)} %fusion.71), channel_id=1, source_target_pairs={{0,4},{1,5},{2,6},{3,7},{4,0},{5,1},{6,2},{7,3},{8,12},{9,13},{10,... | collective-permute-start | bytes 196616 | tf_op jit(solution)/shard_map/ppermute | solution.py:126
  32.0 8.0 %collective-permute-start.6 = (f32[4,16,1024]{2,1,0:T(8,128)S(1)}, f32[4,16,1024]{2,1,0:T(8,128)S(1)}, u32[]{:S(2)}, u32[]{:S(2)}) collective-permute-start(f32[4,16,1024]{2,1,0:T(8,128)S(1)} %pad_maximum_fusion), channel_id=1, source_target_pairs={{0,2},{1,3},{2,0},{3,1},{4,6},{5,7},{6,4},{7,5},{8,10},{9,11},{10,... | collective-permute-start | bytes 786440 | tf_op jit(solution)/shard_map/ppermute | solution.py:126
  40.8 1.3 %collective-permute-start.7 = (f32[16,1024]{1,0:T(8,128)S(1)}, f32[16,1024]{1,0:T(8,128)S(1)}, u32[]{:S(2)}, u32[]{:S(2)}) collective-permute-start(f32[16,1024]{1,0:T(8,128)S(1)} %slice.36), channel_id=1, source_target_pairs={{0,1},{1,0},{2,3},{3,2},{4,5},{5,4},{6,7},{7,6},{8,9},{9,8},{10,11... | collective-permute-start | bytes 196616 | tf_op jit(solution)/shard_map/ppermute | solution.py:134

commit v4 on v3

--- a/solution.py
+++ b/solution.py
@@ -8,7 +8,7 @@
 BLK = 128
 Z_CHUNK = 4
 
-precise = lax.Precision.HIGHEST
+precise = lax.Precision.HIGH
 
 
 def passed_along(value, axis, steps):
@@ -24,7 +24,7 @@
     return lower, upper
 
 
-def stencil_kernel(w_ref, s_ref, sprev_ref, f_ref, vx_ref, vy_ref, vz_ref, d_ref, out_ref):
+def stencil_kernel(w_ref, s_ref, sprev_ref, f_ref, vx_ref, vy_ref, vz_ref, d_ref, out_ref, to_prev_ref, edge_ref):
     c = pl.program_id(0)
     rows, cols = out_ref.shape
     sub = lax.broadcasted_iota(jnp.int32, (rows, cols), 0)
@@ -42,6 +42,10 @@
         f = f_ref[j]
         d = d_ref[j]
         lo_x, up_x = coefs(f, 1, vx_ref[j], d)
+        to_prev_ref[0, pl.ds(z, 1), :] = s[0:1, :]
+        to_prev_ref[1, pl.ds(z, 1), :] = lo_x[0:1, :]
+        edge_ref[0, pl.ds(z, 1), :] = s[rows - 1:rows, :]
+        edge_ref[1, pl.ds(z, 1), :] = up_x[0:1, :]
         lo_y, up_y = coefs(f, 2, vy_ref[j], d)
         lo_z, up_z = coefs(f, 4, vz_ref[j], d)
         s_xm = jnp.where(sub == 0, 0.0, pltpu.roll(s, 1, 0))
@@ -81,8 +85,16 @@
             block,
             block,
         ],
-        out_specs=pl.BlockSpec((rows, cols), lambda c: (0, 0)),
-        out_shape=jax.ShapeDtypeStruct((rows, cols), jnp.float32),
+        out_specs=[
+            pl.BlockSpec((rows, cols), lambda c: (0, 0)),
+            pl.BlockSpec((2, depth, cols), lambda c: (0, 0, 0)),
+            pl.BlockSpec((2, depth, cols), lambda c: (0, 0, 0)),
+        ],
+        out_shape=[
+            jax.ShapeDtypeStruct((rows, cols), jnp.float32),
+            jax.ShapeDtypeStruct((2, depth, cols), jnp.float32),
+            jax.ShapeDtypeStruct((2, depth, cols), jnp.float32),
+        ],
         compiler_params=pltpu.CompilerParams(dimension_semantics=("arbitrary",)),
     )(layer_weight, s, s, f, vx, vy, vz, d)
 
@@ -132,30 +144,6 @@
     if count == 1:
         return own
     return own + lax.ppermute(for_partner, axis, [(i, i ^ 1) for i in range(count)])
-
-
-def edges_kernel(s_lo_ref, s_hi_ref, f_ref, vx_ref, d_ref, first_ref, last_ref, lo_ref, up_ref):
-    first_ref[...] = s_lo_ref[:, 0, :]
-    last_ref[...] = s_hi_ref[:, s_hi_ref.shape[1] - 1, :]
-    lo, up = coefs(f_ref[:, 0, :], 1, vx_ref[:, 0, :], d_ref[:, 0, :])
-    lo_ref[...] = lo
-    up_ref[...] = up
-
-
-def edges(s, f, vx, d):
-    depth, rows, cols = s.shape
-    part = 8 if rows % 8 == 0 else rows
-    lo_block = pl.BlockSpec((depth, part, cols), lambda i: (0, 0, 0))
-    hi_block = pl.BlockSpec((depth, part, cols), lambda i: (0, rows // part - 1, 0))
-    plane = jax.ShapeDtypeStruct((depth, cols), jnp.float32)
-    whole = pl.BlockSpec((depth, cols), lambda i: (0, 0))
-    return pl.pallas_call(
-        edges_kernel,
-        grid=(1,),
-        in_specs=[lo_block, hi_block, lo_block, lo_block, lo_block],
-        out_specs=[whole] * 4,
-        out_shape=[plane] * 4,
-    )(s, s, f, vx, d)
 
 
 def body(
@@ -175,11 +163,10 @@
     me = lax.axis_index("gx")
     depth, rows, cols = adjoint_state.shape
 
-    first_s, last_s, lo_x0, up_x0 = edges(adjoint_state, face_flags, speed_x, dispersion)
-    from_next = passed_along(jnp.stack([first_s, lo_x0]), "gx", -1)
+    partial, to_prev, edge = stencil(layer_weight, adjoint_state, face_flags, speed_x, speed_y, speed_z, dispersion)
+    last_s, up_x0 = edge[0], edge[1]
+    from_next = passed_along(to_prev, "gx", -1)
     from_prev = passed_along(last_s, "gx", 1)
-
-    partial = stencil(layer_weight, adjoint_state, face_flags, speed_x, speed_y, speed_z, dispersion)
 
     corr_first = jnp.sum(layer_weight[:, None] * (-up_x0 * from_prev), axis=0)
     ax_next = -from_next[1] * (from_next[0] - last_s)

time: 45.6 us -> 43 us (0.943)
  Pallas kernels: 7.57 us -> 5.18 us
  matrix products: 3.84 us -> 2.58 us
  local copies, waits for them, and re-layouts: 3.59 us -> 4.43 us
  starting transfers between devices: 13 us -> 13.6 us
    pallas_call x1 -> x0, Pallas kernels: 2.56 us -> none  [edges(): pl.pallas_call(edges_kernel, grid=(1,), in_specs=[lo_block, hi_block, lo_...]
    dot_general x1, matrix products: 1.89 us -> 0.96 us  [body(): jnp.einsum('xrkc,rikc->xri', picked, cov_y.reshape(nyb, BLK, cov_y.shape[...]
    another operation x1 -> x0, other arithmetic: 0.88 us -> none  [body(): from_next = passed_along(jnp.stack([first_s, lo_x0]), 'gx', -1)]
    reduce_sum x1, other arithmetic: 0.09 us -> 0.97 us  [body(): corr_first = jnp.sum(layer_weight[:, None] * (-up_x0 * from_prev), axis=0)]
    squeeze x0 -> x1, local copies, waits for them, and re-layouts: none -> 0.85 us  [body(): last_s, up_x0 = (edge[0], edge[1])]
    ppermute x4, starting transfers between devices: 6.02 us -> 6.59 us  [mixed_rows(): lax.ppermute(buf, axis, [(i, i ^ m) for i in range(count)])]
  transfers between devices with their start and end apart: 8 -> 8, of which waited for: 4 -> 4; matrix products, arithmetic and copies ran while one was open for 11% -> 9% of each run, Pallas kernels for 11% -> 0%
where the time goes in v4:
time: 43 us; the launch traced here: 42.6 us
  starting transfers between devices  13.6 us (32%)
  waiting for transfers between devices  12.5 us (29%)
  Pallas kernels  5.18 us (12%)
  local copies, waits for them, and re-layouts  4.43 us (10%)
  other arithmetic  3.4 us (8%)
  matrix products  2.58 us (6%)
  between operations  1 us (2%)
    ppermute x4, waiting for transfers between devices, mixed_rows(): lax.ppermute(buf, axis, [(i, i ^ m) for i in range(count)])  11.2 us
    ppermute x4, starting transfers between devices, mixed_rows(): lax.ppermute(buf, axis, [(i, i ^ m) for i in range(count)])  6.59 us
    pallas_call x1, Pallas kernels, stencil(): pl.pallas_call(stencil_kernel, grid=(depth // zc,), in_specs=[pl.BlockSpe...  5.18 us
    ppermute x2, starting transfers between devices, passed_along(): lax.ppermute(value, axis, [(source, source + steps) for source in range(f...  3.64 us
    ppermute x1, starting transfers between devices, body(): lax.ppermute(cov_x, 'gx', [(i, i ^ 1) for i in range(count)])  3.3 us
    dot_general x5, matrix products, product(): jnp.dot(cols, piece.reshape(-1, piece.shape[-1]), precision=precise, pref...  1.62 us
    ppermute x1, waiting for transfers between devices, mixed_rows(): lax.ppermute(for_partner, axis, [(i, i ^ 1) for i in range(count)])  1.23 us
    gather x2, local copies, waits for them, and re-layouts, cx_slab(): target = (row_block[:, None] + offsets[row_block]) % nxb  1.12 us
  transfers between devices with their start and end apart: 8, of which 4 were waited for; matrix products, arithmetic and copies ran while one was open for 9% of the time, Pallas kernels for 0%

profile of v4, /device:TPU:0, one launch (start us, length us, event | category | flops | bytes accessed | tf_op | source)
XLA Modules:
  0.0 42.6 jit_solution(10500442253479342785)
XLA Ops:
  0.7 5.2 %shard_map.167 = (f32[16,1024]{1,0:T(8,128)}, f32[2,16,1024]{2,1,0:T(8,128)}, f32[2,16,1024]{2,1,0:T(8,128)}) custom-call(f32[16]{0:T(128)} %w_ref.1, f32[16,16,1024]{2,1,0:T(8,128)} %sprev_ref.1, f32[16,16,1024]{2,1,0:T(8,128)} %sprev_ref.1, s32[16,16,1024]{2,1,0:T(8,128)} %f_ref.1, f32[16,16,1024]{2,1,0:T(8,128)} %vx_ref.1, f32[16,16,1024]{2,1,0:T(8,128)} %vy_ref.1, ...), custom_call_target="tpu_custom_call" | custom-call | tf_op jit(solution)/shard_map/pallas_call | solution.py:75
  5.9 0.8 %slice_bitcast_fusion.1 = f32[16,1024]{1,0:T(8,128)S(1)} fusion(f32[2,16,1024]{2,1,0:T(8,128)} %get-tuple-element.7), kind=kLoop, calls=%fused_computation.47 | loop fusion | bytes 131072 | tf_op jit(solution)/shard_map/squeeze | solution.py:167
  6.7 2.3 %collective-permute-start = (f32[16,1024]{1,0:T(8,128)S(1)}, f32[16,1024]{1,0:T(8,128)S(1)}, u32[]{:S(2)}, u32[]{:S(2)}) collective-permute-start(f32[16,1024]{1,0:T(8,128)S(1)} %slice_bitcast_fusion.1), channel_id=1, source_target_pairs={{0,1},{1,2},{2,3},{3,4},{4,5},{5,6},{6,7},{7,8},{8,9},{9,10},{10,1... | collective-permute-start | bytes 196616 | tf_op jit(solution)/shard_map/ppermute | solution.py:17
  9.1 1.3 %collective-permute-start.1 = (f32[2,16,1024]{2,1,0:T(8,128)}, f32[2,16,1024]{2,1,0:T(8,128)S(1)}, u32[]{:S(2)}, u32[]{:S(2)}) collective-permute-start(f32[2,16,1024]{2,1,0:T(8,128)} %get-tuple-element.8), channel_id=1, source_target_pairs={{1,0},{2,1},{3,2},{4,3},{5,4},{6,5},{7,6},{8,7},{9,8},{10,9},{11,1... | collective-permute-start | bytes 393224 | tf_op jit(solution)/shard_map/ppermute | solution.py:17
  10.4 3.3 %collective-permute-start.2 = (bf16[16,4,128]{2,1,0:T(4,128)(2,1)S(1)}, bf16[16,4,128]{2,1,0:T(4,128)(2,1)S(1)}, u32[]{:S(2)}, u32[]{:S(2)}) collective-permute-start(bf16[16,4,128]{2,1,0:T(4,128)(2,1)S(1)} %copy-done.3), channel_id=1, source_target_pairs={{0,1},{1,0},{2,3},{3,2},{4,5},{5,4},{6,7},{7,6},{8,9},{9,8},{10,11... | collective-permute-start | bytes 49160 | tf_op jit(solution)/shard_map/ppermute | solution.py:177
  13.8 0.6 %gather_fusion.1 = s32[16,4]{1,0:T(8,128)S(1)} fusion(s32[2,4]{1,0:T(2,128)S(1)} %copy-done.1, s32[1024]{0:T(1024)S(1)} %pad_clamp_fusion.2), kind=kCustom, calls=%fused_computation.1 | custom fusion | bytes 576 | tf_op jit(solution)/shard_map/gather | solution.py:117
  14.5 0.6 %gather_fusion = s32[16,4]{1,0:T(8,128)S(1)} fusion(s32[2,4]{1,0:T(2,128)S(1)} %copy-done.1, s32[1024]{0:T(1024)S(1)} %pad_clamp_fusion.3), kind=kCustom, calls=%fused_computation | custom fusion | bytes 576 | tf_op jit(solution)/shard_map/gather | solution.py:117
  15.3 0.1 select_reduce_fusion.1
  15.5 0.1 copy.30
  15.7 0.1 copy.27
  15.8 0.1 select_reduce_fusion
  15.9 0.1 copy.33
  16.0 0.1 pad_maximum_fusion.1
  16.1 0.6 %gather_fusion.2 = f32[4,32,16]{1,2,0:T(8,128)S(1)} fusion(f32[32,16,16]{0,2,1:T(8,128)S(1)} %pad_maximum_fusion.1, s32[1024]{0:T(1024)S(1)} %pad_clamp_fusion.1), kind=kCustom, calls=%fused_computation.2 | custom fusion | bytes 16400 | tf_op jit(solution)/shard_map/jit(_take)/gather | solution.py:131
  16.7 1.0 %fusion.22 = (f32[1024]{0:T(1024)S(1)}, f32[1024]{0:T(1024)S(1)}) fusion(f32[16,1024]{1,0:T(8,128)S(1)} %collective-permute-done, f32[2,16,1024]{2,1,0:T(8,128)} %get-tuple-element.7, f32[16]{0:T(128)S(1)} %copy-done.5, f32[2,16,1024]{2,1,0:T(8,128)S(1)} %collective-permute-done.1), kind=kLoop, calls=%fused_computation.43 | loop fusion | flops 145408 | bytes 335936 | tf_op jit(solution)/shard_map/reduce_sum | solution.py:171
  17.7 0.9 %select_add_fusion = f32[16,1024]{1,0:T(8,128)S(1)} fusion(f32[16,1024]{1,0:T(8,128)} %get-tuple-element.6, f32[1024]{0:T(1024)S(1)} %get-tuple-element.21, f32[1024]{0:T(1024)S(1)} %get-tuple-element.20, pred[16]{0:T(512)(128)(4,1)S(1)} %get-tuple-element.30, pred[16]{0:T(512)(128)(4,1)S(1)} %get-tuple-element.31), kind=kLoop, calls=%fused_computation.46 | loop fusion | flops 65536 | bytes 139296 | tf_op jit(solution)/shard_map/add | solution.py:175
  18.6 0.9 %fusion.73 = f32[1,16,1024]{2,1,0:T(8,128)S(1)} fusion(f32[1024]{0:T(1024)S(1)} %get-tuple-element.21, pred[16]{0:T(512)(128)(4,1)S(1)} %get-tuple-element.30, f32[16,1024]{1,0:T(8,128)} %get-tuple-element.6, f32[1024]{0:T(1024)S(1)} %get-tuple-element.20, pred[16]{0:T(512)(128)(4,1)S(1)} %get-tuple-element.31), kind=kLoop, calls=%fused_computation.131 | loop fusion | flops 65536 | bytes 139296 | tf_op jit(solution)/shard_map/broadcast_in_dim | solution.py:134
  19.6 4.7 %collective-permute-start.5 = (f32[1,16,1024]{2,1,0:T(8,128)S(1)}, f32[1,16,1024]{2,1,0:T(8,128)S(1)}, u32[]{:S(2)}, u32[]{:S(2)}) collective-permute-start(f32[1,16,1024]{2,1,0:T(8,128)S(1)} %fusion.73), channel_id=1, source_target_pairs={{0,12},{1,13},{2,14},{3,15},{4,8},{5,9},{6,10},{7,11},{8,4},{9,5},... | collective-permute-start | bytes 196616 | tf_op jit(solution)/shard_map/ppermute | solution.py:138
  24.3 0.6 %collective-permute-start.3 = (f32[1,16,1024]{2,1,0:T(8,128)S(1)}, f32[1,16,1024]{2,1,0:T(8,128)S(1)}, u32[]{:S(2)}, u32[]{:S(2)}) collective-permute-start(f32[1,16,1024]{2,1,0:T(8,128)S(1)} %fusion.73), channel_id=1, source_target_pairs={{0,4},{1,5},{2,6},{3,7},{4,0},{5,1},{6,2},{7,3},{8,12},{9,13},{10,... | collective-permute-start | bytes 196616 | tf_op jit(solution)/shard_map/ppermute | solution.py:138
  24.9 0.3 fusion.36
  25.3 2.0 %collective-permute-done.5 = f32[1,16,1024]{2,1,0:T(8,128)S(1)} collective-permute-done((f32[1,16,1024]{2,1,0:T(8,128)S(1)}, f32[1,16,1024]{2,1,0:T(8,128)S(1)}, u32[]{:S(2)}, u32[]{:S(2)}) %collective-permute-start.5) | collective-permute-done | bytes 65568 | tf_op jit(solution)/shard_map/ppermute | solution.py:138
  27.2 3.2 %collective-permute-done.4 = f32[1,16,1024]{2,1,0:T(8,128)S(1)} collective-permute-done((f32[1,16,1024]{2,1,0:T(8,128)S(1)}, f32[1,16,1024]{2,1,0:T(8,128)S(1)}, u32[]{:S(2)}, u32[]{:S(2)}) %collective-permute-start.4) | collective-permute-done | bytes 65568 | tf_op jit(solution)/shard_map/ppermute | solution.py:138
  30.4 1.2 %collective-permute-start.6 = (f32[4,16,1024]{2,1,0:T(8,128)S(1)}, f32[4,16,1024]{2,1,0:T(8,128)S(1)}, u32[]{:S(2)}, u32[]{:S(2)}) collective-permute-start(f32[4,16,1024]{2,1,0:T(8,128)S(1)} %pad_maximum_fusion), channel_id=1, source_target_pairs={{0,2},{1,3},{2,0},{3,1},{4,6},{5,7},{6,4},{7,5},{8,10},{9,11},{10,... | collective-permute-start | bytes 786440 | tf_op jit(solution)/shard_map/ppermute | solution.py:138
  31.7 0.3 fusion.17
  32.0 0.3 convolution_add_fusion.1
  32.3 6.1 %collective-permute-done.6 = f32[4,16,1024]{2,1,0:T(8,128)S(1)} collective-permute-done((f32[4,16,1024]{2,1,0:T(8,128)S(1)}, f32[4,16,1024]{2,1,0:T(8,128)S(1)}, u32[]{:S(2)}, u32[]{:S(2)}) %collective-permute-start.6) | collective-permute-done | bytes 262176 | tf_op jit(solution)/shard_map/ppermute | solution.py:138
  38.4 0.3 convolution_bitcast_fusion
  38.7 0.3 fusion.3
  39.2 1.2 %collective-permute-done.7 = f32[16,1024]{1,0:T(8,128)S(1)} collective-permute-done((f32[16,1024]{1,0:T(8,128)S(1)}, f32[16,1024]{1,0:T(8,128)S(1)}, u32[]{:S(2)}, u32[]{:S(2)}) %collective-permute-start.7) | collective-permute-done | bytes 65568 | tf_op jit(solution)/shard_map/ppermute | solution.py:146
  40.4 0.6 %gather_fusion.3 = f32[32,16,128]{2,1,0:T(8,128)S(1)} fusion(f32[16,8,128]{2,0,1:T(8,128)S(1)} %copy_bitcast_fusion.1, s32[1024]{0:T(1024)S(1)} %pad_clamp_fusion), kind=kCustom, calls=%fused_computation.3 | custom fusion | bytes 524416 | tf_op jit(solution)/shard_map/jit(_take)/gather | solution.py:185
  41.0 1.0 %fusion.4 = f32[8,2,8,128]{3,2,1,0:T(8,128)S(1)} fusion(f32[8,128,4,128]{3,2,1,0:T(4,128)S(1)} %bitcast.88, f32[8,4,16,128]{3,2,1,0:T(8,128)S(1)} %bitcast.99, pred[8,4]{1,0:T(8,128)(4,1)S(1)} %copy.27), kind=kOutput, calls=%fused_computation.11 | convolution fusion | flops 50397184 | bytes 2424864 | tf_op jit(solution)/shard_map/xrkc,rikc->xri/dot_general | solution.py:186
  42.0 0.7 %copy.47 = f32[8,2,8,128]{3,2,0,1:T(8,128)} copy(f32[8,2,8,128]{3,2,1,0:T(8,128)S(1)} %fusion.4) | data formatting | bytes 131072 | tf_op jit(solution)/shard_map/reshape | solution.py:192
  (42 shorter events, 0.8 us)
Async XLA Ops:
  0.6 40.4 %copy-start = (f32[1024,4,128]{2,1,0:T(4,128)S(1)}, f32[1024,4,128]{2,1,0:T(4,128)}, u32[]{:S(2)}) copy-start(f32[1024,4,128]{2,1,0:T(4,128)} %param.27) | copy-start | bytes 6291460
  0.6 14.6 %copy-start.6 = (s32[4]{0:T(128)S(1)}, s32[4]{0:T(128)}, u32[]{:S(2)}) copy-start(s32[4]{0:T(128)} %constant.118.clone) | copy-start | bytes 52
  0.7 16.0 %copy-start.5 = (f32[16]{0:T(128)S(1)}, f32[16]{0:T(128)}, u32[]{:S(2)}) copy-start(f32[16]{0:T(128)} %w_ref.1) | copy-start | bytes 196
  0.7 9.7 %copy-start.3 = (bf16[16,4,128]{2,1,0:T(4,128)(2,1)S(1)}, bf16[16,4,128]{2,1,0:T(4,128)(2,1)}, u32[]{:S(2)}) copy-start(bf16[16,4,128]{2,1,0:T(4,128)(2,1)} %param.25) | copy-start | bytes 49156
  0.7 13.1 %copy-start.1 = (s32[2,4]{1,0:T(2,128)S(1)}, s32[2,4]{1,0:T(2,128)}, u32[]{:S(2)}) copy-start(s32[2,4]{1,0:T(2,128)} %param.26) | copy-start | bytes 100
  0.7 14.6 %copy-start.4 = (s32[8,4]{0,1:T(4,128)S(1)}, s32[8,4]{0,1:T(4,128)}, u32[]{:S(2)}) copy-start(s32[8,4]{0,1:T(4,128)} %param.28) | copy-start | bytes 388
  6.7 10.0 %collective-permute-start = (f32[16,1024]{1,0:T(8,128)S(1)}, f32[16,1024]{1,0:T(8,128)S(1)}, u32[]{:S(2)}, u32[]{:S(2)}) collective-permute-start(f32[16,1024]{1,0:T(8,128)S(1)} %slice_bitcast_fusion.1), channel_id=1, source_target_pairs={{0,1},{1,2},{2,3},{3,4},{4,5},{5,6},{6,7},{7,8},{8,9},{9,10},{10,1... | collective-permute-start | bytes 196616 | tf_op jit(solution)/shard_map/ppermute | solution.py:17
  9.1 7.6 %collective-permute-start.1 = (f32[2,16,1024]{2,1,0:T(8,128)}, f32[2,16,1024]{2,1,0:T(8,128)S(1)}, u32[]{:S(2)}, u32[]{:S(2)}) collective-permute-start(f32[2,16,1024]{2,1,0:T(8,128)} %get-tuple-element.8), channel_id=1, source_target_pairs={{1,0},{2,1},{3,2},{4,3},{5,4},{6,5},{7,6},{8,7},{9,8},{10,9},{11,1... | collective-permute-start | bytes 393224 | tf_op jit(solution)/shard_map/ppermute | solution.py:17
  10.4 5.4 %collective-permute-start.2 = (bf16[16,4,128]{2,1,0:T(4,128)(2,1)S(1)}, bf16[16,4,128]{2,1,0:T(4,128)(2,1)S(1)}, u32[]{:S(2)}, u32[]{:S(2)}) collective-permute-start(bf16[16,4,128]{2,1,0:T(4,128)(2,1)S(1)} %copy-done.3), channel_id=1, source_target_pairs={{0,1},{1,0},{2,3},{3,2},{4,5},{5,4},{6,7},{7,6},{8,9},{9,8},{10,11... | collective-permute-start | bytes 49160 | tf_op jit(solution)/shard_map/ppermute | solution.py:177
  18.6 22.4 %copy-start.2 = (f32[16,1024]{1,0:T(8,128)}, f32[16,1024]{1,0:T(8,128)S(1)}, u32[]{:S(2)}) copy-start(f32[16,1024]{1,0:T(8,128)S(1)} %select_add_fusion) | copy-start | bytes 196612
  19.6 7.6 %collective-permute-start.5 = (f32[1,16,1024]{2,1,0:T(8,128)S(1)}, f32[1,16,1024]{2,1,0:T(8,128)S(1)}, u32[]{:S(2)}, u32[]{:S(2)}) collective-permute-start(f32[1,16,1024]{2,1,0:T(8,128)S(1)} %fusion.73), channel_id=1, source_target_pairs={{0,12},{1,13},{2,14},{3,15},{4,8},{5,9},{6,10},{7,11},{8,4},{9,5},... | collective-permute-start | bytes 196616 | tf_op jit(solution)/shard_map/ppermute | solution.py:138
  24.3 6.1 %collective-permute-start.4 = (f32[1,16,1024]{2,1,0:T(8,128)S(1)}, f32[1,16,1024]{2,1,0:T(8,128)S(1)}, u32[]{:S(2)}, u32[]{:S(2)}) collective-permute-start(f32[1,16,1024]{2,1,0:T(8,128)S(1)} %fusion.73), channel_id=1, source_target_pairs={{0,8},{1,9},{2,10},{3,11},{4,12},{5,13},{6,14},{7,15},{8,0},{9,1},... | collective-permute-start | bytes 196616 | tf_op jit(solution)/shard_map/ppermute | solution.py:138
  24.3 6.1 %collective-permute-start.3 = (f32[1,16,1024]{2,1,0:T(8,128)S(1)}, f32[1,16,1024]{2,1,0:T(8,128)S(1)}, u32[]{:S(2)}, u32[]{:S(2)}) collective-permute-start(f32[1,16,1024]{2,1,0:T(8,128)S(1)} %fusion.73), channel_id=1, source_target_pairs={{0,4},{1,5},{2,6},{3,7},{4,0},{5,1},{6,2},{7,3},{8,12},{9,13},{10,... | collective-permute-start | bytes 196616 | tf_op jit(solution)/shard_map/ppermute | solution.py:138
  30.4 8.0 %collective-permute-start.6 = (f32[4,16,1024]{2,1,0:T(8,128)S(1)}, f32[4,16,1024]{2,1,0:T(8,128)S(1)}, u32[]{:S(2)}, u32[]{:S(2)}) collective-permute-start(f32[4,16,1024]{2,1,0:T(8,128)S(1)} %pad_maximum_fusion), channel_id=1, source_target_pairs={{0,2},{1,3},{2,0},{3,1},{4,6},{5,7},{6,4},{7,5},{8,10},{9,11},{10,... | collective-permute-start | bytes 786440 | tf_op jit(solution)/shard_map/ppermute | solution.py:138
  39.1 1.3 %collective-permute-start.7 = (f32[16,1024]{1,0:T(8,128)S(1)}, f32[16,1024]{1,0:T(8,128)S(1)}, u32[]{:S(2)}, u32[]{:S(2)}) collective-permute-start(f32[16,1024]{1,0:T(8,128)S(1)} %slice.44), channel_id=1, source_target_pairs={{0,1},{1,0},{2,3},{3,2},{4,5},{5,4},{6,7},{7,6},{8,9},{9,8},{10,11... | collective-permute-start | bytes 196616 | tf_op jit(solution)/shard_map/ppermute | solution.py:146

commit v5 on v4

--- a/solution.py
+++ b/solution.py
@@ -102,12 +102,17 @@
 def gather_rounds(count):
     bits = []
     bit = count // 2
-    while bit >= 2:
+    while bit >= 4:
         bits.append(bit)
         bit //= 2
     if len(bits) < 2:
         return [[b] for b in bits]
     return [[bits[1], bits[0], bits[0] | bits[1]]] + [[b] for b in bits[2:]]
+
+
+def swap(value, axis, mask):
+    count = lax.axis_size(axis)
+    return lax.ppermute(value, axis, [(i, i ^ mask) for i in range(count)])
 
 
 def cx_slab(cov_rows, offsets, device, rows):
@@ -135,15 +140,15 @@
     entries = [0]
     total = product(buf, entries)
     for masks in gather_rounds(count):
-        others = [lax.ppermute(buf, axis, [(i, i ^ m) for i in range(count)]) for m in masks]
+        others = [swap(buf, axis, m) for m in masks]
         for m, other in zip(masks, others):
             total = total + product(other, [m ^ q for q in entries])
         buf = jnp.concatenate([buf] + others, axis=0)
         entries = entries + [m ^ q for m in masks for q in entries]
-    own, for_partner = total[:rows], total[rows:]
-    if count == 1:
-        return own
-    return own + lax.ppermute(for_partner, axis, [(i, i ^ 1) for i in range(count)])
+    parts = total.reshape(4, rows, total.shape[-1])
+    got = swap(parts[1::2], axis, 1)
+    near = parts[0::2] + got
+    return near[0] + swap(near[1], axis, 2)
 
 
 def body(
@@ -174,10 +179,9 @@
     row = lax.broadcasted_iota(jnp.int32, (rows, cols), 0)
     recharge = partial + jnp.where(row == 0, corr_first[None, :], 0.0) + jnp.where(row == rows - 1, corr_last[None, :], 0.0)
 
-    partner_cov = lax.ppermute(cov_x, "gx", [(i, i ^ 1) for i in range(count)]) if count > 1 else cov_x
-    slab = jnp.concatenate(
-        [cx_slab(cov_x, offsets_x, me, rows), cx_slab(partner_cov, offsets_x, me ^ 1, rows)], axis=0
-    )
+    pair_cov = jnp.stack([cov_x, swap(cov_x, "gx", 1)])
+    quad_cov = jnp.concatenate([pair_cov, swap(pair_cov, "gx", 2)], axis=0)
+    slab = jnp.concatenate([cx_slab(quad_cov[m], offsets_x, me ^ m, rows) for m in range(4)], axis=0)
     mixed = mixed_rows(recharge, slab, "gx")
 
     nyb = offsets_y.shape[0]

time: 43 us -> 41.2 us (0.958)
  waiting for transfers between devices: 12.5 us -> 9.93 us
  other arithmetic: 3.4 us -> 1.28 us
  local copies, waits for them, and re-layouts: 4.43 us -> 6.32 us
  starting transfers between devices: 13.6 us -> 15.1 us
    ppermute x6 -> x7, waiting for transfers between devices: 12.4 us -> 9.93 us  [swap(): return lax.ppermute(value, axis, [(i, i ^ mask) for i in range(count)])]
    ppermute x6 -> x7, starting transfers between devices: 9.96 us -> 11.9 us  [swap(): return lax.ppermute(value, axis, [(i, i ^ mask) for i in range(count)])]
    gather x2 -> x4, local copies, waits for them, and re-layouts: 1.12 us -> 2.25 us  [cx_slab(): target = (row_block[:, None] + offsets[row_block]) % nxb]
    unnamed x14 -> x17, local copies, waits for them, and re-layouts: 0.04 us -> 0.92 us
    reduce_sum x1, other arithmetic: 0.97 us -> 0.09 us  [body(): corr_first = jnp.sum(layer_weight[:, None] * (-up_x0 * from_prev), axis=0)]
    broadcast_in_dim x1, other arithmetic: 0.95 us -> 0.08 us  [mixed_rows(): buf = local[None]]
    add x1, other arithmetic: 0.92 us -> 0.08 us  [body(): partial + jnp.where(row == 0, corr_first[None, :], 0.0)]
    gather x1 -> x0, local copies, waits for them, and re-layouts: 0.55 us -> none  [product(): jnp.take(per_device, me ^ jnp.array(masks, jnp.int32), axis=1)]
  transfers between devices with their start and end apart: 8 -> 9, of which waited for: 4 -> 5; matrix products, arithmetic and copies ran while one was open for 9% -> 15% of each run, Pallas kernels for 0% -> 12%
where the time goes in v5:
time: 41.2 us; the launch traced here: 41 us
  starting transfers between devices  15.1 us (37%)
  waiting for transfers between devices  9.93 us (24%)
  local copies, waits for them, and re-layouts  6.32 us (15%)
  Pallas kernels  5.04 us (12%)
  matrix products  2.21 us (5%)
  other arithmetic  1.28 us (3%)
  between operations  1.06 us (3%)
    ppermute x7, starting transfers between devices, swap(): return lax.ppermute(value, axis, [(i, i ^ mask) for i in range(count)])  11.9 us
    ppermute x7, waiting for transfers between devices, swap(): return lax.ppermute(value, axis, [(i, i ^ mask) for i in range(count)])  9.93 us
    pallas_call x1, Pallas kernels, stencil(): pl.pallas_call(stencil_kernel, grid=(depth // zc,), in_specs=[pl.BlockSpe...  5.04 us
    ppermute x2, starting transfers between devices, passed_along(): lax.ppermute(value, axis, [(source, source + steps) for source in range(f...  3.24 us
    gather x4, local copies, waits for them, and re-layouts, cx_slab(): target = (row_block[:, None] + offsets[row_block]) % nxb  2.25 us
    dot_general x4, matrix products, product(): jnp.dot(cols, piece.reshape(-1, piece.shape[-1]), precision=precise, pref...  1.25 us
    dot_general x1, matrix products, body(): jnp.einsum('xrkc,rikc->xri', picked, cov_y.reshape(nyb, BLK, cov_y.shape[...  0.96 us
    unnamed x17, local copies, waits for them, and re-layouts  0.92 us
  transfers between devices with their start and end apart: 9, of which 5 were waited for; matrix products, arithmetic and copies ran while one was open for 15% of the time, Pallas kernels for 12%

profile of v5, /device:TPU:0, one launch (start us, length us, event | category | flops | bytes accessed | tf_op | source)
XLA Modules:
  0.0 41.0 jit_solution(16619108809611355792)
XLA Ops:
  0.6 0.9 %copy.108 = bf16[16,4,128]{2,0,1:T(8,128)(2,1)S(1)} copy(bf16[16,4,128]{2,1,0:T(4,128)(2,1)} %param.24) | data formatting | bytes 32768 | tf_op args[7]
  1.5 0.5 %collective-permute-start.2 = (bf16[16,4,128]{2,0,1:T(8,128)(2,1)S(1)}, bf16[16,4,128]{2,0,1:T(8,128)(2,1)S(1)}, u32[]{:S(2)}, u32[]{:S(2)}) collective-permute-start(bf16[16,4,128]{2,0,1:T(8,128)(2,1)S(1)} %copy.108), channel_id=1, source_target_pairs={{0,1},{1,0},{2,3},{3,2},{4,5},{5,4},{6,7},{7,6},{8,9},{9,8},{10,11... | collective-permute-start | bytes 49160 | tf_op jit(solution)/shard_map/ppermute | solution.py:115
  2.0 5.0 %shard_map.158 = (f32[16,1024]{1,0:T(8,128)}, f32[2,16,1024]{2,1,0:T(8,128)}, f32[2,16,1024]{2,1,0:T(8,128)}) custom-call(f32[16]{0:T(128)} %w_ref.1, f32[16,16,1024]{2,1,0:T(8,128)} %sprev_ref.1, f32[16,16,1024]{2,1,0:T(8,128)} %sprev_ref.1, s32[16,16,1024]{2,1,0:T(8,128)} %f_ref.1, f32[16,16,1024]{2,1,0:T(8,128)} %vx_ref.1, f32[16,16,1024]{2,1,0:T(8,128)} %vy_ref.1, ...), custom_call_target="tpu_custom_call" | custom-call | tf_op jit(solution)/shard_map/pallas_call | solution.py:75
  7.1 0.9 %slice_bitcast_fusion.3 = f32[16,1024]{1,0:T(8,128)S(1)} fusion(f32[2,16,1024]{2,1,0:T(8,128)} %get-tuple-element.7), kind=kLoop, calls=%fused_computation.42 | loop fusion | bytes 131072 | tf_op jit(solution)/shard_map/squeeze | solution.py:172
  8.0 2.0 %collective-permute-start = (f32[16,1024]{1,0:T(8,128)S(1)}, f32[16,1024]{1,0:T(8,128)S(1)}, u32[]{:S(2)}, u32[]{:S(2)}) collective-permute-start(f32[16,1024]{1,0:T(8,128)S(1)} %slice_bitcast_fusion.3), channel_id=1, source_target_pairs={{0,1},{1,2},{2,3},{3,4},{4,5},{5,6},{6,7},{7,8},{8,9},{9,10},{10,1... | collective-permute-start | bytes 196616 | tf_op jit(solution)/shard_map/ppermute | solution.py:17
  10.0 1.3 %collective-permute-start.1 = (f32[2,16,1024]{2,1,0:T(8,128)}, f32[2,16,1024]{2,1,0:T(8,128)S(1)}, u32[]{:S(2)}, u32[]{:S(2)}) collective-permute-start(f32[2,16,1024]{2,1,0:T(8,128)} %get-tuple-element.8), channel_id=1, source_target_pairs={{1,0},{2,1},{3,2},{4,3},{5,4},{6,5},{7,6},{8,7},{9,8},{10,9},{11,1... | collective-permute-start | bytes 393224 | tf_op jit(solution)/shard_map/ppermute | solution.py:17
  11.4 0.6 %gather_fusion = s32[16,4]{1,0:T(8,128)S(1)} fusion(s32[2,4]{1,0:T(2,128)S(1)} %copy-done.1, s32[1024]{0:T(1024)S(1)} %pad_clamp_fusion.4), kind=kCustom, calls=%fused_computation | custom fusion | bytes 576 | tf_op jit(solution)/shard_map/gather | solution.py:122
  12.2 0.6 %gather_fusion.2 = s32[16,4]{1,0:T(8,128)S(1)} fusion(s32[2,4]{1,0:T(2,128)S(1)} %copy-done.1, s32[1024]{0:T(1024)S(1)} %pad_clamp_fusion.2), kind=kCustom, calls=%fused_computation.2 | custom fusion | bytes 576 | tf_op jit(solution)/shard_map/gather | solution.py:122
  12.9 0.6 %gather_fusion.3 = s32[16,4]{1,0:T(8,128)S(1)} fusion(s32[2,4]{1,0:T(2,128)S(1)} %copy-done.1, s32[1024]{0:T(1024)S(1)} %pad_clamp_fusion.1), kind=kCustom, calls=%fused_computation.3 | custom fusion | bytes 576 | tf_op jit(solution)/shard_map/gather | solution.py:122
  13.7 0.6 %gather_fusion.1 = s32[16,4]{1,0:T(8,128)S(1)} fusion(s32[2,4]{1,0:T(2,128)S(1)} %copy-done.1, s32[1024]{0:T(1024)S(1)} %pad_clamp_fusion.3), kind=kCustom, calls=%fused_computation.1 | custom fusion | bytes 576 | tf_op jit(solution)/shard_map/gather | solution.py:122
  14.5 0.1 copy.89
  14.7 4.9 %collective-permute-start.3 = (bf16[2,16,4,128]{3,1,2,0:T(8,128)(2,1)S(1)}, bf16[2,16,4,128]{3,1,2,0:T(8,128)(2,1)S(1)}, u32[]{:S(2)}, u32[]{:S(2)}) collective-permute-start(bf16[2,16,4,128]{3,1,2,0:T(8,128)(2,1)S(1)} %pad_maximum_fusion.1), channel_id=1, source_target_pairs={{0,2},{1,3},{2,0},{3,1},{4,6},{5,7},{6,4},{7,5},{8,10},{9,11},{10,... | collective-permute-start | bytes 98312 | tf_op jit(solution)/shard_map/ppermute | solution.py:115
  19.7 0.1 copy.90
  19.8 1.7 %collective-permute-done.3 = bf16[2,16,4,128]{3,1,2,0:T(8,128)(2,1)S(1)} collective-permute-done((bf16[2,16,4,128]{3,1,2,0:T(8,128)(2,1)S(1)}, bf16[2,16,4,128]{3,1,2,0:T(8,128)(2,1)S(1)}, u32[]{:S(2)}, u32[]{:S(2)}) %collective-permute-start.3) | collective-permute-done | bytes 32800 | tf_op jit(solution)/shard_map/ppermute | solution.py:115
  21.7 0.1 copy.92
  21.8 0.1 copy.91
  21.9 0.2 pad_maximum_fusion
  22.4 5.1 %collective-permute-start.6 = (f32[1,16,1024]{2,1,0:T(8,128)S(1)}, f32[1,16,1024]{2,1,0:T(8,128)S(1)}, u32[]{:S(2)}, u32[]{:S(2)}) collective-permute-start(f32[1,16,1024]{2,1,0:T(8,128)S(1)} %fusion.65), channel_id=1, source_target_pairs={{0,12},{1,13},{2,14},{3,15},{4,8},{5,9},{6,10},{7,11},{8,4},{9,5},... | collective-permute-start | bytes 196616 | tf_op jit(solution)/shard_map/ppermute | solution.py:115
  27.5 0.6 %collective-permute-start.4 = (f32[1,16,1024]{2,1,0:T(8,128)S(1)}, f32[1,16,1024]{2,1,0:T(8,128)S(1)}, u32[]{:S(2)}, u32[]{:S(2)}) collective-permute-start(f32[1,16,1024]{2,1,0:T(8,128)S(1)} %fusion.65), channel_id=1, source_target_pairs={{0,4},{1,5},{2,6},{3,7},{4,0},{5,1},{6,2},{7,3},{8,12},{9,13},{10,... | collective-permute-start | bytes 196616 | tf_op jit(solution)/shard_map/ppermute | solution.py:115
  28.1 0.3 fusion.32
  28.4 3.3 %collective-permute-done.4 = f32[1,16,1024]{2,1,0:T(8,128)S(1)} collective-permute-done((f32[1,16,1024]{2,1,0:T(8,128)S(1)}, f32[1,16,1024]{2,1,0:T(8,128)S(1)}, u32[]{:S(2)}, u32[]{:S(2)}) %collective-permute-start.4) | collective-permute-done | bytes 65568 | tf_op jit(solution)/shard_map/ppermute | solution.py:115
  31.7 0.3 convolution_add_fusion.1
  32.1 0.3 fusion.17
  32.4 0.2 collective-permute-done.5
  32.6 0.3 fusion.2
  33.1 0.1 copy.68
  33.3 1.0 %collective-permute-done.7 = f32[2,16,1024]{2,1,0:T(8,128)S(1)} collective-permute-done((f32[2,16,1024]{2,1,0:T(8,128)S(1)}, f32[2,16,1024]{2,1,0:T(8,128)S(1)}, u32[]{:S(2)}, u32[]{:S(2)}) %collective-permute-start.7) | collective-permute-done | bytes 131104 | tf_op jit(solution)/shard_map/ppermute | solution.py:115
  34.4 0.7 %collective-permute-start.8 = (f32[16,1024]{1,0:T(8,128)S(1)}, f32[16,1024]{1,0:T(8,128)S(1)}, u32[]{:S(2)}, u32[]{:S(2)}) collective-permute-start(f32[16,1024]{1,0:T(8,128)S(1)} %slice_bitcast_fusion), channel_id=1, source_target_pairs={{0,2},{1,3},{2,0},{3,1},{4,6},{5,7},{6,4},{7,5},{8,10},{9,11},{10,... | collective-permute-start | bytes 196616 | tf_op jit(solution)/shard_map/ppermute | solution.py:115
  35.1 3.6 %collective-permute-done.8 = f32[16,1024]{1,0:T(8,128)S(1)} collective-permute-done((f32[16,1024]{1,0:T(8,128)S(1)}, f32[16,1024]{1,0:T(8,128)S(1)}, u32[]{:S(2)}, u32[]{:S(2)}) %collective-permute-start.8) | collective-permute-done | bytes 65568 | tf_op jit(solution)/shard_map/ppermute | solution.py:115
  38.8 0.6 %gather_fusion.4 = f32[32,16,128]{2,1,0:T(8,128)S(1)} fusion(f32[16,8,128]{2,0,1:T(8,128)S(1)} %copy_bitcast_fusion.1, s32[1024]{0:T(1024)S(1)} %pad_clamp_fusion), kind=kCustom, calls=%fused_computation.4 | custom fusion | bytes 524416 | tf_op jit(solution)/shard_map/jit(_take)/gather | solution.py:189
  39.4 1.0 %fusion.3 = f32[8,2,8,128]{3,2,1,0:T(8,128)S(1)} fusion(f32[8,128,4,128]{3,2,1,0:T(4,128)S(1)} %bitcast.112, f32[8,4,16,128]{3,2,1,0:T(8,128)S(1)} %bitcast.113, pred[8,4]{1,0:T(8,128)(4,1)S(1)} %copy.68), kind=kOutput, calls=%fused_computation.10 | convolution fusion | flops 50397184 | bytes 2424864 | tf_op jit(solution)/shard_map/xrkc,rikc->xri/dot_general | solution.py:190
  40.3 0.7 %copy.107 = f32[8,2,8,128]{3,2,0,1:T(8,128)} copy(f32[8,2,8,128]{3,2,1,0:T(8,128)S(1)} %fusion.3) | data formatting | bytes 131072 | tf_op jit(solution)/shard_map/reshape | solution.py:196
  (62 shorter events, 1.7 us)
Async XLA Ops:
  0.6 38.7 %copy-start = (f32[1024,4,128]{2,1,0:T(4,128)S(1)}, f32[1024,4,128]{2,1,0:T(4,128)}, u32[]{:S(2)}) copy-start(f32[1024,4,128]{2,1,0:T(4,128)} %param.26) | copy-start | bytes 6291460
  1.5 9.8 %copy-start.5 = (bf16[16,4,128]{2,1,0:T(4,128)(2,1)S(1)}, bf16[16,4,128]{2,1,0:T(4,128)(2,1)}, u32[]{:S(2)}) copy-start(bf16[16,4,128]{2,1,0:T(4,128)(2,1)} %param.24) | copy-start | bytes 49156
  1.5 9.9 %copy-start.1 = (s32[2,4]{1,0:T(2,128)S(1)}, s32[2,4]{1,0:T(2,128)}, u32[]{:S(2)}) copy-start(s32[2,4]{1,0:T(2,128)} %param.25) | copy-start | bytes 100
  1.5 13.1 %collective-permute-start.2 = (bf16[16,4,128]{2,0,1:T(8,128)(2,1)S(1)}, bf16[16,4,128]{2,0,1:T(8,128)(2,1)S(1)}, u32[]{:S(2)}, u32[]{:S(2)}) collective-permute-start(bf16[16,4,128]{2,0,1:T(8,128)(2,1)S(1)} %copy.108), channel_id=1, source_target_pairs={{0,1},{1,0},{2,3},{3,2},{4,5},{5,4},{6,7},{7,6},{8,9},{9,8},{10,11... | collective-permute-start | bytes 49160 | tf_op jit(solution)/shard_map/ppermute | solution.py:115
  7.1 15.0 %copy-start.2 = (f32[2,16,1024]{2,1,0:T(8,128)S(1)}, f32[2,16,1024]{2,1,0:T(8,128)}, u32[]{:S(2)}) copy-start(f32[2,16,1024]{2,1,0:T(8,128)} %get-tuple-element.7) | copy-start | bytes 393220
  7.1 15.0 %copy-start.7 = (f32[16]{0:T(128)S(1)}, f32[16]{0:T(128)}, u32[]{:S(2)}) copy-start(f32[16]{0:T(128)} %w_ref.1) | copy-start | bytes 196
  7.1 15.1 %copy-start.3 = (f32[16,1024]{1,0:T(8,128)S(1)}, f32[16,1024]{1,0:T(8,128)}, u32[]{:S(2)}) copy-start(f32[16,1024]{1,0:T(8,128)} %get-tuple-element.6) | copy-start | bytes 196612
  8.0 14.0 %collective-permute-start = (f32[16,1024]{1,0:T(8,128)S(1)}, f32[16,1024]{1,0:T(8,128)S(1)}, u32[]{:S(2)}, u32[]{:S(2)}) collective-permute-start(f32[16,1024]{1,0:T(8,128)S(1)} %slice_bitcast_fusion.3), channel_id=1, source_target_pairs={{0,1},{1,2},{2,3},{3,4},{4,5},{5,6},{6,7},{7,8},{8,9},{9,10},{10,1... | collective-permute-start | bytes 196616 | tf_op jit(solution)/shard_map/ppermute | solution.py:17
  10.0 12.1 %collective-permute-start.1 = (f32[2,16,1024]{2,1,0:T(8,128)}, f32[2,16,1024]{2,1,0:T(8,128)S(1)}, u32[]{:S(2)}, u32[]{:S(2)}) collective-permute-start(f32[2,16,1024]{2,1,0:T(8,128)} %get-tuple-element.8), channel_id=1, source_target_pairs={{1,0},{2,1},{3,2},{4,3},{5,4},{6,5},{7,6},{8,7},{9,8},{10,9},{11,1... | collective-permute-start | bytes 393224 | tf_op jit(solution)/shard_map/ppermute | solution.py:17
  14.7 6.8 %collective-permute-start.3 = (bf16[2,16,4,128]{3,1,2,0:T(8,128)(2,1)S(1)}, bf16[2,16,4,128]{3,1,2,0:T(8,128)(2,1)S(1)}, u32[]{:S(2)}, u32[]{:S(2)}) collective-permute-start(bf16[2,16,4,128]{3,1,2,0:T(8,128)(2,1)S(1)} %pad_maximum_fusion.1), channel_id=1, source_target_pairs={{0,2},{1,3},{2,0},{3,1},{4,6},{5,7},{6,4},{7,5},{8,10},{9,11},{10,... | collective-permute-start | bytes 98312 | tf_op jit(solution)/shard_map/ppermute | solution.py:115
  19.8 13.3 %copy-start.6 = (s32[8,4]{0,1:T(4,128)S(1)}, s32[8,4]{0,1:T(4,128)}, u32[]{:S(2)}) copy-start(s32[8,4]{0,1:T(4,128)} %param.27) | copy-start | bytes 388
  22.4 18.0 %copy-start.4 = (f32[16,1024]{1,0:T(8,128)}, f32[16,1024]{1,0:T(8,128)S(1)}, u32[]{:S(2)}) copy-start(f32[16,1024]{1,0:T(8,128)S(1)} %select_add_fusion) | copy-start | bytes 196612
  22.4 9.7 %collective-permute-start.6 = (f32[1,16,1024]{2,1,0:T(8,128)S(1)}, f32[1,16,1024]{2,1,0:T(8,128)S(1)}, u32[]{:S(2)}, u32[]{:S(2)}) collective-permute-start(f32[1,16,1024]{2,1,0:T(8,128)S(1)} %fusion.65), channel_id=1, source_target_pairs={{0,12},{1,13},{2,14},{3,15},{4,8},{5,9},{6,10},{7,11},{8,4},{9,5},... | collective-permute-start | bytes 196616 | tf_op jit(solution)/shard_map/ppermute | solution.py:115
  27.5 5.2 %collective-permute-start.5 = (f32[1,16,1024]{2,1,0:T(8,128)S(1)}, f32[1,16,1024]{2,1,0:T(8,128)S(1)}, u32[]{:S(2)}, u32[]{:S(2)}) collective-permute-start(f32[1,16,1024]{2,1,0:T(8,128)S(1)} %fusion.65), channel_id=1, source_target_pairs={{0,8},{1,9},{2,10},{3,11},{4,12},{5,13},{6,14},{7,15},{8,0},{9,1},... | collective-permute-start | bytes 196616 | tf_op jit(solution)/shard_map/ppermute | solution.py:115
  27.5 4.3 %collective-permute-start.4 = (f32[1,16,1024]{2,1,0:T(8,128)S(1)}, f32[1,16,1024]{2,1,0:T(8,128)S(1)}, u32[]{:S(2)}, u32[]{:S(2)}) collective-permute-start(f32[1,16,1024]{2,1,0:T(8,128)S(1)} %fusion.65), channel_id=1, source_target_pairs={{0,4},{1,5},{2,6},{3,7},{4,0},{5,1},{6,2},{7,3},{8,12},{9,13},{10,... | collective-permute-start | bytes 196616 | tf_op jit(solution)/shard_map/ppermute | solution.py:115
  33.0 1.4 %collective-permute-start.7 = (f32[2,16,1024]{2,1,0:T(8,128)S(1)}, f32[2,16,1024]{2,1,0:T(8,128)S(1)}, u32[]{:S(2)}, u32[]{:S(2)}) collective-permute-start(f32[2,16,1024]{2,1,0:T(8,128)S(1)} %slice.37), channel_id=1, source_target_pairs={{0,1},{1,0},{2,3},{3,2},{4,5},{5,4},{6,7},{7,6},{8,9},{9,8},{10,11... | collective-permute-start | bytes 393224 | tf_op jit(solution)/shard_map/ppermute | solution.py:115
  34.4 4.3 %collective-permute-start.8 = (f32[16,1024]{1,0:T(8,128)S(1)}, f32[16,1024]{1,0:T(8,128)S(1)}, u32[]{:S(2)}, u32[]{:S(2)}) collective-permute-start(f32[16,1024]{1,0:T(8,128)S(1)} %slice_bitcast_fusion), channel_id=1, source_target_pairs={{0,2},{1,3},{2,0},{3,1},{4,6},{5,7},{6,4},{7,5},{8,10},{9,11},{10,... | collective-permute-start | bytes 196616 | tf_op jit(solution)/shard_map/ppermute | solution.py:115

commit v6 on v5

--- a/solution.py
+++ b/solution.py
@@ -6,7 +6,7 @@
 from jax.sharding import PartitionSpec as P
 
 BLK = 128
-Z_CHUNK = 4
+Z_CHUNK = 8
 
 precise = lax.Precision.HIGH
 
@@ -24,7 +24,7 @@
     return lower, upper
 
 
-def stencil_kernel(w_ref, s_ref, sprev_ref, f_ref, vx_ref, vy_ref, vz_ref, d_ref, out_ref, to_prev_ref, edge_ref):
+def stencil_kernel(w_ref, s_ref, sprev_ref, f_ref, vx_ref, vy_ref, vz_ref, d_ref, out_ref, to_prev_ref, last_ref, up_ref):
     c = pl.program_id(0)
     rows, cols = out_ref.shape
     sub = lax.broadcasted_iota(jnp.int32, (rows, cols), 0)
@@ -44,8 +44,8 @@
         lo_x, up_x = coefs(f, 1, vx_ref[j], d)
         to_prev_ref[0, pl.ds(z, 1), :] = s[0:1, :]
         to_prev_ref[1, pl.ds(z, 1), :] = lo_x[0:1, :]
-        edge_ref[0, pl.ds(z, 1), :] = s[rows - 1:rows, :]
-        edge_ref[1, pl.ds(z, 1), :] = up_x[0:1, :]
+        last_ref[pl.ds(z, 1), :] = s[rows - 1:rows, :]
+        up_ref[pl.ds(z, 1), :] = up_x[0:1, :]
         lo_y, up_y = coefs(f, 2, vy_ref[j], d)
         lo_z, up_z = coefs(f, 4, vz_ref[j], d)
         s_xm = jnp.where(sub == 0, 0.0, pltpu.roll(s, 1, 0))
@@ -88,12 +88,14 @@
         out_specs=[
             pl.BlockSpec((rows, cols), lambda c: (0, 0)),
             pl.BlockSpec((2, depth, cols), lambda c: (0, 0, 0)),
-            pl.BlockSpec((2, depth, cols), lambda c: (0, 0, 0)),
+            pl.BlockSpec((depth, cols), lambda c: (0, 0)),
+            pl.BlockSpec((depth, cols), lambda c: (0, 0)),
         ],
         out_shape=[
             jax.ShapeDtypeStruct((rows, cols), jnp.float32),
             jax.ShapeDtypeStruct((2, depth, cols), jnp.float32),
-            jax.ShapeDtypeStruct((2, depth, cols), jnp.float32),
+            jax.ShapeDtypeStruct((depth, cols), jnp.float32),
+            jax.ShapeDtypeStruct((depth, cols), jnp.float32),
         ],
         compiler_params=pltpu.CompilerParams(dimension_semantics=("arbitrary",)),
     )(layer_weight, s, s, f, vx, vy, vz, d)
@@ -168,8 +170,9 @@
     me = lax.axis_index("gx")
     depth, rows, cols = adjoint_state.shape
 
-    partial, to_prev, edge = stencil(layer_weight, adjoint_state, face_flags, speed_x, speed_y, speed_z, dispersion)
-    last_s, up_x0 = edge[0], edge[1]
+    partial, to_prev, last_s, up_x0 = stencil(
+        layer_weight, adjoint_state, face_flags, speed_x, speed_y, speed_z, dispersion
+    )
     from_next = passed_along(to_prev, "gx", -1)
     from_prev = passed_along(last_s, "gx", 1)
 
@@ -179,9 +182,9 @@
     row = lax.broadcasted_iota(jnp.int32, (rows, cols), 0)
     recharge = partial + jnp.where(row == 0, corr_first[None, :], 0.0) + jnp.where(row == rows - 1, corr_last[None, :], 0.0)
 
-    pair_cov = jnp.stack([cov_x, swap(cov_x, "gx", 1)])
-    quad_cov = jnp.concatenate([pair_cov, swap(pair_cov, "gx", 2)], axis=0)
-    slab = jnp.concatenate([cx_slab(quad_cov[m], offsets_x, me ^ m, rows) for m in range(4)], axis=0)
+    own_slab = cx_slab(cov_x, offsets_x, me, rows)
+    pair_slab = jnp.concatenate([own_slab, swap(own_slab, "gx", 1)], axis=0)
+    slab = jnp.concatenate([pair_slab, swap(pair_slab, "gx", 2)], axis=0)
     mixed = mixed_rows(recharge, slab, "gx")
 
     nyb = offsets_y.shape[0]

time: 41.2 us -> 42.1 us (1.022)
  waiting for transfers between devices: 9.93 us -> 12.6 us
  local copies, waits for them, and re-layouts: 6.32 us -> 4.03 us
  other arithmetic: 1.28 us -> 3.21 us
  starting transfers between devices: 15.1 us -> 14.3 us
  Pallas kernels: 5.04 us -> 4.48 us
    ppermute x7, waiting for transfers between devices: 9.93 us -> 12.6 us  [swap(): return lax.ppermute(value, axis, [(i, i ^ mask) for i in range(count)])]
    squeeze x1 -> x0, local copies, waits for them, and re-layouts: 0.9 us -> none  [body(): last_s, up_x0 = (edge[0], edge[1])]
    unnamed x17 -> x8, local copies, waits for them, and re-layouts: 0.92 us -> 0.03 us
    reduce_sum x1, other arithmetic: 0.09 us -> 0.97 us  [body(): corr_first = jnp.sum(layer_weight[:, None] * (-up_x0 * from_prev), axis=0)]
    gather x4 -> x1, local copies, waits for them, and re-layouts: 2.25 us -> 1.38 us  [cx_slab(): target = (row_block[:, None] + offsets[row_block]) % nxb]
    add x1, other arithmetic: 0.08 us -> 0.92 us  [body(): partial + jnp.where(row == 0, corr_first[None, :], 0.0)]
    broadcast_in_dim x1, other arithmetic: 0.08 us -> 0.92 us  [mixed_rows(): buf = local[None]]
    ppermute x7, starting transfers between devices: 11.9 us -> 11.1 us  [swap(): return lax.ppermute(value, axis, [(i, i ^ mask) for i in range(count)])]
  transfers between devices with their start and end apart: 9 -> 9, of which waited for: 5 -> 5; matrix products, arithmetic and copies ran while one was open for 15% -> 4% of each run, Pallas kernels for 12% -> 11%
where the time goes in v6:
time: 42.1 us; the launch traced here: 41.8 us
  starting transfers between devices  14.3 us (34%)
  waiting for transfers between devices  12.6 us (30%)
  Pallas kernels  4.48 us (11%)
  local copies, waits for them, and re-layouts  4.03 us (10%)
  other arithmetic  3.21 us (8%)
  matrix products  2.22 us (5%)
  between operations  0.9 us (2%)
    ppermute x7, waiting for transfers between devices, swap(): return lax.ppermute(value, axis, [(i, i ^ mask) for i in range(count)])  12.6 us
    ppermute x7, starting transfers between devices, swap(): return lax.ppermute(value, axis, [(i, i ^ mask) for i in range(count)])  11.1 us
    pallas_call x1, Pallas kernels, stencil(): pl.pallas_call(stencil_kernel, grid=(depth // zc,), in_specs=[pl.BlockSpe...  4.48 us
    ppermute x2, starting transfers between devices, passed_along(): lax.ppermute(value, axis, [(source, source + steps) for source in range(f...  3.26 us
    gather x1, local copies, waits for them, and re-layouts, cx_slab(): target = (row_block[:, None] + offsets[row_block]) % nxb  1.38 us
    dot_general x4, matrix products, product(): jnp.dot(cols, piece.reshape(-1, piece.shape[-1]), precision=precise, pref...  1.26 us
    reduce_sum x1, other arithmetic, body(): corr_first = jnp.sum(layer_weight[:, None] * (-up_x0 * from_prev), axis=0)  0.97 us
    dot_general x1, matrix products, body(): jnp.einsum('xrkc,rikc->xri', picked, cov_y.reshape(nyb, BLK, cov_y.shape[...  0.96 us
  transfers between devices with their start and end apart: 9, of which 5 were waited for; matrix products, arithmetic and copies ran while one was open for 4% of the time, Pallas kernels for 11%

profile of v6, /device:TPU:0, one launch (start us, length us, event | category | flops | bytes accessed | tf_op | source)
XLA Modules:
  0.0 41.8 jit_solution(8476489843801679968)
XLA Ops:
  0.7 1.4 %gather_fusion = s32[16,4]{1,0:T(8,128)S(1)} fusion(s32[2,4]{1,0:T(2,128)} %param.25, s32[1024]{0:T(1024)S(1)} %pad_clamp_fusion.1), kind=kCustom, calls=%fused_computation | custom fusion | bytes 576 | tf_op jit(solution)/shard_map/gather | solution.py:124
  2.2 0.1 copy.47
  2.3 0.7 %copy.48 = f32[16,4,128]{2,0,1:T(8,128)S(1)} copy(bf16[16,4,128]{2,1,0:T(4,128)(2,1)} %param.24) | data formatting | bytes 49152 | tf_op jit(solution)/shard_map/convert_element_type | solution.py:127
  3.0 0.1 select_reduce_fusion
  3.1 0.5 %collective-permute-start.2 = (f32[16,256]{1,0:T(8,128)S(1)}, f32[16,256]{1,0:T(8,128)S(1)}, u32[]{:S(2)}, u32[]{:S(2)}) collective-permute-start(f32[16,256]{1,0:T(8,128)S(1)} %copy_bitcast_fusion.2), channel_id=1, source_target_pairs={{0,1},{1,0},{2,3},{3,2},{4,5},{5,4},{6,7},{7,6},{8,9},{9,8},{10,11... | collective-permute-start | bytes 49160 | tf_op jit(solution)/shard_map/ppermute | solution.py:117
  3.6 4.5 %shard_map.158 = (f32[16,1024]{1,0:T(8,128)}, f32[2,16,1024]{2,1,0:T(8,128)}, f32[16,1024]{1,0:T(8,128)}, f32[16,1024]{1,0:T(8,128)}) custom-call(f32[16]{0:T(128)} %w_ref.1, f32[16,16,1024]{2,1,0:T(8,128)} %sprev_ref.1, f32[16,16,1024]{2,1,0:T(8,128)} %sprev_ref.1, s32[16,16,1024]{2,1,0:T(8,128)} %f_ref.1, f32[16,16,1024]{2,1,0:T(8,128)} %vx_ref.1, ...), custom_call_target="tpu_custom_call" | custom-call | tf_op jit(solution)/shard_map/pallas_call | solution.py:75
  8.1 2.0 %collective-permute-start = (f32[16,1024]{1,0:T(8,128)}, f32[16,1024]{1,0:T(8,128)S(1)}, u32[]{:S(2)}, u32[]{:S(2)}) collective-permute-start(f32[16,1024]{1,0:T(8,128)} %get-tuple-element.9), channel_id=1, source_target_pairs={{0,1},{1,2},{2,3},{3,4},{4,5},{5,6},{6,7},{7,8},{8,9},{9,10},{10,1... | collective-permute-start | bytes 196616 | tf_op jit(solution)/shard_map/ppermute | solution.py:17
  10.1 1.3 %collective-permute-start.1 = (f32[2,16,1024]{2,1,0:T(8,128)}, f32[2,16,1024]{2,1,0:T(8,128)S(1)}, u32[]{:S(2)}, u32[]{:S(2)}) collective-permute-start(f32[2,16,1024]{2,1,0:T(8,128)} %get-tuple-element.10), channel_id=1, source_target_pairs={{1,0},{2,1},{3,2},{4,3},{5,4},{6,5},{7,6},{8,7},{9,8},{10,9},{11,1... | collective-permute-start | bytes 393224 | tf_op jit(solution)/shard_map/ppermute | solution.py:17
  11.4 0.1 copy.51
  11.5 4.9 %collective-permute-start.3 = (f32[32,256]{0,1:T(8,128)S(1)}, f32[32,256]{0,1:T(8,128)S(1)}, u32[]{:S(2)}, u32[]{:S(2)}) collective-permute-start(f32[32,256]{0,1:T(8,128)S(1)} %copy.51), channel_id=1, source_target_pairs={{0,2},{1,3},{2,0},{3,1},{4,6},{5,7},{6,4},{7,5},{8,10},{9,11},{10,... | collective-permute-start | bytes 98312 | tf_op jit(solution)/shard_map/ppermute | solution.py:117
  16.4 0.1 copy.59
  16.5 0.1 copy.60
  16.6 5.0 %collective-permute-done.3 = f32[32,256]{0,1:T(8,128)S(1)} collective-permute-done((f32[32,256]{0,1:T(8,128)S(1)}, f32[32,256]{0,1:T(8,128)S(1)}, u32[]{:S(2)}, u32[]{:S(2)}) %collective-permute-start.3) | collective-permute-done | bytes 32800 | tf_op jit(solution)/shard_map/ppermute | solution.py:117
  21.6 0.1 pad_maximum_fusion
  21.8 1.0 %multiply_reduce_fusion = (f32[1024]{0:T(1024)S(1)}, f32[1024]{0:T(1024)S(1)}) fusion(f32[16,1024]{1,0:T(8,128)S(1)} %collective-permute-done, f32[16,1024]{1,0:T(8,128)} %get-tuple-element.8, f32[16]{0:T(128)S(1)} %copy-done.3, f32[16,1024]{1,0:T(8,128)} %get-tuple-element.9, f32[2,16,1024]{2,1,0:T(8,128)S(1)} %collective-permute-done.1), kind=kLoop, calls=%fused_computation.33 | loop fusion | flops 145408 | bytes 335936 | tf_op jit(solution)/shard_map/reduce_sum | solution.py:179
  22.7 0.9 %fusion.55 = f32[1,16,1024]{2,1,0:T(8,128)S(1)} fusion(f32[1024]{0:T(1024)S(1)} %get-tuple-element.23, pred[16]{0:T(512)(128)(4,1)S(1)} %get-tuple-element.26, f32[16,1024]{1,0:T(8,128)} %get-tuple-element.7, f32[1024]{0:T(1024)S(1)} %get-tuple-element.22, pred[16]{0:T(512)(128)(4,1)S(1)} %get-tuple-element.27), kind=kLoop, calls=%fused_computation.91 | loop fusion | flops 65536 | bytes 139296 | tf_op jit(solution)/shard_map/broadcast_in_dim | solution.py:141
  23.7 0.9 %select_add_fusion = f32[16,1024]{1,0:T(8,128)S(1)} fusion(f32[16,1024]{1,0:T(8,128)} %get-tuple-element.7, f32[1024]{0:T(1024)S(1)} %get-tuple-element.23, f32[1024]{0:T(1024)S(1)} %get-tuple-element.22, pred[16]{0:T(512)(128)(4,1)S(1)} %get-tuple-element.26, pred[16]{0:T(512)(128)(4,1)S(1)} %get-tuple-element.27), kind=kLoop, calls=%fused_computation.32 | loop fusion | flops 65536 | bytes 139296 | tf_op jit(solution)/shard_map/add | solution.py:183
  24.6 3.7 %collective-permute-start.6 = (f32[1,16,1024]{2,1,0:T(8,128)S(1)}, f32[1,16,1024]{2,1,0:T(8,128)S(1)}, u32[]{:S(2)}, u32[]{:S(2)}) collective-permute-start(f32[1,16,1024]{2,1,0:T(8,128)S(1)} %fusion.55), channel_id=1, source_target_pairs={{0,12},{1,13},{2,14},{3,15},{4,8},{5,9},{6,10},{7,11},{8,4},{9,5},... | collective-permute-start | bytes 196616 | tf_op jit(solution)/shard_map/ppermute | solution.py:117
  28.3 0.8 %collective-permute-start.4 = (f32[1,16,1024]{2,1,0:T(8,128)S(1)}, f32[1,16,1024]{2,1,0:T(8,128)S(1)}, u32[]{:S(2)}, u32[]{:S(2)}) collective-permute-start(f32[1,16,1024]{2,1,0:T(8,128)S(1)} %fusion.55), channel_id=1, source_target_pairs={{0,4},{1,5},{2,6},{3,7},{4,0},{5,1},{6,2},{7,3},{8,12},{9,13},{10,... | collective-permute-start | bytes 196616 | tf_op jit(solution)/shard_map/ppermute | solution.py:117
  29.0 0.3 fusion.25
  29.4 3.2 %collective-permute-done.4 = f32[1,16,1024]{2,1,0:T(8,128)S(1)} collective-permute-done((f32[1,16,1024]{2,1,0:T(8,128)S(1)}, f32[1,16,1024]{2,1,0:T(8,128)S(1)}, u32[]{:S(2)}, u32[]{:S(2)}) %collective-permute-start.4) | collective-permute-done | bytes 65568 | tf_op jit(solution)/shard_map/ppermute | solution.py:117
  32.5 0.3 convolution_add_fusion.1
  32.9 0.3 fusion.17
  33.2 0.2 collective-permute-done.5
  33.4 0.3 fusion.2
  33.9 0.1 copy.46
  34.1 1.0 %collective-permute-done.7 = f32[2,16,1024]{2,1,0:T(8,128)S(1)} collective-permute-done((f32[2,16,1024]{2,1,0:T(8,128)S(1)}, f32[2,16,1024]{2,1,0:T(8,128)S(1)}, u32[]{:S(2)}, u32[]{:S(2)}) %collective-permute-start.7) | collective-permute-done | bytes 131104 | tf_op jit(solution)/shard_map/ppermute | solution.py:117
  35.2 1.1 %collective-permute-start.8 = (f32[16,1024]{1,0:T(8,128)S(1)}, f32[16,1024]{1,0:T(8,128)S(1)}, u32[]{:S(2)}, u32[]{:S(2)}) collective-permute-start(f32[16,1024]{1,0:T(8,128)S(1)} %slice_bitcast_fusion), channel_id=1, source_target_pairs={{0,2},{1,3},{2,0},{3,1},{4,6},{5,7},{6,4},{7,5},{8,10},{9,11},{10,... | collective-permute-start | bytes 196616 | tf_op jit(solution)/shard_map/ppermute | solution.py:117
  36.4 3.2 %collective-permute-done.8 = f32[16,1024]{1,0:T(8,128)S(1)} collective-permute-done((f32[16,1024]{1,0:T(8,128)S(1)}, f32[16,1024]{1,0:T(8,128)S(1)}, u32[]{:S(2)}, u32[]{:S(2)}) %collective-permute-start.8) | collective-permute-done | bytes 65568 | tf_op jit(solution)/shard_map/ppermute | solution.py:117
  39.6 0.6 %gather_fusion.1 = f32[32,16,128]{2,1,0:T(8,128)S(1)} fusion(f32[16,8,128]{2,0,1:T(8,128)S(1)} %copy_bitcast_fusion.1, s32[1024]{0:T(1024)S(1)} %pad_clamp_fusion), kind=kCustom, calls=%fused_computation.1 | custom fusion | bytes 524416 | tf_op jit(solution)/shard_map/jit(_take)/gather | solution.py:192
  40.2 1.0 %fusion.3 = f32[8,2,8,128]{3,2,1,0:T(8,128)S(1)} fusion(f32[8,128,4,128]{3,2,1,0:T(4,128)S(1)} %bitcast.86, f32[8,4,16,128]{3,2,1,0:T(8,128)S(1)} %bitcast.87, pred[8,4]{1,0:T(8,128)(4,1)S(1)} %copy.46), kind=kOutput, calls=%fused_computation.7 | convolution fusion | flops 50397184 | bytes 2424864 | tf_op jit(solution)/shard_map/xrkc,rikc->xri/dot_general | solution.py:193
  41.1 0.7 %copy.72 = f32[8,2,8,128]{3,2,0,1:T(8,128)} copy(f32[8,2,8,128]{3,2,1,0:T(8,128)S(1)} %fusion.3) | data formatting | bytes 131072 | tf_op jit(solution)/shard_map/reshape | solution.py:199
  (30 shorter events, 0.5 us)
Async XLA Ops:
  0.6 39.5 %copy-start = (f32[1024,4,128]{2,1,0:T(4,128)S(1)}, f32[1024,4,128]{2,1,0:T(4,128)}, u32[]{:S(2)}) copy-start(f32[1024,4,128]{2,1,0:T(4,128)} %param.26) | copy-start | bytes 6291460
  3.1 18.7 %copy-start.3 = (f32[16]{0:T(128)S(1)}, f32[16]{0:T(128)}, u32[]{:S(2)}) copy-start(f32[16]{0:T(128)} %w_ref.1) | copy-start | bytes 196
  3.1 8.3 %collective-permute-start.2 = (f32[16,256]{1,0:T(8,128)S(1)}, f32[16,256]{1,0:T(8,128)S(1)}, u32[]{:S(2)}, u32[]{:S(2)}) collective-permute-start(f32[16,256]{1,0:T(8,128)S(1)} %copy_bitcast_fusion.2), channel_id=1, source_target_pairs={{0,1},{1,0},{2,3},{3,2},{4,5},{5,4},{6,7},{7,6},{8,9},{9,8},{10,11... | collective-permute-start | bytes 49160 | tf_op jit(solution)/shard_map/ppermute | solution.py:117
  8.1 25.7 %copy-start.2 = (s32[8,4]{0,1:T(4,128)S(1)}, s32[8,4]{0,1:T(4,128)}, u32[]{:S(2)}) copy-start(s32[8,4]{0,1:T(4,128)} %param.27) | copy-start | bytes 388
  8.1 13.6 %collective-permute-start = (f32[16,1024]{1,0:T(8,128)}, f32[16,1024]{1,0:T(8,128)S(1)}, u32[]{:S(2)}, u32[]{:S(2)}) collective-permute-start(f32[16,1024]{1,0:T(8,128)} %get-tuple-element.9), channel_id=1, source_target_pairs={{0,1},{1,2},{2,3},{3,4},{4,5},{5,6},{6,7},{7,8},{8,9},{9,10},{10,1... | collective-permute-start | bytes 196616 | tf_op jit(solution)/shard_map/ppermute | solution.py:17
  10.1 11.7 %collective-permute-start.1 = (f32[2,16,1024]{2,1,0:T(8,128)}, f32[2,16,1024]{2,1,0:T(8,128)S(1)}, u32[]{:S(2)}, u32[]{:S(2)}) collective-permute-start(f32[2,16,1024]{2,1,0:T(8,128)} %get-tuple-element.10), channel_id=1, source_target_pairs={{1,0},{2,1},{3,2},{4,3},{5,4},{6,5},{7,6},{8,7},{9,8},{10,9},{11,1... | collective-permute-start | bytes 393224 | tf_op jit(solution)/shard_map/ppermute | solution.py:17
  11.5 10.1 %collective-permute-start.3 = (f32[32,256]{0,1:T(8,128)S(1)}, f32[32,256]{0,1:T(8,128)S(1)}, u32[]{:S(2)}, u32[]{:S(2)}) collective-permute-start(f32[32,256]{0,1:T(8,128)S(1)} %copy.51), channel_id=1, source_target_pairs={{0,2},{1,3},{2,0},{3,1},{4,6},{5,7},{6,4},{7,5},{8,10},{9,11},{10,... | collective-permute-start | bytes 98312 | tf_op jit(solution)/shard_map/ppermute | solution.py:117
  24.6 16.5 %copy-start.1 = (f32[16,1024]{1,0:T(8,128)}, f32[16,1024]{1,0:T(8,128)S(1)}, u32[]{:S(2)}) copy-start(f32[16,1024]{1,0:T(8,128)S(1)} %select_add_fusion) | copy-start | bytes 196612
  24.6 8.3 %collective-permute-start.6 = (f32[1,16,1024]{2,1,0:T(8,128)S(1)}, f32[1,16,1024]{2,1,0:T(8,128)S(1)}, u32[]{:S(2)}, u32[]{:S(2)}) collective-permute-start(f32[1,16,1024]{2,1,0:T(8,128)S(1)} %fusion.55), channel_id=1, source_target_pairs={{0,12},{1,13},{2,14},{3,15},{4,8},{5,9},{6,10},{7,11},{8,4},{9,5},... | collective-permute-start | bytes 196616 | tf_op jit(solution)/shard_map/ppermute | solution.py:117
  28.3 5.2 %collective-permute-start.5 = (f32[1,16,1024]{2,1,0:T(8,128)S(1)}, f32[1,16,1024]{2,1,0:T(8,128)S(1)}, u32[]{:S(2)}, u32[]{:S(2)}) collective-permute-start(f32[1,16,1024]{2,1,0:T(8,128)S(1)} %fusion.55), channel_id=1, source_target_pairs={{0,8},{1,9},{2,10},{3,11},{4,12},{5,13},{6,14},{7,15},{8,0},{9,1},... | collective-permute-start | bytes 196616 | tf_op jit(solution)/shard_map/ppermute | solution.py:117
  28.3 4.3 %collective-permute-start.4 = (f32[1,16,1024]{2,1,0:T(8,128)S(1)}, f32[1,16,1024]{2,1,0:T(8,128)S(1)}, u32[]{:S(2)}, u32[]{:S(2)}) collective-permute-start(f32[1,16,1024]{2,1,0:T(8,128)S(1)} %fusion.55), channel_id=1, source_target_pairs={{0,4},{1,5},{2,6},{3,7},{4,0},{5,1},{6,2},{7,3},{8,12},{9,13},{10,... | collective-permute-start | bytes 196616 | tf_op jit(solution)/shard_map/ppermute | solution.py:117
  33.8 1.4 %collective-permute-start.7 = (f32[2,16,1024]{2,1,0:T(8,128)S(1)}, f32[2,16,1024]{2,1,0:T(8,128)S(1)}, u32[]{:S(2)}, u32[]{:S(2)}) collective-permute-start(f32[2,16,1024]{2,1,0:T(8,128)S(1)} %slice.21), channel_id=1, source_target_pairs={{0,1},{1,0},{2,3},{3,2},{4,5},{5,4},{6,7},{7,6},{8,9},{9,8},{10,11... | collective-permute-start | bytes 393224 | tf_op jit(solution)/shard_map/ppermute | solution.py:117
  35.2 4.3 %collective-permute-start.8 = (f32[16,1024]{1,0:T(8,128)S(1)}, f32[16,1024]{1,0:T(8,128)S(1)}, u32[]{:S(2)}, u32[]{:S(2)}) collective-permute-start(f32[16,1024]{1,0:T(8,128)S(1)} %slice_bitcast_fusion), channel_id=1, source_target_pairs={{0,2},{1,3},{2,0},{3,1},{4,6},{5,7},{6,4},{7,5},{8,10},{9,11},{10,... | collective-permute-start | bytes 196616 | tf_op jit(solution)/shard_map/ppermute | solution.py:117

commit v7 on v6

--- a/solution.py
+++ b/solution.py
@@ -101,6 +101,25 @@
     )(layer_weight, s, s, f, vx, vy, vz, d)
 
 
+def fix_kernel(w_ref, partial_ref, up_ref, prev_ref, next_ref, last_ref, out_ref):
+    rows, cols = partial_ref.shape
+    w = w_ref[...]
+    corr_first = jnp.sum(w * (-up_ref[...] * prev_ref[...]), axis=0, keepdims=True)
+    ax_next = -next_ref[1] * (next_ref[0] - last_ref[...])
+    corr_last = jnp.sum(w * ax_next, axis=0, keepdims=True)
+    row = lax.broadcasted_iota(jnp.int32, (rows, cols), 0)
+    out_ref[...] = (
+        partial_ref[...] + jnp.where(row == 0, corr_first, 0.0) + jnp.where(row == rows - 1, corr_last, 0.0)
+    )
+
+
+def corrected(w_col, partial, up_x0, from_prev, from_next, last_s):
+    return pl.pallas_call(
+        fix_kernel,
+        out_shape=jax.ShapeDtypeStruct(partial.shape, jnp.float32),
+    )(w_col, partial, up_x0, from_prev, from_next, last_s)
+
+
 def gather_rounds(count):
     bits = []
     bit = count // 2
@@ -176,15 +195,10 @@
     from_next = passed_along(to_prev, "gx", -1)
     from_prev = passed_along(last_s, "gx", 1)
 
-    corr_first = jnp.sum(layer_weight[:, None] * (-up_x0 * from_prev), axis=0)
-    ax_next = -from_next[1] * (from_next[0] - last_s)
-    corr_last = jnp.sum(layer_weight[:, None] * ax_next, axis=0)
-    row = lax.broadcasted_iota(jnp.int32, (rows, cols), 0)
-    recharge = partial + jnp.where(row == 0, corr_first[None, :], 0.0) + jnp.where(row == rows - 1, corr_last[None, :], 0.0)
+    recharge = corrected(layer_weight[:, None], partial, up_x0, from_prev, from_next, last_s)
 
     own_slab = cx_slab(cov_x, offsets_x, me, rows)
-    pair_slab = jnp.concatenate([own_slab, swap(own_slab, "gx", 1)], axis=0)
-    slab = jnp.concatenate([pair_slab, swap(pair_slab, "gx", 2)], axis=0)
+    slab = jnp.concatenate([own_slab] + [swap(own_slab, "gx", m) for m in (1, 2, 3)], axis=0)
     mixed = mixed_rows(recharge, slab, "gx")
 
     nyb = offsets_y.shape[0]

time: 42.1 us -> 41.3 us (0.981)
  other arithmetic: 3.21 us -> 0.42 us
  Pallas kernels: 4.48 us -> 6.38 us
  matrix products: 2.22 us -> 3.07 us
  waiting for transfers between devices: 12.6 us -> 11.8 us
    pallas_call x0 -> x1, Pallas kernels: none -> 1.75 us  [corrected(): pl.pallas_call(fix_kernel, out_shape=jax.ShapeDtypeStruct(partial.shape,...]
    reduce_sum x1 -> x0, other arithmetic: 0.97 us -> none  [body(): corr_first = jnp.sum(layer_weight[:, None] * (-up_x0 * from_prev), axis=0)]
    add x1 -> x0, other arithmetic: 0.92 us -> none  [body(): partial + jnp.where(row == 0, corr_first[None, :], 0.0)]
    broadcast_in_dim x1 -> x0, other arithmetic: 0.92 us -> none  [mixed_rows(): buf = local[None]]
    dot_general x4, matrix products: 1.26 us -> 2.11 us  [product(): jnp.dot(cols, piece.reshape(-1, piece.shape[-1]), precision=precise, pref...]
    gather x1, local copies, waits for them, and re-layouts: 1.38 us -> 0.56 us  [cx_slab(): target = (row_block[:, None] + offsets[row_block]) % nxb]
    ppermute x7 -> x8, waiting for transfers between devices: 12.6 us -> 11.8 us  [swap(): return lax.ppermute(value, axis, [(i, i ^ mask) for i in range(count)])]
    convert_element_type x1, local copies, waits for them, and re-layouts: 0.72 us -> 0.01 us  [cx_slab(): cov_rows.astype(jnp.float32)[:, :, None, :]]
  transfers between devices with their start and end apart: 9 -> 10, of which waited for: 5 -> 7; matrix products, arithmetic and copies ran while one was open for 4% -> 7% of each run, Pallas kernels for 11% -> 0%
where the time goes in v7:
time: 41.3 us; the launch traced here: 41 us
  starting transfers between devices  14.5 us (35%)
  waiting for transfers between devices  11.8 us (29%)
  Pallas kernels  6.38 us (15%)
  local copies, waits for them, and re-layouts  3.92 us (9%)
  matrix products  3.07 us (7%)
  between operations  0.92 us (2%)
  other arithmetic  0.42 us (1%)
    ppermute x8, waiting for transfers between devices, swap(): return lax.ppermute(value, axis, [(i, i ^ mask) for i in range(count)])  11.8 us
    ppermute x8, starting transfers between devices, swap(): return lax.ppermute(value, axis, [(i, i ^ mask) for i in range(count)])  10.9 us
    pallas_call x1, Pallas kernels, stencil(): pl.pallas_call(stencil_kernel, grid=(depth // zc,), in_specs=[pl.BlockSpe...  4.63 us
    ppermute x2, starting transfers between devices, passed_along(): lax.ppermute(value, axis, [(source, source + steps) for source in range(f...  3.65 us
    dot_general x4, matrix products, product(): jnp.dot(cols, piece.reshape(-1, piece.shape[-1]), precision=precise, pref...  2.11 us
    pallas_call x1, Pallas kernels, corrected(): pl.pallas_call(fix_kernel, out_shape=jax.ShapeDtypeStruct(partial.shape,...  1.75 us
    dot_general x1, matrix products, body(): jnp.einsum('xrkc,rikc->xri', picked, cov_y.reshape(nyb, BLK, cov_y.shape[...  0.96 us
  transfers between devices with their start and end apart: 10, of which 7 were waited for; matrix products, arithmetic and copies ran while one was open for 7% of the time, Pallas kernels for 0%

profile of v7, /device:TPU:0, one launch (start us, length us, event | category | flops | bytes accessed | tf_op | source)
XLA Modules:
  0.0 41.0 jit_solution(6452221689271247450)
XLA Ops:
  0.7 4.6 %shard_map.158 = (f32[16,1024]{1,0:T(8,128)}, f32[2,16,1024]{2,1,0:T(8,128)}, f32[16,1024]{1,0:T(8,128)}, f32[16,1024]{1,0:T(8,128)}) custom-call(f32[16]{0:T(128)} %w_ref.1, f32[16,16,1024]{2,1,0:T(8,128)} %sprev_ref.1, f32[16,16,1024]{2,1,0:T(8,128)} %sprev_ref.1, s32[16,16,1024]{2,1,0:T(8,128)} %f_ref.1, f32[16,16,1024]{2,1,0:T(8,128)} %vx_ref.1, ...), custom_call_target="tpu_custom_call" | custom-call | tf_op jit(solution)/shard_map/pallas_call | solution.py:75
  5.3 2.4 %collective-permute-start = (f32[16,1024]{1,0:T(8,128)}, f32[16,1024]{1,0:T(8,128)S(1)}, u32[]{:S(2)}, u32[]{:S(2)}) collective-permute-start(f32[16,1024]{1,0:T(8,128)} %get-tuple-element.9.last_ref), channel_id=1, source_target_pairs={{0,1},{1,2},{2,3},{3,4},{4,5},{5,6},{6,7},{7,8},{8,9},{9,10},{10,1... | collective-permute-start | bytes 196616 | tf_op jit(solution)/shard_map/ppermute | solution.py:17
  7.7 1.3 %collective-permute-start.1 = (f32[2,16,1024]{2,1,0:T(8,128)}, f32[2,16,1024]{2,1,0:T(8,128)S(1)}, u32[]{:S(2)}, u32[]{:S(2)}) collective-permute-start(f32[2,16,1024]{2,1,0:T(8,128)} %get-tuple-element.10), channel_id=1, source_target_pairs={{1,0},{2,1},{3,2},{4,3},{5,4},{6,5},{7,6},{8,7},{9,8},{10,9},{11,1... | collective-permute-start | bytes 393224 | tf_op jit(solution)/shard_map/ppermute | solution.py:17
  9.0 0.6 %gather_fusion = s32[16,4]{1,0:T(8,128)S(1)} fusion(s32[2,4]{1,0:T(2,128)S(1)} %copy-done.1, s32[1024]{0:T(1024)S(1)} %pad_clamp_fusion.1), kind=kCustom, calls=%fused_computation | custom fusion | bytes 576 | tf_op jit(solution)/shard_map/gather | solution.py:143
  9.9 3.3 %collective-permute-start.2 = (f32[16,256]{1,0:T(8,128)S(1)}, f32[16,256]{1,0:T(8,128)S(1)}, u32[]{:S(2)}, u32[]{:S(2)}) collective-permute-start(f32[16,256]{1,0:T(8,128)S(1)} %copy_bitcast_fusion.2), channel_id=1, source_target_pairs={{0,1},{1,0},{2,3},{3,2},{4,5},{5,4},{6,7},{7,6},{8,9},{9,8},{10,11... | collective-permute-start | bytes 49160 | tf_op jit(solution)/shard_map/ppermute | solution.py:136
  13.2 1.7 %collective-permute-start.3 = (f32[16,256]{1,0:T(8,128)S(1)}, f32[16,256]{1,0:T(8,128)S(1)}, u32[]{:S(2)}, u32[]{:S(2)}) collective-permute-start(f32[16,256]{1,0:T(8,128)S(1)} %copy_bitcast_fusion.2), channel_id=1, source_target_pairs={{0,2},{1,3},{2,0},{3,1},{4,6},{5,7},{6,4},{7,5},{8,10},{9,11},{10,... | collective-permute-start | bytes 49160 | tf_op jit(solution)/shard_map/ppermute | solution.py:136
  15.0 0.1 copy.61
  15.1 0.7 %copy.46.w_ref = f32[16,1]{1,0:T(8,128)} copy(f32[16,1]{0,1:T(1,128)S(1)} %bitcast.85) | data formatting | bytes 128 | tf_op jit(solution)/shard_map/broadcast_in_dim | solution.py:198
  15.8 0.1 copy.62
  15.9 1.4 %collective-permute-done.3 = f32[16,256]{1,0:T(8,128)S(1)} collective-permute-done((f32[16,256]{1,0:T(8,128)S(1)}, f32[16,256]{1,0:T(8,128)S(1)}, u32[]{:S(2)}, u32[]{:S(2)}) %collective-permute-start.3) | collective-permute-done | bytes 16416 | tf_op jit(solution)/shard_map/ppermute | solution.py:136
  17.3 0.1 copy.63
  17.4 0.7 %collective-permute-done.4 = f32[16,256]{1,0:T(8,128)S(1)} collective-permute-done((f32[16,256]{1,0:T(8,128)S(1)}, f32[16,256]{1,0:T(8,128)S(1)}, u32[]{:S(2)}, u32[]{:S(2)}) %collective-permute-start.4) | collective-permute-done | bytes 16416 | tf_op jit(solution)/shard_map/ppermute | solution.py:136
  18.1 0.1 copy.64
  18.2 0.6 %copy-done.3 = f32[16,1024]{1,0:T(8,128)} copy-done((f32[16,1024]{1,0:T(8,128)}, f32[16,1024]{1,0:T(8,128)S(1)}, u32[]{:S(2)}) %copy-start.3) | copy-done | bytes 65560
  18.9 1.7 %shard_map.159 = f32[16,1024]{1,0:T(8,128)} custom-call(f32[16,1]{1,0:T(8,128)} %copy.46.w_ref, f32[16,1024]{1,0:T(8,128)} %get-tuple-element.7.partial_ref, f32[16,1024]{1,0:T(8,128)} %get-tuple-element.8.up_ref, f32[16,1024]{1,0:T(8,128)} %copy-done.3, f32[2,16,1024]{2,1,0:T(8,128)} %copy-done.2, f32[16,1024]{1,0:T(8,128)} %get-tuple-element.9.last_ref), custom_call_target="tpu_custom_call" | custom-call | tf_op jit(solution)/shard_map/pallas_call | solution.py:117
  20.6 2.8 %collective-permute-start.6 = (f32[1,16,1024]{2,1,0:T(8,128)}, f32[1,16,1024]{2,1,0:T(8,128)S(1)}, u32[]{:S(2)}, u32[]{:S(2)}) collective-permute-start(f32[1,16,1024]{2,1,0:T(8,128)} %bitcast.81), channel_id=1, source_target_pairs={{0,8},{1,9},{2,10},{3,11},{4,12},{5,13},{6,14},{7,15},{8,0},{9,1},... | collective-permute-start | bytes 196616 | tf_op jit(solution)/shard_map/ppermute | solution.py:136
  23.4 0.2 pad_maximum_fusion
  23.6 1.6 %collective-permute-start.5 = (f32[1,16,1024]{2,1,0:T(8,128)}, f32[1,16,1024]{2,1,0:T(8,128)S(1)}, u32[]{:S(2)}, u32[]{:S(2)}) collective-permute-start(f32[1,16,1024]{2,1,0:T(8,128)} %bitcast.82), channel_id=1, source_target_pairs={{0,4},{1,5},{2,6},{3,7},{4,0},{5,1},{6,2},{7,3},{8,12},{9,13},{10,... | collective-permute-start | bytes 196616 | tf_op jit(solution)/shard_map/ppermute | solution.py:136
  25.3 1.6 %collective-permute-done.6 = f32[1,16,1024]{2,1,0:T(8,128)S(1)} collective-permute-done((f32[1,16,1024]{2,1,0:T(8,128)}, f32[1,16,1024]{2,1,0:T(8,128)S(1)}, u32[]{:S(2)}, u32[]{:S(2)}) %collective-permute-start.6) | collective-permute-done | bytes 65568 | tf_op jit(solution)/shard_map/ppermute | solution.py:136
  26.8 0.3 fusion.15
  27.2 1.0 %collective-permute-done.5 = f32[1,16,1024]{2,1,0:T(8,128)S(1)} collective-permute-done((f32[1,16,1024]{2,1,0:T(8,128)}, f32[1,16,1024]{2,1,0:T(8,128)S(1)}, u32[]{:S(2)}, u32[]{:S(2)}) %collective-permute-start.5) | collective-permute-done | bytes 65568 | tf_op jit(solution)/shard_map/ppermute | solution.py:136
  28.2 0.3 fusion.17
  28.5 3.1 %collective-permute-done.7 = f32[1,16,1024]{2,1,0:T(8,128)S(1)} collective-permute-done((f32[1,16,1024]{2,1,0:T(8,128)}, f32[1,16,1024]{2,1,0:T(8,128)S(1)}, u32[]{:S(2)}, u32[]{:S(2)}) %collective-permute-start.7) | collective-permute-done | bytes 65568 | tf_op jit(solution)/shard_map/ppermute | solution.py:136
  31.5 0.3 fusion.13
  31.8 1.2 %fusion.3 = f32[64,1024]{1,0:T(8,128)S(1)} fusion(f32[64,1024]{1,0:T(8,128)S(1)} %fusion.13, f32[64,1024]{1,0:T(8,128)S(1)} %fusion.15, f32[64,1024]{1,0:T(8,128)S(1)} %fusion.17, f32[16,1024]{1,0:T(8,128)} %shard_map.159, f32[64,16,16]{0,2,1:T(8,128)S(1)} %pad_maximum_fusion, s32[]{:T(128)} %bitcast.8, pred[]{:T(512)} %bitcast.2), kind=kOutput, calls=%fused_computation.6 | convolution fusion | flops 6489088 | bytes 1122309 | tf_op jit(solution)/shard_map/dot_general | solution.py:158
  33.3 0.1 copy.47
  33.4 1.0 %collective-permute-done.8 = f32[2,16,1024]{2,1,0:T(8,128)S(1)} collective-permute-done((f32[2,16,1024]{2,1,0:T(8,128)S(1)}, f32[2,16,1024]{2,1,0:T(8,128)S(1)}, u32[]{:S(2)}, u32[]{:S(2)}) %collective-permute-start.8) | collective-permute-done | bytes 131104 | tf_op jit(solution)/shard_map/ppermute | solution.py:136
  34.5 1.3 %collective-permute-start.9 = (f32[16,1024]{1,0:T(8,128)S(1)}, f32[16,1024]{1,0:T(8,128)S(1)}, u32[]{:S(2)}, u32[]{:S(2)}) collective-permute-start(f32[16,1024]{1,0:T(8,128)S(1)} %slice_bitcast_fusion), channel_id=1, source_target_pairs={{0,2},{1,3},{2,0},{3,1},{4,6},{5,7},{6,4},{7,5},{8,10},{9,11},{10,... | collective-permute-start | bytes 196616 | tf_op jit(solution)/shard_map/ppermute | solution.py:136
  35.8 3.1 %collective-permute-done.9 = f32[16,1024]{1,0:T(8,128)S(1)} collective-permute-done((f32[16,1024]{1,0:T(8,128)S(1)}, f32[16,1024]{1,0:T(8,128)S(1)}, u32[]{:S(2)}, u32[]{:S(2)}) %collective-permute-start.9) | collective-permute-done | bytes 65568 | tf_op jit(solution)/shard_map/ppermute | solution.py:136
  38.8 0.6 %gather_fusion.1 = f32[32,16,128]{2,1,0:T(8,128)S(1)} fusion(f32[16,8,128]{2,0,1:T(8,128)S(1)} %copy_bitcast_fusion.1, s32[1024]{0:T(1024)S(1)} %pad_clamp_fusion), kind=kCustom, calls=%fused_computation.1 | custom fusion | bytes 524416 | tf_op jit(solution)/shard_map/jit(_take)/gather | solution.py:206
  39.4 1.0 %fusion.4 = f32[8,2,8,128]{3,2,1,0:T(8,128)S(1)} fusion(f32[8,128,4,128]{3,2,1,0:T(4,128)S(1)} %bitcast.73, f32[8,4,16,128]{3,2,1,0:T(8,128)S(1)} %bitcast.76, pred[8,4]{1,0:T(8,128)(4,1)S(1)} %copy.47), kind=kOutput, calls=%fused_computation.7 | convolution fusion | flops 50397184 | bytes 2424864 | tf_op jit(solution)/shard_map/xrkc,rikc->xri/dot_general | solution.py:207
  40.4 0.7 %copy.76 = f32[8,2,8,128]{3,2,0,1:T(8,128)} copy(f32[8,2,8,128]{3,2,1,0:T(8,128)S(1)} %fusion.4) | data formatting | bytes 131072 | tf_op jit(solution)/shard_map/reshape | solution.py:213
  (36 shorter events, 0.8 us)
Async XLA Ops:
  0.6 38.8 %copy-start = (f32[1024,4,128]{2,1,0:T(4,128)S(1)}, f32[1024,4,128]{2,1,0:T(4,128)}, u32[]{:S(2)}) copy-start(f32[1024,4,128]{2,1,0:T(4,128)} %param.26) | copy-start | bytes 6291460
  0.6 14.5 %copy-start.6 = (f32[16]{0:T(128)S(1)}, f32[16]{0:T(128)}, u32[]{:S(2)}) copy-start(f32[16]{0:T(128)} %w_ref.1) | copy-start | bytes 196
  0.7 8.4 %copy-start.1 = (s32[2,4]{1,0:T(2,128)S(1)}, s32[2,4]{1,0:T(2,128)}, u32[]{:S(2)}) copy-start(s32[2,4]{1,0:T(2,128)} %param.25) | copy-start | bytes 100
  0.7 9.1 %copy-start.4 = (bf16[16,4,128]{2,1,0:T(4,128)(2,1)S(1)}, bf16[16,4,128]{2,1,0:T(4,128)(2,1)}, u32[]{:S(2)}) copy-start(bf16[16,4,128]{2,1,0:T(4,128)(2,1)} %param.24) | copy-start | bytes 49156
  5.3 12.9 %collective-permute-start = (f32[16,1024]{1,0:T(8,128)}, f32[16,1024]{1,0:T(8,128)S(1)}, u32[]{:S(2)}, u32[]{:S(2)}) collective-permute-start(f32[16,1024]{1,0:T(8,128)} %get-tuple-element.9.last_ref), channel_id=1, source_target_pairs={{0,1},{1,2},{2,3},{3,4},{4,5},{5,6},{6,7},{7,8},{8,9},{9,10},{10,1... | collective-permute-start | bytes 196616 | tf_op jit(solution)/shard_map/ppermute | solution.py:17
  7.7 10.5 %collective-permute-start.1 = (f32[2,16,1024]{2,1,0:T(8,128)}, f32[2,16,1024]{2,1,0:T(8,128)S(1)}, u32[]{:S(2)}, u32[]{:S(2)}) collective-permute-start(f32[2,16,1024]{2,1,0:T(8,128)} %get-tuple-element.10), channel_id=1, source_target_pairs={{1,0},{2,1},{3,2},{4,3},{5,4},{6,5},{7,6},{8,7},{9,8},{10,9},{11,1... | collective-permute-start | bytes 393224 | tf_op jit(solution)/shard_map/ppermute | solution.py:17
  9.9 23.2 %copy-start.5 = (s32[8,4]{0,1:T(4,128)S(1)}, s32[8,4]{0,1:T(4,128)}, u32[]{:S(2)}) copy-start(s32[8,4]{0,1:T(4,128)} %param.27) | copy-start | bytes 388
  9.9 5.9 %collective-permute-start.2 = (f32[16,256]{1,0:T(8,128)S(1)}, f32[16,256]{1,0:T(8,128)S(1)}, u32[]{:S(2)}, u32[]{:S(2)}) collective-permute-start(f32[16,256]{1,0:T(8,128)S(1)} %copy_bitcast_fusion.2), channel_id=1, source_target_pairs={{0,1},{1,0},{2,3},{3,2},{4,5},{5,4},{6,7},{7,6},{8,9},{9,8},{10,11... | collective-permute-start | bytes 49160 | tf_op jit(solution)/shard_map/ppermute | solution.py:136
  13.2 4.1 %collective-permute-start.3 = (f32[16,256]{1,0:T(8,128)S(1)}, f32[16,256]{1,0:T(8,128)S(1)}, u32[]{:S(2)}, u32[]{:S(2)}) collective-permute-start(f32[16,256]{1,0:T(8,128)S(1)} %copy_bitcast_fusion.2), channel_id=1, source_target_pairs={{0,2},{1,3},{2,0},{3,1},{4,6},{5,7},{6,4},{7,5},{8,10},{9,11},{10,... | collective-permute-start | bytes 49160 | tf_op jit(solution)/shard_map/ppermute | solution.py:136
  14.9 3.2 %collective-permute-start.4 = (f32[16,256]{1,0:T(8,128)S(1)}, f32[16,256]{1,0:T(8,128)S(1)}, u32[]{:S(2)}, u32[]{:S(2)}) collective-permute-start(f32[16,256]{1,0:T(8,128)S(1)} %copy_bitcast_fusion.2), channel_id=1, source_target_pairs={{0,3},{1,2},{2,1},{3,0},{4,7},{5,6},{6,5},{7,4},{8,11},{9,10},{10,... | collective-permute-start | bytes 49160 | tf_op jit(solution)/shard_map/ppermute | solution.py:136
  18.2 0.6 %copy-start.3 = (f32[16,1024]{1,0:T(8,128)}, f32[16,1024]{1,0:T(8,128)S(1)}, u32[]{:S(2)}) copy-start(f32[16,1024]{1,0:T(8,128)S(1)} %collective-permute-done.prev_ref) | copy-start | bytes 196612
  18.2 0.7 %copy-start.2 = (f32[2,16,1024]{2,1,0:T(8,128)}, f32[2,16,1024]{2,1,0:T(8,128)S(1)}, u32[]{:S(2)}) copy-start(f32[2,16,1024]{2,1,0:T(8,128)S(1)} %collective-permute-done.1.next_ref) | copy-start | bytes 393220
  20.6 6.2 %collective-permute-start.6 = (f32[1,16,1024]{2,1,0:T(8,128)}, f32[1,16,1024]{2,1,0:T(8,128)S(1)}, u32[]{:S(2)}, u32[]{:S(2)}) collective-permute-start(f32[1,16,1024]{2,1,0:T(8,128)} %bitcast.81), channel_id=1, source_target_pairs={{0,8},{1,9},{2,10},{3,11},{4,12},{5,13},{6,14},{7,15},{8,0},{9,1},... | collective-permute-start | bytes 196616 | tf_op jit(solution)/shard_map/ppermute | solution.py:136
  23.6 4.5 %collective-permute-start.5 = (f32[1,16,1024]{2,1,0:T(8,128)}, f32[1,16,1024]{2,1,0:T(8,128)S(1)}, u32[]{:S(2)}, u32[]{:S(2)}) collective-permute-start(f32[1,16,1024]{2,1,0:T(8,128)} %bitcast.82), channel_id=1, source_target_pairs={{0,4},{1,5},{2,6},{3,7},{4,0},{5,1},{6,2},{7,3},{8,12},{9,13},{10,... | collective-permute-start | bytes 196616 | tf_op jit(solution)/shard_map/ppermute | solution.py:136
  25.3 6.3 %collective-permute-start.7 = (f32[1,16,1024]{2,1,0:T(8,128)}, f32[1,16,1024]{2,1,0:T(8,128)S(1)}, u32[]{:S(2)}, u32[]{:S(2)}) collective-permute-start(f32[1,16,1024]{2,1,0:T(8,128)} %bitcast.83), channel_id=1, source_target_pairs={{0,12},{1,13},{2,14},{3,15},{4,8},{5,9},{6,10},{7,11},{8,4},{9,5},... | collective-permute-start | bytes 196616 | tf_op jit(solution)/shard_map/ppermute | solution.py:136
  33.0 1.4 %collective-permute-start.8 = (f32[2,16,1024]{2,1,0:T(8,128)S(1)}, f32[2,16,1024]{2,1,0:T(8,128)S(1)}, u32[]{:S(2)}, u32[]{:S(2)}) collective-permute-start(f32[2,16,1024]{2,1,0:T(8,128)S(1)} %slice.13), channel_id=1, source_target_pairs={{0,1},{1,0},{2,3},{3,2},{4,5},{5,4},{6,7},{7,6},{8,9},{9,8},{10,11... | collective-permute-start | bytes 393224 | tf_op jit(solution)/shard_map/ppermute | solution.py:136
  34.5 4.3 %collective-permute-start.9 = (f32[16,1024]{1,0:T(8,128)S(1)}, f32[16,1024]{1,0:T(8,128)S(1)}, u32[]{:S(2)}, u32[]{:S(2)}) collective-permute-start(f32[16,1024]{1,0:T(8,128)S(1)} %slice_bitcast_fusion), channel_id=1, source_target_pairs={{0,2},{1,3},{2,0},{3,1},{4,6},{5,7},{6,4},{7,5},{8,10},{9,11},{10,... | collective-permute-start | bytes 196616 | tf_op jit(solution)/shard_map/ppermute | solution.py:136

commit v8 on v7

--- a/solution.py
+++ b/solution.py
@@ -152,9 +152,10 @@
     me = lax.axis_index(axis)
     rows = local.shape[0]
     per_device = slab.reshape(slab.shape[0], count, rows)
+    relative = jnp.take(per_device, me ^ jnp.arange(count, dtype=jnp.int32), axis=1)
 
     def product(piece, masks):
-        cols = jnp.take(per_device, me ^ jnp.array(masks, jnp.int32), axis=1).reshape(slab.shape[0], -1)
+        cols = jnp.concatenate([relative[:, m, :] for m in masks], axis=1)
         return jnp.dot(cols, piece.reshape(-1, piece.shape[-1]), precision=precise, preferred_element_type=jnp.float32)
 
     buf = local[None]

time: 41.3 us -> 43.1 us (1.044)
  local copies, waits for them, and re-layouts: 3.92 us -> 6.02 us
  waiting for transfers between devices: 11.8 us -> 11.3 us
    ppermute x8, waiting for transfers between devices: 11.8 us -> 9.81 us  [swap(): return lax.ppermute(value, axis, [(i, i ^ mask) for i in range(count)])]
    ppermute x2, waiting for transfers between devices: 0.01 us -> 1.44 us  [passed_along(): lax.ppermute(value, axis, [(source, source + steps) for source in range(f...]
    gather x1, local copies, waits for them, and re-layouts: 0.56 us -> 1.38 us  [cx_slab(): target = (row_block[:, None] + offsets[row_block]) % nxb]
    convert_element_type x1, local copies, waits for them, and re-layouts: 0.01 us -> 0.72 us  [cx_slab(): cov_rows.astype(jnp.float32)[:, :, None, :]]
    ppermute x8, starting transfers between devices: 10.9 us -> 11.5 us  [swap(): return lax.ppermute(value, axis, [(i, i ^ mask) for i in range(count)])]
    gather x0 -> x1, local copies, waits for them, and re-layouts: none -> 0.57 us  [mixed_rows(): jnp.take(per_device, me ^ jnp.arange(count, dtype=jnp.int32), axis=1)]
  transfers between devices with their start and end apart: 10 -> 10, of which waited for: 7 -> 6; matrix products, arithmetic and copies ran while one was open for 7% -> 7% of each run, Pallas kernels for 0% -> 10%
where the time goes in v8:
time: 43.1 us; the launch traced here: 42.8 us
  starting transfers between devices  14.8 us (34%)
  waiting for transfers between devices  11.3 us (26%)
  Pallas kernels  6.23 us (14%)
  local copies, waits for them, and re-layouts  6.02 us (14%)
  matrix products  3.05 us (7%)
  between operations  0.88 us (2%)
  other arithmetic  0.53 us (1%)
    ppermute x8, starting transfers between devices, swap(): return lax.ppermute(value, axis, [(i, i ^ mask) for i in range(count)])  11.5 us
    ppermute x8, waiting for transfers between devices, swap(): return lax.ppermute(value, axis, [(i, i ^ mask) for i in range(count)])  9.81 us
    pallas_call x1, Pallas kernels, stencil(): pl.pallas_call(stencil_kernel, grid=(depth // zc,), in_specs=[pl.BlockSpe...  4.48 us
    ppermute x2, starting transfers between devices, passed_along(): lax.ppermute(value, axis, [(source, source + steps) for source in range(f...  3.34 us
    dot_general x4, matrix products, product(): jnp.dot(cols, piece.reshape(-1, piece.shape[-1]), precision=precise, pref...  2.09 us
    pallas_call x1, Pallas kernels, corrected(): pl.pallas_call(fix_kernel, out_shape=jax.ShapeDtypeStruct(partial.shape,...  1.75 us
    ppermute x2, waiting for transfers between devices, passed_along(): lax.ppermute(value, axis, [(source, source + steps) for source in range(f...  1.44 us
    gather x1, local copies, waits for them, and re-layouts, cx_slab(): target = (row_block[:, None] + offsets[row_block]) % nxb  1.38 us
  transfers between devices with their start and end apart: 10, of which 6 were waited for; matrix products, arithmetic and copies ran while one was open for 7% of the time, Pallas kernels for 10%

profile of v8, /device:TPU:0, one launch (start us, length us, event | category | flops | bytes accessed | tf_op | source)
XLA Modules:
  0.0 42.8 jit_solution(7285372269703259223)
XLA Ops:
  0.7 1.4 %gather_fusion = s32[16,4]{1,0:T(8,128)S(1)} fusion(s32[2,4]{1,0:T(2,128)} %param.19, s32[1024]{0:T(1024)S(1)} %pad_clamp_fusion.2), kind=kCustom, calls=%fused_computation | custom fusion | bytes 576 | tf_op jit(solution)/shard_map/gather | solution.py:143
  2.3 0.7 %copy.40 = f32[16,4,128]{2,0,1:T(8,128)S(1)} copy(bf16[16,4,128]{2,1,0:T(4,128)(2,1)} %param.18) | data formatting | bytes 49152 | tf_op jit(solution)/shard_map/convert_element_type | solution.py:146
  3.1 0.5 %collective-permute-start.2 = (f32[16,256]{1,0:T(8,128)S(1)}, f32[16,256]{1,0:T(8,128)S(1)}, u32[]{:S(2)}, u32[]{:S(2)}) collective-permute-start(f32[16,256]{1,0:T(8,128)S(1)} %copy_bitcast_fusion.2), channel_id=1, source_target_pairs={{0,1},{1,0},{2,3},{3,2},{4,5},{5,4},{6,7},{7,6},{8,9},{9,8},{10,11... | collective-permute-start | bytes 49160 | tf_op jit(solution)/shard_map/ppermute | solution.py:136
  3.6 2.6 %collective-permute-start.3 = (f32[16,256]{1,0:T(8,128)S(1)}, f32[16,256]{1,0:T(8,128)S(1)}, u32[]{:S(2)}, u32[]{:S(2)}) collective-permute-start(f32[16,256]{1,0:T(8,128)S(1)} %copy_bitcast_fusion.2), channel_id=1, source_target_pairs={{0,2},{1,3},{2,0},{3,1},{4,6},{5,7},{6,4},{7,5},{8,10},{9,11},{10,... | collective-permute-start | bytes 49160 | tf_op jit(solution)/shard_map/ppermute | solution.py:136
  6.3 4.5 %shard_map.122 = (f32[16,1024]{1,0:T(8,128)}, f32[2,16,1024]{2,1,0:T(8,128)}, f32[16,1024]{1,0:T(8,128)}, f32[16,1024]{1,0:T(8,128)}) custom-call(f32[16]{0:T(128)} %w_ref.1, f32[16,16,1024]{2,1,0:T(8,128)} %sprev_ref.1, f32[16,16,1024]{2,1,0:T(8,128)} %sprev_ref.1, s32[16,16,1024]{2,1,0:T(8,128)} %f_ref.1, f32[16,16,1024]{2,1,0:T(8,128)} %vx_ref.1, ...), custom_call_target="tpu_custom_call" | custom-call | tf_op jit(solution)/shard_map/pallas_call | solution.py:75
  10.7 2.0 %collective-permute-start = (f32[16,1024]{1,0:T(8,128)}, f32[16,1024]{1,0:T(8,128)S(1)}, u32[]{:S(2)}, u32[]{:S(2)}) collective-permute-start(f32[16,1024]{1,0:T(8,128)} %get-tuple-element.8.last_ref), channel_id=1, source_target_pairs={{0,1},{1,2},{2,3},{3,4},{4,5},{5,6},{6,7},{7,8},{8,9},{9,10},{10,1... | collective-permute-start | bytes 196616 | tf_op jit(solution)/shard_map/ppermute | solution.py:17
  12.8 1.3 %collective-permute-start.1 = (f32[2,16,1024]{2,1,0:T(8,128)}, f32[2,16,1024]{2,1,0:T(8,128)S(1)}, u32[]{:S(2)}, u32[]{:S(2)}) collective-permute-start(f32[2,16,1024]{2,1,0:T(8,128)} %get-tuple-element.9), channel_id=1, source_target_pairs={{1,0},{2,1},{3,2},{4,3},{5,4},{6,5},{7,6},{8,7},{9,8},{10,9},{11,1... | collective-permute-start | bytes 393224 | tf_op jit(solution)/shard_map/ppermute | solution.py:17
  14.1 0.1 copy.41
  14.2 0.7 %copy.37.w_ref = f32[16,1]{1,0:T(8,128)} copy(f32[16,1]{0,1:T(1,128)S(1)} %bitcast.80) | data formatting | bytes 128 | tf_op jit(solution)/shard_map/broadcast_in_dim | solution.py:199
  14.9 0.1 copy.43
  15.0 0.1 copy.44
  15.1 0.1 copy.45
  15.2 0.2 pad_maximum_fusion
  15.4 0.6 %gather_fusion.1 = f32[16,64,16]{1,2,0:T(8,128)S(1)} fusion(f32[64,16,16]{0,2,1:T(8,128)S(1)} %pad_maximum_fusion, s32[1024]{0:T(1024)S(1)} %pad_clamp_fusion.1), kind=kCustom, calls=%fused_computation.1 | custom fusion | bytes 131136 | tf_op jit(solution)/shard_map/jit(_take)/gather | solution.py:155
  16.0 1.4 %collective-permute-done.1.next_ref = f32[2,16,1024]{2,1,0:T(8,128)S(1)} collective-permute-done((f32[2,16,1024]{2,1,0:T(8,128)}, f32[2,16,1024]{2,1,0:T(8,128)S(1)}, u32[]{:S(2)}, u32[]{:S(2)}) %collective-permute-start.1) | collective-permute-done | bytes 131104 | tf_op jit(solution)/shard_map/ppermute | solution.py:17
  17.5 0.6 %copy-done.1 = f32[2,16,1024]{2,1,0:T(8,128)} copy-done((f32[2,16,1024]{2,1,0:T(8,128)}, f32[2,16,1024]{2,1,0:T(8,128)S(1)}, u32[]{:S(2)}) %copy-start.1) | copy-done | bytes 131096
  18.1 1.7 %shard_map.123 = f32[16,1024]{1,0:T(8,128)} custom-call(f32[16,1]{1,0:T(8,128)} %copy.37.w_ref, f32[16,1024]{1,0:T(8,128)} %get-tuple-element.6.partial_ref, f32[16,1024]{1,0:T(8,128)} %get-tuple-element.7.up_ref, f32[16,1024]{1,0:T(8,128)} %copy-done.2, f32[2,16,1024]{2,1,0:T(8,128)} %copy-done.1, f32[16,1024]{1,0:T(8,128)} %get-tuple-element.8.last_ref), custom_call_target="tpu_custom_call" | custom-call | tf_op jit(solution)/shard_map/pallas_call | solution.py:117
  19.8 5.4 %collective-permute-start.6 = (f32[1,16,1024]{2,1,0:T(8,128)}, f32[1,16,1024]{2,1,0:T(8,128)S(1)}, u32[]{:S(2)}, u32[]{:S(2)}) collective-permute-start(f32[1,16,1024]{2,1,0:T(8,128)} %bitcast.76), channel_id=1, source_target_pairs={{0,8},{1,9},{2,10},{3,11},{4,12},{5,13},{6,14},{7,15},{8,0},{9,1},... | collective-permute-start | bytes 196616 | tf_op jit(solution)/shard_map/ppermute | solution.py:136
  25.3 1.6 %collective-permute-start.5 = (f32[1,16,1024]{2,1,0:T(8,128)}, f32[1,16,1024]{2,1,0:T(8,128)S(1)}, u32[]{:S(2)}, u32[]{:S(2)}) collective-permute-start(f32[1,16,1024]{2,1,0:T(8,128)} %bitcast.77), channel_id=1, source_target_pairs={{0,4},{1,5},{2,6},{3,7},{4,0},{5,1},{6,2},{7,3},{8,12},{9,13},{10,... | collective-permute-start | bytes 196616 | tf_op jit(solution)/shard_map/ppermute | solution.py:136
  27.0 2.6 %collective-permute-done.6 = f32[1,16,1024]{2,1,0:T(8,128)S(1)} collective-permute-done((f32[1,16,1024]{2,1,0:T(8,128)}, f32[1,16,1024]{2,1,0:T(8,128)S(1)}, u32[]{:S(2)}, u32[]{:S(2)}) %collective-permute-start.6) | collective-permute-done | bytes 65568 | tf_op jit(solution)/shard_map/ppermute | solution.py:136
  29.6 0.3 fusion.15
  29.9 0.3 collective-permute-done.5
  30.3 0.3 fusion.17
  30.6 2.7 %collective-permute-done.7 = f32[1,16,1024]{2,1,0:T(8,128)S(1)} collective-permute-done((f32[1,16,1024]{2,1,0:T(8,128)}, f32[1,16,1024]{2,1,0:T(8,128)S(1)}, u32[]{:S(2)}, u32[]{:S(2)}) %collective-permute-start.7) | collective-permute-done | bytes 65568 | tf_op jit(solution)/shard_map/ppermute | solution.py:136
  33.3 0.3 fusion.13
  33.6 1.2 %fusion.3 = f32[64,1024]{1,0:T(8,128)S(1)} fusion(f32[64,1024]{1,0:T(8,128)S(1)} %fusion.13, f32[64,1024]{1,0:T(8,128)S(1)} %fusion.15, f32[64,1024]{1,0:T(8,128)S(1)} %fusion.17, f32[16,1024]{1,0:T(8,128)} %shard_map.123, f32[64,16,16]{0,2,1:T(8,128)S(1)} %select_bitcast_fusion), kind=kOutput, calls=%fused_computation.7 | convolution fusion | flops 6488064 | bytes 1122304 | tf_op jit(solution)/shard_map/dot_general | solution.py:159
  35.1 1.0 %collective-permute-done.8 = f32[2,16,1024]{2,1,0:T(8,128)S(1)} collective-permute-done((f32[2,16,1024]{2,1,0:T(8,128)S(1)}, f32[2,16,1024]{2,1,0:T(8,128)S(1)}, u32[]{:S(2)}, u32[]{:S(2)}) %collective-permute-start.8) | collective-permute-done | bytes 131104 | tf_op jit(solution)/shard_map/ppermute | solution.py:136
  36.2 1.2 %collective-permute-start.9 = (f32[16,1024]{1,0:T(8,128)S(1)}, f32[16,1024]{1,0:T(8,128)S(1)}, u32[]{:S(2)}, u32[]{:S(2)}) collective-permute-start(f32[16,1024]{1,0:T(8,128)S(1)} %slice_bitcast_fusion), channel_id=1, source_target_pairs={{0,2},{1,3},{2,0},{3,1},{4,6},{5,7},{6,4},{7,5},{8,10},{9,11},{10,... | collective-permute-start | bytes 196616 | tf_op jit(solution)/shard_map/ppermute | solution.py:136
  37.4 3.1 %collective-permute-done.9 = f32[16,1024]{1,0:T(8,128)S(1)} collective-permute-done((f32[16,1024]{1,0:T(8,128)S(1)}, f32[16,1024]{1,0:T(8,128)S(1)}, u32[]{:S(2)}, u32[]{:S(2)}) %collective-permute-start.9) | collective-permute-done | bytes 65568 | tf_op jit(solution)/shard_map/ppermute | solution.py:136
  40.6 0.6 %gather_fusion.2 = f32[32,16,128]{2,1,0:T(8,128)S(1)} fusion(f32[16,8,128]{2,0,1:T(8,128)S(1)} %copy_bitcast_fusion.1, s32[1024]{0:T(1024)S(1)} %pad_clamp_fusion), kind=kCustom, calls=%fused_computation.2 | custom fusion | bytes 524416 | tf_op jit(solution)/shard_map/jit(_take)/gather | solution.py:207
  41.2 1.0 %fusion.4 = f32[8,2,8,128]{3,2,1,0:T(8,128)S(1)} fusion(f32[8,128,4,128]{3,2,1,0:T(4,128)S(1)} %bitcast.68, f32[8,4,16,128]{3,2,1,0:T(8,128)S(1)} %bitcast.71, pred[8,4]{1,0:T(8,128)(4,1)S(1)} %copy.38), kind=kOutput, calls=%fused_computation.8 | convolution fusion | flops 50397184 | bytes 2424864 | tf_op jit(solution)/shard_map/xrkc,rikc->xri/dot_general | solution.py:208
  42.1 0.7 %copy.61 = f32[8,2,8,128]{3,2,0,1:T(8,128)} copy(f32[8,2,8,128]{3,2,1,0:T(8,128)S(1)} %fusion.4) | data formatting | bytes 131072 | tf_op jit(solution)/shard_map/reshape | solution.py:214
  (37 shorter events, 0.9 us)
Async XLA Ops:
  0.6 40.5 %copy-start = (f32[1024,4,128]{2,1,0:T(4,128)S(1)}, f32[1024,4,128]{2,1,0:T(4,128)}, u32[]{:S(2)}) copy-start(f32[1024,4,128]{2,1,0:T(4,128)} %param.20) | copy-start | bytes 6291460
  3.1 11.1 %copy-start.4 = (f32[16]{0:T(128)S(1)}, f32[16]{0:T(128)}, u32[]{:S(2)}) copy-start(f32[16]{0:T(128)} %w_ref.1) | copy-start | bytes 196
  3.1 11.8 %collective-permute-start.2 = (f32[16,256]{1,0:T(8,128)S(1)}, f32[16,256]{1,0:T(8,128)S(1)}, u32[]{:S(2)}, u32[]{:S(2)}) collective-permute-start(f32[16,256]{1,0:T(8,128)S(1)} %copy_bitcast_fusion.2), channel_id=1, source_target_pairs={{0,1},{1,0},{2,3},{3,2},{4,5},{5,4},{6,7},{7,6},{8,9},{9,8},{10,11... | collective-permute-start | bytes 49160 | tf_op jit(solution)/shard_map/ppermute | solution.py:136
  3.6 11.4 %collective-permute-start.3 = (f32[16,256]{1,0:T(8,128)S(1)}, f32[16,256]{1,0:T(8,128)S(1)}, u32[]{:S(2)}, u32[]{:S(2)}) collective-permute-start(f32[16,256]{1,0:T(8,128)S(1)} %copy_bitcast_fusion.2), channel_id=1, source_target_pairs={{0,2},{1,3},{2,0},{3,1},{4,6},{5,7},{6,4},{7,5},{8,10},{9,11},{10,... | collective-permute-start | bytes 49160 | tf_op jit(solution)/shard_map/ppermute | solution.py:136
  6.2 8.9 %collective-permute-start.4 = (f32[16,256]{1,0:T(8,128)S(1)}, f32[16,256]{1,0:T(8,128)S(1)}, u32[]{:S(2)}, u32[]{:S(2)}) collective-permute-start(f32[16,256]{1,0:T(8,128)S(1)} %copy_bitcast_fusion.2), channel_id=1, source_target_pairs={{0,3},{1,2},{2,1},{3,0},{4,7},{5,6},{6,5},{7,4},{8,11},{9,10},{10,... | collective-permute-start | bytes 49160 | tf_op jit(solution)/shard_map/ppermute | solution.py:136
  10.7 5.3 %collective-permute-start = (f32[16,1024]{1,0:T(8,128)}, f32[16,1024]{1,0:T(8,128)S(1)}, u32[]{:S(2)}, u32[]{:S(2)}) collective-permute-start(f32[16,1024]{1,0:T(8,128)} %get-tuple-element.8.last_ref), channel_id=1, source_target_pairs={{0,1},{1,2},{2,3},{3,4},{4,5},{5,6},{6,7},{7,8},{8,9},{9,10},{10,1... | collective-permute-start | bytes 196616 | tf_op jit(solution)/shard_map/ppermute | solution.py:17
  12.8 4.7 %collective-permute-start.1 = (f32[2,16,1024]{2,1,0:T(8,128)}, f32[2,16,1024]{2,1,0:T(8,128)S(1)}, u32[]{:S(2)}, u32[]{:S(2)}) collective-permute-start(f32[2,16,1024]{2,1,0:T(8,128)} %get-tuple-element.9), channel_id=1, source_target_pairs={{1,0},{2,1},{3,2},{4,3},{5,4},{6,5},{7,6},{8,7},{9,8},{10,9},{11,1... | collective-permute-start | bytes 393224 | tf_op jit(solution)/shard_map/ppermute | solution.py:17
  15.4 19.4 %copy-start.3 = (s32[8,4]{0,1:T(4,128)S(1)}, s32[8,4]{0,1:T(4,128)}, u32[]{:S(2)}) copy-start(s32[8,4]{0,1:T(4,128)} %param.21) | copy-start | bytes 388
  16.0 1.5 %copy-start.2 = (f32[16,1024]{1,0:T(8,128)}, f32[16,1024]{1,0:T(8,128)S(1)}, u32[]{:S(2)}) copy-start(f32[16,1024]{1,0:T(8,128)S(1)} %collective-permute-done.prev_ref) | copy-start | bytes 196612
  17.4 0.7 %copy-start.1 = (f32[2,16,1024]{2,1,0:T(8,128)}, f32[2,16,1024]{2,1,0:T(8,128)S(1)}, u32[]{:S(2)}) copy-start(f32[2,16,1024]{2,1,0:T(8,128)S(1)} %collective-permute-done.1.next_ref) | copy-start | bytes 393220
  19.8 9.8 %collective-permute-start.6 = (f32[1,16,1024]{2,1,0:T(8,128)}, f32[1,16,1024]{2,1,0:T(8,128)S(1)}, u32[]{:S(2)}, u32[]{:S(2)}) collective-permute-start(f32[1,16,1024]{2,1,0:T(8,128)} %bitcast.76), channel_id=1, source_target_pairs={{0,8},{1,9},{2,10},{3,11},{4,12},{5,13},{6,14},{7,15},{8,0},{9,1},... | collective-permute-start | bytes 196616 | tf_op jit(solution)/shard_map/ppermute | solution.py:136
  25.3 4.9 %collective-permute-start.5 = (f32[1,16,1024]{2,1,0:T(8,128)}, f32[1,16,1024]{2,1,0:T(8,128)S(1)}, u32[]{:S(2)}, u32[]{:S(2)}) collective-permute-start(f32[1,16,1024]{2,1,0:T(8,128)} %bitcast.77), channel_id=1, source_target_pairs={{0,4},{1,5},{2,6},{3,7},{4,0},{5,1},{6,2},{7,3},{8,12},{9,13},{10,... | collective-permute-start | bytes 196616 | tf_op jit(solution)/shard_map/ppermute | solution.py:136
  27.0 6.3 %collective-permute-start.7 = (f32[1,16,1024]{2,1,0:T(8,128)}, f32[1,16,1024]{2,1,0:T(8,128)S(1)}, u32[]{:S(2)}, u32[]{:S(2)}) collective-permute-start(f32[1,16,1024]{2,1,0:T(8,128)} %bitcast.78), channel_id=1, source_target_pairs={{0,12},{1,13},{2,14},{3,15},{4,8},{5,9},{6,10},{7,11},{8,4},{9,5},... | collective-permute-start | bytes 196616 | tf_op jit(solution)/shard_map/ppermute | solution.py:136
  34.8 1.4 %collective-permute-start.8 = (f32[2,16,1024]{2,1,0:T(8,128)S(1)}, f32[2,16,1024]{2,1,0:T(8,128)S(1)}, u32[]{:S(2)}, u32[]{:S(2)}) collective-permute-start(f32[2,16,1024]{2,1,0:T(8,128)S(1)} %slice.29), channel_id=1, source_target_pairs={{0,1},{1,0},{2,3},{3,2},{4,5},{5,4},{6,7},{7,6},{8,9},{9,8},{10,11... | collective-permute-start | bytes 393224 | tf_op jit(solution)/shard_map/ppermute | solution.py:136
  36.2 4.3 %collective-permute-start.9 = (f32[16,1024]{1,0:T(8,128)S(1)}, f32[16,1024]{1,0:T(8,128)S(1)}, u32[]{:S(2)}, u32[]{:S(2)}) collective-permute-start(f32[16,1024]{1,0:T(8,128)S(1)} %slice_bitcast_fusion), channel_id=1, source_target_pairs={{0,2},{1,3},{2,0},{3,1},{4,6},{5,7},{6,4},{7,5},{8,10},{9,11},{10,... | collective-permute-start | bytes 196616 | tf_op jit(solution)/shard_map/ppermute | solution.py:136

commit v9 on v7

--- a/solution.py
+++ b/solution.py
@@ -50,19 +50,19 @@
         lo_z, up_z = coefs(f, 4, vz_ref[j], d)
         s_xm = jnp.where(sub == 0, 0.0, pltpu.roll(s, 1, 0))
         jx = s - s_xm
-        ax = -lo_x * jx
+        ax = lo_x * jx
         ax_next = jnp.where(sub == rows - 1, 0.0, pltpu.roll(ax, rows - 1, 0))
-        img = up_x * jx + ax_next
+        img = up_x * jx - ax_next
         s_ym = jnp.where(lane == 0, 0.0, pltpu.roll(s, 1, 1))
         jy = s - s_ym
-        ay = -lo_y * jy
+        ay = lo_y * jy
         ay_next = jnp.where(lane == cols - 1, 0.0, pltpu.roll(ay, cols - 1, 1))
-        img = img + (up_y * jy + ay_next)
+        img = img + (up_y * jy - ay_next)
         jz = s - prev
         img = img + up_z * jz
         acc = acc + w_ref[z] * img
         w_before = jnp.where(z > 0, w_ref[jnp.maximum(z - 1, 0)], 0.0)
-        acc = acc + w_before * (-lo_z * jz)
+        acc = acc - w_before * (lo_z * jz)
         prev = s
     out_ref[...] += acc
 
@@ -103,21 +103,27 @@
 
 def fix_kernel(w_ref, partial_ref, up_ref, prev_ref, next_ref, last_ref, out_ref):
     rows, cols = partial_ref.shape
-    w = w_ref[...]
-    corr_first = jnp.sum(w * (-up_ref[...] * prev_ref[...]), axis=0, keepdims=True)
-    ax_next = -next_ref[1] * (next_ref[0] - last_ref[...])
-    corr_last = jnp.sum(w * ax_next, axis=0, keepdims=True)
+    depth = up_ref.shape[0]
+    corr_first = jnp.zeros((1, cols), jnp.float32)
+    corr_last = jnp.zeros((1, cols), jnp.float32)
+    for z in range(depth):
+        w = w_ref[z]
+        corr_first = corr_first - w * (up_ref[pl.ds(z, 1), :] * prev_ref[pl.ds(z, 1), :])
+        jump = next_ref[0, pl.ds(z, 1), :] - last_ref[pl.ds(z, 1), :]
+        corr_last = corr_last - w * (next_ref[1, pl.ds(z, 1), :] * jump)
     row = lax.broadcasted_iota(jnp.int32, (rows, cols), 0)
     out_ref[...] = (
         partial_ref[...] + jnp.where(row == 0, corr_first, 0.0) + jnp.where(row == rows - 1, corr_last, 0.0)
     )
 
 
-def corrected(w_col, partial, up_x0, from_prev, from_next, last_s):
+def corrected(w, partial, up_x0, from_prev, from_next, last_s):
+    vmem = pl.BlockSpec(memory_space=pltpu.VMEM)
     return pl.pallas_call(
         fix_kernel,
+        in_specs=[pl.BlockSpec(memory_space=pltpu.SMEM)] + [vmem] * 5,
         out_shape=jax.ShapeDtypeStruct(partial.shape, jnp.float32),
-    )(w_col, partial, up_x0, from_prev, from_next, last_s)
+    )(w, partial, up_x0, from_prev, from_next, last_s)
 
 
 def gather_rounds(count):
@@ -195,7 +201,7 @@
     from_next = passed_along(to_prev, "gx", -1)
     from_prev = passed_along(last_s, "gx", 1)
 
-    recharge = corrected(layer_weight[:, None], partial, up_x0, from_prev, from_next, last_s)
+    recharge = corrected(layer_weight, partial, up_x0, from_prev, from_next, last_s)
 
     own_slab = cx_slab(cov_x, offsets_x, me, rows)
     slab = jnp.concatenate([own_slab] + [swap(own_slab, "gx", m) for m in (1, 2, 3)], axis=0)

time: 41.3 us -> 41.2 us (level)
  waiting for transfers between devices: 11.8 us -> 12.5 us
  local copies, waits for them, and re-layouts: 3.92 us -> 3.24 us
    ppermute x8, waiting for transfers between devices: 11.8 us -> 12.5 us  [swap(): return lax.ppermute(value, axis, [(i, i ^ mask) for i in range(count)])]
    broadcast_in_dim x1 -> x0, local copies, waits for them, and re-layouts: 0.68 us -> none  [body(): layer_weight[:, None]]
  transfers between devices with their start and end apart: 10 -> 10, of which waited for: 7 -> 7; matrix products, arithmetic and copies ran while one was open for 7% -> 6% of each run, Pallas kernels for 0% -> 0%
where the time goes in v9:
time: 41.2 us; the launch traced here: 41 us
  starting transfers between devices  14.5 us (35%)
  waiting for transfers between devices  12.5 us (30%)
  Pallas kernels  6.3 us (15%)
  local copies, waits for them, and re-layouts  3.24 us (8%)
  matrix products  3.07 us (7%)
  between operations  0.91 us (2%)
  other arithmetic  0.42 us (1%)
    ppermute x8, waiting for transfers between devices, swap(): return lax.ppermute(value, axis, [(i, i ^ mask) for i in range(count)])  12.5 us
    ppermute x8, starting transfers between devices, swap(): return lax.ppermute(value, axis, [(i, i ^ mask) for i in range(count)])  10.9 us
    pallas_call x1, Pallas kernels, stencil(): pl.pallas_call(stencil_kernel, grid=(depth // zc,), in_specs=[pl.BlockSpe...  4.6 us
    ppermute x2, starting transfers between devices, passed_along(): lax.ppermute(value, axis, [(source, source + steps) for source in range(f...  3.65 us
    dot_general x4, matrix products, product(): jnp.dot(cols, piece.reshape(-1, piece.shape[-1]), precision=precise, pref...  2.12 us
    pallas_call x1, Pallas kernels, corrected(): pl.pallas_call(fix_kernel, in_specs=[pl.BlockSpec(memory_space=pltpu.SMEM...  1.69 us
    dot_general x1, matrix products, body(): jnp.einsum('xrkc,rikc->xri', picked, cov_y.reshape(nyb, BLK, cov_y.shape[...  0.96 us
  transfers between devices with their start and end apart: 10, of which 7 were waited for; matrix products, arithmetic and copies ran while one was open for 6% of the time, Pallas kernels for 0%

profile of v9, /device:TPU:0, one launch (start us, length us, event | category | flops | bytes accessed | tf_op | source)
XLA Modules:
  0.0 41.0 jit_solution(1009859843302887459)
XLA Ops:
  0.7 4.6 %shard_map.158 = (f32[16,1024]{1,0:T(8,128)}, f32[2,16,1024]{2,1,0:T(8,128)}, f32[16,1024]{1,0:T(8,128)}, f32[16,1024]{1,0:T(8,128)}) custom-call(f32[16]{0:T(128)} %w_ref.3, f32[16,16,1024]{2,1,0:T(8,128)} %sprev_ref.1, f32[16,16,1024]{2,1,0:T(8,128)} %sprev_ref.1, s32[16,16,1024]{2,1,0:T(8,128)} %f_ref.1, f32[16,16,1024]{2,1,0:T(8,128)} %vx_ref.1, ...), custom_call_target="tpu_custom_call" | custom-call | tf_op jit(solution)/shard_map/pallas_call | solution.py:75
  5.3 2.4 %collective-permute-start = (f32[16,1024]{1,0:T(8,128)}, f32[16,1024]{1,0:T(8,128)S(1)}, u32[]{:S(2)}, u32[]{:S(2)}) collective-permute-start(f32[16,1024]{1,0:T(8,128)} %get-tuple-element.9.last_ref), channel_id=1, source_target_pairs={{0,1},{1,2},{2,3},{3,4},{4,5},{5,6},{6,7},{7,8},{8,9},{9,10},{10,1... | collective-permute-start | bytes 196616 | tf_op jit(solution)/shard_map/ppermute | solution.py:17
  7.6 1.3 %collective-permute-start.1 = (f32[2,16,1024]{2,1,0:T(8,128)}, f32[2,16,1024]{2,1,0:T(8,128)S(1)}, u32[]{:S(2)}, u32[]{:S(2)}) collective-permute-start(f32[2,16,1024]{2,1,0:T(8,128)} %get-tuple-element.10), channel_id=1, source_target_pairs={{1,0},{2,1},{3,2},{4,3},{5,4},{6,5},{7,6},{8,7},{9,8},{10,9},{11,1... | collective-permute-start | bytes 393224 | tf_op jit(solution)/shard_map/ppermute | solution.py:17
  9.0 0.6 %gather_fusion = s32[16,4]{1,0:T(8,128)S(1)} fusion(s32[2,4]{1,0:T(2,128)S(1)} %copy-done.1, s32[1024]{0:T(1024)S(1)} %pad_clamp_fusion.1), kind=kCustom, calls=%fused_computation | custom fusion | bytes 576 | tf_op jit(solution)/shard_map/gather | solution.py:149
  9.8 0.1 select_reduce_fusion
  9.9 3.3 %collective-permute-start.2 = (f32[16,256]{1,0:T(8,128)S(1)}, f32[16,256]{1,0:T(8,128)S(1)}, u32[]{:S(2)}, u32[]{:S(2)}) collective-permute-start(f32[16,256]{1,0:T(8,128)S(1)} %copy_bitcast_fusion.2), channel_id=1, source_target_pairs={{0,1},{1,0},{2,3},{3,2},{4,5},{5,4},{6,7},{7,6},{8,9},{9,8},{10,11... | collective-permute-start | bytes 49160 | tf_op jit(solution)/shard_map/ppermute | solution.py:142
  13.2 1.7 %collective-permute-start.3 = (f32[16,256]{1,0:T(8,128)S(1)}, f32[16,256]{1,0:T(8,128)S(1)}, u32[]{:S(2)}, u32[]{:S(2)}) collective-permute-start(f32[16,256]{1,0:T(8,128)S(1)} %copy_bitcast_fusion.2), channel_id=1, source_target_pairs={{0,2},{1,3},{2,0},{3,1},{4,6},{5,7},{6,4},{7,5},{8,10},{9,11},{10,... | collective-permute-start | bytes 49160 | tf_op jit(solution)/shard_map/ppermute | solution.py:142
  14.9 0.1 copy.55
  15.1 0.1 copy.56
  15.2 2.1 %collective-permute-done.3 = f32[16,256]{1,0:T(8,128)S(1)} collective-permute-done((f32[16,256]{1,0:T(8,128)S(1)}, f32[16,256]{1,0:T(8,128)S(1)}, u32[]{:S(2)}, u32[]{:S(2)}) %collective-permute-start.3) | collective-permute-done | bytes 16416 | tf_op jit(solution)/shard_map/ppermute | solution.py:142
  17.3 0.1 copy.57
  17.4 0.7 %collective-permute-done.4 = f32[16,256]{1,0:T(8,128)S(1)} collective-permute-done((f32[16,256]{1,0:T(8,128)S(1)}, f32[16,256]{1,0:T(8,128)S(1)}, u32[]{:S(2)}, u32[]{:S(2)}) %collective-permute-start.4) | collective-permute-done | bytes 16416 | tf_op jit(solution)/shard_map/ppermute | solution.py:142
  18.0 0.1 copy.58
  18.2 0.6 %copy-done.3 = f32[16,1024]{1,0:T(8,128)} copy-done((f32[16,1024]{1,0:T(8,128)}, f32[16,1024]{1,0:T(8,128)S(1)}, u32[]{:S(2)}) %copy-start.3) | copy-done | bytes 65560
  18.8 1.7 %shard_map.159 = f32[16,1024]{1,0:T(8,128)} custom-call(f32[16]{0:T(128)} %w_ref.3, f32[16,1024]{1,0:T(8,128)} %get-tuple-element.7.partial_ref, f32[16,1024]{1,0:T(8,128)} %get-tuple-element.8.up_ref, f32[16,1024]{1,0:T(8,128)} %copy-done.3, f32[2,16,1024]{2,1,0:T(8,128)} %copy-done.2, f32[16,1024]{1,0:T(8,128)} %get-tuple-element.9.last_ref), custom_call_target="tpu_custom_call" | custom-call | tf_op jit(solution)/shard_map/pallas_call | solution.py:122
  20.5 2.8 %collective-permute-start.6 = (f32[1,16,1024]{2,1,0:T(8,128)}, f32[1,16,1024]{2,1,0:T(8,128)S(1)}, u32[]{:S(2)}, u32[]{:S(2)}) collective-permute-start(f32[1,16,1024]{2,1,0:T(8,128)} %bitcast.80), channel_id=1, source_target_pairs={{0,8},{1,9},{2,10},{3,11},{4,12},{5,13},{6,14},{7,15},{8,0},{9,1},... | collective-permute-start | bytes 196616 | tf_op jit(solution)/shard_map/ppermute | solution.py:142
  23.3 0.2 pad_maximum_fusion
  23.5 1.6 %collective-permute-start.5 = (f32[1,16,1024]{2,1,0:T(8,128)}, f32[1,16,1024]{2,1,0:T(8,128)S(1)}, u32[]{:S(2)}, u32[]{:S(2)}) collective-permute-start(f32[1,16,1024]{2,1,0:T(8,128)} %bitcast.81), channel_id=1, source_target_pairs={{0,4},{1,5},{2,6},{3,7},{4,0},{5,1},{6,2},{7,3},{8,12},{9,13},{10,... | collective-permute-start | bytes 196616 | tf_op jit(solution)/shard_map/ppermute | solution.py:142
  25.2 1.6 %collective-permute-done.6 = f32[1,16,1024]{2,1,0:T(8,128)S(1)} collective-permute-done((f32[1,16,1024]{2,1,0:T(8,128)}, f32[1,16,1024]{2,1,0:T(8,128)S(1)}, u32[]{:S(2)}, u32[]{:S(2)}) %collective-permute-start.6) | collective-permute-done | bytes 65568 | tf_op jit(solution)/shard_map/ppermute | solution.py:142
  26.7 0.3 fusion.15
  27.1 1.0 %collective-permute-done.5 = f32[1,16,1024]{2,1,0:T(8,128)S(1)} collective-permute-done((f32[1,16,1024]{2,1,0:T(8,128)}, f32[1,16,1024]{2,1,0:T(8,128)S(1)}, u32[]{:S(2)}, u32[]{:S(2)}) %collective-permute-start.5) | collective-permute-done | bytes 65568 | tf_op jit(solution)/shard_map/ppermute | solution.py:142
  28.1 0.3 fusion.17
  28.4 3.1 %collective-permute-done.7 = f32[1,16,1024]{2,1,0:T(8,128)S(1)} collective-permute-done((f32[1,16,1024]{2,1,0:T(8,128)}, f32[1,16,1024]{2,1,0:T(8,128)S(1)}, u32[]{:S(2)}, u32[]{:S(2)}) %collective-permute-start.7) | collective-permute-done | bytes 65568 | tf_op jit(solution)/shard_map/ppermute | solution.py:142
  31.4 0.3 fusion.13
  31.7 1.2 %fusion.3 = f32[64,1024]{1,0:T(8,128)S(1)} fusion(f32[64,1024]{1,0:T(8,128)S(1)} %fusion.13, f32[64,1024]{1,0:T(8,128)S(1)} %fusion.15, f32[64,1024]{1,0:T(8,128)S(1)} %fusion.17, f32[16,1024]{1,0:T(8,128)} %shard_map.159, f32[64,16,16]{0,2,1:T(8,128)S(1)} %pad_maximum_fusion, s32[]{:T(128)} %bitcast.7, pred[]{:T(512)} %bitcast.1), kind=kOutput, calls=%fused_computation.6 | convolution fusion | flops 6489088 | bytes 1122309 | tf_op jit(solution)/shard_map/dot_general | solution.py:164
  33.2 0.1 copy.41
  33.3 1.0 %collective-permute-done.8 = f32[2,16,1024]{2,1,0:T(8,128)S(1)} collective-permute-done((f32[2,16,1024]{2,1,0:T(8,128)S(1)}, f32[2,16,1024]{2,1,0:T(8,128)S(1)}, u32[]{:S(2)}, u32[]{:S(2)}) %collective-permute-start.8) | collective-permute-done | bytes 131104 | tf_op jit(solution)/shard_map/ppermute | solution.py:142
  34.4 1.3 %collective-permute-start.9 = (f32[16,1024]{1,0:T(8,128)S(1)}, f32[16,1024]{1,0:T(8,128)S(1)}, u32[]{:S(2)}, u32[]{:S(2)}) collective-permute-start(f32[16,1024]{1,0:T(8,128)S(1)} %slice_bitcast_fusion), channel_id=1, source_target_pairs={{0,2},{1,3},{2,0},{3,1},{4,6},{5,7},{6,4},{7,5},{8,10},{9,11},{10,... | collective-permute-start | bytes 196616 | tf_op jit(solution)/shard_map/ppermute | solution.py:142
  35.7 3.1 %collective-permute-done.9 = f32[16,1024]{1,0:T(8,128)S(1)} collective-permute-done((f32[16,1024]{1,0:T(8,128)S(1)}, f32[16,1024]{1,0:T(8,128)S(1)}, u32[]{:S(2)}, u32[]{:S(2)}) %collective-permute-start.9) | collective-permute-done | bytes 65568 | tf_op jit(solution)/shard_map/ppermute | solution.py:142
  38.7 0.6 %gather_fusion.1 = f32[32,16,128]{2,1,0:T(8,128)S(1)} fusion(f32[16,8,128]{2,0,1:T(8,128)S(1)} %copy_bitcast_fusion.1, s32[1024]{0:T(1024)S(1)} %pad_clamp_fusion), kind=kCustom, calls=%fused_computation.1 | custom fusion | bytes 524416 | tf_op jit(solution)/shard_map/jit(_take)/gather | solution.py:212
  39.3 1.0 %fusion.4 = f32[8,2,8,128]{3,2,1,0:T(8,128)S(1)} fusion(f32[8,128,4,128]{3,2,1,0:T(4,128)S(1)} %bitcast.72, f32[8,4,16,128]{3,2,1,0:T(8,128)S(1)} %bitcast.75, pred[8,4]{1,0:T(8,128)(4,1)S(1)} %copy.41), kind=kOutput, calls=%fused_computation.7 | convolution fusion | flops 50397184 | bytes 2424864 | tf_op jit(solution)/shard_map/xrkc,rikc->xri/dot_general | solution.py:213
  40.3 0.7 %copy.70 = f32[8,2,8,128]{3,2,0,1:T(8,128)} copy(f32[8,2,8,128]{3,2,1,0:T(8,128)S(1)} %fusion.4) | data formatting | bytes 131072 | tf_op jit(solution)/shard_map/reshape | solution.py:219
  (33 shorter events, 0.7 us)
Async XLA Ops:
  0.6 38.7 %copy-start = (f32[1024,4,128]{2,1,0:T(4,128)S(1)}, f32[1024,4,128]{2,1,0:T(4,128)}, u32[]{:S(2)}) copy-start(f32[1024,4,128]{2,1,0:T(4,128)} %param.26) | copy-start | bytes 6291460
  0.6 8.4 %copy-start.1 = (s32[2,4]{1,0:T(2,128)S(1)}, s32[2,4]{1,0:T(2,128)}, u32[]{:S(2)}) copy-start(s32[2,4]{1,0:T(2,128)} %param.25) | copy-start | bytes 100
  0.7 9.1 %copy-start.4 = (bf16[16,4,128]{2,1,0:T(4,128)(2,1)S(1)}, bf16[16,4,128]{2,1,0:T(4,128)(2,1)}, u32[]{:S(2)}) copy-start(bf16[16,4,128]{2,1,0:T(4,128)(2,1)} %param.24) | copy-start | bytes 49156
  5.3 12.9 %collective-permute-start = (f32[16,1024]{1,0:T(8,128)}, f32[16,1024]{1,0:T(8,128)S(1)}, u32[]{:S(2)}, u32[]{:S(2)}) collective-permute-start(f32[16,1024]{1,0:T(8,128)} %get-tuple-element.9.last_ref), channel_id=1, source_target_pairs={{0,1},{1,2},{2,3},{3,4},{4,5},{5,6},{6,7},{7,8},{8,9},{9,10},{10,1... | collective-permute-start | bytes 196616 | tf_op jit(solution)/shard_map/ppermute | solution.py:17
  7.6 10.5 %collective-permute-start.1 = (f32[2,16,1024]{2,1,0:T(8,128)}, f32[2,16,1024]{2,1,0:T(8,128)S(1)}, u32[]{:S(2)}, u32[]{:S(2)}) collective-permute-start(f32[2,16,1024]{2,1,0:T(8,128)} %get-tuple-element.10), channel_id=1, source_target_pairs={{1,0},{2,1},{3,2},{4,3},{5,4},{6,5},{7,6},{8,7},{9,8},{10,9},{11,1... | collective-permute-start | bytes 393224 | tf_op jit(solution)/shard_map/ppermute | solution.py:17
  9.9 23.2 %copy-start.5 = (s32[8,4]{0,1:T(4,128)S(1)}, s32[8,4]{0,1:T(4,128)}, u32[]{:S(2)}) copy-start(s32[8,4]{0,1:T(4,128)} %param.27) | copy-start | bytes 388
  9.9 5.2 %collective-permute-start.2 = (f32[16,256]{1,0:T(8,128)S(1)}, f32[16,256]{1,0:T(8,128)S(1)}, u32[]{:S(2)}, u32[]{:S(2)}) collective-permute-start(f32[16,256]{1,0:T(8,128)S(1)} %copy_bitcast_fusion.2), channel_id=1, source_target_pairs={{0,1},{1,0},{2,3},{3,2},{4,5},{5,4},{6,7},{7,6},{8,9},{9,8},{10,11... | collective-permute-start | bytes 49160 | tf_op jit(solution)/shard_map/ppermute | solution.py:142
  13.2 4.1 %collective-permute-start.3 = (f32[16,256]{1,0:T(8,128)S(1)}, f32[16,256]{1,0:T(8,128)S(1)}, u32[]{:S(2)}, u32[]{:S(2)}) collective-permute-start(f32[16,256]{1,0:T(8,128)S(1)} %copy_bitcast_fusion.2), channel_id=1, source_target_pairs={{0,2},{1,3},{2,0},{3,1},{4,6},{5,7},{6,4},{7,5},{8,10},{9,11},{10,... | collective-permute-start | bytes 49160 | tf_op jit(solution)/shard_map/ppermute | solution.py:142
  14.9 3.2 %collective-permute-start.4 = (f32[16,256]{1,0:T(8,128)S(1)}, f32[16,256]{1,0:T(8,128)S(1)}, u32[]{:S(2)}, u32[]{:S(2)}) collective-permute-start(f32[16,256]{1,0:T(8,128)S(1)} %copy_bitcast_fusion.2), channel_id=1, source_target_pairs={{0,3},{1,2},{2,1},{3,0},{4,7},{5,6},{6,5},{7,4},{8,11},{9,10},{10,... | collective-permute-start | bytes 49160 | tf_op jit(solution)/shard_map/ppermute | solution.py:142
  18.1 0.6 %copy-start.3 = (f32[16,1024]{1,0:T(8,128)}, f32[16,1024]{1,0:T(8,128)S(1)}, u32[]{:S(2)}) copy-start(f32[16,1024]{1,0:T(8,128)S(1)} %collective-permute-done.prev_ref) | copy-start | bytes 196612
  18.2 0.7 %copy-start.2 = (f32[2,16,1024]{2,1,0:T(8,128)}, f32[2,16,1024]{2,1,0:T(8,128)S(1)}, u32[]{:S(2)}) copy-start(f32[2,16,1024]{2,1,0:T(8,128)S(1)} %collective-permute-done.1.next_ref) | copy-start | bytes 393220
  20.5 6.2 %collective-permute-start.6 = (f32[1,16,1024]{2,1,0:T(8,128)}, f32[1,16,1024]{2,1,0:T(8,128)S(1)}, u32[]{:S(2)}, u32[]{:S(2)}) collective-permute-start(f32[1,16,1024]{2,1,0:T(8,128)} %bitcast.80), channel_id=1, source_target_pairs={{0,8},{1,9},{2,10},{3,11},{4,12},{5,13},{6,14},{7,15},{8,0},{9,1},... | collective-permute-start | bytes 196616 | tf_op jit(solution)/shard_map/ppermute | solution.py:142
  23.5 4.5 %collective-permute-start.5 = (f32[1,16,1024]{2,1,0:T(8,128)}, f32[1,16,1024]{2,1,0:T(8,128)S(1)}, u32[]{:S(2)}, u32[]{:S(2)}) collective-permute-start(f32[1,16,1024]{2,1,0:T(8,128)} %bitcast.81), channel_id=1, source_target_pairs={{0,4},{1,5},{2,6},{3,7},{4,0},{5,1},{6,2},{7,3},{8,12},{9,13},{10,... | collective-permute-start | bytes 196616 | tf_op jit(solution)/shard_map/ppermute | solution.py:142
  25.2 6.3 %collective-permute-start.7 = (f32[1,16,1024]{2,1,0:T(8,128)}, f32[1,16,1024]{2,1,0:T(8,128)S(1)}, u32[]{:S(2)}, u32[]{:S(2)}) collective-permute-start(f32[1,16,1024]{2,1,0:T(8,128)} %bitcast.82), channel_id=1, source_target_pairs={{0,12},{1,13},{2,14},{3,15},{4,8},{5,9},{6,10},{7,11},{8,4},{9,5},... | collective-permute-start | bytes 196616 | tf_op jit(solution)/shard_map/ppermute | solution.py:142
  32.9 1.4 %collective-permute-start.8 = (f32[2,16,1024]{2,1,0:T(8,128)S(1)}, f32[2,16,1024]{2,1,0:T(8,128)S(1)}, u32[]{:S(2)}, u32[]{:S(2)}) collective-permute-start(f32[2,16,1024]{2,1,0:T(8,128)S(1)} %slice.13), channel_id=1, source_target_pairs={{0,1},{1,0},{2,3},{3,2},{4,5},{5,4},{6,7},{7,6},{8,9},{9,8},{10,11... | collective-permute-start | bytes 393224 | tf_op jit(solution)/shard_map/ppermute | solution.py:142
  34.4 4.3 %collective-permute-start.9 = (f32[16,1024]{1,0:T(8,128)S(1)}, f32[16,1024]{1,0:T(8,128)S(1)}, u32[]{:S(2)}, u32[]{:S(2)}) collective-permute-start(f32[16,1024]{1,0:T(8,128)S(1)} %slice_bitcast_fusion), channel_id=1, source_target_pairs={{0,2},{1,3},{2,0},{3,1},{4,6},{5,7},{6,4},{7,5},{8,10},{9,11},{10,... | collective-permute-start | bytes 196616 | tf_op jit(solution)/shard_map/ppermute | solution.py:142

commit v10 on v9

--- a/solution.py
+++ b/solution.py
@@ -101,7 +101,7 @@
     )(layer_weight, s, s, f, vx, vy, vz, d)
 
 
-def fix_kernel(w_ref, partial_ref, up_ref, prev_ref, next_ref, last_ref, out_ref):
+def fix_kernel(w_ref, partial_ref, up_ref, prev_ref, next_ref, last_ref, out_ref, corr_ref):
     rows, cols = partial_ref.shape
     depth = up_ref.shape[0]
     corr_first = jnp.zeros((1, cols), jnp.float32)
@@ -115,6 +115,8 @@
     out_ref[...] = (
         partial_ref[...] + jnp.where(row == 0, corr_first, 0.0) + jnp.where(row == rows - 1, corr_last, 0.0)
     )
+    corr_ref[0:1, :] = corr_first
+    corr_ref[1:2, :] = corr_last
 
 
 def corrected(w, partial, up_x0, from_prev, from_next, last_s):
@@ -122,7 +124,11 @@
     return pl.pallas_call(
         fix_kernel,
         in_specs=[pl.BlockSpec(memory_space=pltpu.SMEM)] + [vmem] * 5,
-        out_shape=jax.ShapeDtypeStruct(partial.shape, jnp.float32),
+        out_specs=[vmem, vmem],
+        out_shape=[
+            jax.ShapeDtypeStruct(partial.shape, jnp.float32),
+            jax.ShapeDtypeStruct((2, partial.shape[1]), jnp.float32),
+        ],
     )(w, partial, up_x0, from_prev, from_next, last_s)
 
 
@@ -153,25 +159,47 @@
     return slab.reshape(rows, -1)
 
 
-def mixed_rows(local, slab, axis):
+def gather_pieces(local, axis):
+    buf = local[None]
+    entries = [0]
+    pieces = []
+    for masks in gather_rounds(lax.axis_size(axis)):
+        others = [swap(buf, axis, m) for m in masks]
+        for m, other in zip(masks, others):
+            pieces.append((other, [m ^ q for q in entries]))
+        buf = jnp.concatenate([buf] + others, axis=0)
+        entries = entries + [m ^ q for m in masks for q in entries]
+    return pieces
+
+
+def mixed_rows(partial, recharge, corr, slab, axis):
     count = lax.axis_size(axis)
     me = lax.axis_index(axis)
-    rows = local.shape[0]
+    rows = partial.shape[0]
     per_device = slab.reshape(slab.shape[0], count, rows)
 
-    def product(piece, masks):
-        cols = jnp.take(per_device, me ^ jnp.array(masks, jnp.int32), axis=1).reshape(slab.shape[0], -1)
-        return jnp.dot(cols, piece.reshape(-1, piece.shape[-1]), precision=precise, preferred_element_type=jnp.float32)
-
-    buf = local[None]
-    entries = [0]
-    total = product(buf, entries)
-    for masks in gather_rounds(count):
-        others = [swap(buf, axis, m) for m in masks]
-        for m, other in zip(masks, others):
-            total = total + product(other, [m ^ q for q in entries])
-        buf = jnp.concatenate([buf] + others, axis=0)
-        entries = entries + [m ^ q for m in masks for q in entries]
+    def columns(masks):
+        return jnp.take(per_device, me ^ jnp.array(masks, jnp.int32), axis=1)
+
+    def dot(cols, piece):
+        return jnp.dot(
+            cols.reshape(slab.shape[0], -1),
+            piece.reshape(-1, piece.shape[-1]),
+            precision=precise,
+            preferred_element_type=jnp.float32,
+        )
+
+    bulk = gather_pieces(partial, axis)
+    total = dot(columns([0]), recharge[None])
+    taken = []
+    for piece, masks in bulk:
+        cols = columns(masks)
+        taken.append(cols)
+        total = total + dot(cols, piece)
+    fixes = gather_pieces(corr, axis)
+    for (piece, masks), cols in zip(fixes, taken):
+        edge_cols = jnp.stack([cols[:, :, 0], cols[:, :, rows - 1]], axis=2)
+        total = total + dot(edge_cols, piece)
     parts = total.reshape(4, rows, total.shape[-1])
     got = swap(parts[1::2], axis, 1)
     near = parts[0::2] + got
@@ -201,11 +229,11 @@
     from_next = passed_along(to_prev, "gx", -1)
     from_prev = passed_along(last_s, "gx", 1)
 
-    recharge = corrected(layer_weight, partial, up_x0, from_prev, from_next, last_s)
+    recharge, corr = corrected(layer_weight, partial, up_x0, from_prev, from_next, last_s)
 
     own_slab = cx_slab(cov_x, offsets_x, me, rows)
     slab = jnp.concatenate([own_slab] + [swap(own_slab, "gx", m) for m in (1, 2, 3)], axis=0)
-    mixed = mixed_rows(recharge, slab, "gx")
+    mixed = mixed_rows(partial, recharge, corr, slab, "gx")
 
     nyb = offsets_y.shape[0]
     col_block = (jnp.arange(nyb)[:, None] + offsets_y) % nyb

time: 41.2 us -> 47.5 us (1.15)
  starting transfers between devices: 14.5 us -> 18.5 us
  local copies, waits for them, and re-layouts: 3.24 us -> 4.78 us
  matrix products: 3.07 us -> 4.11 us
    ppermute x8 -> x11, starting transfers between devices: 10.9 us -> 15.5 us  [swap(): return lax.ppermute(value, axis, [(i, i ^ mask) for i in range(count)])]
    ppermute x8 -> x11, waiting for transfers between devices: 12.5 us -> 11.2 us  [swap(): return lax.ppermute(value, axis, [(i, i ^ mask) for i in range(count)])]
    ppermute x2, waiting for transfers between devices: 0.01 us -> 1.16 us  [passed_along(): lax.ppermute(value, axis, [(source, source + steps) for source in range(f...]
    dot_general x4 -> x7, matrix products: 2.12 us -> 3.15 us  [dot(): jnp.dot(cols.reshape(slab.shape[0], -1), piece.reshape(-1, piece.shape[-1...]
    gather x1, local copies, waits for them, and re-layouts: 0.56 us -> 1.38 us  [cx_slab(): target = (row_block[:, None] + offsets[row_block]) % nxb]
    convert_element_type x1, local copies, waits for them, and re-layouts: 0.01 us -> 0.72 us  [cx_slab(): cov_rows.astype(jnp.float32)[:, :, None, :]]
    ppermute x2, starting transfers between devices: 3.65 us -> 2.98 us  [passed_along(): lax.ppermute(value, axis, [(source, source + steps) for source in range(f...]
  transfers between devices with their start and end apart: 10 -> 13, of which waited for: 7 -> 6; matrix products, arithmetic and copies ran while one was open for 6% -> 5% of each run, Pallas kernels for 0% -> 13%
where the time goes in v10:
time: 47.5 us; the launch traced here: 47.2 us
  starting transfers between devices  18.5 us (39%)
  waiting for transfers between devices  12.3 us (26%)
  Pallas kernels  6.15 us (13%)
  local copies, waits for them, and re-layouts  4.78 us (10%)
  matrix products  4.11 us (9%)
  between operations  0.92 us (2%)
    ppermute x11, starting transfers between devices, swap(): return lax.ppermute(value, axis, [(i, i ^ mask) for i in range(count)])  15.5 us
    ppermute x11, waiting for transfers between devices, swap(): return lax.ppermute(value, axis, [(i, i ^ mask) for i in range(count)])  11.2 us
    pallas_call x1, Pallas kernels, stencil(): pl.pallas_call(stencil_kernel, grid=(depth // zc,), in_specs=[pl.BlockSpe...  4.45 us
    dot_general x7, matrix products, dot(): jnp.dot(cols.reshape(slab.shape[0], -1), piece.reshape(-1, piece.shape[-1...  3.15 us
    ppermute x2, starting transfers between devices, passed_along(): lax.ppermute(value, axis, [(source, source + steps) for source in range(f...  2.98 us
    pallas_call x1, Pallas kernels, corrected(): pl.pallas_call(fix_kernel, in_specs=[pl.BlockSpec(memory_space=pltpu.SMEM...  1.7 us
    gather x1, local copies, waits for them, and re-layouts, cx_slab(): target = (row_block[:, None] + offsets[row_block]) % nxb  1.38 us
    ppermute x2, waiting for transfers between devices, passed_along(): lax.ppermute(value, axis, [(source, source + steps) for source in range(f...  1.16 us
  transfers between devices with their start and end apart: 13, of which 6 were waited for; matrix products, arithmetic and copies ran while one was open for 5% of the time, Pallas kernels for 13%

profile of v10, /device:TPU:0, one launch (start us, length us, event | category | flops | bytes accessed | tf_op | source)
XLA Modules:
  0.0 47.2 jit_solution(3988650482556147147)
XLA Ops:
  0.7 1.4 %gather_fusion = s32[16,4]{1,0:T(8,128)S(1)} fusion(s32[2,4]{1,0:T(2,128)} %param.25, s32[1024]{0:T(1024)S(1)} %pad_clamp_fusion.1), kind=kCustom, calls=%fused_computation | custom fusion | bytes 576 | tf_op jit(solution)/shard_map/gather | solution.py:155
  2.3 0.7 %copy.50 = f32[16,4,128]{2,0,1:T(8,128)S(1)} copy(bf16[16,4,128]{2,1,0:T(4,128)(2,1)} %param.24) | data formatting | bytes 49152 | tf_op jit(solution)/shard_map/convert_element_type | solution.py:158
  3.1 0.5 %collective-permute-start.2 = (f32[16,256]{1,0:T(8,128)S(1)}, f32[16,256]{1,0:T(8,128)S(1)}, u32[]{:S(2)}, u32[]{:S(2)}) collective-permute-start(f32[16,256]{1,0:T(8,128)S(1)} %copy_bitcast_fusion.2), channel_id=1, source_target_pairs={{0,1},{1,0},{2,3},{3,2},{4,5},{5,4},{6,7},{7,6},{8,9},{9,8},{10,11... | collective-permute-start | bytes 49160 | tf_op jit(solution)/shard_map/ppermute | solution.py:148
  3.6 2.6 %collective-permute-start.3 = (f32[16,256]{1,0:T(8,128)S(1)}, f32[16,256]{1,0:T(8,128)S(1)}, u32[]{:S(2)}, u32[]{:S(2)}) collective-permute-start(f32[16,256]{1,0:T(8,128)S(1)} %copy_bitcast_fusion.2), channel_id=1, source_target_pairs={{0,2},{1,3},{2,0},{3,1},{4,6},{5,7},{6,4},{7,5},{8,10},{9,11},{10,... | collective-permute-start | bytes 49160 | tf_op jit(solution)/shard_map/ppermute | solution.py:148
  6.2 4.5 %shard_map.158 = (f32[16,1024]{1,0:T(8,128)}, f32[2,16,1024]{2,1,0:T(8,128)}, f32[16,1024]{1,0:T(8,128)}, f32[16,1024]{1,0:T(8,128)}) custom-call(f32[16]{0:T(128)} %w_ref.3, f32[16,16,1024]{2,1,0:T(8,128)} %sprev_ref.1, f32[16,16,1024]{2,1,0:T(8,128)} %sprev_ref.1, s32[16,16,1024]{2,1,0:T(8,128)} %f_ref.1, f32[16,16,1024]{2,1,0:T(8,128)} %vx_ref.1, ...), custom_call_target="tpu_custom_call" | custom-call | tf_op jit(solution)/shard_map/pallas_call | solution.py:75
  10.7 3.9 %collective-permute-start.7 = (f32[1,16,1024]{2,1,0:T(8,128)}, f32[1,16,1024]{2,1,0:T(8,128)S(1)}, u32[]{:S(2)}, u32[]{:S(2)}) collective-permute-start(f32[1,16,1024]{2,1,0:T(8,128)} %bitcast.100), channel_id=1, source_target_pairs={{0,12},{1,13},{2,14},{3,15},{4,8},{5,9},{6,10},{7,11},{8,4},{9,5},... | collective-permute-start | bytes 196616 | tf_op jit(solution)/shard_map/ppermute | solution.py:148
  14.7 0.7 %collective-permute-start.5 = (f32[1,16,1024]{2,1,0:T(8,128)}, f32[1,16,1024]{2,1,0:T(8,128)S(1)}, u32[]{:S(2)}, u32[]{:S(2)}) collective-permute-start(f32[1,16,1024]{2,1,0:T(8,128)} %bitcast.102), channel_id=1, source_target_pairs={{0,4},{1,5},{2,6},{3,7},{4,0},{5,1},{6,2},{7,3},{8,12},{9,13},{10,... | collective-permute-start | bytes 196616 | tf_op jit(solution)/shard_map/ppermute | solution.py:148
  15.5 1.7 %collective-permute-start = (f32[16,1024]{1,0:T(8,128)}, f32[16,1024]{1,0:T(8,128)S(1)}, u32[]{:S(2)}, u32[]{:S(2)}) collective-permute-start(f32[16,1024]{1,0:T(8,128)} %get-tuple-element.11.last_ref), channel_id=1, source_target_pairs={{0,1},{1,2},{2,3},{3,4},{4,5},{5,6},{6,7},{7,8},{8,9},{9,10},{10,1... | collective-permute-start | bytes 196616 | tf_op jit(solution)/shard_map/ppermute | solution.py:17
  17.2 0.1 copy.64
  17.3 1.3 %collective-permute-start.1 = (f32[2,16,1024]{2,1,0:T(8,128)}, f32[2,16,1024]{2,1,0:T(8,128)S(1)}, u32[]{:S(2)}, u32[]{:S(2)}) collective-permute-start(f32[2,16,1024]{2,1,0:T(8,128)} %get-tuple-element.12), channel_id=1, source_target_pairs={{1,0},{2,1},{3,2},{4,3},{5,4},{6,5},{7,6},{8,7},{9,8},{10,9},{11,1... | collective-permute-start | bytes 393224 | tf_op jit(solution)/shard_map/ppermute | solution.py:17
  18.7 0.2 pad_maximum_fusion
  19.0 0.3 fusion.16
  19.3 1.5 %collective-permute-done.6 = f32[1,16,1024]{2,1,0:T(8,128)S(1)} collective-permute-done((f32[1,16,1024]{2,1,0:T(8,128)}, f32[1,16,1024]{2,1,0:T(8,128)S(1)}, u32[]{:S(2)}, u32[]{:S(2)}) %collective-permute-start.6) | collective-permute-done | bytes 65568 | tf_op jit(solution)/shard_map/ppermute | solution.py:148
  20.8 0.3 fusion.18
  21.1 1.2 %collective-permute-done.1.next_ref = f32[2,16,1024]{2,1,0:T(8,128)S(1)} collective-permute-done((f32[2,16,1024]{2,1,0:T(8,128)}, f32[2,16,1024]{2,1,0:T(8,128)S(1)}, u32[]{:S(2)}, u32[]{:S(2)}) %collective-permute-start.1) | collective-permute-done | bytes 131104 | tf_op jit(solution)/shard_map/ppermute | solution.py:17
  22.3 0.6 %copy-done.1 = f32[2,16,1024]{2,1,0:T(8,128)} copy-done((f32[2,16,1024]{2,1,0:T(8,128)}, f32[2,16,1024]{2,1,0:T(8,128)S(1)}, u32[]{:S(2)}) %copy-start.1) | copy-done | bytes 131096
  22.9 1.7 %shard_map.159 = (f32[16,1024]{1,0:T(8,128)}, f32[2,1024]{1,0:T(2,128)}) custom-call(f32[16]{0:T(128)} %w_ref.3, f32[16,1024]{1,0:T(8,128)} %get-tuple-element.9.partial_ref, f32[16,1024]{1,0:T(8,128)} %get-tuple-element.10.up_ref, f32[16,1024]{1,0:T(8,128)} %copy-done.2, f32[2,16,1024]{2,1,0:T(8,128)} %copy-done.1, f32[16,1024]{1,0:T(8,128)} %get-tuple-element.11.last_ref), custom_call_target="tpu_custom_call" | custom-call | tf_op jit(solution)/shard_map/pallas_call | solution.py:124
  24.6 4.1 %collective-permute-start.8 = (f32[1,2,1024]{2,1,0:T(2,128)}, f32[1,2,1024]{2,1,0:T(2,128)S(1)}, u32[]{:S(2)}, u32[]{:S(2)}) collective-permute-start(f32[1,2,1024]{2,1,0:T(2,128)} %bitcast.103), channel_id=1, source_target_pairs={{0,4},{1,5},{2,6},{3,7},{4,0},{5,1},{6,2},{7,3},{8,12},{9,13},{10,... | collective-permute-start | bytes 24584 | tf_op jit(solution)/shard_map/ppermute | solution.py:148
  28.7 0.3 fusion.20
  29.0 3.0 %collective-permute-start.9 = (f32[1,2,1024]{2,1,0:T(2,128)}, f32[1,2,1024]{2,1,0:T(2,128)S(1)}, u32[]{:S(2)}, u32[]{:S(2)}) collective-permute-start(f32[1,2,1024]{2,1,0:T(2,128)} %bitcast.104), channel_id=1, source_target_pairs={{0,8},{1,9},{2,10},{3,11},{4,12},{5,13},{6,14},{7,15},{8,0},{9,1},... | collective-permute-start | bytes 24584 | tf_op jit(solution)/shard_map/ppermute | solution.py:148
  32.0 0.3 fusion.27
  32.3 1.5 %collective-permute-done.9 = f32[1,2,1024]{2,1,0:T(2,128)S(1)} collective-permute-done((f32[1,2,1024]{2,1,0:T(2,128)}, f32[1,2,1024]{2,1,0:T(2,128)S(1)}, u32[]{:S(2)}, u32[]{:S(2)}) %collective-permute-start.9) | collective-permute-done | bytes 8224 | tf_op jit(solution)/shard_map/ppermute | solution.py:148
  33.8 0.3 fusion.25
  34.2 3.5 %collective-permute-done.10 = f32[1,2,1024]{2,1,0:T(2,128)S(1)} collective-permute-done((f32[1,2,1024]{2,1,0:T(2,128)}, f32[1,2,1024]{2,1,0:T(2,128)S(1)}, u32[]{:S(2)}, u32[]{:S(2)}) %collective-permute-start.10) | collective-permute-done | bytes 8224 | tf_op jit(solution)/shard_map/ppermute | solution.py:148
  37.6 0.3 fusion.23
  38.0 1.2 %fusion.6 = f32[64,1024]{1,0:T(8,128)S(1)} fusion(f32[64,1024]{1,0:T(8,128)S(1)} %fusion.23, f32[64,1024]{1,0:T(8,128)S(1)} %fusion.25, f32[64,1024]{1,0:T(8,128)S(1)} %fusion.27, f32[64,1024]{1,0:T(8,128)S(1)} %fusion.16, f32[64,1024]{1,0:T(8,128)S(1)} %fusion.18, f32[64,1024]{1,0:T(8,128)S(1)} %fusion.20, f32[16,1024]{1,0:T(8,128)} %get-tuple-element.7, ...), kind=kOutput, calls=%fused_computation.9 | convolution fusion | flops 6685696 | bytes 1908741 | tf_op jit(solution)/shard_map/dot_general | solution.py:185
  39.6 1.0 %collective-permute-done.11 = f32[2,16,1024]{2,1,0:T(8,128)S(1)} collective-permute-done((f32[2,16,1024]{2,1,0:T(8,128)S(1)}, f32[2,16,1024]{2,1,0:T(8,128)S(1)}, u32[]{:S(2)}, u32[]{:S(2)}) %collective-permute-start.11) | collective-permute-done | bytes 131104 | tf_op jit(solution)/shard_map/ppermute | solution.py:148
  40.7 0.7 %collective-permute-start.12 = (f32[16,1024]{1,0:T(8,128)S(1)}, f32[16,1024]{1,0:T(8,128)S(1)}, u32[]{:S(2)}, u32[]{:S(2)}) collective-permute-start(f32[16,1024]{1,0:T(8,128)S(1)} %slice_bitcast_fusion), channel_id=1, source_target_pairs={{0,2},{1,3},{2,0},{3,1},{4,6},{5,7},{6,4},{7,5},{8,10},{9,11},{10,... | collective-permute-start | bytes 196616 | tf_op jit(solution)/shard_map/ppermute | solution.py:148
  41.3 3.7 %collective-permute-done.12 = f32[16,1024]{1,0:T(8,128)S(1)} collective-permute-done((f32[16,1024]{1,0:T(8,128)S(1)}, f32[16,1024]{1,0:T(8,128)S(1)}, u32[]{:S(2)}, u32[]{:S(2)}) %collective-permute-start.12) | collective-permute-done | bytes 65568 | tf_op jit(solution)/shard_map/ppermute | solution.py:148
  45.0 0.6 %gather_fusion.1 = f32[32,16,128]{2,1,0:T(8,128)S(1)} fusion(f32[16,8,128]{2,0,1:T(8,128)S(1)} %copy_bitcast_fusion.1, s32[1024]{0:T(1024)S(1)} %pad_clamp_fusion), kind=kCustom, calls=%fused_computation.1 | custom fusion | bytes 524416 | tf_op jit(solution)/shard_map/jit(_take)/gather | solution.py:240
  45.6 1.0 %fusion.7 = f32[8,2,8,128]{3,2,1,0:T(8,128)S(1)} fusion(f32[8,128,4,128]{3,2,1,0:T(4,128)S(1)} %bitcast.91, f32[8,4,16,128]{3,2,1,0:T(8,128)S(1)} %bitcast.94, pred[8,4]{1,0:T(8,128)(4,1)S(1)} %copy.48), kind=kOutput, calls=%fused_computation.10 | convolution fusion | flops 50397184 | bytes 2424864 | tf_op jit(solution)/shard_map/xrkc,rikc->xri/dot_general | solution.py:241
  46.6 0.7 %copy.77 = f32[8,2,8,128]{3,2,0,1:T(8,128)} copy(f32[8,2,8,128]{3,2,1,0:T(8,128)S(1)} %fusion.7) | data formatting | bytes 131072 | tf_op jit(solution)/shard_map/reshape | solution.py:247
  (42 shorter events, 1.1 us)
Async XLA Ops:
  0.6 45.0 %copy-start = (f32[1024,4,128]{2,1,0:T(4,128)S(1)}, f32[1024,4,128]{2,1,0:T(4,128)}, u32[]{:S(2)}) copy-start(f32[1024,4,128]{2,1,0:T(4,128)} %param.26) | copy-start | bytes 6291460
  3.1 11.6 %collective-permute-start.2 = (f32[16,256]{1,0:T(8,128)S(1)}, f32[16,256]{1,0:T(8,128)S(1)}, u32[]{:S(2)}, u32[]{:S(2)}) collective-permute-start(f32[16,256]{1,0:T(8,128)S(1)} %copy_bitcast_fusion.2), channel_id=1, source_target_pairs={{0,1},{1,0},{2,3},{3,2},{4,5},{5,4},{6,7},{7,6},{8,9},{9,8},{10,11... | collective-permute-start | bytes 49160 | tf_op jit(solution)/shard_map/ppermute | solution.py:148
  3.6 11.9 %collective-permute-start.3 = (f32[16,256]{1,0:T(8,128)S(1)}, f32[16,256]{1,0:T(8,128)S(1)}, u32[]{:S(2)}, u32[]{:S(2)}) collective-permute-start(f32[16,256]{1,0:T(8,128)S(1)} %copy_bitcast_fusion.2), channel_id=1, source_target_pairs={{0,2},{1,3},{2,0},{3,1},{4,6},{5,7},{6,4},{7,5},{8,10},{9,11},{10,... | collective-permute-start | bytes 49160 | tf_op jit(solution)/shard_map/ppermute | solution.py:148
  6.2 11.2 %collective-permute-start.4 = (f32[16,256]{1,0:T(8,128)S(1)}, f32[16,256]{1,0:T(8,128)S(1)}, u32[]{:S(2)}, u32[]{:S(2)}) collective-permute-start(f32[16,256]{1,0:T(8,128)S(1)} %copy_bitcast_fusion.2), channel_id=1, source_target_pairs={{0,3},{1,2},{2,1},{3,0},{4,7},{5,6},{6,5},{7,4},{8,11},{9,10},{10,... | collective-permute-start | bytes 49160 | tf_op jit(solution)/shard_map/ppermute | solution.py:148
  10.7 8.3 %collective-permute-start.7 = (f32[1,16,1024]{2,1,0:T(8,128)}, f32[1,16,1024]{2,1,0:T(8,128)S(1)}, u32[]{:S(2)}, u32[]{:S(2)}) collective-permute-start(f32[1,16,1024]{2,1,0:T(8,128)} %bitcast.100), channel_id=1, source_target_pairs={{0,12},{1,13},{2,14},{3,15},{4,8},{5,9},{6,10},{7,11},{8,4},{9,5},... | collective-permute-start | bytes 196616 | tf_op jit(solution)/shard_map/ppermute | solution.py:148
  14.6 6.2 %collective-permute-start.6 = (f32[1,16,1024]{2,1,0:T(8,128)}, f32[1,16,1024]{2,1,0:T(8,128)S(1)}, u32[]{:S(2)}, u32[]{:S(2)}) collective-permute-start(f32[1,16,1024]{2,1,0:T(8,128)} %bitcast.101), channel_id=1, source_target_pairs={{0,8},{1,9},{2,10},{3,11},{4,12},{5,13},{6,14},{7,15},{8,0},{9,1},... | collective-permute-start | bytes 196616 | tf_op jit(solution)/shard_map/ppermute | solution.py:148
  14.7 13.9 %collective-permute-start.5 = (f32[1,16,1024]{2,1,0:T(8,128)}, f32[1,16,1024]{2,1,0:T(8,128)S(1)}, u32[]{:S(2)}, u32[]{:S(2)}) collective-permute-start(f32[1,16,1024]{2,1,0:T(8,128)} %bitcast.102), channel_id=1, source_target_pairs={{0,4},{1,5},{2,6},{3,7},{4,0},{5,1},{6,2},{7,3},{8,12},{9,13},{10,... | collective-permute-start | bytes 196616 | tf_op jit(solution)/shard_map/ppermute | solution.py:148
  15.5 5.6 %collective-permute-start = (f32[16,1024]{1,0:T(8,128)}, f32[16,1024]{1,0:T(8,128)S(1)}, u32[]{:S(2)}, u32[]{:S(2)}) collective-permute-start(f32[16,1024]{1,0:T(8,128)} %get-tuple-element.11.last_ref), channel_id=1, source_target_pairs={{0,1},{1,2},{2,3},{3,4},{4,5},{5,6},{6,7},{7,8},{8,9},{9,10},{10,1... | collective-permute-start | bytes 196616 | tf_op jit(solution)/shard_map/ppermute | solution.py:17
  17.3 4.9 %collective-permute-start.1 = (f32[2,16,1024]{2,1,0:T(8,128)}, f32[2,16,1024]{2,1,0:T(8,128)S(1)}, u32[]{:S(2)}, u32[]{:S(2)}) collective-permute-start(f32[2,16,1024]{2,1,0:T(8,128)} %get-tuple-element.12), channel_id=1, source_target_pairs={{1,0},{2,1},{3,2},{4,3},{5,4},{6,5},{7,6},{8,7},{9,8},{10,9},{11,1... | collective-permute-start | bytes 393224 | tf_op jit(solution)/shard_map/ppermute | solution.py:17
  19.3 20.0 %copy-start.3 = (s32[8,4]{0,1:T(4,128)S(1)}, s32[8,4]{0,1:T(4,128)}, u32[]{:S(2)}) copy-start(s32[8,4]{0,1:T(4,128)} %param.27) | copy-start | bytes 388
  21.1 1.2 %copy-start.2 = (f32[16,1024]{1,0:T(8,128)}, f32[16,1024]{1,0:T(8,128)S(1)}, u32[]{:S(2)}) copy-start(f32[16,1024]{1,0:T(8,128)S(1)} %collective-permute-done.prev_ref) | copy-start | bytes 196612
  22.3 0.6 %copy-start.1 = (f32[2,16,1024]{2,1,0:T(8,128)}, f32[2,16,1024]{2,1,0:T(8,128)S(1)}, u32[]{:S(2)}) copy-start(f32[2,16,1024]{2,1,0:T(8,128)S(1)} %collective-permute-done.1.next_ref) | copy-start | bytes 393220
  24.6 7.4 %collective-permute-start.8 = (f32[1,2,1024]{2,1,0:T(2,128)}, f32[1,2,1024]{2,1,0:T(2,128)S(1)}, u32[]{:S(2)}, u32[]{:S(2)}) collective-permute-start(f32[1,2,1024]{2,1,0:T(2,128)} %bitcast.103), channel_id=1, source_target_pairs={{0,4},{1,5},{2,6},{3,7},{4,0},{5,1},{6,2},{7,3},{8,12},{9,13},{10,... | collective-permute-start | bytes 24584 | tf_op jit(solution)/shard_map/ppermute | solution.py:148
  29.0 4.8 %collective-permute-start.9 = (f32[1,2,1024]{2,1,0:T(2,128)}, f32[1,2,1024]{2,1,0:T(2,128)S(1)}, u32[]{:S(2)}, u32[]{:S(2)}) collective-permute-start(f32[1,2,1024]{2,1,0:T(2,128)} %bitcast.104), channel_id=1, source_target_pairs={{0,8},{1,9},{2,10},{3,11},{4,12},{5,13},{6,14},{7,15},{8,0},{9,1},... | collective-permute-start | bytes 24584 | tf_op jit(solution)/shard_map/ppermute | solution.py:148
  32.0 5.7 %collective-permute-start.10 = (f32[1,2,1024]{2,1,0:T(2,128)}, f32[1,2,1024]{2,1,0:T(2,128)S(1)}, u32[]{:S(2)}, u32[]{:S(2)}) collective-permute-start(f32[1,2,1024]{2,1,0:T(2,128)} %bitcast.105), channel_id=1, source_target_pairs={{0,12},{1,13},{2,14},{3,15},{4,8},{5,9},{6,10},{7,11},{8,4},{9,5},... | collective-permute-start | bytes 24584 | tf_op jit(solution)/shard_map/ppermute | solution.py:148
  39.2 1.4 %collective-permute-start.11 = (f32[2,16,1024]{2,1,0:T(8,128)S(1)}, f32[2,16,1024]{2,1,0:T(8,128)S(1)}, u32[]{:S(2)}, u32[]{:S(2)}) collective-permute-start(f32[2,16,1024]{2,1,0:T(8,128)S(1)} %slice.37), channel_id=1, source_target_pairs={{0,1},{1,0},{2,3},{3,2},{4,5},{5,4},{6,7},{7,6},{8,9},{9,8},{10,11... | collective-permute-start | bytes 393224 | tf_op jit(solution)/shard_map/ppermute | solution.py:148
  40.7 4.3 %collective-permute-start.12 = (f32[16,1024]{1,0:T(8,128)S(1)}, f32[16,1024]{1,0:T(8,128)S(1)}, u32[]{:S(2)}, u32[]{:S(2)}) collective-permute-start(f32[16,1024]{1,0:T(8,128)S(1)} %slice_bitcast_fusion), channel_id=1, source_target_pairs={{0,2},{1,3},{2,0},{3,1},{4,6},{5,7},{6,4},{7,5},{8,10},{9,11},{10,... | collective-permute-start | bytes 196616 | tf_op jit(solution)/shard_map/ppermute | solution.py:148

commit v11 on v9

--- a/solution.py
+++ b/solution.py
@@ -209,14 +209,13 @@
 
     nyb = offsets_y.shape[0]
     col_block = (jnp.arange(nyb)[:, None] + offsets_y) % nyb
-    picked = jnp.take(mixed.reshape(rows, nyb, BLK), col_block, axis=1)
-    prior = jnp.einsum(
-        "xrkc,rikc->xri",
-        picked,
-        cov_y.reshape(nyb, BLK, cov_y.shape[1], BLK),
-        precision=precise,
-        preferred_element_type=jnp.float32,
-    ).reshape(rows, cols)
+    ny = cov_y.shape[0]
+    row_target = jnp.repeat(col_block, BLK, axis=0)
+    hit = row_target[:, :, None, None] == jnp.arange(nyb)[None, None, :, None]
+    dense_y = jnp.sum(jnp.where(hit, cov_y[:, :, None, :], 0.0), axis=1).reshape(ny, nyb * BLK)
+    prior = lax.dot_general(
+        mixed, dense_y, (((1,), (1,)), ((), ())), precision=precise, preferred_element_type=jnp.float32
+    )
     return (recharge, prior)
 
 

time: 41.2 us -> 47.9 us (1.16)
  other arithmetic: 0.42 us -> 6.54 us
  waiting for transfers between devices: 12.5 us -> 9.6 us
  matrix products: 3.07 us -> 4.86 us
  starting transfers between devices: 14.5 us -> 15.5 us
  local copies, waits for them, and re-layouts: 3.24 us -> 4.04 us
    reduce_sum x0 -> x1, other arithmetic: none -> 6.11 us  [body(): jnp.sum(jnp.where(hit, cov_y[:, :, None, :], 0.0), axis=1)]
    ppermute x8, waiting for transfers between devices: 12.5 us -> 7.12 us  [swap(): return lax.ppermute(value, axis, [(i, i ^ mask) for i in range(count)])]
    ppermute x2, waiting for transfers between devices: 0.01 us -> 2.48 us  [passed_along(): lax.ppermute(value, axis, [(source, source + steps) for source in range(f...]
    dot_general x1, matrix products: 0.96 us -> 2.74 us  [body(): lax.dot_general(mixed, dense_y, (((1,), (1,)), ((), ())), precision=preci...]
    eq x0 -> x1, local copies, waits for them, and re-layouts: none -> 0.91 us  [body(): hit = row_target[:, :, None, None] == jnp.arange(nyb)[None, None, :, None]]
    ppermute x8, starting transfers between devices: 10.9 us -> 11.7 us  [swap(): return lax.ppermute(value, axis, [(i, i ^ mask) for i in range(count)])]
    convert_element_type x1, local copies, waits for them, and re-layouts: 0.01 us -> 0.72 us  [cx_slab(): cov_rows.astype(jnp.float32)[:, :, None, :]]
    unnamed x12, local copies, waits for them, and re-layouts: 0.68 us -> 1.34 us
  transfers between devices with their start and end apart: 10 -> 10, of which waited for: 7 -> 3; matrix products, arithmetic and copies ran while one was open for 6% -> 18% of each run, Pallas kernels for 0% -> 9%
where the time goes in v11:
time: 47.9 us; the launch traced here: 47.6 us
  starting transfers between devices  15.5 us (32%)
  waiting for transfers between devices  9.6 us (20%)
  other arithmetic  6.54 us (14%)
  Pallas kernels  6.15 us (13%)
  matrix products  4.86 us (10%)
  local copies, waits for them, and re-layouts  4.04 us (8%)
  between operations  0.89 us (2%)
    ppermute x8, starting transfers between devices, swap(): return lax.ppermute(value, axis, [(i, i ^ mask) for i in range(count)])  11.7 us
    ppermute x8, waiting for transfers between devices, swap(): return lax.ppermute(value, axis, [(i, i ^ mask) for i in range(count)])  7.12 us
    reduce_sum x1, other arithmetic, body(): jnp.sum(jnp.where(hit, cov_y[:, :, None, :], 0.0), axis=1)  6.11 us
    pallas_call x1, Pallas kernels, stencil(): pl.pallas_call(stencil_kernel, grid=(depth // zc,), in_specs=[pl.BlockSpe...  4.45 us
    ppermute x2, starting transfers between devices, passed_along(): lax.ppermute(value, axis, [(source, source + steps) for source in range(f...  3.8 us
    dot_general x1, matrix products, body(): lax.dot_general(mixed, dense_y, (((1,), (1,)), ((), ())), precision=preci...  2.74 us
    ppermute x2, waiting for transfers between devices, passed_along(): lax.ppermute(value, axis, [(source, source + steps) for source in range(f...  2.48 us
    dot_general x4, matrix products, product(): jnp.dot(cols, piece.reshape(-1, piece.shape[-1]), precision=precise, pref...  2.12 us
  transfers between devices with their start and end apart: 10, of which 3 were waited for; matrix products, arithmetic and copies ran while one was open for 18% of the time, Pallas kernels for 9%

profile of v11, /device:TPU:0, one launch (start us, length us, event | category | flops | bytes accessed | tf_op | source)
XLA Modules:
  0.0 47.6 jit_solution(806688736852682365)
XLA Ops:
  0.7 0.6 %copy-done = s32[2,4]{1,0:T(2,128)S(1)} copy-done((s32[2,4]{1,0:T(2,128)S(1)}, s32[2,4]{1,0:T(2,128)}, u32[]{:S(2)}) %copy-start) | copy-done | bytes 56
  1.3 0.6 %gather_fusion = s32[16,4]{1,0:T(8,128)S(1)} fusion(s32[2,4]{1,0:T(2,128)S(1)} %copy-done, s32[1024]{0:T(1024)S(1)} %pad_clamp_fusion), kind=kCustom, calls=%fused_computation | custom fusion | bytes 576 | tf_op jit(solution)/shard_map/gather | solution.py:149
  1.9 0.1 add_select_fusion
  2.0 0.1 copy.22
  2.1 0.7 %copy.23 = f32[16,4,128]{2,0,1:T(8,128)S(1)} copy(bf16[16,4,128]{2,1,0:T(4,128)(2,1)} %param.24) | data formatting | bytes 49152 | tf_op jit(solution)/shard_map/convert_element_type | solution.py:152
  2.8 0.1 select_reduce_fusion.1
  2.9 2.4 %collective-permute-start.4 = (f32[16,256]{1,0:T(8,128)S(1)}, f32[16,256]{1,0:T(8,128)S(1)}, u32[]{:S(2)}, u32[]{:S(2)}) collective-permute-start(f32[16,256]{1,0:T(8,128)S(1)} %copy_bitcast_fusion.1), channel_id=1, source_target_pairs={{0,3},{1,2},{2,1},{3,0},{4,7},{5,6},{6,5},{7,4},{8,11},{9,10},{10,... | collective-permute-start | bytes 49160 | tf_op jit(solution)/shard_map/ppermute | solution.py:142
  5.3 0.6 %collective-permute-start.3 = (f32[16,256]{1,0:T(8,128)S(1)}, f32[16,256]{1,0:T(8,128)S(1)}, u32[]{:S(2)}, u32[]{:S(2)}) collective-permute-start(f32[16,256]{1,0:T(8,128)S(1)} %copy_bitcast_fusion.1), channel_id=1, source_target_pairs={{0,2},{1,3},{2,0},{3,1},{4,6},{5,7},{6,4},{7,5},{8,10},{9,11},{10,... | collective-permute-start | bytes 49160 | tf_op jit(solution)/shard_map/ppermute | solution.py:142
  6.0 4.5 %shard_map.158 = (f32[16,1024]{1,0:T(8,128)}, f32[2,16,1024]{2,1,0:T(8,128)}, f32[16,1024]{1,0:T(8,128)}, f32[16,1024]{1,0:T(8,128)}) custom-call(f32[16]{0:T(128)} %w_ref.3, f32[16,16,1024]{2,1,0:T(8,128)} %sprev_ref.1, f32[16,16,1024]{2,1,0:T(8,128)} %sprev_ref.1, s32[16,16,1024]{2,1,0:T(8,128)} %f_ref.1, f32[16,16,1024]{2,1,0:T(8,128)} %vx_ref.1, ...), custom_call_target="tpu_custom_call" | custom-call | tf_op jit(solution)/shard_map/pallas_call | solution.py:75
  10.5 2.5 %collective-permute-start = (f32[16,1024]{1,0:T(8,128)}, f32[16,1024]{1,0:T(8,128)S(1)}, u32[]{:S(2)}, u32[]{:S(2)}) collective-permute-start(f32[16,1024]{1,0:T(8,128)} %get-tuple-element.9.last_ref), channel_id=1, source_target_pairs={{0,1},{1,2},{2,3},{3,4},{4,5},{5,6},{6,7},{7,8},{8,9},{9,10},{10,1... | collective-permute-start | bytes 196616 | tf_op jit(solution)/shard_map/ppermute | solution.py:17
  13.0 1.3 %collective-permute-start.1 = (f32[2,16,1024]{2,1,0:T(8,128)}, f32[2,16,1024]{2,1,0:T(8,128)S(1)}, u32[]{:S(2)}, u32[]{:S(2)}) collective-permute-start(f32[2,16,1024]{2,1,0:T(8,128)} %get-tuple-element.10), channel_id=1, source_target_pairs={{1,0},{2,1},{3,2},{4,3},{5,4},{6,5},{7,6},{8,7},{9,8},{10,9},{11,1... | collective-permute-start | bytes 393224 | tf_op jit(solution)/shard_map/ppermute | solution.py:17
  14.4 0.1 copy.31
  14.5 0.1 copy.32
  14.6 0.1 copy.33
  14.7 0.1 copy.34
  14.8 2.5 %collective-permute-done.1.next_ref = f32[2,16,1024]{2,1,0:T(8,128)S(1)} collective-permute-done((f32[2,16,1024]{2,1,0:T(8,128)}, f32[2,16,1024]{2,1,0:T(8,128)S(1)}, u32[]{:S(2)}, u32[]{:S(2)}) %collective-permute-start.1) | collective-permute-done | bytes 131104 | tf_op jit(solution)/shard_map/ppermute | solution.py:17
  17.3 0.6 %copy-done.2 = f32[2,16,1024]{2,1,0:T(8,128)} copy-done((f32[2,16,1024]{2,1,0:T(8,128)}, f32[2,16,1024]{2,1,0:T(8,128)S(1)}, u32[]{:S(2)}) %copy-start.2) | copy-done | bytes 131096
  18.0 1.7 %shard_map.159 = f32[16,1024]{1,0:T(8,128)} custom-call(f32[16]{0:T(128)} %w_ref.3, f32[16,1024]{1,0:T(8,128)} %get-tuple-element.7.partial_ref, f32[16,1024]{1,0:T(8,128)} %get-tuple-element.8.up_ref, f32[16,1024]{1,0:T(8,128)} %copy-done.3, f32[2,16,1024]{2,1,0:T(8,128)} %copy-done.2, f32[16,1024]{1,0:T(8,128)} %get-tuple-element.9.last_ref), custom_call_target="tpu_custom_call" | custom-call | tf_op jit(solution)/shard_map/pallas_call | solution.py:122
  19.7 4.4 %collective-permute-start.5 = (f32[1,16,1024]{2,1,0:T(8,128)}, f32[1,16,1024]{2,1,0:T(8,128)S(1)}, u32[]{:S(2)}, u32[]{:S(2)}) collective-permute-start(f32[1,16,1024]{2,1,0:T(8,128)} %bitcast.69), channel_id=1, source_target_pairs={{0,4},{1,5},{2,6},{3,7},{4,0},{5,1},{6,2},{7,3},{8,12},{9,13},{10,... | collective-permute-start | bytes 196616 | tf_op jit(solution)/shard_map/ppermute | solution.py:142
  24.1 0.2 pad_maximum_fusion
  24.2 2.5 %collective-permute-start.7 = (f32[1,16,1024]{2,1,0:T(8,128)}, f32[1,16,1024]{2,1,0:T(8,128)S(1)}, u32[]{:S(2)}, u32[]{:S(2)}) collective-permute-start(f32[1,16,1024]{2,1,0:T(8,128)} %bitcast.70), channel_id=1, source_target_pairs={{0,12},{1,13},{2,14},{3,15},{4,8},{5,9},{6,10},{7,11},{8,4},{9,5},... | collective-permute-start | bytes 196616 | tf_op jit(solution)/shard_map/ppermute | solution.py:142
  26.8 0.2 collective-permute-start.6
  27.0 0.3 fusion.11
  27.3 6.7 %collective-permute-done.6 = f32[1,16,1024]{2,1,0:T(8,128)S(1)} collective-permute-done((f32[1,16,1024]{2,1,0:T(8,128)}, f32[1,16,1024]{2,1,0:T(8,128)S(1)}, u32[]{:S(2)}, u32[]{:S(2)}) %collective-permute-start.6) | collective-permute-done | bytes 65568 | tf_op jit(solution)/shard_map/ppermute | solution.py:142
  34.0 0.3 fusion.9
  34.3 0.3 fusion.7
  34.7 1.2 %fusion.4 = f32[64,1024]{1,0:T(8,128)S(1)} fusion(f32[64,1024]{1,0:T(8,128)S(1)} %fusion.7, f32[64,1024]{1,0:T(8,128)S(1)} %fusion.9, f32[64,1024]{1,0:T(8,128)S(1)} %fusion.11, f32[16,1024]{1,0:T(8,128)} %shard_map.159, f32[64,16,16]{0,2,1:T(8,128)S(1)} %pad_maximum_fusion, s32[]{:T(128)} %bitcast.7, pred[]{:T(512)} %bitcast.1), kind=kOutput, calls=%fused_computation.7 | convolution fusion | flops 6489088 | bytes 1122309 | tf_op jit(solution)/shard_map/dot_general | solution.py:164
  36.0 0.9 %copy.30 = pred[1024,4,8]{2,1,0:T(4,128)(4,1)S(1)} copy(pred[1024,4,8]{0,2,1:T(8,128)(4,1)S(1)} %iota_compare_fusion) | data formatting | bytes 65536 | tf_op jit(solution)/shard_map/eq | solution.py:214
  36.9 0.4 collective-permute-done.8
  37.3 1.4 %collective-permute-start.9 = (f32[16,1024]{1,0:T(8,128)S(1)}, f32[16,1024]{1,0:T(8,128)S(1)}, u32[]{:S(2)}, u32[]{:S(2)}) collective-permute-start(f32[16,1024]{1,0:T(8,128)S(1)} %slice_bitcast_fusion), channel_id=1, source_target_pairs={{0,2},{1,3},{2,0},{3,1},{4,6},{5,7},{6,4},{7,5},{8,10},{9,11},{10,... | collective-permute-start | bytes 196616 | tf_op jit(solution)/shard_map/ppermute | solution.py:142
  38.7 6.1 %select_reduce_fusion = f32[1024,8,128]{2,1,0:T(8,128)S(1)} fusion(f32[1024,4,128]{2,1,0:T(4,128)S(1)} %copy-done.1, pred[1024,4,8]{2,1,0:T(4,128)(4,1)S(1)} %copy.30), kind=kLoop, calls=%fused_computation.1 | loop fusion | flops 7340032 | bytes 6324224 | tf_op jit(solution)/shard_map/reduce_sum | solution.py:215
  44.9 2.7 %fusion = f32[16,1024]{1,0:T(8,128)} fusion(f32[128,8,8,128]{3,2,1,0:T(8,128)S(1)} %bitcast.62, f32[16,1024]{1,0:T(8,128)S(1)} %collective-permute-done.9, f32[2,16,1024]{2,1,0:T(8,128)S(1)} %slice_add_fusion), kind=kOutput, calls=%fused_computation.2 | convolution fusion | flops 100679680 | bytes 4390912 | tf_op jit(solution)/shard_map/dot_general | solution.py:216
  (29 shorter events, 0.4 us)
Async XLA Ops:
  0.6 0.7 %copy-start = (s32[2,4]{1,0:T(2,128)S(1)}, s32[2,4]{1,0:T(2,128)}, u32[]{:S(2)}) copy-start(s32[2,4]{1,0:T(2,128)} %param.25) | copy-start | bytes 100
  0.6 13.6 %copy-start.4 = (s32[8,4]{0,1:T(4,128)S(1)}, s32[8,4]{0,1:T(4,128)}, u32[]{:S(2)}) copy-start(s32[8,4]{0,1:T(4,128)} %param.27) | copy-start | bytes 388
  2.9 11.9 %collective-permute-start.4 = (f32[16,256]{1,0:T(8,128)S(1)}, f32[16,256]{1,0:T(8,128)S(1)}, u32[]{:S(2)}, u32[]{:S(2)}) collective-permute-start(f32[16,256]{1,0:T(8,128)S(1)} %copy_bitcast_fusion.1), channel_id=1, source_target_pairs={{0,3},{1,2},{2,1},{3,0},{4,7},{5,6},{6,5},{7,4},{8,11},{9,10},{10,... | collective-permute-start | bytes 49160 | tf_op jit(solution)/shard_map/ppermute | solution.py:142
  5.3 9.3 %collective-permute-start.3 = (f32[16,256]{1,0:T(8,128)S(1)}, f32[16,256]{1,0:T(8,128)S(1)}, u32[]{:S(2)}, u32[]{:S(2)}) collective-permute-start(f32[16,256]{1,0:T(8,128)S(1)} %copy_bitcast_fusion.1), channel_id=1, source_target_pairs={{0,2},{1,3},{2,0},{3,1},{4,6},{5,7},{6,4},{7,5},{8,10},{9,11},{10,... | collective-permute-start | bytes 49160 | tf_op jit(solution)/shard_map/ppermute | solution.py:142
  6.0 8.6 %collective-permute-start.2 = (f32[16,256]{1,0:T(8,128)S(1)}, f32[16,256]{1,0:T(8,128)S(1)}, u32[]{:S(2)}, u32[]{:S(2)}) collective-permute-start(f32[16,256]{1,0:T(8,128)S(1)} %copy_bitcast_fusion.1), channel_id=1, source_target_pairs={{0,1},{1,0},{2,3},{3,2},{4,5},{5,4},{6,7},{7,6},{8,9},{9,8},{10,11... | collective-permute-start | bytes 49160 | tf_op jit(solution)/shard_map/ppermute | solution.py:142
  10.5 28.3 %copy-start.1 = (f32[1024,4,128]{2,1,0:T(4,128)S(1)}, f32[1024,4,128]{2,1,0:T(4,128)}, u32[]{:S(2)}) copy-start(f32[1024,4,128]{2,1,0:T(4,128)} %param.26) | copy-start | bytes 6291460
  10.5 4.4 %collective-permute-start = (f32[16,1024]{1,0:T(8,128)}, f32[16,1024]{1,0:T(8,128)S(1)}, u32[]{:S(2)}, u32[]{:S(2)}) collective-permute-start(f32[16,1024]{1,0:T(8,128)} %get-tuple-element.9.last_ref), channel_id=1, source_target_pairs={{0,1},{1,2},{2,3},{3,4},{4,5},{5,6},{6,7},{7,8},{8,9},{9,10},{10,1... | collective-permute-start | bytes 196616 | tf_op jit(solution)/shard_map/ppermute | solution.py:17
  13.0 4.3 %collective-permute-start.1 = (f32[2,16,1024]{2,1,0:T(8,128)}, f32[2,16,1024]{2,1,0:T(8,128)S(1)}, u32[]{:S(2)}, u32[]{:S(2)}) collective-permute-start(f32[2,16,1024]{2,1,0:T(8,128)} %get-tuple-element.10), channel_id=1, source_target_pairs={{1,0},{2,1},{3,2},{4,3},{5,4},{6,5},{7,6},{8,7},{9,8},{10,9},{11,1... | collective-permute-start | bytes 393224 | tf_op jit(solution)/shard_map/ppermute | solution.py:17
  14.8 2.5 %copy-start.3 = (f32[16,1024]{1,0:T(8,128)}, f32[16,1024]{1,0:T(8,128)S(1)}, u32[]{:S(2)}) copy-start(f32[16,1024]{1,0:T(8,128)S(1)} %collective-permute-done.prev_ref) | copy-start | bytes 196612
  17.3 0.6 %copy-start.2 = (f32[2,16,1024]{2,1,0:T(8,128)}, f32[2,16,1024]{2,1,0:T(8,128)S(1)}, u32[]{:S(2)}) copy-start(f32[2,16,1024]{2,1,0:T(8,128)S(1)} %collective-permute-done.1.next_ref) | copy-start | bytes 393220
  19.7 7.3 %collective-permute-start.5 = (f32[1,16,1024]{2,1,0:T(8,128)}, f32[1,16,1024]{2,1,0:T(8,128)S(1)}, u32[]{:S(2)}, u32[]{:S(2)}) collective-permute-start(f32[1,16,1024]{2,1,0:T(8,128)} %bitcast.69), channel_id=1, source_target_pairs={{0,4},{1,5},{2,6},{3,7},{4,0},{5,1},{6,2},{7,3},{8,12},{9,13},{10,... | collective-permute-start | bytes 196616 | tf_op jit(solution)/shard_map/ppermute | solution.py:142
  24.2 10.1 %collective-permute-start.7 = (f32[1,16,1024]{2,1,0:T(8,128)}, f32[1,16,1024]{2,1,0:T(8,128)S(1)}, u32[]{:S(2)}, u32[]{:S(2)}) collective-permute-start(f32[1,16,1024]{2,1,0:T(8,128)} %bitcast.70), channel_id=1, source_target_pairs={{0,12},{1,13},{2,14},{3,15},{4,8},{5,9},{6,10},{7,11},{8,4},{9,5},... | collective-permute-start | bytes 196616 | tf_op jit(solution)/shard_map/ppermute | solution.py:142
  26.8 7.2 %collective-permute-start.6 = (f32[1,16,1024]{2,1,0:T(8,128)}, f32[1,16,1024]{2,1,0:T(8,128)S(1)}, u32[]{:S(2)}, u32[]{:S(2)}) collective-permute-start(f32[1,16,1024]{2,1,0:T(8,128)} %bitcast.71), channel_id=1, source_target_pairs={{0,8},{1,9},{2,10},{3,11},{4,12},{5,13},{6,14},{7,15},{8,0},{9,1},... | collective-permute-start | bytes 196616 | tf_op jit(solution)/shard_map/ppermute | solution.py:142
  35.9 1.4 %collective-permute-start.8 = (f32[2,16,1024]{2,1,0:T(8,128)S(1)}, f32[2,16,1024]{2,1,0:T(8,128)S(1)}, u32[]{:S(2)}, u32[]{:S(2)}) collective-permute-start(f32[2,16,1024]{2,1,0:T(8,128)S(1)} %slice.13), channel_id=1, source_target_pairs={{0,1},{1,0},{2,3},{3,2},{4,5},{5,4},{6,7},{7,6},{8,9},{9,8},{10,11... | collective-permute-start | bytes 393224 | tf_op jit(solution)/shard_map/ppermute | solution.py:142
  37.3 7.5 %collective-permute-start.9 = (f32[16,1024]{1,0:T(8,128)S(1)}, f32[16,1024]{1,0:T(8,128)S(1)}, u32[]{:S(2)}, u32[]{:S(2)}) collective-permute-start(f32[16,1024]{1,0:T(8,128)S(1)} %slice_bitcast_fusion), channel_id=1, source_target_pairs={{0,2},{1,3},{2,0},{3,1},{4,6},{5,7},{6,4},{7,5},{8,10},{9,11},{10,... | collective-permute-start | bytes 196616 | tf_op jit(solution)/shard_map/ppermute | solution.py:142

commit v12 on v9

--- a/solution.py
+++ b/solution.py
@@ -173,9 +173,7 @@
         buf = jnp.concatenate([buf] + others, axis=0)
         entries = entries + [m ^ q for m in masks for q in entries]
     parts = total.reshape(4, rows, total.shape[-1])
-    got = swap(parts[1::2], axis, 1)
-    near = parts[0::2] + got
-    return near[0] + swap(near[1], axis, 2)
+    return parts[0] + (swap(parts[1], axis, 1) + swap(parts[2], axis, 2) + swap(parts[3], axis, 3))
 
 
 def body(

time: 41.2 us -> 42.9 us (1.041)
  local copies, waits for them, and re-layouts: 3.24 us -> 4.78 us
  starting transfers between devices: 14.5 us -> 15.7 us
  waiting for transfers between devices: 12.5 us -> 11.6 us
    ppermute x8 -> x9, waiting for transfers between devices: 12.5 us -> 9.01 us  [swap(): return lax.ppermute(value, axis, [(i, i ^ mask) for i in range(count)])]
    ppermute x2, waiting for transfers between devices: 0.01 us -> 2.6 us  [passed_along(): lax.ppermute(value, axis, [(source, source + steps) for source in range(f...]
    ppermute x8 -> x9, starting transfers between devices: 10.9 us -> 12.4 us  [swap(): return lax.ppermute(value, axis, [(i, i ^ mask) for i in range(count)])]
    gather x1, local copies, waits for them, and re-layouts: 0.56 us -> 1.38 us  [cx_slab(): target = (row_block[:, None] + offsets[row_block]) % nxb]
    convert_element_type x1, local copies, waits for them, and re-layouts: 0.01 us -> 0.72 us  [cx_slab(): cov_rows.astype(jnp.float32)[:, :, None, :]]
  transfers between devices with their start and end apart: 10 -> 11, of which waited for: 7 -> 6; matrix products, arithmetic and copies ran while one was open for 6% -> 3% of each run, Pallas kernels for 0% -> 10%
where the time goes in v12:
time: 42.9 us; the launch traced here: 42.6 us
  starting transfers between devices  15.7 us (37%)
  waiting for transfers between devices  11.6 us (27%)
  Pallas kernels  6.15 us (14%)
  local copies, waits for them, and re-layouts  4.78 us (11%)
  matrix products  3.06 us (7%)
  between operations  0.85 us (2%)
    ppermute x9, starting transfers between devices, swap(): return lax.ppermute(value, axis, [(i, i ^ mask) for i in range(count)])  12.4 us
    ppermute x9, waiting for transfers between devices, swap(): return lax.ppermute(value, axis, [(i, i ^ mask) for i in range(count)])  9.01 us
    pallas_call x1, Pallas kernels, stencil(): pl.pallas_call(stencil_kernel, grid=(depth // zc,), in_specs=[pl.BlockSpe...  4.45 us
    ppermute x2, starting transfers between devices, passed_along(): lax.ppermute(value, axis, [(source, source + steps) for source in range(f...  3.34 us
    ppermute x2, waiting for transfers between devices, passed_along(): lax.ppermute(value, axis, [(source, source + steps) for source in range(f...  2.6 us
    dot_general x4, matrix products, product(): jnp.dot(cols, piece.reshape(-1, piece.shape[-1]), precision=precise, pref...  2.1 us
    pallas_call x1, Pallas kernels, corrected(): pl.pallas_call(fix_kernel, in_specs=[pl.BlockSpec(memory_space=pltpu.SMEM...  1.69 us
    gather x1, local copies, waits for them, and re-layouts, cx_slab(): target = (row_block[:, None] + offsets[row_block]) % nxb  1.38 us
  transfers between devices with their start and end apart: 11, of which 6 were waited for; matrix products, arithmetic and copies ran while one was open for 3% of the time, Pallas kernels for 10%

profile of v12, /device:TPU:0, one launch (start us, length us, event | category | flops | bytes accessed | tf_op | source)
XLA Modules:
  0.0 42.6 jit_solution(2698135202644485456)
XLA Ops:
  0.7 1.4 %gather_fusion = s32[16,4]{1,0:T(8,128)S(1)} fusion(s32[2,4]{1,0:T(2,128)} %param.25, s32[1024]{0:T(1024)S(1)} %pad_clamp_fusion.1), kind=kCustom, calls=%fused_computation | custom fusion | bytes 576 | tf_op jit(solution)/shard_map/gather | solution.py:149
  2.3 0.7 %copy.40 = f32[16,4,128]{2,0,1:T(8,128)S(1)} copy(bf16[16,4,128]{2,1,0:T(4,128)(2,1)} %param.24) | data formatting | bytes 49152 | tf_op jit(solution)/shard_map/convert_element_type | solution.py:152
  3.1 0.5 %collective-permute-start.2 = (f32[16,256]{1,0:T(8,128)S(1)}, f32[16,256]{1,0:T(8,128)S(1)}, u32[]{:S(2)}, u32[]{:S(2)}) collective-permute-start(f32[16,256]{1,0:T(8,128)S(1)} %copy_bitcast_fusion.2), channel_id=1, source_target_pairs={{0,1},{1,0},{2,3},{3,2},{4,5},{5,4},{6,7},{7,6},{8,9},{9,8},{10,11... | collective-permute-start | bytes 49160 | tf_op jit(solution)/shard_map/ppermute | solution.py:142
  3.6 2.6 %collective-permute-start.3 = (f32[16,256]{1,0:T(8,128)S(1)}, f32[16,256]{1,0:T(8,128)S(1)}, u32[]{:S(2)}, u32[]{:S(2)}) collective-permute-start(f32[16,256]{1,0:T(8,128)S(1)} %copy_bitcast_fusion.2), channel_id=1, source_target_pairs={{0,2},{1,3},{2,0},{3,1},{4,6},{5,7},{6,4},{7,5},{8,10},{9,11},{10,... | collective-permute-start | bytes 49160 | tf_op jit(solution)/shard_map/ppermute | solution.py:142
  6.3 4.5 %shard_map.158 = (f32[16,1024]{1,0:T(8,128)}, f32[2,16,1024]{2,1,0:T(8,128)}, f32[16,1024]{1,0:T(8,128)}, f32[16,1024]{1,0:T(8,128)}) custom-call(f32[16]{0:T(128)} %w_ref.3, f32[16,16,1024]{2,1,0:T(8,128)} %sprev_ref.1, f32[16,16,1024]{2,1,0:T(8,128)} %sprev_ref.1, s32[16,16,1024]{2,1,0:T(8,128)} %f_ref.1, f32[16,16,1024]{2,1,0:T(8,128)} %vx_ref.1, ...), custom_call_target="tpu_custom_call" | custom-call | tf_op jit(solution)/shard_map/pallas_call | solution.py:75
  10.7 2.0 %collective-permute-start = (f32[16,1024]{1,0:T(8,128)}, f32[16,1024]{1,0:T(8,128)S(1)}, u32[]{:S(2)}, u32[]{:S(2)}) collective-permute-start(f32[16,1024]{1,0:T(8,128)} %get-tuple-element.9.last_ref), channel_id=1, source_target_pairs={{0,1},{1,2},{2,3},{3,4},{4,5},{5,6},{6,7},{7,8},{8,9},{9,10},{10,1... | collective-permute-start | bytes 196616 | tf_op jit(solution)/shard_map/ppermute | solution.py:17
  12.8 1.3 %collective-permute-start.1 = (f32[2,16,1024]{2,1,0:T(8,128)}, f32[2,16,1024]{2,1,0:T(8,128)S(1)}, u32[]{:S(2)}, u32[]{:S(2)}) collective-permute-start(f32[2,16,1024]{2,1,0:T(8,128)} %get-tuple-element.10), channel_id=1, source_target_pairs={{1,0},{2,1},{3,2},{4,3},{5,4},{6,5},{7,6},{8,7},{9,8},{10,9},{11,1... | collective-permute-start | bytes 393224 | tf_op jit(solution)/shard_map/ppermute | solution.py:17
  14.1 0.1 copy.52
  14.5 0.1 copy.53
  14.6 0.1 copy.54
  14.7 0.1 copy.55
  14.8 2.6 %collective-permute-done.1.next_ref = f32[2,16,1024]{2,1,0:T(8,128)S(1)} collective-permute-done((f32[2,16,1024]{2,1,0:T(8,128)}, f32[2,16,1024]{2,1,0:T(8,128)S(1)}, u32[]{:S(2)}, u32[]{:S(2)}) %collective-permute-start.1) | collective-permute-done | bytes 131104 | tf_op jit(solution)/shard_map/ppermute | solution.py:17
  17.4 0.7 %copy-done.1 = f32[2,16,1024]{2,1,0:T(8,128)} copy-done((f32[2,16,1024]{2,1,0:T(8,128)}, f32[2,16,1024]{2,1,0:T(8,128)S(1)}, u32[]{:S(2)}) %copy-start.1) | copy-done | bytes 131096
  18.1 1.7 %shard_map.159 = f32[16,1024]{1,0:T(8,128)} custom-call(f32[16]{0:T(128)} %w_ref.3, f32[16,1024]{1,0:T(8,128)} %get-tuple-element.7.partial_ref, f32[16,1024]{1,0:T(8,128)} %get-tuple-element.8.up_ref, f32[16,1024]{1,0:T(8,128)} %copy-done.2, f32[2,16,1024]{2,1,0:T(8,128)} %copy-done.1, f32[16,1024]{1,0:T(8,128)} %get-tuple-element.9.last_ref), custom_call_target="tpu_custom_call" | custom-call | tf_op jit(solution)/shard_map/pallas_call | solution.py:122
  19.8 5.4 %collective-permute-start.6 = (f32[1,16,1024]{2,1,0:T(8,128)}, f32[1,16,1024]{2,1,0:T(8,128)S(1)}, u32[]{:S(2)}, u32[]{:S(2)}) collective-permute-start(f32[1,16,1024]{2,1,0:T(8,128)} %bitcast.68), channel_id=1, source_target_pairs={{0,8},{1,9},{2,10},{3,11},{4,12},{5,13},{6,14},{7,15},{8,0},{9,1},... | collective-permute-start | bytes 196616 | tf_op jit(solution)/shard_map/ppermute | solution.py:142
  25.2 0.2 pad_maximum_fusion
  25.3 1.6 %collective-permute-start.5 = (f32[1,16,1024]{2,1,0:T(8,128)}, f32[1,16,1024]{2,1,0:T(8,128)S(1)}, u32[]{:S(2)}, u32[]{:S(2)}) collective-permute-start(f32[1,16,1024]{2,1,0:T(8,128)} %bitcast.69), channel_id=1, source_target_pairs={{0,4},{1,5},{2,6},{3,7},{4,0},{5,1},{6,2},{7,3},{8,12},{9,13},{10,... | collective-permute-start | bytes 196616 | tf_op jit(solution)/shard_map/ppermute | solution.py:142
  27.0 2.6 %collective-permute-done.6 = f32[1,16,1024]{2,1,0:T(8,128)S(1)} collective-permute-done((f32[1,16,1024]{2,1,0:T(8,128)}, f32[1,16,1024]{2,1,0:T(8,128)S(1)}, u32[]{:S(2)}, u32[]{:S(2)}) %collective-permute-start.6) | collective-permute-done | bytes 65568 | tf_op jit(solution)/shard_map/ppermute | solution.py:142
  29.6 0.3 fusion.14
  29.9 0.4 collective-permute-done.5
  30.3 0.3 fusion.16
  30.6 2.7 %collective-permute-done.7 = f32[1,16,1024]{2,1,0:T(8,128)S(1)} collective-permute-done((f32[1,16,1024]{2,1,0:T(8,128)}, f32[1,16,1024]{2,1,0:T(8,128)S(1)}, u32[]{:S(2)}, u32[]{:S(2)}) %collective-permute-start.7) | collective-permute-done | bytes 65568 | tf_op jit(solution)/shard_map/ppermute | solution.py:142
  33.3 0.3 fusion.12
  33.6 1.2 %fusion.3 = f32[64,1024]{1,0:T(8,128)S(1)} fusion(f32[64,1024]{1,0:T(8,128)S(1)} %fusion.12, f32[64,1024]{1,0:T(8,128)S(1)} %fusion.14, f32[64,1024]{1,0:T(8,128)S(1)} %fusion.16, f32[16,1024]{1,0:T(8,128)} %shard_map.159, f32[64,16,16]{0,2,1:T(8,128)S(1)} %pad_maximum_fusion, s32[]{:T(128)} %bitcast.7, pred[]{:T(512)} %bitcast.1), kind=kOutput, calls=%fused_computation.6 | convolution fusion | flops 6489088 | bytes 1122309 | tf_op jit(solution)/shard_map/dot_general | solution.py:164
  34.8 0.7 %collective-permute-start.10 = (f32[16,1024]{1,0:T(8,128)S(1)}, f32[16,1024]{1,0:T(8,128)S(1)}, u32[]{:S(2)}, u32[]{:S(2)}) collective-permute-start(f32[16,1024]{1,0:T(8,128)S(1)} %get-tuple-element.25), channel_id=1, source_target_pairs={{0,3},{1,2},{2,1},{3,0},{4,7},{5,6},{6,5},{7,4},{8,11},{9,10},{10,... | collective-permute-start | bytes 196616 | tf_op jit(solution)/shard_map/ppermute | solution.py:142
  35.5 0.6 %collective-permute-start.8 = (f32[16,1024]{1,0:T(8,128)S(1)}, f32[16,1024]{1,0:T(8,128)S(1)}, u32[]{:S(2)}, u32[]{:S(2)}) collective-permute-start(f32[16,1024]{1,0:T(8,128)S(1)} %get-tuple-element.26), channel_id=1, source_target_pairs={{0,1},{1,0},{2,3},{3,2},{4,5},{5,4},{6,7},{7,6},{8,9},{9,8},{10,11... | collective-permute-start | bytes 196616 | tf_op jit(solution)/shard_map/ppermute | solution.py:142
  36.1 0.9 %collective-permute-start.9 = (f32[16,1024]{1,0:T(8,128)S(1)}, f32[16,1024]{1,0:T(8,128)S(1)}, u32[]{:S(2)}, u32[]{:S(2)}) collective-permute-start(f32[16,1024]{1,0:T(8,128)S(1)} %get-tuple-element.24), channel_id=1, source_target_pairs={{0,2},{1,3},{2,0},{3,1},{4,6},{5,7},{6,4},{7,5},{8,10},{9,11},{10,... | collective-permute-start | bytes 196616 | tf_op jit(solution)/shard_map/ppermute | solution.py:142
  37.0 1.9 %collective-permute-done.10 = f32[16,1024]{1,0:T(8,128)S(1)} collective-permute-done((f32[16,1024]{1,0:T(8,128)S(1)}, f32[16,1024]{1,0:T(8,128)S(1)}, u32[]{:S(2)}, u32[]{:S(2)}) %collective-permute-start.10) | collective-permute-done | bytes 65568 | tf_op jit(solution)/shard_map/ppermute | solution.py:142
  38.9 1.4 %collective-permute-done.9 = f32[16,1024]{1,0:T(8,128)S(1)} collective-permute-done((f32[16,1024]{1,0:T(8,128)S(1)}, f32[16,1024]{1,0:T(8,128)S(1)}, u32[]{:S(2)}, u32[]{:S(2)}) %collective-permute-start.9) | collective-permute-done | bytes 65568 | tf_op jit(solution)/shard_map/ppermute | solution.py:142
  40.4 0.6 %gather_fusion.1 = f32[32,16,128]{2,1,0:T(8,128)S(1)} fusion(f32[16,8,128]{2,0,1:T(8,128)S(1)} %copy_bitcast_fusion.1, s32[1024]{0:T(1024)S(1)} %pad_clamp_fusion), kind=kCustom, calls=%fused_computation.1 | custom fusion | bytes 524416 | tf_op jit(solution)/shard_map/jit(_take)/gather | solution.py:210
  41.0 1.0 %fusion.4 = f32[8,2,8,128]{3,2,1,0:T(8,128)S(1)} fusion(f32[8,128,4,128]{3,2,1,0:T(4,128)S(1)} %bitcast.62, f32[8,4,16,128]{3,2,1,0:T(8,128)S(1)} %bitcast.63, pred[8,4]{1,0:T(8,128)(4,1)S(1)} %copy.38), kind=kOutput, calls=%fused_computation.7 | convolution fusion | flops 50397184 | bytes 2424864 | tf_op jit(solution)/shard_map/xrkc,rikc->xri/dot_general | solution.py:211
  41.9 0.7 %copy.67 = f32[8,2,8,128]{3,2,0,1:T(8,128)} copy(f32[8,2,8,128]{3,2,1,0:T(8,128)S(1)} %fusion.4) | data formatting | bytes 131072 | tf_op jit(solution)/shard_map/reshape | solution.py:217
  (29 shorter events, 0.7 us)
Async XLA Ops:
  0.6 40.4 %copy-start = (f32[1024,4,128]{2,1,0:T(4,128)S(1)}, f32[1024,4,128]{2,1,0:T(4,128)}, u32[]{:S(2)}) copy-start(f32[1024,4,128]{2,1,0:T(4,128)} %param.26) | copy-start | bytes 6291460
  3.1 11.0 %copy-start.3 = (s32[8,4]{0,1:T(4,128)S(1)}, s32[8,4]{0,1:T(4,128)}, u32[]{:S(2)}) copy-start(s32[8,4]{0,1:T(4,128)} %param.27) | copy-start | bytes 388
  3.1 11.4 %collective-permute-start.2 = (f32[16,256]{1,0:T(8,128)S(1)}, f32[16,256]{1,0:T(8,128)S(1)}, u32[]{:S(2)}, u32[]{:S(2)}) collective-permute-start(f32[16,256]{1,0:T(8,128)S(1)} %copy_bitcast_fusion.2), channel_id=1, source_target_pairs={{0,1},{1,0},{2,3},{3,2},{4,5},{5,4},{6,7},{7,6},{8,9},{9,8},{10,11... | collective-permute-start | bytes 49160 | tf_op jit(solution)/shard_map/ppermute | solution.py:142
  3.6 11.0 %collective-permute-start.3 = (f32[16,256]{1,0:T(8,128)S(1)}, f32[16,256]{1,0:T(8,128)S(1)}, u32[]{:S(2)}, u32[]{:S(2)}) collective-permute-start(f32[16,256]{1,0:T(8,128)S(1)} %copy_bitcast_fusion.2), channel_id=1, source_target_pairs={{0,2},{1,3},{2,0},{3,1},{4,6},{5,7},{6,4},{7,5},{8,10},{9,11},{10,... | collective-permute-start | bytes 49160 | tf_op jit(solution)/shard_map/ppermute | solution.py:142
  6.2 8.5 %collective-permute-start.4 = (f32[16,256]{1,0:T(8,128)S(1)}, f32[16,256]{1,0:T(8,128)S(1)}, u32[]{:S(2)}, u32[]{:S(2)}) collective-permute-start(f32[16,256]{1,0:T(8,128)S(1)} %copy_bitcast_fusion.2), channel_id=1, source_target_pairs={{0,3},{1,2},{2,1},{3,0},{4,7},{5,6},{6,5},{7,4},{8,11},{9,10},{10,... | collective-permute-start | bytes 49160 | tf_op jit(solution)/shard_map/ppermute | solution.py:142
  10.7 4.1 %collective-permute-start = (f32[16,1024]{1,0:T(8,128)}, f32[16,1024]{1,0:T(8,128)S(1)}, u32[]{:S(2)}, u32[]{:S(2)}) collective-permute-start(f32[16,1024]{1,0:T(8,128)} %get-tuple-element.9.last_ref), channel_id=1, source_target_pairs={{0,1},{1,2},{2,3},{3,4},{4,5},{5,6},{6,7},{7,8},{8,9},{9,10},{10,1... | collective-permute-start | bytes 196616 | tf_op jit(solution)/shard_map/ppermute | solution.py:17
  12.8 4.7 %collective-permute-start.1 = (f32[2,16,1024]{2,1,0:T(8,128)}, f32[2,16,1024]{2,1,0:T(8,128)S(1)}, u32[]{:S(2)}, u32[]{:S(2)}) collective-permute-start(f32[2,16,1024]{2,1,0:T(8,128)} %get-tuple-element.10), channel_id=1, source_target_pairs={{1,0},{2,1},{3,2},{4,3},{5,4},{6,5},{7,6},{8,7},{9,8},{10,9},{11,1... | collective-permute-start | bytes 393224 | tf_op jit(solution)/shard_map/ppermute | solution.py:17
  14.8 2.6 %copy-start.2 = (f32[16,1024]{1,0:T(8,128)}, f32[16,1024]{1,0:T(8,128)S(1)}, u32[]{:S(2)}) copy-start(f32[16,1024]{1,0:T(8,128)S(1)} %collective-permute-done.prev_ref) | copy-start | bytes 196612
  17.4 0.7 %copy-start.1 = (f32[2,16,1024]{2,1,0:T(8,128)}, f32[2,16,1024]{2,1,0:T(8,128)S(1)}, u32[]{:S(2)}) copy-start(f32[2,16,1024]{2,1,0:T(8,128)S(1)} %collective-permute-done.1.next_ref) | copy-start | bytes 393220
  19.8 9.8 %collective-permute-start.6 = (f32[1,16,1024]{2,1,0:T(8,128)}, f32[1,16,1024]{2,1,0:T(8,128)S(1)}, u32[]{:S(2)}, u32[]{:S(2)}) collective-permute-start(f32[1,16,1024]{2,1,0:T(8,128)} %bitcast.68), channel_id=1, source_target_pairs={{0,8},{1,9},{2,10},{3,11},{4,12},{5,13},{6,14},{7,15},{8,0},{9,1},... | collective-permute-start | bytes 196616 | tf_op jit(solution)/shard_map/ppermute | solution.py:142
  25.3 4.9 %collective-permute-start.5 = (f32[1,16,1024]{2,1,0:T(8,128)}, f32[1,16,1024]{2,1,0:T(8,128)S(1)}, u32[]{:S(2)}, u32[]{:S(2)}) collective-permute-start(f32[1,16,1024]{2,1,0:T(8,128)} %bitcast.69), channel_id=1, source_target_pairs={{0,4},{1,5},{2,6},{3,7},{4,0},{5,1},{6,2},{7,3},{8,12},{9,13},{10,... | collective-permute-start | bytes 196616 | tf_op jit(solution)/shard_map/ppermute | solution.py:142
  27.0 6.3 %collective-permute-start.7 = (f32[1,16,1024]{2,1,0:T(8,128)}, f32[1,16,1024]{2,1,0:T(8,128)S(1)}, u32[]{:S(2)}, u32[]{:S(2)}) collective-permute-start(f32[1,16,1024]{2,1,0:T(8,128)} %bitcast.70), channel_id=1, source_target_pairs={{0,12},{1,13},{2,14},{3,15},{4,8},{5,9},{6,10},{7,11},{8,4},{9,5},... | collective-permute-start | bytes 196616 | tf_op jit(solution)/shard_map/ppermute | solution.py:142
  34.8 4.1 %collective-permute-start.10 = (f32[16,1024]{1,0:T(8,128)S(1)}, f32[16,1024]{1,0:T(8,128)S(1)}, u32[]{:S(2)}, u32[]{:S(2)}) collective-permute-start(f32[16,1024]{1,0:T(8,128)S(1)} %get-tuple-element.25), channel_id=1, source_target_pairs={{0,3},{1,2},{2,1},{3,0},{4,7},{5,6},{6,5},{7,4},{8,11},{9,10},{10,... | collective-permute-start | bytes 196616 | tf_op jit(solution)/shard_map/ppermute | solution.py:142
  35.5 3.4 %collective-permute-start.8 = (f32[16,1024]{1,0:T(8,128)S(1)}, f32[16,1024]{1,0:T(8,128)S(1)}, u32[]{:S(2)}, u32[]{:S(2)}) collective-permute-start(f32[16,1024]{1,0:T(8,128)S(1)} %get-tuple-element.26), channel_id=1, source_target_pairs={{0,1},{1,0},{2,3},{3,2},{4,5},{5,4},{6,7},{7,6},{8,9},{9,8},{10,11... | collective-permute-start | bytes 196616 | tf_op jit(solution)/shard_map/ppermute | solution.py:142
  36.1 4.3 %collective-permute-start.9 = (f32[16,1024]{1,0:T(8,128)S(1)}, f32[16,1024]{1,0:T(8,128)S(1)}, u32[]{:S(2)}, u32[]{:S(2)}) collective-permute-start(f32[16,1024]{1,0:T(8,128)S(1)} %get-tuple-element.24), channel_id=1, source_target_pairs={{0,2},{1,3},{2,0},{3,1},{4,6},{5,7},{6,4},{7,5},{8,10},{9,11},{10,... | collective-permute-start | bytes 196616 | tf_op jit(solution)/shard_map/ppermute | solution.py:142

commit v13 on v9

--- a/solution.py
+++ b/solution.py
@@ -204,7 +204,8 @@
     recharge = corrected(layer_weight, partial, up_x0, from_prev, from_next, last_s)
 
     own_slab = cx_slab(cov_x, offsets_x, me, rows)
-    slab = jnp.concatenate([own_slab] + [swap(own_slab, "gx", m) for m in (1, 2, 3)], axis=0)
+    late_slab, _ = lax.optimization_barrier((own_slab, recharge))
+    slab = jnp.concatenate([own_slab] + [swap(late_slab, "gx", m) for m in (1, 2, 3)], axis=0)
     mixed = mixed_rows(recharge, slab, "gx")
 
     nyb = offsets_y.shape[0]

time: 41.2 us -> 41 us (level)
  starting transfers between devices: 14.5 us -> 15.8 us
  matrix products: 3.07 us -> 2.24 us
  waiting for transfers between devices: 12.5 us -> 11.9 us
    ppermute x8, waiting for transfers between devices: 12.5 us -> 8.57 us  [swap(): return lax.ppermute(value, axis, [(i, i ^ mask) for i in range(count)])]
    ppermute x2, waiting for transfers between devices: 0.01 us -> 3.31 us  [passed_along(): lax.ppermute(value, axis, [(source, source + steps) for source in range(f...]
    ppermute x8, starting transfers between devices: 10.9 us -> 12.2 us  [swap(): return lax.ppermute(value, axis, [(i, i ^ mask) for i in range(count)])]
    dot_general x4, matrix products: 2.12 us -> 1.28 us  [product(): jnp.dot(cols, piece.reshape(-1, piece.shape[-1]), precision=precise, pref...]
  transfers between devices with their start and end apart: 10 -> 10, of which waited for: 7 -> 4; matrix products, arithmetic and copies ran while one was open for 6% -> 6% of each run, Pallas kernels for 0% -> 0%
where the time goes in v13:
time: 41 us; the launch traced here: 40.8 us
  starting transfers between devices  15.8 us (39%)
  waiting for transfers between devices  11.9 us (29%)
  Pallas kernels  6.3 us (15%)
  local copies, waits for them, and re-layouts  3.25 us (8%)
  matrix products  2.24 us (5%)
  between operations  0.93 us (2%)
  other arithmetic  0.42 us (1%)
    ppermute x8, starting transfers between devices, swap(): return lax.ppermute(value, axis, [(i, i ^ mask) for i in range(count)])  12.2 us
    ppermute x8, waiting for transfers between devices, swap(): return lax.ppermute(value, axis, [(i, i ^ mask) for i in range(count)])  8.57 us
    pallas_call x1, Pallas kernels, stencil(): pl.pallas_call(stencil_kernel, grid=(depth // zc,), in_specs=[pl.BlockSpe...  4.6 us
    ppermute x2, starting transfers between devices, passed_along(): lax.ppermute(value, axis, [(source, source + steps) for source in range(f...  3.65 us
    ppermute x2, waiting for transfers between devices, passed_along(): lax.ppermute(value, axis, [(source, source + steps) for source in range(f...  3.31 us
    pallas_call x1, Pallas kernels, corrected(): pl.pallas_call(fix_kernel, in_specs=[pl.BlockSpec(memory_space=pltpu.SMEM...  1.69 us
    dot_general x4, matrix products, product(): jnp.dot(cols, piece.reshape(-1, piece.shape[-1]), precision=precise, pref...  1.28 us
    dot_general x1, matrix products, body(): jnp.einsum('xrkc,rikc->xri', picked, cov_y.reshape(nyb, BLK, cov_y.shape[...  0.96 us
  transfers between devices with their start and end apart: 10, of which 4 were waited for; matrix products, arithmetic and copies ran while one was open for 6% of the time, Pallas kernels for 0%

profile of v13, /device:TPU:0, one launch (start us, length us, event | category | flops | bytes accessed | tf_op | source)
XLA Modules:
  0.0 40.8 jit_solution(17681577374229530224)
XLA Ops:
  0.7 4.6 %shard_map.158 = (f32[16,1024]{1,0:T(8,128)}, f32[2,16,1024]{2,1,0:T(8,128)}, f32[16,1024]{1,0:T(8,128)}, f32[16,1024]{1,0:T(8,128)}) custom-call(f32[16]{0:T(128)} %w_ref.3, f32[16,16,1024]{2,1,0:T(8,128)} %sprev_ref.1, f32[16,16,1024]{2,1,0:T(8,128)} %sprev_ref.1, s32[16,16,1024]{2,1,0:T(8,128)} %f_ref.1, f32[16,16,1024]{2,1,0:T(8,128)} %vx_ref.1, ...), custom_call_target="tpu_custom_call" | custom-call | tf_op jit(solution)/shard_map/pallas_call | solution.py:75
  5.3 2.4 %collective-permute-start = (f32[16,1024]{1,0:T(8,128)}, f32[16,1024]{1,0:T(8,128)S(1)}, u32[]{:S(2)}, u32[]{:S(2)}) collective-permute-start(f32[16,1024]{1,0:T(8,128)} %get-tuple-element.10.last_ref), channel_id=1, source_target_pairs={{0,1},{1,2},{2,3},{3,4},{4,5},{5,6},{6,7},{7,8},{8,9},{9,10},{10,1... | collective-permute-start | bytes 196616 | tf_op jit(solution)/shard_map/ppermute | solution.py:17
  7.6 1.3 %collective-permute-start.1 = (f32[2,16,1024]{2,1,0:T(8,128)}, f32[2,16,1024]{2,1,0:T(8,128)S(1)}, u32[]{:S(2)}, u32[]{:S(2)}) collective-permute-start(f32[2,16,1024]{2,1,0:T(8,128)} %get-tuple-element.11), channel_id=1, source_target_pairs={{1,0},{2,1},{3,2},{4,3},{5,4},{6,5},{7,6},{8,7},{9,8},{10,9},{11,1... | collective-permute-start | bytes 393224 | tf_op jit(solution)/shard_map/ppermute | solution.py:17
  9.0 0.6 %gather_fusion = s32[16,4]{1,0:T(8,128)S(1)} fusion(s32[2,4]{1,0:T(2,128)S(1)} %copy-done.1, s32[1024]{0:T(1024)S(1)} %pad_clamp_fusion.1), kind=kCustom, calls=%fused_computation | custom fusion | bytes 576 | tf_op jit(solution)/shard_map/gather | solution.py:149
  9.7 0.1 copy.42
  9.8 0.1 select_reduce_fusion
  9.9 3.3 %collective-permute-done.1.next_ref = f32[2,16,1024]{2,1,0:T(8,128)S(1)} collective-permute-done((f32[2,16,1024]{2,1,0:T(8,128)}, f32[2,16,1024]{2,1,0:T(8,128)S(1)}, u32[]{:S(2)}, u32[]{:S(2)}) %collective-permute-start.1) | collective-permute-done | bytes 131104 | tf_op jit(solution)/shard_map/ppermute | solution.py:17
  13.2 0.7 %copy-done.3 = f32[2,16,1024]{2,1,0:T(8,128)} copy-done((f32[2,16,1024]{2,1,0:T(8,128)}, f32[2,16,1024]{2,1,0:T(8,128)S(1)}, u32[]{:S(2)}) %copy-start.3) | copy-done | bytes 131096
  13.9 1.7 %shard_map.159 = f32[16,1024]{1,0:T(8,128)} custom-call(f32[16]{0:T(128)} %w_ref.3, f32[16,1024]{1,0:T(8,128)} %get-tuple-element.8.partial_ref, f32[16,1024]{1,0:T(8,128)} %get-tuple-element.9.up_ref, f32[16,1024]{1,0:T(8,128)} %copy-done.4, f32[2,16,1024]{2,1,0:T(8,128)} %copy-done.3, f32[16,1024]{1,0:T(8,128)} %get-tuple-element.10.last_ref), custom_call_target="tpu_custom_call" | custom-call | tf_op jit(solution)/shard_map/pallas_call | solution.py:122
  15.6 3.5 %collective-permute-start.2 = (f32[16,256]{1,0:T(8,128)S(1)}, f32[16,256]{1,0:T(8,128)S(1)}, u32[]{:S(2)}, u32[]{:S(2)}) collective-permute-start(f32[16,256]{1,0:T(8,128)S(1)} %copy_bitcast_fusion.2), channel_id=1, source_target_pairs={{0,1},{1,0},{2,3},{3,2},{4,5},{5,4},{6,7},{7,6},{8,9},{9,8},{10,11... | collective-permute-start | bytes 49160 | tf_op jit(solution)/shard_map/ppermute | solution.py:142
  19.1 2.4 %collective-permute-start.3 = (f32[16,256]{1,0:T(8,128)S(1)}, f32[16,256]{1,0:T(8,128)S(1)}, u32[]{:S(2)}, u32[]{:S(2)}) collective-permute-start(f32[16,256]{1,0:T(8,128)S(1)} %copy_bitcast_fusion.2), channel_id=1, source_target_pairs={{0,2},{1,3},{2,0},{3,1},{4,6},{5,7},{6,4},{7,5},{8,10},{9,11},{10,... | collective-permute-start | bytes 49160 | tf_op jit(solution)/shard_map/ppermute | solution.py:142
  21.5 0.1 copy.55
  21.7 1.6 %collective-permute-start.5 = (f32[1,16,1024]{2,1,0:T(8,128)}, f32[1,16,1024]{2,1,0:T(8,128)S(1)}, u32[]{:S(2)}, u32[]{:S(2)}) collective-permute-start(f32[1,16,1024]{2,1,0:T(8,128)} %bitcast.80), channel_id=1, source_target_pairs={{0,4},{1,5},{2,6},{3,7},{4,0},{5,1},{6,2},{7,3},{8,12},{9,13},{10,... | collective-permute-start | bytes 196616 | tf_op jit(solution)/shard_map/ppermute | solution.py:142
  23.3 1.5 %collective-permute-start.6 = (f32[1,16,1024]{2,1,0:T(8,128)}, f32[1,16,1024]{2,1,0:T(8,128)S(1)}, u32[]{:S(2)}, u32[]{:S(2)}) collective-permute-start(f32[1,16,1024]{2,1,0:T(8,128)} %bitcast.81), channel_id=1, source_target_pairs={{0,8},{1,9},{2,10},{3,11},{4,12},{5,13},{6,14},{7,15},{8,0},{9,1},... | collective-permute-start | bytes 196616 | tf_op jit(solution)/shard_map/ppermute | solution.py:142
  24.8 1.3 %collective-permute-start.7 = (f32[1,16,1024]{2,1,0:T(8,128)}, f32[1,16,1024]{2,1,0:T(8,128)S(1)}, u32[]{:S(2)}, u32[]{:S(2)}) collective-permute-start(f32[1,16,1024]{2,1,0:T(8,128)} %bitcast.82), channel_id=1, source_target_pairs={{0,12},{1,13},{2,14},{3,15},{4,8},{5,9},{6,10},{7,11},{8,4},{9,5},... | collective-permute-start | bytes 196616 | tf_op jit(solution)/shard_map/ppermute | solution.py:142
  26.1 0.1 copy.56
  26.2 0.1 copy.57
  26.4 0.1 copy.58
  26.5 0.2 pad_maximum_fusion
  26.6 0.3 fusion.17
  27.0 4.8 %collective-permute-done.6 = f32[1,16,1024]{2,1,0:T(8,128)S(1)} collective-permute-done((f32[1,16,1024]{2,1,0:T(8,128)}, f32[1,16,1024]{2,1,0:T(8,128)S(1)}, u32[]{:S(2)}, u32[]{:S(2)}) %collective-permute-start.6) | collective-permute-done | bytes 65568 | tf_op jit(solution)/shard_map/ppermute | solution.py:142
  31.8 0.3 fusion.15
  32.1 0.3 fusion.13
  32.4 0.3 fusion.3
  32.9 0.1 copy.50
  33.1 0.1 copy.41
  33.2 1.0 %collective-permute-done.8 = f32[2,16,1024]{2,1,0:T(8,128)S(1)} collective-permute-done((f32[2,16,1024]{2,1,0:T(8,128)S(1)}, f32[2,16,1024]{2,1,0:T(8,128)S(1)}, u32[]{:S(2)}, u32[]{:S(2)}) %collective-permute-start.8) | collective-permute-done | bytes 131104 | tf_op jit(solution)/shard_map/ppermute | solution.py:142
  34.3 1.6 %collective-permute-start.9 = (f32[16,1024]{1,0:T(8,128)S(1)}, f32[16,1024]{1,0:T(8,128)S(1)}, u32[]{:S(2)}, u32[]{:S(2)}) collective-permute-start(f32[16,1024]{1,0:T(8,128)S(1)} %slice_bitcast_fusion), channel_id=1, source_target_pairs={{0,2},{1,3},{2,0},{3,1},{4,6},{5,7},{6,4},{7,5},{8,10},{9,11},{10,... | collective-permute-start | bytes 196616 | tf_op jit(solution)/shard_map/ppermute | solution.py:142
  35.9 2.7 %collective-permute-done.9 = f32[16,1024]{1,0:T(8,128)S(1)} collective-permute-done((f32[16,1024]{1,0:T(8,128)S(1)}, f32[16,1024]{1,0:T(8,128)S(1)}, u32[]{:S(2)}, u32[]{:S(2)}) %collective-permute-start.9) | collective-permute-done | bytes 65568 | tf_op jit(solution)/shard_map/ppermute | solution.py:142
  38.6 0.6 %gather_fusion.1 = f32[32,16,128]{2,1,0:T(8,128)S(1)} fusion(f32[16,8,128]{2,0,1:T(8,128)S(1)} %copy_bitcast_fusion.1, s32[1024]{0:T(1024)S(1)} %pad_clamp_fusion), kind=kCustom, calls=%fused_computation.1 | custom fusion | bytes 524416 | tf_op jit(solution)/shard_map/jit(_take)/gather | solution.py:213
  39.2 1.0 %fusion.4 = f32[8,2,8,128]{3,2,1,0:T(8,128)S(1)} fusion(f32[8,128,4,128]{3,2,1,0:T(4,128)S(1)} %bitcast.72, f32[8,4,16,128]{3,2,1,0:T(8,128)S(1)} %bitcast.75, pred[8,4]{1,0:T(8,128)(4,1)S(1)} %copy.41), kind=kOutput, calls=%fused_computation.7 | convolution fusion | flops 50397184 | bytes 2424864 | tf_op jit(solution)/shard_map/xrkc,rikc->xri/dot_general | solution.py:214
  40.2 0.7 %copy.70 = f32[8,2,8,128]{3,2,0,1:T(8,128)} copy(f32[8,2,8,128]{3,2,1,0:T(8,128)S(1)} %fusion.4) | data formatting | bytes 131072 | tf_op jit(solution)/shard_map/reshape | solution.py:220
  (35 shorter events, 0.4 us)
Async XLA Ops:
  0.6 38.6 %copy-start = (f32[1024,4,128]{2,1,0:T(4,128)S(1)}, f32[1024,4,128]{2,1,0:T(4,128)}, u32[]{:S(2)}) copy-start(f32[1024,4,128]{2,1,0:T(4,128)} %param.26) | copy-start | bytes 6291460
  0.6 8.4 %copy-start.1 = (s32[2,4]{1,0:T(2,128)S(1)}, s32[2,4]{1,0:T(2,128)}, u32[]{:S(2)}) copy-start(s32[2,4]{1,0:T(2,128)} %param.25) | copy-start | bytes 100
  0.7 9.1 %copy-start.5 = (bf16[16,4,128]{2,1,0:T(4,128)(2,1)S(1)}, bf16[16,4,128]{2,1,0:T(4,128)(2,1)}, u32[]{:S(2)}) copy-start(bf16[16,4,128]{2,1,0:T(4,128)(2,1)} %param.24) | copy-start | bytes 49156
  5.3 4.6 %collective-permute-start = (f32[16,1024]{1,0:T(8,128)}, f32[16,1024]{1,0:T(8,128)S(1)}, u32[]{:S(2)}, u32[]{:S(2)}) collective-permute-start(f32[16,1024]{1,0:T(8,128)} %get-tuple-element.10.last_ref), channel_id=1, source_target_pairs={{0,1},{1,2},{2,3},{3,4},{4,5},{5,6},{6,7},{7,8},{8,9},{9,10},{10,1... | collective-permute-start | bytes 196616 | tf_op jit(solution)/shard_map/ppermute | solution.py:17
  7.6 5.6 %collective-permute-start.1 = (f32[2,16,1024]{2,1,0:T(8,128)}, f32[2,16,1024]{2,1,0:T(8,128)S(1)}, u32[]{:S(2)}, u32[]{:S(2)}) collective-permute-start(f32[2,16,1024]{2,1,0:T(8,128)} %get-tuple-element.11), channel_id=1, source_target_pairs={{1,0},{2,1},{3,2},{4,3},{5,4},{6,5},{7,6},{8,7},{9,8},{10,9},{11,1... | collective-permute-start | bytes 393224 | tf_op jit(solution)/shard_map/ppermute | solution.py:17
  9.9 23.0 %copy-start.6 = (s32[8,4]{0,1:T(4,128)S(1)}, s32[8,4]{0,1:T(4,128)}, u32[]{:S(2)}) copy-start(s32[8,4]{0,1:T(4,128)} %param.27) | copy-start | bytes 388
  9.9 3.3 %copy-start.4 = (f32[16,1024]{1,0:T(8,128)}, f32[16,1024]{1,0:T(8,128)S(1)}, u32[]{:S(2)}) copy-start(f32[16,1024]{1,0:T(8,128)S(1)} %collective-permute-done.prev_ref) | copy-start | bytes 196612
  13.2 0.7 %copy-start.3 = (f32[2,16,1024]{2,1,0:T(8,128)}, f32[2,16,1024]{2,1,0:T(8,128)S(1)}, u32[]{:S(2)}) copy-start(f32[2,16,1024]{2,1,0:T(8,128)S(1)} %collective-permute-done.1.next_ref) | copy-start | bytes 393220
  15.6 16.9 %copy-start.2 = (f32[16,1024]{1,0:T(8,128)S(1)}, f32[16,1024]{1,0:T(8,128)}, u32[]{:S(2)}) copy-start(f32[16,1024]{1,0:T(8,128)} %shard_map.159) | copy-start | bytes 196612
  15.6 9.3 %collective-permute-start.2 = (f32[16,256]{1,0:T(8,128)S(1)}, f32[16,256]{1,0:T(8,128)S(1)}, u32[]{:S(2)}, u32[]{:S(2)}) collective-permute-start(f32[16,256]{1,0:T(8,128)S(1)} %copy_bitcast_fusion.2), channel_id=1, source_target_pairs={{0,1},{1,0},{2,3},{3,2},{4,5},{5,4},{6,7},{7,6},{8,9},{9,8},{10,11... | collective-permute-start | bytes 49160 | tf_op jit(solution)/shard_map/ppermute | solution.py:142
  19.1 7.1 %collective-permute-start.3 = (f32[16,256]{1,0:T(8,128)S(1)}, f32[16,256]{1,0:T(8,128)S(1)}, u32[]{:S(2)}, u32[]{:S(2)}) collective-permute-start(f32[16,256]{1,0:T(8,128)S(1)} %copy_bitcast_fusion.2), channel_id=1, source_target_pairs={{0,2},{1,3},{2,0},{3,1},{4,6},{5,7},{6,4},{7,5},{8,10},{9,11},{10,... | collective-permute-start | bytes 49160 | tf_op jit(solution)/shard_map/ppermute | solution.py:142
  21.5 4.8 %collective-permute-start.4 = (f32[16,256]{1,0:T(8,128)S(1)}, f32[16,256]{1,0:T(8,128)S(1)}, u32[]{:S(2)}, u32[]{:S(2)}) collective-permute-start(f32[16,256]{1,0:T(8,128)S(1)} %copy_bitcast_fusion.2), channel_id=1, source_target_pairs={{0,3},{1,2},{2,1},{3,0},{4,7},{5,6},{6,5},{7,4},{8,11},{9,10},{10,... | collective-permute-start | bytes 49160 | tf_op jit(solution)/shard_map/ppermute | solution.py:142
  21.7 4.9 %collective-permute-start.5 = (f32[1,16,1024]{2,1,0:T(8,128)}, f32[1,16,1024]{2,1,0:T(8,128)S(1)}, u32[]{:S(2)}, u32[]{:S(2)}) collective-permute-start(f32[1,16,1024]{2,1,0:T(8,128)} %bitcast.80), channel_id=1, source_target_pairs={{0,4},{1,5},{2,6},{3,7},{4,0},{5,1},{6,2},{7,3},{8,12},{9,13},{10,... | collective-permute-start | bytes 196616 | tf_op jit(solution)/shard_map/ppermute | solution.py:142
  23.3 8.5 %collective-permute-start.6 = (f32[1,16,1024]{2,1,0:T(8,128)}, f32[1,16,1024]{2,1,0:T(8,128)S(1)}, u32[]{:S(2)}, u32[]{:S(2)}) collective-permute-start(f32[1,16,1024]{2,1,0:T(8,128)} %bitcast.81), channel_id=1, source_target_pairs={{0,8},{1,9},{2,10},{3,11},{4,12},{5,13},{6,14},{7,15},{8,0},{9,1},... | collective-permute-start | bytes 196616 | tf_op jit(solution)/shard_map/ppermute | solution.py:142
  24.8 7.3 %collective-permute-start.7 = (f32[1,16,1024]{2,1,0:T(8,128)}, f32[1,16,1024]{2,1,0:T(8,128)S(1)}, u32[]{:S(2)}, u32[]{:S(2)}) collective-permute-start(f32[1,16,1024]{2,1,0:T(8,128)} %bitcast.82), channel_id=1, source_target_pairs={{0,12},{1,13},{2,14},{3,15},{4,8},{5,9},{6,10},{7,11},{8,4},{9,5},... | collective-permute-start | bytes 196616 | tf_op jit(solution)/shard_map/ppermute | solution.py:142
  32.8 1.4 %collective-permute-start.8 = (f32[2,16,1024]{2,1,0:T(8,128)S(1)}, f32[2,16,1024]{2,1,0:T(8,128)S(1)}, u32[]{:S(2)}, u32[]{:S(2)}) collective-permute-start(f32[2,16,1024]{2,1,0:T(8,128)S(1)} %slice.13), channel_id=1, source_target_pairs={{0,1},{1,0},{2,3},{3,2},{4,5},{5,4},{6,7},{7,6},{8,9},{9,8},{10,11... | collective-permute-start | bytes 393224 | tf_op jit(solution)/shard_map/ppermute | solution.py:142
  34.3 4.3 %collective-permute-start.9 = (f32[16,1024]{1,0:T(8,128)S(1)}, f32[16,1024]{1,0:T(8,128)S(1)}, u32[]{:S(2)}, u32[]{:S(2)}) collective-permute-start(f32[16,1024]{1,0:T(8,128)S(1)} %slice_bitcast_fusion), channel_id=1, source_target_pairs={{0,2},{1,3},{2,0},{3,1},{4,6},{5,7},{6,4},{7,5},{8,10},{9,11},{10,... | collective-permute-start | bytes 196616 | tf_op jit(solution)/shard_map/ppermute | solution.py:142

commit v14 on v12

--- a/solution.py
+++ b/solution.py
@@ -3,9 +3,10 @@
 from jax import lax
 from jax.experimental import pallas as pl
 from jax.experimental.pallas import tpu as pltpu
-from jax.sharding import PartitionSpec as P
+from jax.sharding import Mesh, PartitionSpec as P
 
 BLK = 128
+AX = ("zq", "xq", "cq")
 Z_CHUNK = 8
 
 precise = lax.Precision.HIGH
@@ -157,23 +158,16 @@
     count = lax.axis_size(axis)
     me = lax.axis_index(axis)
     rows = local.shape[0]
+    lines = count // 4
     per_device = slab.reshape(slab.shape[0], count, rows)
-
-    def product(piece, masks):
-        cols = jnp.take(per_device, me ^ jnp.array(masks, jnp.int32), axis=1).reshape(slab.shape[0], -1)
-        return jnp.dot(cols, piece.reshape(-1, piece.shape[-1]), precision=precise, preferred_element_type=jnp.float32)
-
-    buf = local[None]
-    entries = [0]
-    total = product(buf, entries)
-    for masks in gather_rounds(count):
-        others = [swap(buf, axis, m) for m in masks]
-        for m, other in zip(masks, others):
-            total = total + product(other, [m ^ q for q in entries])
-        buf = jnp.concatenate([buf] + others, axis=0)
-        entries = entries + [m ^ q for m in masks for q in entries]
+    devices = jnp.arange(lines, dtype=jnp.int32) * 4 + me % 4
+    cols = jnp.take(per_device, devices, axis=1).reshape(slab.shape[0], -1)
+    spread = jnp.broadcast_to(local[None], (lines,) + local.shape)
+    got = lax.all_to_all(spread, axis[0], 0, 0, tiled=True)
+    total = jnp.dot(cols, got.reshape(-1, local.shape[-1]), precision=precise, preferred_element_type=jnp.float32)
     parts = total.reshape(4, rows, total.shape[-1])
-    return parts[0] + (swap(parts[1], axis, 1) + swap(parts[2], axis, 2) + swap(parts[3], axis, 3))
+    near = parts[0::2] + swap(parts[1::2], axis, 1)
+    return near[0] + swap(near[1], axis, 2)
 
 
 def body(
@@ -189,21 +183,21 @@
     cov_y,
     offsets_y,
 ):
-    count = lax.axis_size("gx")
-    me = lax.axis_index("gx")
+    count = lax.axis_size(AX)
+    me = lax.axis_index(AX)
     depth, rows, cols = adjoint_state.shape
 
     partial, to_prev, last_s, up_x0 = stencil(
         layer_weight, adjoint_state, face_flags, speed_x, speed_y, speed_z, dispersion
     )
-    from_next = passed_along(to_prev, "gx", -1)
-    from_prev = passed_along(last_s, "gx", 1)
+    from_next = passed_along(to_prev, AX, -1)
+    from_prev = passed_along(last_s, AX, 1)
 
     recharge = corrected(layer_weight, partial, up_x0, from_prev, from_next, last_s)
 
     own_slab = cx_slab(cov_x, offsets_x, me, rows)
-    slab = jnp.concatenate([own_slab] + [swap(own_slab, "gx", m) for m in (1, 2, 3)], axis=0)
-    mixed = mixed_rows(recharge, slab, "gx")
+    slab = jnp.concatenate([own_slab] + [swap(own_slab, AX, m) for m in (1, 2, 3)], axis=0)
+    mixed = mixed_rows(recharge, slab, AX)
 
     nyb = offsets_y.shape[0]
     col_block = (jnp.arange(nyb)[:, None] + offsets_y) % nyb
@@ -219,22 +213,13 @@
 
 
 def solution(mesh):
+    count = mesh.shape["gx"]
+    split = Mesh(mesh.devices.reshape(mesh.shape["grp"], count // 4, 2, 2), ("grp",) + AX)
+    field = P(None, ("grp",) + AX, None)
     return jax.shard_map(
         body,
-        mesh=mesh,
-        in_specs=(
-            P(None, ("grp", "gx"), None),
-            P(None, ("grp", "gx"), None),
-            P(None, ("grp", "gx"), None),
-            P(None, ("grp", "gx"), None),
-            P(None, ("grp", "gx"), None),
-            P(None, ("grp", "gx"), None),
-            P(),
-            P("gx", None, None),
-            P(),
-            P(),
-            P(),
-        ),
-        out_specs=(P(("grp", "gx"), None), P(("grp", "gx"), None)),
+        mesh=split,
+        in_specs=(field, field, field, field, field, field, P(), P(AX, None, None), P(), P(), P()),
+        out_specs=(P(("grp",) + AX, None), P(("grp",) + AX, None)),
         check_vma=False,
     )

time: 42.9 us -> 47.5 us (1.11)
  waiting for transfers between devices: 11.6 us -> 16.2 us
  local copies, waits for them, and re-layouts: 4.78 us -> 7 us
  matrix products: 3.06 us -> 1.27 us
  starting transfers between devices: 15.7 us -> 15.1 us
    all_to_all x0 -> x1, waiting for transfers between devices: none -> 8.4 us  [mixed_rows(): got = lax.all_to_all(spread, axis[0], 0, 0, tiled=True)]
    ppermute x9 -> x5, starting transfers between devices: 12.4 us -> 4.08 us  [swap(): return lax.ppermute(value, axis, [(i, i ^ mask) for i in range(count)])]
    all_to_all x0 -> x1, starting transfers between devices: none -> 7.69 us  [mixed_rows(): got = lax.all_to_all(spread, axis[0], 0, 0, tiled=True)]
    ppermute x9 -> x5, waiting for transfers between devices: 9.01 us -> 4.52 us  [swap(): return lax.ppermute(value, axis, [(i, i ^ mask) for i in range(count)])]
    dot_general x4 -> x1, matrix products: 2.1 us -> 0.32 us  [mixed_rows(): jnp.dot(cols, got.reshape(-1, local.shape[-1]), precision=precise, prefer...]
    broadcast_in_dim x0 -> x1, local copies, waits for them, and re-layouts: none -> 1.56 us  [mixed_rows(): spread = jnp.broadcast_to(local[None], (lines,) + local.shape)]
    ppermute x2, waiting for transfers between devices: 2.6 us -> 3.3 us  [passed_along(): lax.ppermute(value, axis, [(source, source + steps) for source in range(f...]
    gather x0 -> x1, local copies, waits for them, and re-layouts: none -> 0.55 us  [mixed_rows(): cols = jnp.take(per_device, devices, axis=1).reshape(slab.shape[0], -1)]
  transfers between devices with their start and end apart: 11 -> 8, of which waited for: 6 -> 4; matrix products, arithmetic and copies ran while one was open for 3% -> 7% of each run, Pallas kernels for 10% -> 13%
where the time goes in v14:
time: 47.5 us; the launch traced here: 47.1 us
  waiting for transfers between devices  16.2 us (34%)
  starting transfers between devices  15.1 us (32%)
  local copies, waits for them, and re-layouts  7 us (15%)
  Pallas kernels  6.15 us (13%)
  matrix products  1.27 us (3%)
  between operations  0.86 us (2%)
  other arithmetic  0.52 us (1%)
    all_to_all x1, waiting for transfers between devices, mixed_rows(): got = lax.all_to_all(spread, axis[0], 0, 0, tiled=True)  8.4 us
    all_to_all x1, starting transfers between devices, mixed_rows(): got = lax.all_to_all(spread, axis[0], 0, 0, tiled=True)  7.69 us
    ppermute x5, waiting for transfers between devices, swap(): return lax.ppermute(value, axis, [(i, i ^ mask) for i in range(count)])  4.52 us
    pallas_call x1, Pallas kernels, stencil(): pl.pallas_call(stencil_kernel, grid=(depth // zc,), in_specs=[pl.BlockSpe...  4.45 us
    ppermute x5, starting transfers between devices, swap(): return lax.ppermute(value, axis, [(i, i ^ mask) for i in range(count)])  4.08 us
    ppermute x2, starting transfers between devices, passed_along(): lax.ppermute(value, axis, [(source, source + steps) for source in range(f...  3.34 us
    ppermute x2, waiting for transfers between devices, passed_along(): lax.ppermute(value, axis, [(source, source + steps) for source in range(f...  3.3 us
    pallas_call x1, Pallas kernels, corrected(): pl.pallas_call(fix_kernel, in_specs=[pl.BlockSpec(memory_space=pltpu.SMEM...  1.69 us
  transfers between devices with their start and end apart: 8, of which 4 were waited for; matrix products, arithmetic and copies ran while one was open for 7% of the time, Pallas kernels for 13%

profile of v14, /device:TPU:0, one launch (start us, length us, event | category | flops | bytes accessed | tf_op | source)
XLA Modules:
  0.0 47.1 jit_solution(11655781611578655981)
XLA Ops:
  0.7 1.4 %gather_fusion = s32[16,4]{1,0:T(8,128)S(1)} fusion(s32[2,4]{1,0:T(2,128)} %param.19, s32[1024]{0:T(1024)S(1)} %pad_clamp_fusion.2), kind=kCustom, calls=%fused_computation | custom fusion | bytes 576 | tf_op jit(solution)/shard_map/gather | solution.py:150
  2.2 0.1 copy.33
  2.3 0.7 %copy.34 = f32[16,4,128]{2,0,1:T(8,128)S(1)} copy(bf16[16,4,128]{2,1,0:T(4,128)(2,1)} %param.18) | data formatting | bytes 49152 | tf_op jit(solution)/shard_map/convert_element_type | solution.py:153
  3.0 0.1 select_reduce_fusion
  3.1 0.5 %collective-permute-start.2 = (f32[16,256]{1,0:T(8,128)S(1)}, f32[16,256]{1,0:T(8,128)S(1)}, u32[]{:S(2)}, u32[]{:S(2)}) collective-permute-start(f32[16,256]{1,0:T(8,128)S(1)} %copy_bitcast_fusion.2), channel_id=1, source_target_pairs={{0,1},{1,0},{2,3},{3,2},{4,5},{5,4},{6,7},{7,6},{8,9},{9,8},{10,11... | collective-permute-start | bytes 49160 | tf_op jit(solution)/shard_map/ppermute | solution.py:143
  3.6 2.6 %collective-permute-start.3 = (f32[16,256]{1,0:T(8,128)S(1)}, f32[16,256]{1,0:T(8,128)S(1)}, u32[]{:S(2)}, u32[]{:S(2)}) collective-permute-start(f32[16,256]{1,0:T(8,128)S(1)} %copy_bitcast_fusion.2), channel_id=1, source_target_pairs={{0,2},{1,3},{2,0},{3,1},{4,6},{5,7},{6,4},{7,5},{8,10},{9,11},{10,... | collective-permute-start | bytes 49160 | tf_op jit(solution)/shard_map/ppermute | solution.py:143
  6.2 4.5 %shard_map.122 = (f32[16,1024]{1,0:T(8,128)}, f32[2,16,1024]{2,1,0:T(8,128)}, f32[16,1024]{1,0:T(8,128)}, f32[16,1024]{1,0:T(8,128)}) custom-call(f32[16]{0:T(128)} %w_ref.3, f32[16,16,1024]{2,1,0:T(8,128)} %sprev_ref.1, f32[16,16,1024]{2,1,0:T(8,128)} %sprev_ref.1, s32[16,16,1024]{2,1,0:T(8,128)} %f_ref.1, f32[16,16,1024]{2,1,0:T(8,128)} %vx_ref.1, ...), custom_call_target="tpu_custom_call" | custom-call | tf_op jit(solution)/shard_map/pallas_call | solution.py:76
  10.7 2.0 %collective-permute-start = (f32[16,1024]{1,0:T(8,128)}, f32[16,1024]{1,0:T(8,128)S(1)}, u32[]{:S(2)}, u32[]{:S(2)}) collective-permute-start(f32[16,1024]{1,0:T(8,128)} %get-tuple-element.8.last_ref), channel_id=1, source_target_pairs={{0,1},{1,2},{2,3},{3,4},{4,5},{5,6},{6,7},{7,8},{8,9},{9,10},{10,1... | collective-permute-start | bytes 196616 | tf_op jit(solution)/shard_map/ppermute | solution.py:18
  12.8 1.3 %collective-permute-start.1 = (f32[2,16,1024]{2,1,0:T(8,128)}, f32[2,16,1024]{2,1,0:T(8,128)S(1)}, u32[]{:S(2)}, u32[]{:S(2)}) collective-permute-start(f32[2,16,1024]{2,1,0:T(8,128)} %get-tuple-element.9), channel_id=1, source_target_pairs={{1,0},{2,1},{3,2},{4,3},{5,4},{6,5},{7,6},{8,7},{9,8},{10,9},{11,1... | collective-permute-start | bytes 393224 | tf_op jit(solution)/shard_map/ppermute | solution.py:18
  14.1 3.3 %collective-permute-done.1.next_ref = f32[2,16,1024]{2,1,0:T(8,128)S(1)} collective-permute-done((f32[2,16,1024]{2,1,0:T(8,128)}, f32[2,16,1024]{2,1,0:T(8,128)S(1)}, u32[]{:S(2)}, u32[]{:S(2)}) %collective-permute-start.1) | collective-permute-done | bytes 131104 | tf_op jit(solution)/shard_map/ppermute | solution.py:18
  17.4 0.6 %copy-done.1 = f32[2,16,1024]{2,1,0:T(8,128)} copy-done((f32[2,16,1024]{2,1,0:T(8,128)}, f32[2,16,1024]{2,1,0:T(8,128)S(1)}, u32[]{:S(2)}) %copy-start.1) | copy-done | bytes 131096
  18.1 1.7 %shard_map.123 = f32[16,1024]{1,0:T(8,128)} custom-call(f32[16]{0:T(128)} %w_ref.3, f32[16,1024]{1,0:T(8,128)} %get-tuple-element.6.partial_ref, f32[16,1024]{1,0:T(8,128)} %get-tuple-element.7.up_ref, f32[16,1024]{1,0:T(8,128)} %copy-done.2, f32[2,16,1024]{2,1,0:T(8,128)} %copy-done.1, f32[16,1024]{1,0:T(8,128)} %get-tuple-element.8.last_ref), custom_call_target="tpu_custom_call" | custom-call | tf_op jit(solution)/shard_map/pallas_call | solution.py:123
  19.8 1.6 %broadcast_in_dim.60 = f32[4,16,1024]{2,1,0:T(8,128)} broadcast(f32[16,1024]{1,0:T(8,128)} %shard_map.123), dimensions={1,2} | broadcast | bytes 327680 | tf_op jit(solution)/shard_map/broadcast_in_dim | solution.py:165
  21.3 7.7 %all-to-all-start = ((f32[4,16,1024]{2,1,0:T(8,128)}), f32[4,16,1024]{2,1,0:T(8,128)S(1)}, u32[]{:S(2)}, u32[]{:S(2)}) async-start(f32[4,16,1024]{2,1,0:T(8,128)} %broadcast_in_dim.60), calls=%async_computation | async-start | bytes 524288 | tf_op jit(solution)/shard_map/all_to_all | solution.py:166
  29.0 0.1 copy.35
  29.1 0.1 copy.37
  29.2 0.1 copy.38
  29.3 0.1 copy.39
  29.4 0.2 pad_maximum_fusion
  29.6 0.6 %gather_fusion.1 = f32[4,64,16]{1,2,0:T(8,128)S(1)} fusion(f32[64,16,16]{0,2,1:T(8,128)S(1)} %pad_maximum_fusion, s32[1024]{0:T(1024)S(1)} %pad_clamp_fusion.1), kind=kCustom, calls=%fused_computation.1 | custom fusion | bytes 32784 | tf_op jit(solution)/shard_map/jit(_take)/gather | solution.py:164
  30.3 0.1 reshape.214
  30.4 8.4 %all-to-all-done = f32[4,16,1024]{2,1,0:T(8,128)S(1)} async-done(((f32[4,16,1024]{2,1,0:T(8,128)}), f32[4,16,1024]{2,1,0:T(8,128)S(1)}, u32[]{:S(2)}, u32[]{:S(2)}) %all-to-all-start) | async-done | bytes 262176 | tf_op jit(solution)/shard_map/all_to_all | solution.py:166
  38.8 0.3 fusion.7
  39.2 0.1 copy.41
  39.3 0.1 reshape.204
  39.4 0.1 copy.32
  39.5 1.0 %collective-permute-done.5 = f32[2,16,1024]{2,1,0:T(8,128)S(1)} collective-permute-done((f32[2,16,1024]{2,1,0:T(8,128)S(1)}, f32[2,16,1024]{2,1,0:T(8,128)S(1)}, u32[]{:S(2)}, u32[]{:S(2)}) %collective-permute-start.5) | collective-permute-done | bytes 131104 | tf_op jit(solution)/shard_map/ppermute | solution.py:143
  40.6 0.9 %collective-permute-start.6 = (f32[16,1024]{1,0:T(8,128)S(1)}, f32[16,1024]{1,0:T(8,128)S(1)}, u32[]{:S(2)}, u32[]{:S(2)}) collective-permute-start(f32[16,1024]{1,0:T(8,128)S(1)} %slice_bitcast_fusion), channel_id=1, source_target_pairs={{0,2},{1,3},{2,0},{3,1},{4,6},{5,7},{6,4},{7,5},{8,10},{9,11},{10,... | collective-permute-start | bytes 196616 | tf_op jit(solution)/shard_map/ppermute | solution.py:143
  41.4 3.5 %collective-permute-done.6 = f32[16,1024]{1,0:T(8,128)S(1)} collective-permute-done((f32[16,1024]{1,0:T(8,128)S(1)}, f32[16,1024]{1,0:T(8,128)S(1)}, u32[]{:S(2)}, u32[]{:S(2)}) %collective-permute-start.6) | collective-permute-done | bytes 65568 | tf_op jit(solution)/shard_map/ppermute | solution.py:143
  44.9 0.6 %gather_fusion.2 = f32[32,16,128]{2,1,0:T(8,128)S(1)} fusion(f32[16,8,128]{2,0,1:T(8,128)S(1)} %copy_bitcast_fusion.1, s32[1024]{0:T(1024)S(1)} %pad_clamp_fusion), kind=kCustom, calls=%fused_computation.2 | custom fusion | bytes 524416 | tf_op jit(solution)/shard_map/jit(_take)/gather | solution.py:204
  45.5 1.0 %fusion.2 = f32[8,2,8,128]{3,2,1,0:T(8,128)S(1)} fusion(f32[8,128,4,128]{3,2,1,0:T(4,128)S(1)} %bitcast.49, f32[8,4,16,128]{3,2,1,0:T(8,128)S(1)} %bitcast.50, pred[8,4]{1,0:T(8,128)(4,1)S(1)} %copy.32), kind=kOutput, calls=%fused_computation.5 | convolution fusion | flops 50397184 | bytes 2424864 | tf_op jit(solution)/shard_map/xrkc,rikc->xri/dot_general | solution.py:205
  46.5 0.7 %copy.59 = f32[8,2,8,128]{3,2,0,1:T(8,128)} copy(f32[8,2,8,128]{3,2,1,0:T(8,128)S(1)} %fusion.2) | data formatting | bytes 131072 | tf_op jit(solution)/shard_map/reshape | solution.py:211
  (29 shorter events, 0.5 us)
Async XLA Ops:
  0.6 44.9 %copy-start = (f32[1024,4,128]{2,1,0:T(4,128)S(1)}, f32[1024,4,128]{2,1,0:T(4,128)}, u32[]{:S(2)}) copy-start(f32[1024,4,128]{2,1,0:T(4,128)} %param.20) | copy-start | bytes 6291460
  3.1 26.0 %collective-permute-start.2 = (f32[16,256]{1,0:T(8,128)S(1)}, f32[16,256]{1,0:T(8,128)S(1)}, u32[]{:S(2)}, u32[]{:S(2)}) collective-permute-start(f32[16,256]{1,0:T(8,128)S(1)} %copy_bitcast_fusion.2), channel_id=1, source_target_pairs={{0,1},{1,0},{2,3},{3,2},{4,5},{5,4},{6,7},{7,6},{8,9},{9,8},{10,11... | collective-permute-start | bytes 49160 | tf_op jit(solution)/shard_map/ppermute | solution.py:143
  3.6 25.6 %collective-permute-start.3 = (f32[16,256]{1,0:T(8,128)S(1)}, f32[16,256]{1,0:T(8,128)S(1)}, u32[]{:S(2)}, u32[]{:S(2)}) collective-permute-start(f32[16,256]{1,0:T(8,128)S(1)} %copy_bitcast_fusion.2), channel_id=1, source_target_pairs={{0,2},{1,3},{2,0},{3,1},{4,6},{5,7},{6,4},{7,5},{8,10},{9,11},{10,... | collective-permute-start | bytes 49160 | tf_op jit(solution)/shard_map/ppermute | solution.py:143
  6.2 23.2 %collective-permute-start.4 = (f32[16,256]{1,0:T(8,128)S(1)}, f32[16,256]{1,0:T(8,128)S(1)}, u32[]{:S(2)}, u32[]{:S(2)}) collective-permute-start(f32[16,256]{1,0:T(8,128)S(1)} %copy_bitcast_fusion.2), channel_id=1, source_target_pairs={{0,3},{1,2},{2,1},{3,0},{4,7},{5,6},{6,5},{7,4},{8,11},{9,10},{10,... | collective-permute-start | bytes 49160 | tf_op jit(solution)/shard_map/ppermute | solution.py:143
  10.7 28.5 %copy-start.3 = (s32[8,4]{0,1:T(4,128)S(1)}, s32[8,4]{0,1:T(4,128)}, u32[]{:S(2)}) copy-start(s32[8,4]{0,1:T(4,128)} %param.21) | copy-start | bytes 388
  10.7 3.4 %collective-permute-start = (f32[16,1024]{1,0:T(8,128)}, f32[16,1024]{1,0:T(8,128)S(1)}, u32[]{:S(2)}, u32[]{:S(2)}) collective-permute-start(f32[16,1024]{1,0:T(8,128)} %get-tuple-element.8.last_ref), channel_id=1, source_target_pairs={{0,1},{1,2},{2,3},{3,4},{4,5},{5,6},{6,7},{7,8},{8,9},{9,10},{10,1... | collective-permute-start | bytes 196616 | tf_op jit(solution)/shard_map/ppermute | solution.py:18
  12.8 4.7 %collective-permute-start.1 = (f32[2,16,1024]{2,1,0:T(8,128)}, f32[2,16,1024]{2,1,0:T(8,128)S(1)}, u32[]{:S(2)}, u32[]{:S(2)}) collective-permute-start(f32[2,16,1024]{2,1,0:T(8,128)} %get-tuple-element.9), channel_id=1, source_target_pairs={{1,0},{2,1},{3,2},{4,3},{5,4},{6,5},{7,6},{8,7},{9,8},{10,9},{11,1... | collective-permute-start | bytes 393224 | tf_op jit(solution)/shard_map/ppermute | solution.py:18
  14.1 3.3 %copy-start.2 = (f32[16,1024]{1,0:T(8,128)}, f32[16,1024]{1,0:T(8,128)S(1)}, u32[]{:S(2)}) copy-start(f32[16,1024]{1,0:T(8,128)S(1)} %collective-permute-done.prev_ref) | copy-start | bytes 196612
  17.4 0.7 %copy-start.1 = (f32[2,16,1024]{2,1,0:T(8,128)}, f32[2,16,1024]{2,1,0:T(8,128)S(1)}, u32[]{:S(2)}) copy-start(f32[2,16,1024]{2,1,0:T(8,128)S(1)} %collective-permute-done.1.next_ref) | copy-start | bytes 393220
  21.3 17.5 %all-to-all-start = ((f32[4,16,1024]{2,1,0:T(8,128)}), f32[4,16,1024]{2,1,0:T(8,128)S(1)}, u32[]{:S(2)}, u32[]{:S(2)}) async-start(f32[4,16,1024]{2,1,0:T(8,128)} %broadcast_in_dim.60), calls=%async_computation | async-start | bytes 524288 | tf_op jit(solution)/shard_map/all_to_all | solution.py:166
  39.1 1.4 %collective-permute-start.5 = (f32[2,16,1024]{2,1,0:T(8,128)S(1)}, f32[2,16,1024]{2,1,0:T(8,128)S(1)}, u32[]{:S(2)}, u32[]{:S(2)}) collective-permute-start(f32[2,16,1024]{2,1,0:T(8,128)S(1)} %slice.13), channel_id=1, source_target_pairs={{0,1},{1,0},{2,3},{3,2},{4,5},{5,4},{6,7},{7,6},{8,9},{9,8},{10,11... | collective-permute-start | bytes 393224 | tf_op jit(solution)/shard_map/ppermute | solution.py:143
  40.6 4.3 %collective-permute-start.6 = (f32[16,1024]{1,0:T(8,128)S(1)}, f32[16,1024]{1,0:T(8,128)S(1)}, u32[]{:S(2)}, u32[]{:S(2)}) collective-permute-start(f32[16,1024]{1,0:T(8,128)S(1)} %slice_bitcast_fusion), channel_id=1, source_target_pairs={{0,2},{1,3},{2,0},{3,1},{4,6},{5,7},{6,4},{7,5},{8,10},{9,11},{10,... | collective-permute-start | bytes 196616 | tf_op jit(solution)/shard_map/ppermute | solution.py:143

commit v15 on v9

--- a/solution.py
+++ b/solution.py
@@ -204,7 +204,9 @@
     recharge = corrected(layer_weight, partial, up_x0, from_prev, from_next, last_s)
 
     own_slab = cx_slab(cov_x, offsets_x, me, rows)
-    slab = jnp.concatenate([own_slab] + [swap(own_slab, "gx", m) for m in (1, 2, 3)], axis=0)
+    pair_slab = jnp.concatenate([own_slab, swap(own_slab, "gx", 1)], axis=0)
+    late_pair, _ = lax.optimization_barrier((pair_slab, recharge))
+    slab = jnp.concatenate([pair_slab, swap(late_pair, "gx", 2)], axis=0)
     mixed = mixed_rows(recharge, slab, "gx")
 
     nyb = offsets_y.shape[0]

time: 41.2 us -> 39.6 us (0.961)
  waiting for transfers between devices: 12.5 us -> 9.88 us
  starting transfers between devices: 14.5 us -> 16.5 us
  matrix products: 3.07 us -> 2.23 us
    ppermute x8 -> x7, waiting for transfers between devices: 12.5 us -> 8.81 us  [swap(): return lax.ppermute(value, axis, [(i, i ^ mask) for i in range(count)])]
    ppermute x8 -> x7, starting transfers between devices: 10.9 us -> 13.3 us  [swap(): return lax.ppermute(value, axis, [(i, i ^ mask) for i in range(count)])]
    ppermute x2, waiting for transfers between devices: 0.01 us -> 1.07 us  [passed_along(): lax.ppermute(value, axis, [(source, source + steps) for source in range(f...]
    dot_general x4, matrix products: 2.12 us -> 1.27 us  [product(): jnp.dot(cols, piece.reshape(-1, piece.shape[-1]), precision=precise, pref...]
    ppermute x2, starting transfers between devices: 3.65 us -> 3.21 us  [passed_along(): lax.ppermute(value, axis, [(source, source + steps) for source in range(f...]
  transfers between devices with their start and end apart: 10 -> 9, of which waited for: 7 -> 5; matrix products, arithmetic and copies ran while one was open for 6% -> 5% of each run, Pallas kernels for 0% -> 0%
where the time goes in v15:
time: 39.6 us; the launch traced here: 39.4 us
  starting transfers between devices  16.5 us (42%)
  waiting for transfers between devices  9.88 us (25%)
  Pallas kernels  6.3 us (16%)
  local copies, waits for them, and re-layouts  3.16 us (8%)
  matrix products  2.23 us (6%)
  between operations  0.91 us (2%)
    ppermute x7, starting transfers between devices, swap(): return lax.ppermute(value, axis, [(i, i ^ mask) for i in range(count)])  13.3 us
    ppermute x7, waiting for transfers between devices, swap(): return lax.ppermute(value, axis, [(i, i ^ mask) for i in range(count)])  8.81 us
    pallas_call x1, Pallas kernels, stencil(): pl.pallas_call(stencil_kernel, grid=(depth // zc,), in_specs=[pl.BlockSpe...  4.6 us
    ppermute x2, starting transfers between devices, passed_along(): lax.ppermute(value, axis, [(source, source + steps) for source in range(f...  3.21 us
    pallas_call x1, Pallas kernels, corrected(): pl.pallas_call(fix_kernel, in_specs=[pl.BlockSpec(memory_space=pltpu.SMEM...  1.69 us
    dot_general x4, matrix products, product(): jnp.dot(cols, piece.reshape(-1, piece.shape[-1]), precision=precise, pref...  1.27 us
    ppermute x2, waiting for transfers between devices, passed_along(): lax.ppermute(value, axis, [(source, source + steps) for source in range(f...  1.07 us
    dot_general x1, matrix products, body(): jnp.einsum('xrkc,rikc->xri', picked, cov_y.reshape(nyb, BLK, cov_y.shape[...  0.96 us
  transfers between devices with their start and end apart: 9, of which 5 were waited for; matrix products, arithmetic and copies ran while one was open for 5% of the time, Pallas kernels for 0%

profile of v15, /device:TPU:0, one launch (start us, length us, event | category | flops | bytes accessed | tf_op | source)
XLA Modules:
  0.0 39.4 jit_solution(3645048155122969632)
XLA Ops:
  0.7 4.6 %shard_map.158 = (f32[16,1024]{1,0:T(8,128)}, f32[2,16,1024]{2,1,0:T(8,128)}, f32[16,1024]{1,0:T(8,128)}, f32[16,1024]{1,0:T(8,128)}) custom-call(f32[16]{0:T(128)} %w_ref.3, f32[16,16,1024]{2,1,0:T(8,128)} %sprev_ref.1, f32[16,16,1024]{2,1,0:T(8,128)} %sprev_ref.1, s32[16,16,1024]{2,1,0:T(8,128)} %f_ref.1, f32[16,16,1024]{2,1,0:T(8,128)} %vx_ref.1, ...), custom_call_target="tpu_custom_call" | custom-call | tf_op jit(solution)/shard_map/pallas_call | solution.py:75
  5.3 1.3 %collective-permute-start.1 = (f32[2,16,1024]{2,1,0:T(8,128)}, f32[2,16,1024]{2,1,0:T(8,128)S(1)}, u32[]{:S(2)}, u32[]{:S(2)}) collective-permute-start(f32[2,16,1024]{2,1,0:T(8,128)} %get-tuple-element.11), channel_id=1, source_target_pairs={{1,0},{2,1},{3,2},{4,3},{5,4},{6,5},{7,6},{8,7},{9,8},{10,9},{11,1... | collective-permute-start | bytes 393224 | tf_op jit(solution)/shard_map/ppermute | solution.py:17
  6.7 0.6 %gather_fusion = s32[16,4]{1,0:T(8,128)S(1)} fusion(s32[2,4]{1,0:T(2,128)S(1)} %copy-done.1, s32[1024]{0:T(1024)S(1)} %pad_clamp_fusion.1), kind=kCustom, calls=%fused_computation | custom fusion | bytes 576 | tf_op jit(solution)/shard_map/gather | solution.py:149
  7.3 0.1 copy.47
  7.4 0.1 select_reduce_fusion
  7.5 1.2 %collective-permute-start.2 = (f32[16,256]{1,0:T(8,128)S(1)}, f32[16,256]{1,0:T(8,128)S(1)}, u32[]{:S(2)}, u32[]{:S(2)}) collective-permute-start(f32[16,256]{1,0:T(8,128)S(1)} %copy_bitcast_fusion.2), channel_id=1, source_target_pairs={{0,1},{1,0},{2,3},{3,2},{4,5},{5,4},{6,7},{7,6},{8,9},{9,8},{10,11... | collective-permute-start | bytes 49160 | tf_op jit(solution)/shard_map/ppermute | solution.py:142
  8.7 1.9 %collective-permute-start = (f32[16,1024]{1,0:T(8,128)}, f32[16,1024]{1,0:T(8,128)S(1)}, u32[]{:S(2)}, u32[]{:S(2)}) collective-permute-start(f32[16,1024]{1,0:T(8,128)} %get-tuple-element.10.last_ref), channel_id=1, source_target_pairs={{0,1},{1,2},{2,3},{3,4},{4,5},{5,6},{6,7},{7,8},{8,9},{9,10},{10,1... | collective-permute-start | bytes 196616 | tf_op jit(solution)/shard_map/ppermute | solution.py:17
  10.6 1.1 %collective-permute-done.prev_ref = f32[16,1024]{1,0:T(8,128)S(1)} collective-permute-done((f32[16,1024]{1,0:T(8,128)}, f32[16,1024]{1,0:T(8,128)S(1)}, u32[]{:S(2)}, u32[]{:S(2)}) %collective-permute-start) | collective-permute-done | bytes 65568 | tf_op jit(solution)/shard_map/ppermute | solution.py:17
  11.7 0.6 %copy-done.4 = f32[16,1024]{1,0:T(8,128)} copy-done((f32[16,1024]{1,0:T(8,128)}, f32[16,1024]{1,0:T(8,128)S(1)}, u32[]{:S(2)}) %copy-start.4) | copy-done | bytes 65560
  12.4 1.7 %shard_map.159 = f32[16,1024]{1,0:T(8,128)} custom-call(f32[16]{0:T(128)} %w_ref.3, f32[16,1024]{1,0:T(8,128)} %get-tuple-element.8.partial_ref, f32[16,1024]{1,0:T(8,128)} %get-tuple-element.9.up_ref, f32[16,1024]{1,0:T(8,128)} %copy-done.4, f32[2,16,1024]{2,1,0:T(8,128)} %copy-done.3, f32[16,1024]{1,0:T(8,128)} %get-tuple-element.10.last_ref), custom_call_target="tpu_custom_call" | custom-call | tf_op jit(solution)/shard_map/pallas_call | solution.py:122
  14.1 0.1 copy.51
  14.2 5.8 %collective-permute-start.3 = (f32[32,256]{0,1:T(8,128)S(1)}, f32[32,256]{0,1:T(8,128)S(1)}, u32[]{:S(2)}, u32[]{:S(2)}) collective-permute-start(f32[32,256]{0,1:T(8,128)S(1)} %copy.51), channel_id=1, source_target_pairs={{0,2},{1,3},{2,0},{3,1},{4,6},{5,7},{6,4},{7,5},{8,10},{9,11},{10,... | collective-permute-start | bytes 98312 | tf_op jit(solution)/shard_map/ppermute | solution.py:142
  20.0 0.1 copy.59
  20.1 0.1 copy.60
  20.2 1.6 %collective-permute-start.4 = (f32[1,16,1024]{2,1,0:T(8,128)}, f32[1,16,1024]{2,1,0:T(8,128)S(1)}, u32[]{:S(2)}, u32[]{:S(2)}) collective-permute-start(f32[1,16,1024]{2,1,0:T(8,128)} %bitcast.77), channel_id=1, source_target_pairs={{0,4},{1,5},{2,6},{3,7},{4,0},{5,1},{6,2},{7,3},{8,12},{9,13},{10,... | collective-permute-start | bytes 196616 | tf_op jit(solution)/shard_map/ppermute | solution.py:142
  21.8 2.6 %collective-permute-start.5 = (f32[1,16,1024]{2,1,0:T(8,128)}, f32[1,16,1024]{2,1,0:T(8,128)S(1)}, u32[]{:S(2)}, u32[]{:S(2)}) collective-permute-start(f32[1,16,1024]{2,1,0:T(8,128)} %bitcast.78), channel_id=1, source_target_pairs={{0,8},{1,9},{2,10},{3,11},{4,12},{5,13},{6,14},{7,15},{8,0},{9,1},... | collective-permute-start | bytes 196616 | tf_op jit(solution)/shard_map/ppermute | solution.py:142
  24.4 0.2 collective-permute-start.6
  24.6 0.1 pad_maximum_fusion
  24.8 0.3 fusion.17
  25.1 3.8 %collective-permute-done.5 = f32[1,16,1024]{2,1,0:T(8,128)S(1)} collective-permute-done((f32[1,16,1024]{2,1,0:T(8,128)}, f32[1,16,1024]{2,1,0:T(8,128)S(1)}, u32[]{:S(2)}, u32[]{:S(2)}) %collective-permute-start.5) | collective-permute-done | bytes 65568 | tf_op jit(solution)/shard_map/ppermute | solution.py:142
  28.9 0.3 fusion.15
  29.2 1.5 %collective-permute-done.6 = f32[1,16,1024]{2,1,0:T(8,128)S(1)} collective-permute-done((f32[1,16,1024]{2,1,0:T(8,128)}, f32[1,16,1024]{2,1,0:T(8,128)S(1)}, u32[]{:S(2)}, u32[]{:S(2)}) %collective-permute-start.6) | collective-permute-done | bytes 65568 | tf_op jit(solution)/shard_map/ppermute | solution.py:142
  30.7 0.3 fusion.13
  31.0 0.3 fusion.3
  31.6 0.1 reshape.273
  31.7 0.1 copy.46
  31.8 1.0 %collective-permute-done.7 = f32[2,16,1024]{2,1,0:T(8,128)S(1)} collective-permute-done((f32[2,16,1024]{2,1,0:T(8,128)S(1)}, f32[2,16,1024]{2,1,0:T(8,128)S(1)}, u32[]{:S(2)}, u32[]{:S(2)}) %collective-permute-start.7) | collective-permute-done | bytes 131104 | tf_op jit(solution)/shard_map/ppermute | solution.py:142
  32.8 1.8 %collective-permute-start.8 = (f32[16,1024]{1,0:T(8,128)S(1)}, f32[16,1024]{1,0:T(8,128)S(1)}, u32[]{:S(2)}, u32[]{:S(2)}) collective-permute-start(f32[16,1024]{1,0:T(8,128)S(1)} %slice_bitcast_fusion), channel_id=1, source_target_pairs={{0,2},{1,3},{2,0},{3,1},{4,6},{5,7},{6,4},{7,5},{8,10},{9,11},{10,... | collective-permute-start | bytes 196616 | tf_op jit(solution)/shard_map/ppermute | solution.py:142
  34.7 2.5 %collective-permute-done.8 = f32[16,1024]{1,0:T(8,128)S(1)} collective-permute-done((f32[16,1024]{1,0:T(8,128)S(1)}, f32[16,1024]{1,0:T(8,128)S(1)}, u32[]{:S(2)}, u32[]{:S(2)}) %collective-permute-start.8) | collective-permute-done | bytes 65568 | tf_op jit(solution)/shard_map/ppermute | solution.py:142
  37.2 0.6 %gather_fusion.1 = f32[32,16,128]{2,1,0:T(8,128)S(1)} fusion(f32[16,8,128]{2,0,1:T(8,128)S(1)} %copy_bitcast_fusion.1, s32[1024]{0:T(1024)S(1)} %pad_clamp_fusion), kind=kCustom, calls=%fused_computation.1 | custom fusion | bytes 524416 | tf_op jit(solution)/shard_map/jit(_take)/gather | solution.py:214
  37.8 1.0 %fusion.4 = f32[8,2,8,128]{3,2,1,0:T(8,128)S(1)} fusion(f32[8,128,4,128]{3,2,1,0:T(4,128)S(1)} %bitcast.71, f32[8,4,16,128]{3,2,1,0:T(8,128)S(1)} %bitcast.74, pred[8,4]{1,0:T(8,128)(4,1)S(1)} %copy.46), kind=kOutput, calls=%fused_computation.7 | convolution fusion | flops 50397184 | bytes 2424864 | tf_op jit(solution)/shard_map/xrkc,rikc->xri/dot_general | solution.py:215
  38.7 0.7 %copy.72 = f32[8,2,8,128]{3,2,0,1:T(8,128)} copy(f32[8,2,8,128]{3,2,1,0:T(8,128)S(1)} %fusion.4) | data formatting | bytes 131072 | tf_op jit(solution)/shard_map/reshape | solution.py:221
  (33 shorter events, 0.4 us)
Async XLA Ops:
  0.6 37.1 %copy-start = (f32[1024,4,128]{2,1,0:T(4,128)S(1)}, f32[1024,4,128]{2,1,0:T(4,128)}, u32[]{:S(2)}) copy-start(f32[1024,4,128]{2,1,0:T(4,128)} %param.26) | copy-start | bytes 6291460
  0.6 6.0 %copy-start.1 = (s32[2,4]{1,0:T(2,128)S(1)}, s32[2,4]{1,0:T(2,128)}, u32[]{:S(2)}) copy-start(s32[2,4]{1,0:T(2,128)} %param.25) | copy-start | bytes 100
  0.7 6.7 %copy-start.5 = (bf16[16,4,128]{2,1,0:T(4,128)(2,1)S(1)}, bf16[16,4,128]{2,1,0:T(4,128)(2,1)}, u32[]{:S(2)}) copy-start(bf16[16,4,128]{2,1,0:T(4,128)(2,1)} %param.24) | copy-start | bytes 49156
  5.3 6.4 %collective-permute-start.1 = (f32[2,16,1024]{2,1,0:T(8,128)}, f32[2,16,1024]{2,1,0:T(8,128)S(1)}, u32[]{:S(2)}, u32[]{:S(2)}) collective-permute-start(f32[2,16,1024]{2,1,0:T(8,128)} %get-tuple-element.11), channel_id=1, source_target_pairs={{1,0},{2,1},{3,2},{4,3},{5,4},{6,5},{7,6},{8,7},{9,8},{10,9},{11,1... | collective-permute-start | bytes 393224 | tf_op jit(solution)/shard_map/ppermute | solution.py:17
  6.6 24.8 %copy-start.6 = (s32[8,4]{0,1:T(4,128)S(1)}, s32[8,4]{0,1:T(4,128)}, u32[]{:S(2)}) copy-start(s32[8,4]{0,1:T(4,128)} %param.27) | copy-start | bytes 388
  7.5 3.1 %collective-permute-start.2 = (f32[16,256]{1,0:T(8,128)S(1)}, f32[16,256]{1,0:T(8,128)S(1)}, u32[]{:S(2)}, u32[]{:S(2)}) collective-permute-start(f32[16,256]{1,0:T(8,128)S(1)} %copy_bitcast_fusion.2), channel_id=1, source_target_pairs={{0,1},{1,0},{2,3},{3,2},{4,5},{5,4},{6,7},{7,6},{8,9},{9,8},{10,11... | collective-permute-start | bytes 49160 | tf_op jit(solution)/shard_map/ppermute | solution.py:142
  8.7 3.0 %collective-permute-start = (f32[16,1024]{1,0:T(8,128)}, f32[16,1024]{1,0:T(8,128)S(1)}, u32[]{:S(2)}, u32[]{:S(2)}) collective-permute-start(f32[16,1024]{1,0:T(8,128)} %get-tuple-element.10.last_ref), channel_id=1, source_target_pairs={{0,1},{1,2},{2,3},{3,4},{4,5},{5,6},{6,7},{7,8},{8,9},{9,10},{10,1... | collective-permute-start | bytes 196616 | tf_op jit(solution)/shard_map/ppermute | solution.py:17
  11.7 0.6 %copy-start.4 = (f32[16,1024]{1,0:T(8,128)}, f32[16,1024]{1,0:T(8,128)S(1)}, u32[]{:S(2)}) copy-start(f32[16,1024]{1,0:T(8,128)S(1)} %collective-permute-done.prev_ref) | copy-start | bytes 196612
  11.7 0.7 %copy-start.3 = (f32[2,16,1024]{2,1,0:T(8,128)}, f32[2,16,1024]{2,1,0:T(8,128)S(1)}, u32[]{:S(2)}) copy-start(f32[2,16,1024]{2,1,0:T(8,128)S(1)} %collective-permute-done.1.next_ref) | copy-start | bytes 393220
  14.1 16.9 %copy-start.2 = (f32[16,1024]{1,0:T(8,128)S(1)}, f32[16,1024]{1,0:T(8,128)}, u32[]{:S(2)}) copy-start(f32[16,1024]{1,0:T(8,128)} %shard_map.159) | copy-start | bytes 196612
  14.2 10.4 %collective-permute-start.3 = (f32[32,256]{0,1:T(8,128)S(1)}, f32[32,256]{0,1:T(8,128)S(1)}, u32[]{:S(2)}, u32[]{:S(2)}) collective-permute-start(f32[32,256]{0,1:T(8,128)S(1)} %copy.51), channel_id=1, source_target_pairs={{0,2},{1,3},{2,0},{3,1},{4,6},{5,7},{6,4},{7,5},{8,10},{9,11},{10,... | collective-permute-start | bytes 98312 | tf_op jit(solution)/shard_map/ppermute | solution.py:142
  20.2 4.6 %collective-permute-start.4 = (f32[1,16,1024]{2,1,0:T(8,128)}, f32[1,16,1024]{2,1,0:T(8,128)S(1)}, u32[]{:S(2)}, u32[]{:S(2)}) collective-permute-start(f32[1,16,1024]{2,1,0:T(8,128)} %bitcast.77), channel_id=1, source_target_pairs={{0,4},{1,5},{2,6},{3,7},{4,0},{5,1},{6,2},{7,3},{8,12},{9,13},{10,... | collective-permute-start | bytes 196616 | tf_op jit(solution)/shard_map/ppermute | solution.py:142
  21.8 7.1 %collective-permute-start.5 = (f32[1,16,1024]{2,1,0:T(8,128)}, f32[1,16,1024]{2,1,0:T(8,128)S(1)}, u32[]{:S(2)}, u32[]{:S(2)}) collective-permute-start(f32[1,16,1024]{2,1,0:T(8,128)} %bitcast.78), channel_id=1, source_target_pairs={{0,8},{1,9},{2,10},{3,11},{4,12},{5,13},{6,14},{7,15},{8,0},{9,1},... | collective-permute-start | bytes 196616 | tf_op jit(solution)/shard_map/ppermute | solution.py:142
  24.4 6.3 %collective-permute-start.6 = (f32[1,16,1024]{2,1,0:T(8,128)}, f32[1,16,1024]{2,1,0:T(8,128)S(1)}, u32[]{:S(2)}, u32[]{:S(2)}) collective-permute-start(f32[1,16,1024]{2,1,0:T(8,128)} %bitcast.79), channel_id=1, source_target_pairs={{0,12},{1,13},{2,14},{3,15},{4,8},{5,9},{6,10},{7,11},{8,4},{9,5},... | collective-permute-start | bytes 196616 | tf_op jit(solution)/shard_map/ppermute | solution.py:142
  31.4 1.4 %collective-permute-start.7 = (f32[2,16,1024]{2,1,0:T(8,128)S(1)}, f32[2,16,1024]{2,1,0:T(8,128)S(1)}, u32[]{:S(2)}, u32[]{:S(2)}) collective-permute-start(f32[2,16,1024]{2,1,0:T(8,128)S(1)} %slice.13), channel_id=1, source_target_pairs={{0,1},{1,0},{2,3},{3,2},{4,5},{5,4},{6,7},{7,6},{8,9},{9,8},{10,11... | collective-permute-start | bytes 393224 | tf_op jit(solution)/shard_map/ppermute | solution.py:142
  32.8 4.3 %collective-permute-start.8 = (f32[16,1024]{1,0:T(8,128)S(1)}, f32[16,1024]{1,0:T(8,128)S(1)}, u32[]{:S(2)}, u32[]{:S(2)}) collective-permute-start(f32[16,1024]{1,0:T(8,128)S(1)} %slice_bitcast_fusion), channel_id=1, source_target_pairs={{0,2},{1,3},{2,0},{3,1},{4,6},{5,7},{6,4},{7,5},{8,10},{9,11},{10,... | collective-permute-start | bytes 196616 | tf_op jit(solution)/shard_map/ppermute | solution.py:142

commit v16 on v15

--- a/solution.py
+++ b/solution.py
@@ -24,7 +24,9 @@
     return lower, upper
 
 
-def stencil_kernel(w_ref, s_ref, sprev_ref, f_ref, vx_ref, vy_ref, vz_ref, d_ref, out_ref, to_prev_ref, last_ref, up_ref):
+def stencil_kernel(
+    w_ref, s_ref, sprev_ref, f_ref, vx_ref, vy_ref, vz_ref, d_ref, planes_ref, out_ref, to_prev_ref, last_ref, up_ref
+):
     c = pl.program_id(0)
     rows, cols = out_ref.shape
     sub = lax.broadcasted_iota(jnp.int32, (rows, cols), 0)
@@ -33,6 +35,8 @@
     @pl.when(c == 0)
     def _():
         out_ref[...] = jnp.zeros_like(out_ref)
+        to_prev_ref[2:] = planes_ref[...]
+        last_ref[1:] = planes_ref[...]
 
     prev = jnp.where(c > 0, sprev_ref[0], 0.0)
     acc = jnp.zeros((rows, cols), jnp.float32)
@@ -44,7 +48,7 @@
         lo_x, up_x = coefs(f, 1, vx_ref[j], d)
         to_prev_ref[0, pl.ds(z, 1), :] = s[0:1, :]
         to_prev_ref[1, pl.ds(z, 1), :] = lo_x[0:1, :]
-        last_ref[pl.ds(z, 1), :] = s[rows - 1:rows, :]
+        last_ref[0, pl.ds(z, 1), :] = s[rows - 1:rows, :]
         up_ref[pl.ds(z, 1), :] = up_x[0:1, :]
         lo_y, up_y = coefs(f, 2, vy_ref[j], d)
         lo_z, up_z = coefs(f, 4, vz_ref[j], d)
@@ -67,8 +71,9 @@
     out_ref[...] += acc
 
 
-def stencil(layer_weight, s, f, vx, vy, vz, d):
+def stencil(layer_weight, s, f, vx, vy, vz, d, planes):
     depth, rows, cols = s.shape
+    extra = planes.shape[0]
     zc = Z_CHUNK if depth % Z_CHUNK == 0 else depth
     block = pl.BlockSpec((zc, rows, cols), lambda c: (c, 0, 0))
     prev_block = pl.BlockSpec((1, rows, cols), lambda c: (jnp.maximum(c * zc - 1, 0), 0, 0))
@@ -84,21 +89,22 @@
             block,
             block,
             block,
+            pl.BlockSpec(planes.shape, lambda c: (0, 0, 0)),
         ],
         out_specs=[
             pl.BlockSpec((rows, cols), lambda c: (0, 0)),
-            pl.BlockSpec((2, depth, cols), lambda c: (0, 0, 0)),
-            pl.BlockSpec((depth, cols), lambda c: (0, 0)),
+            pl.BlockSpec((2 + extra, depth, cols), lambda c: (0, 0, 0)),
+            pl.BlockSpec((1 + extra, depth, cols), lambda c: (0, 0, 0)),
             pl.BlockSpec((depth, cols), lambda c: (0, 0)),
         ],
         out_shape=[
             jax.ShapeDtypeStruct((rows, cols), jnp.float32),
-            jax.ShapeDtypeStruct((2, depth, cols), jnp.float32),
-            jax.ShapeDtypeStruct((depth, cols), jnp.float32),
+            jax.ShapeDtypeStruct((2 + extra, depth, cols), jnp.float32),
+            jax.ShapeDtypeStruct((1 + extra, depth, cols), jnp.float32),
             jax.ShapeDtypeStruct((depth, cols), jnp.float32),
         ],
         compiler_params=pltpu.CompilerParams(dimension_semantics=("arbitrary",)),
-    )(layer_weight, s, s, f, vx, vy, vz, d)
+    )(layer_weight, s, s, f, vx, vy, vz, d, planes)
 
 
 def fix_kernel(w_ref, partial_ref, up_ref, prev_ref, next_ref, last_ref, out_ref):
@@ -108,8 +114,8 @@
     corr_last = jnp.zeros((1, cols), jnp.float32)
     for z in range(depth):
         w = w_ref[z]
-        corr_first = corr_first - w * (up_ref[pl.ds(z, 1), :] * prev_ref[pl.ds(z, 1), :])
-        jump = next_ref[0, pl.ds(z, 1), :] - last_ref[pl.ds(z, 1), :]
+        corr_first = corr_first - w * (up_ref[pl.ds(z, 1), :] * prev_ref[0, pl.ds(z, 1), :])
+        jump = next_ref[0, pl.ds(z, 1), :] - last_ref[0, pl.ds(z, 1), :]
         corr_last = corr_last - w * (next_ref[1, pl.ds(z, 1), :] * jump)
     row = lax.broadcasted_iota(jnp.int32, (rows, cols), 0)
     out_ref[...] = (
@@ -195,16 +201,24 @@
     me = lax.axis_index("gx")
     depth, rows, cols = adjoint_state.shape
 
-    partial, to_prev, last_s, up_x0 = stencil(
-        layer_weight, adjoint_state, face_flags, speed_x, speed_y, speed_z, dispersion
+    own_slab = cx_slab(cov_x, offsets_x, me, rows)
+    flat = own_slab.reshape(-1)
+    plane = depth * cols
+    extra = -(-flat.shape[0] // plane)
+    planes = jnp.pad(flat, (0, extra * plane - flat.shape[0])).reshape(extra, depth, cols)
+    partial, to_prev, last_ext, up_x0 = stencil(
+        layer_weight, adjoint_state, face_flags, speed_x, speed_y, speed_z, dispersion, planes
     )
     from_next = passed_along(to_prev, "gx", -1)
-    from_prev = passed_along(last_s, "gx", 1)
-
-    recharge = corrected(layer_weight, partial, up_x0, from_prev, from_next, last_s)
-
-    own_slab = cx_slab(cov_x, offsets_x, me, rows)
-    pair_slab = jnp.concatenate([own_slab, swap(own_slab, "gx", 1)], axis=0)
+    from_prev = passed_along(last_ext, "gx", 1)
+
+    recharge = corrected(layer_weight, partial, up_x0, from_prev, from_next, last_ext)
+
+    size = own_slab.size
+    from_up = from_next[2:].reshape(-1)[:size].reshape(own_slab.shape)
+    from_down = from_prev[1:].reshape(-1)[:size].reshape(own_slab.shape)
+    partner_slab = jnp.where(me % 2 == 0, from_up, from_down)
+    pair_slab = jnp.concatenate([own_slab, partner_slab], axis=0)
     late_pair, _ = lax.optimization_barrier((pair_slab, recharge))
     slab = jnp.concatenate([pair_slab, swap(late_pair, "gx", 2)], axis=0)
     mixed = mixed_rows(recharge, slab, "gx")

time: 39.6 us -> 43.5 us (1.098)
  waiting for transfers between devices: 9.88 us -> 13.5 us
  starting transfers between devices: 16.5 us -> 14 us
  local copies, waits for them, and re-layouts: 3.16 us -> 5.44 us
    ppermute x2, waiting for transfers between devices: 1.07 us -> 4.31 us  [passed_along(): lax.ppermute(value, axis, [(source, source + steps) for source in range(f...]
    ppermute x7 -> x6, starting transfers between devices: 13.3 us -> 10.4 us  [swap(): return lax.ppermute(value, axis, [(i, i ^ mask) for i in range(count)])]
    gather x1, local copies, waits for them, and re-layouts: 0.56 us -> 1.38 us  [cx_slab(): target = (row_block[:, None] + offsets[row_block]) % nxb]
    convert_element_type x1, local copies, waits for them, and re-layouts: 0.01 us -> 0.72 us  [cx_slab(): cov_rows.astype(jnp.float32)[:, :, None, :]]
    reshape x0 -> x1, local copies, waits for them, and re-layouts: none -> 0.65 us  [body(): jnp.pad(flat, (0, extra * plane - flat.shape[0]))]
    ppermute x2, starting transfers between devices: 3.21 us -> 3.66 us  [passed_along(): lax.ppermute(value, axis, [(source, source + steps) for source in range(f...]
    ppermute x7 -> x6, waiting for transfers between devices: 8.81 us -> 9.23 us  [swap(): return lax.ppermute(value, axis, [(i, i ^ mask) for i in range(count)])]
  transfers between devices with their start and end apart: 9 -> 8, of which waited for: 5 -> 5; matrix products, arithmetic and copies ran while one was open for 5% -> 3% of each run, Pallas kernels for 0% -> 0%
where the time goes in v16:
time: 43.5 us; the launch traced here: 43.2 us
  starting transfers between devices  14 us (32%)
  waiting for transfers between devices  13.5 us (31%)
  Pallas kernels  6.63 us (15%)
  local copies, waits for them, and re-layouts  5.44 us (13%)
  matrix products  2.24 us (5%)
  between operations  0.92 us (2%)
    ppermute x6, starting transfers between devices, swap(): return lax.ppermute(value, axis, [(i, i ^ mask) for i in range(count)])  10.4 us
    ppermute x6, waiting for transfers between devices, swap(): return lax.ppermute(value, axis, [(i, i ^ mask) for i in range(count)])  9.23 us
    pallas_call x1, Pallas kernels, stencil(): pl.pallas_call(stencil_kernel, grid=(depth // zc,), in_specs=[pl.BlockSpe...  4.79 us
    ppermute x2, waiting for transfers between devices, passed_along(): lax.ppermute(value, axis, [(source, source + steps) for source in range(f...  4.31 us
    ppermute x2, starting transfers between devices, passed_along(): lax.ppermute(value, axis, [(source, source + steps) for source in range(f...  3.66 us
    pallas_call x1, Pallas kernels, corrected(): pl.pallas_call(fix_kernel, in_specs=[pl.BlockSpec(memory_space=pltpu.SMEM...  1.84 us
    gather x1, local copies, waits for them, and re-layouts, cx_slab(): target = (row_block[:, None] + offsets[row_block]) % nxb  1.38 us
    dot_general x4, matrix products, product(): jnp.dot(cols, piece.reshape(-1, piece.shape[-1]), precision=precise, pref...  1.28 us
  transfers between devices with their start and end apart: 8, of which 5 were waited for; matrix products, arithmetic and copies ran while one was open for 3% of the time, Pallas kernels for 0%

profile of v16, /device:TPU:0, one launch (start us, length us, event | category | flops | bytes accessed | tf_op | source)
XLA Modules:
  0.0 43.2 jit_solution(5143861585798641781)
XLA Ops:
  0.7 1.4 %gather_fusion = s32[16,4]{1,0:T(8,128)S(1)} fusion(s32[2,4]{1,0:T(2,128)} %param.25, s32[1024]{0:T(1024)S(1)} %pad_clamp_fusion.1), kind=kCustom, calls=%fused_computation | custom fusion | bytes 576 | tf_op jit(solution)/shard_map/gather | solution.py:155
  2.3 0.7 %copy.54 = f32[16,4,128]{2,0,1:T(8,128)S(1)} copy(bf16[16,4,128]{2,1,0:T(4,128)(2,1)} %param.24) | data formatting | bytes 49152 | tf_op jit(solution)/shard_map/convert_element_type | solution.py:158
  3.1 0.6 %reshape.177.planes_ref = f32[1,16,1024]{2,1,0:T(8,128)} reshape(f32[16384]{0:T(1024)S(1)} %pad.4) | data formatting | bytes 131072 | tf_op jit(solution)/shard_map/reshape | solution.py:208
  3.8 4.8 %shard_map.158 = (f32[16,1024]{1,0:T(8,128)}, f32[3,16,1024]{2,1,0:T(8,128)}, f32[2,16,1024]{2,1,0:T(8,128)}, f32[16,1024]{1,0:T(8,128)}) custom-call(f32[16]{0:T(128)} %w_ref.3, f32[16,16,1024]{2,1,0:T(8,128)} %sprev_ref.1, f32[16,16,1024]{2,1,0:T(8,128)} %sprev_ref.1, s32[16,16,1024]{2,1,0:T(8,128)} %f_ref.1, f32[16,16,1024]{2,1,0:T(8,128)} %vx_ref.1, ...), custom_call_target="tpu_custom_call" | custom-call | tf_op jit(solution)/shard_map/pallas_call | solution.py:80
  8.6 2.4 %collective-permute-start = (f32[2,16,1024]{2,1,0:T(8,128)}, f32[2,16,1024]{2,1,0:T(8,128)S(1)}, u32[]{:S(2)}, u32[]{:S(2)}) collective-permute-start(f32[2,16,1024]{2,1,0:T(8,128)} %get-tuple-element.10.last_ref), channel_id=1, source_target_pairs={{0,1},{1,2},{2,3},{3,4},{4,5},{5,6},{6,7},{7,8},{8,9},{9,10},{10,1... | collective-permute-start | bytes 393224 | tf_op jit(solution)/shard_map/ppermute | solution.py:17
  10.9 1.3 %collective-permute-start.1 = (f32[3,16,1024]{2,1,0:T(8,128)}, f32[3,16,1024]{2,1,0:T(8,128)S(1)}, u32[]{:S(2)}, u32[]{:S(2)}) collective-permute-start(f32[3,16,1024]{2,1,0:T(8,128)} %get-tuple-element.11), channel_id=1, source_target_pairs={{1,0},{2,1},{3,2},{4,3},{5,4},{6,5},{7,6},{8,7},{9,8},{10,9},{11,1... | collective-permute-start | bytes 589832 | tf_op jit(solution)/shard_map/ppermute | solution.py:17
  12.3 4.3 %collective-permute-done.1.next_ref = f32[3,16,1024]{2,1,0:T(8,128)S(1)} collective-permute-done((f32[3,16,1024]{2,1,0:T(8,128)}, f32[3,16,1024]{2,1,0:T(8,128)S(1)}, u32[]{:S(2)}, u32[]{:S(2)}) %collective-permute-start.1) | collective-permute-done | bytes 196640 | tf_op jit(solution)/shard_map/ppermute | solution.py:17
  16.6 0.6 %copy-done.2 = f32[3,16,1024]{2,1,0:T(8,128)} copy-done((f32[3,16,1024]{2,1,0:T(8,128)}, f32[3,16,1024]{2,1,0:T(8,128)S(1)}, u32[]{:S(2)}) %copy-start.2) | copy-done | bytes 196632
  17.3 1.8 %shard_map.159 = f32[16,1024]{1,0:T(8,128)} custom-call(f32[16]{0:T(128)} %w_ref.3, f32[16,1024]{1,0:T(8,128)} %get-tuple-element.8.partial_ref, f32[16,1024]{1,0:T(8,128)} %get-tuple-element.9.up_ref, f32[2,16,1024]{2,1,0:T(8,128)} %copy-done.3, f32[3,16,1024]{2,1,0:T(8,128)} %copy-done.2, f32[2,16,1024]{2,1,0:T(8,128)} %get-tuple-element.10.last_ref), custom_call_target="tpu_custom_call" | custom-call | tf_op jit(solution)/shard_map/pallas_call | solution.py:128
  19.1 0.1 copy.59
  19.2 4.0 %collective-permute-start.2 = (f32[32,256]{0,1:T(8,128)S(1)}, f32[32,256]{0,1:T(8,128)S(1)}, u32[]{:S(2)}, u32[]{:S(2)}) collective-permute-start(f32[32,256]{0,1:T(8,128)S(1)} %copy.59), channel_id=1, source_target_pairs={{0,2},{1,3},{2,0},{3,1},{4,6},{5,7},{6,4},{7,5},{8,10},{9,11},{10,... | collective-permute-start | bytes 98312 | tf_op jit(solution)/shard_map/ppermute | solution.py:148
  23.2 0.1 copy.67
  23.4 0.1 select_n.103
  23.5 1.6 %collective-permute-start.3 = (f32[1,16,1024]{2,1,0:T(8,128)}, f32[1,16,1024]{2,1,0:T(8,128)S(1)}, u32[]{:S(2)}, u32[]{:S(2)}) collective-permute-start(f32[1,16,1024]{2,1,0:T(8,128)} %bitcast.76), channel_id=1, source_target_pairs={{0,4},{1,5},{2,6},{3,7},{4,0},{5,1},{6,2},{7,3},{8,12},{9,13},{10,... | collective-permute-start | bytes 196616 | tf_op jit(solution)/shard_map/ppermute | solution.py:148
  25.1 2.6 %collective-permute-start.4 = (f32[1,16,1024]{2,1,0:T(8,128)}, f32[1,16,1024]{2,1,0:T(8,128)S(1)}, u32[]{:S(2)}, u32[]{:S(2)}) collective-permute-start(f32[1,16,1024]{2,1,0:T(8,128)} %bitcast.77), channel_id=1, source_target_pairs={{0,8},{1,9},{2,10},{3,11},{4,12},{5,13},{6,14},{7,15},{8,0},{9,1},... | collective-permute-start | bytes 196616 | tf_op jit(solution)/shard_map/ppermute | solution.py:148
  27.7 0.2 collective-permute-start.5
  27.9 0.1 copy.61
  28.1 0.1 pad_maximum_fusion
  28.2 0.3 fusion.17
  28.5 3.0 %collective-permute-done.4 = f32[1,16,1024]{2,1,0:T(8,128)S(1)} collective-permute-done((f32[1,16,1024]{2,1,0:T(8,128)}, f32[1,16,1024]{2,1,0:T(8,128)S(1)}, u32[]{:S(2)}, u32[]{:S(2)}) %collective-permute-start.4) | collective-permute-done | bytes 65568 | tf_op jit(solution)/shard_map/ppermute | solution.py:148
  31.5 0.3 fusion.15
  31.8 2.5 %collective-permute-done.5 = f32[1,16,1024]{2,1,0:T(8,128)S(1)} collective-permute-done((f32[1,16,1024]{2,1,0:T(8,128)}, f32[1,16,1024]{2,1,0:T(8,128)S(1)}, u32[]{:S(2)}, u32[]{:S(2)}) %collective-permute-start.5) | collective-permute-done | bytes 65568 | tf_op jit(solution)/shard_map/ppermute | solution.py:148
  34.4 0.3 fusion.13
  34.7 0.3 fusion.3
  35.1 0.5 %collective-permute-start.6 = (f32[2,16,1024]{2,1,0:T(8,128)S(1)}, f32[2,16,1024]{2,1,0:T(8,128)S(1)}, u32[]{:S(2)}, u32[]{:S(2)}) collective-permute-start(f32[2,16,1024]{2,1,0:T(8,128)S(1)} %slice.27), channel_id=1, source_target_pairs={{0,1},{1,0},{2,3},{3,2},{4,5},{5,4},{6,7},{7,6},{8,9},{9,8},{10,11... | collective-permute-start | bytes 393224 | tf_op jit(solution)/shard_map/ppermute | solution.py:148
  35.7 0.1 copy.56
  35.8 0.7 %collective-permute-done.6 = f32[2,16,1024]{2,1,0:T(8,128)S(1)} collective-permute-done((f32[2,16,1024]{2,1,0:T(8,128)S(1)}, f32[2,16,1024]{2,1,0:T(8,128)S(1)}, u32[]{:S(2)}, u32[]{:S(2)}) %collective-permute-start.6) | collective-permute-done | bytes 131104 | tf_op jit(solution)/shard_map/ppermute | solution.py:148
  36.5 1.4 %collective-permute-start.7 = (f32[16,1024]{1,0:T(8,128)S(1)}, f32[16,1024]{1,0:T(8,128)S(1)}, u32[]{:S(2)}, u32[]{:S(2)}) collective-permute-start(f32[16,1024]{1,0:T(8,128)S(1)} %slice_bitcast_fusion), channel_id=1, source_target_pairs={{0,2},{1,3},{2,0},{3,1},{4,6},{5,7},{6,4},{7,5},{8,10},{9,11},{10,... | collective-permute-start | bytes 196616 | tf_op jit(solution)/shard_map/ppermute | solution.py:148
  38.0 3.0 %collective-permute-done.7 = f32[16,1024]{1,0:T(8,128)S(1)} collective-permute-done((f32[16,1024]{1,0:T(8,128)S(1)}, f32[16,1024]{1,0:T(8,128)S(1)}, u32[]{:S(2)}, u32[]{:S(2)}) %collective-permute-start.7) | collective-permute-done | bytes 65568 | tf_op jit(solution)/shard_map/ppermute | solution.py:148
  41.0 0.6 %gather_fusion.1 = f32[32,16,128]{2,1,0:T(8,128)S(1)} fusion(f32[16,8,128]{2,0,1:T(8,128)S(1)} %copy_bitcast_fusion.1, s32[1024]{0:T(1024)S(1)} %pad_clamp_fusion), kind=kCustom, calls=%fused_computation.1 | custom fusion | bytes 524416 | tf_op jit(solution)/shard_map/jit(_take)/gather | solution.py:228
  41.6 1.0 %fusion.4 = f32[8,2,8,128]{3,2,1,0:T(8,128)S(1)} fusion(f32[8,128,4,128]{3,2,1,0:T(4,128)S(1)} %bitcast.71, f32[8,4,16,128]{3,2,1,0:T(8,128)S(1)} %bitcast.74, pred[8,4]{1,0:T(8,128)(4,1)S(1)} %copy.56), kind=kOutput, calls=%fused_computation.7 | convolution fusion | flops 50397184 | bytes 2424864 | tf_op jit(solution)/shard_map/xrkc,rikc->xri/dot_general | solution.py:229
  42.5 0.7 %copy.79 = f32[8,2,8,128]{3,2,0,1:T(8,128)} copy(f32[8,2,8,128]{3,2,1,0:T(8,128)S(1)} %fusion.4) | data formatting | bytes 131072 | tf_op jit(solution)/shard_map/reshape | solution.py:235
  (33 shorter events, 0.6 us)
Async XLA Ops:
  0.6 41.0 %copy-start = (f32[1024,4,128]{2,1,0:T(4,128)S(1)}, f32[1024,4,128]{2,1,0:T(4,128)}, u32[]{:S(2)}) copy-start(f32[1024,4,128]{2,1,0:T(4,128)} %param.26) | copy-start | bytes 6291460
  8.6 3.7 %collective-permute-start = (f32[2,16,1024]{2,1,0:T(8,128)}, f32[2,16,1024]{2,1,0:T(8,128)S(1)}, u32[]{:S(2)}, u32[]{:S(2)}) collective-permute-start(f32[2,16,1024]{2,1,0:T(8,128)} %get-tuple-element.10.last_ref), channel_id=1, source_target_pairs={{0,1},{1,2},{2,3},{3,4},{4,5},{5,6},{6,7},{7,8},{8,9},{9,10},{10,1... | collective-permute-start | bytes 393224 | tf_op jit(solution)/shard_map/ppermute | solution.py:17
  10.9 5.6 %collective-permute-start.1 = (f32[3,16,1024]{2,1,0:T(8,128)}, f32[3,16,1024]{2,1,0:T(8,128)S(1)}, u32[]{:S(2)}, u32[]{:S(2)}) collective-permute-start(f32[3,16,1024]{2,1,0:T(8,128)} %get-tuple-element.11), channel_id=1, source_target_pairs={{1,0},{2,1},{3,2},{4,3},{5,4},{6,5},{7,6},{8,7},{9,8},{10,9},{11,1... | collective-permute-start | bytes 589832 | tf_op jit(solution)/shard_map/ppermute | solution.py:17
  12.3 4.4 %copy-start.3 = (f32[2,16,1024]{2,1,0:T(8,128)}, f32[2,16,1024]{2,1,0:T(8,128)S(1)}, u32[]{:S(2)}) copy-start(f32[2,16,1024]{2,1,0:T(8,128)S(1)} %collective-permute-done.prev_ref) | copy-start | bytes 393220
  16.6 0.7 %copy-start.2 = (f32[3,16,1024]{2,1,0:T(8,128)}, f32[3,16,1024]{2,1,0:T(8,128)S(1)}, u32[]{:S(2)}) copy-start(f32[3,16,1024]{2,1,0:T(8,128)S(1)} %collective-permute-done.1.next_ref) | copy-start | bytes 589828
  17.3 18.3 %copy-start.4 = (s32[8,4]{0,1:T(4,128)S(1)}, s32[8,4]{0,1:T(4,128)}, u32[]{:S(2)}) copy-start(s32[8,4]{0,1:T(4,128)} %param.27) | copy-start | bytes 388
  19.1 15.6 %copy-start.1 = (f32[16,1024]{1,0:T(8,128)S(1)}, f32[16,1024]{1,0:T(8,128)}, u32[]{:S(2)}) copy-start(f32[16,1024]{1,0:T(8,128)} %shard_map.159) | copy-start | bytes 196612
  19.2 8.9 %collective-permute-start.2 = (f32[32,256]{0,1:T(8,128)S(1)}, f32[32,256]{0,1:T(8,128)S(1)}, u32[]{:S(2)}, u32[]{:S(2)}) collective-permute-start(f32[32,256]{0,1:T(8,128)S(1)} %copy.59), channel_id=1, source_target_pairs={{0,2},{1,3},{2,0},{3,1},{4,6},{5,7},{6,4},{7,5},{8,10},{9,11},{10,... | collective-permute-start | bytes 98312 | tf_op jit(solution)/shard_map/ppermute | solution.py:148
  23.5 4.7 %collective-permute-start.3 = (f32[1,16,1024]{2,1,0:T(8,128)}, f32[1,16,1024]{2,1,0:T(8,128)S(1)}, u32[]{:S(2)}, u32[]{:S(2)}) collective-permute-start(f32[1,16,1024]{2,1,0:T(8,128)} %bitcast.76), channel_id=1, source_target_pairs={{0,4},{1,5},{2,6},{3,7},{4,0},{5,1},{6,2},{7,3},{8,12},{9,13},{10,... | collective-permute-start | bytes 196616 | tf_op jit(solution)/shard_map/ppermute | solution.py:148
  25.1 6.4 %collective-permute-start.4 = (f32[1,16,1024]{2,1,0:T(8,128)}, f32[1,16,1024]{2,1,0:T(8,128)S(1)}, u32[]{:S(2)}, u32[]{:S(2)}) collective-permute-start(f32[1,16,1024]{2,1,0:T(8,128)} %bitcast.77), channel_id=1, source_target_pairs={{0,8},{1,9},{2,10},{3,11},{4,12},{5,13},{6,14},{7,15},{8,0},{9,1},... | collective-permute-start | bytes 196616 | tf_op jit(solution)/shard_map/ppermute | solution.py:148
  27.7 6.7 %collective-permute-start.5 = (f32[1,16,1024]{2,1,0:T(8,128)}, f32[1,16,1024]{2,1,0:T(8,128)S(1)}, u32[]{:S(2)}, u32[]{:S(2)}) collective-permute-start(f32[1,16,1024]{2,1,0:T(8,128)} %bitcast.78), channel_id=1, source_target_pairs={{0,12},{1,13},{2,14},{3,15},{4,8},{5,9},{6,10},{7,11},{8,4},{9,5},... | collective-permute-start | bytes 196616 | tf_op jit(solution)/shard_map/ppermute | solution.py:148
  35.1 1.4 %collective-permute-start.6 = (f32[2,16,1024]{2,1,0:T(8,128)S(1)}, f32[2,16,1024]{2,1,0:T(8,128)S(1)}, u32[]{:S(2)}, u32[]{:S(2)}) collective-permute-start(f32[2,16,1024]{2,1,0:T(8,128)S(1)} %slice.27), channel_id=1, source_target_pairs={{0,1},{1,0},{2,3},{3,2},{4,5},{5,4},{6,7},{7,6},{8,9},{9,8},{10,11... | collective-permute-start | bytes 393224 | tf_op jit(solution)/shard_map/ppermute | solution.py:148
  36.5 4.4 %collective-permute-start.7 = (f32[16,1024]{1,0:T(8,128)S(1)}, f32[16,1024]{1,0:T(8,128)S(1)}, u32[]{:S(2)}, u32[]{:S(2)}) collective-permute-start(f32[16,1024]{1,0:T(8,128)S(1)} %slice_bitcast_fusion), channel_id=1, source_target_pairs={{0,2},{1,3},{2,0},{3,1},{4,6},{5,7},{6,4},{7,5},{8,10},{9,11},{10,... | collective-permute-start | bytes 196616 | tf_op jit(solution)/shard_map/ppermute | solution.py:148

commit v17 on v15

--- a/solution.py
+++ b/solution.py
@@ -211,7 +211,10 @@
 
     nyb = offsets_y.shape[0]
     col_block = (jnp.arange(nyb)[:, None] + offsets_y) % nyb
-    picked = jnp.take(mixed.reshape(rows, nyb, BLK), col_block, axis=1)
+    blocks_y = mixed.reshape(rows, nyb, BLK)
+    fixed = [blocks_y, jnp.roll(blocks_y, 1, axis=1), jnp.roll(blocks_y, -(nyb // 2), axis=1)]
+    rest = jnp.take(blocks_y, col_block[:, 3:], axis=1)
+    picked = jnp.concatenate([jnp.stack(fixed, axis=2), rest], axis=2)
     prior = jnp.einsum(
         "xrkc,rikc->xri",
         picked,

time: 39.6 us -> 39.4 us (level)
  waiting for transfers between devices: 9.88 us -> 10.4 us
  starting transfers between devices: 16.5 us -> 16 us
    ppermute x7, waiting for transfers between devices: 8.81 us -> 10.4 us  [swap(): return lax.ppermute(value, axis, [(i, i ^ mask) for i in range(count)])]
    ppermute x2, waiting for transfers between devices: 1.07 us -> 0.01 us  [passed_along(): lax.ppermute(value, axis, [(source, source + steps) for source in range(f...]
    ppermute x7, starting transfers between devices: 13.3 us -> 12.3 us  [swap(): return lax.ppermute(value, axis, [(i, i ^ mask) for i in range(count)])]
    ppermute x2, starting transfers between devices: 3.21 us -> 3.65 us  [passed_along(): lax.ppermute(value, axis, [(source, source + steps) for source in range(f...]
where the time goes in v17:
time: 39.4 us; the launch traced here: 39.2 us
  starting transfers between devices  16 us (41%)
  waiting for transfers between devices  10.4 us (26%)
  Pallas kernels  6.29 us (16%)
  local copies, waits for them, and re-layouts  2.91 us (7%)
  matrix products  2.2 us (6%)
  between operations  0.95 us (2%)
  other arithmetic  0.49 us (1%)
    ppermute x7, starting transfers between devices, swap(): return lax.ppermute(value, axis, [(i, i ^ mask) for i in range(count)])  12.3 us
    ppermute x7, waiting for transfers between devices, swap(): return lax.ppermute(value, axis, [(i, i ^ mask) for i in range(count)])  10.4 us
    pallas_call x1, Pallas kernels, stencil(): pl.pallas_call(stencil_kernel, grid=(depth // zc,), in_specs=[pl.BlockSpe...  4.6 us
    ppermute x2, starting transfers between devices, passed_along(): lax.ppermute(value, axis, [(source, source + steps) for source in range(f...  3.65 us
    pallas_call x1, Pallas kernels, corrected(): pl.pallas_call(fix_kernel, in_specs=[pl.BlockSpec(memory_space=pltpu.SMEM...  1.69 us
    dot_general x4, matrix products, product(): jnp.dot(cols, piece.reshape(-1, piece.shape[-1]), precision=precise, pref...  1.28 us
    dot_general x1, matrix products, body(): jnp.einsum('xrkc,rikc->xri', picked, cov_y.reshape(nyb, BLK, cov_y.shape[...  0.92 us
  transfers between devices with their start and end apart: 9, of which 5 were waited for; matrix products, arithmetic and copies ran while one was open for 5% of the time, Pallas kernels for 0%

profile of v17, /device:TPU:0, one launch (start us, length us, event | category | flops | bytes accessed | tf_op | source)
XLA Modules:
  0.0 39.2 jit_solution(13441093379923687387)
XLA Ops:
  0.7 4.6 %shard_map.158 = (f32[16,1024]{1,0:T(8,128)}, f32[2,16,1024]{2,1,0:T(8,128)}, f32[16,1024]{1,0:T(8,128)}, f32[16,1024]{1,0:T(8,128)}) custom-call(f32[16]{0:T(128)} %w_ref.3, f32[16,16,1024]{2,1,0:T(8,128)} %sprev_ref.1, f32[16,16,1024]{2,1,0:T(8,128)} %sprev_ref.1, s32[16,16,1024]{2,1,0:T(8,128)} %f_ref.1, f32[16,16,1024]{2,1,0:T(8,128)} %vx_ref.1, ...), custom_call_target="tpu_custom_call" | custom-call | tf_op jit(solution)/shard_map/pallas_call | solution.py:75
  5.3 2.4 %collective-permute-start = (f32[16,1024]{1,0:T(8,128)}, f32[16,1024]{1,0:T(8,128)S(1)}, u32[]{:S(2)}, u32[]{:S(2)}) collective-permute-start(f32[16,1024]{1,0:T(8,128)} %get-tuple-element.10.last_ref), channel_id=1, source_target_pairs={{0,1},{1,2},{2,3},{3,4},{4,5},{5,6},{6,7},{7,8},{8,9},{9,10},{10,1... | collective-permute-start | bytes 196616 | tf_op jit(solution)/shard_map/ppermute | solution.py:17
  7.6 1.3 %collective-permute-start.1 = (f32[2,16,1024]{2,1,0:T(8,128)}, f32[2,16,1024]{2,1,0:T(8,128)S(1)}, u32[]{:S(2)}, u32[]{:S(2)}) collective-permute-start(f32[2,16,1024]{2,1,0:T(8,128)} %get-tuple-element.11), channel_id=1, source_target_pairs={{1,0},{2,1},{3,2},{4,3},{5,4},{6,5},{7,6},{8,7},{9,8},{10,9},{11,1... | collective-permute-start | bytes 393224 | tf_op jit(solution)/shard_map/ppermute | solution.py:17
  9.0 0.6 %gather_fusion = s32[16,4]{1,0:T(8,128)S(1)} fusion(s32[2,4]{1,0:T(2,128)S(1)} %copy-done.1, s32[1024]{0:T(1024)S(1)} %pad_clamp_fusion.1), kind=kCustom, calls=%fused_computation | custom fusion | bytes 576 | tf_op jit(solution)/shard_map/gather | solution.py:149
  9.6 0.1 add_select_fusion
  9.7 0.1 copy.57
  9.8 0.1 select_reduce_fusion
  9.9 3.3 %collective-permute-start.2 = (f32[16,256]{1,0:T(8,128)S(1)}, f32[16,256]{1,0:T(8,128)S(1)}, u32[]{:S(2)}, u32[]{:S(2)}) collective-permute-start(f32[16,256]{1,0:T(8,128)S(1)} %copy_bitcast_fusion.2), channel_id=1, source_target_pairs={{0,1},{1,0},{2,3},{3,2},{4,5},{5,4},{6,7},{7,6},{8,9},{9,8},{10,11... | collective-permute-start | bytes 49160 | tf_op jit(solution)/shard_map/ppermute | solution.py:142
  13.2 0.8 %collective-permute-done.2 = f32[16,256]{1,0:T(8,128)S(1)} collective-permute-done((f32[16,256]{1,0:T(8,128)S(1)}, f32[16,256]{1,0:T(8,128)S(1)}, u32[]{:S(2)}, u32[]{:S(2)}) %collective-permute-start.2) | collective-permute-done | bytes 16416 | tf_op jit(solution)/shard_map/ppermute | solution.py:142
  14.0 0.6 %copy-done.4 = f32[16,1024]{1,0:T(8,128)} copy-done((f32[16,1024]{1,0:T(8,128)}, f32[16,1024]{1,0:T(8,128)S(1)}, u32[]{:S(2)}) %copy-start.4) | copy-done | bytes 65560
  14.7 1.7 %shard_map.159 = f32[16,1024]{1,0:T(8,128)} custom-call(f32[16]{0:T(128)} %w_ref.3, f32[16,1024]{1,0:T(8,128)} %get-tuple-element.8.partial_ref, f32[16,1024]{1,0:T(8,128)} %get-tuple-element.9.up_ref, f32[16,1024]{1,0:T(8,128)} %copy-done.4, f32[2,16,1024]{2,1,0:T(8,128)} %copy-done.3, f32[16,1024]{1,0:T(8,128)} %get-tuple-element.10.last_ref), custom_call_target="tpu_custom_call" | custom-call | tf_op jit(solution)/shard_map/pallas_call | solution.py:122
  16.4 0.1 copy.61
  16.5 2.6 %collective-permute-start.3 = (f32[32,256]{0,1:T(8,128)S(1)}, f32[32,256]{0,1:T(8,128)S(1)}, u32[]{:S(2)}, u32[]{:S(2)}) collective-permute-start(f32[32,256]{0,1:T(8,128)S(1)} %copy.61), channel_id=1, source_target_pairs={{0,2},{1,3},{2,0},{3,1},{4,6},{5,7},{6,4},{7,5},{8,10},{9,11},{10,... | collective-permute-start | bytes 98312 | tf_op jit(solution)/shard_map/ppermute | solution.py:142
  19.1 0.1 copy.73
  19.3 0.1 copy.74
  19.4 1.6 %collective-permute-start.4 = (f32[1,16,1024]{2,1,0:T(8,128)}, f32[1,16,1024]{2,1,0:T(8,128)S(1)}, u32[]{:S(2)}, u32[]{:S(2)}) collective-permute-start(f32[1,16,1024]{2,1,0:T(8,128)} %bitcast.94), channel_id=1, source_target_pairs={{0,4},{1,5},{2,6},{3,7},{4,0},{5,1},{6,2},{7,3},{8,12},{9,13},{10,... | collective-permute-start | bytes 196616 | tf_op jit(solution)/shard_map/ppermute | solution.py:142
  21.0 2.6 %collective-permute-start.5 = (f32[1,16,1024]{2,1,0:T(8,128)}, f32[1,16,1024]{2,1,0:T(8,128)S(1)}, u32[]{:S(2)}, u32[]{:S(2)}) collective-permute-start(f32[1,16,1024]{2,1,0:T(8,128)} %bitcast.95), channel_id=1, source_target_pairs={{0,8},{1,9},{2,10},{3,11},{4,12},{5,13},{6,14},{7,15},{8,0},{9,1},... | collective-permute-start | bytes 196616 | tf_op jit(solution)/shard_map/ppermute | solution.py:142
  23.6 0.2 collective-permute-start.6
  23.8 0.1 pad_maximum_fusion
  24.0 0.3 fusion.19
  24.3 3.1 %collective-permute-done.5 = f32[1,16,1024]{2,1,0:T(8,128)S(1)} collective-permute-done((f32[1,16,1024]{2,1,0:T(8,128)}, f32[1,16,1024]{2,1,0:T(8,128)S(1)}, u32[]{:S(2)}, u32[]{:S(2)}) %collective-permute-start.5) | collective-permute-done | bytes 65568 | tf_op jit(solution)/shard_map/ppermute | solution.py:142
  27.4 0.3 fusion.17
  27.8 2.5 %collective-permute-done.6 = f32[1,16,1024]{2,1,0:T(8,128)S(1)} collective-permute-done((f32[1,16,1024]{2,1,0:T(8,128)}, f32[1,16,1024]{2,1,0:T(8,128)S(1)}, u32[]{:S(2)}, u32[]{:S(2)}) %collective-permute-start.6) | collective-permute-done | bytes 65568 | tf_op jit(solution)/shard_map/ppermute | solution.py:142
  30.2 0.3 fusion.15
  30.6 0.3 fusion.3
  30.9 0.5 %collective-permute-start.7 = (f32[2,16,1024]{2,1,0:T(8,128)S(1)}, f32[2,16,1024]{2,1,0:T(8,128)S(1)}, u32[]{:S(2)}, u32[]{:S(2)}) collective-permute-start(f32[2,16,1024]{2,1,0:T(8,128)S(1)} %slice.32), channel_id=1, source_target_pairs={{0,1},{1,0},{2,3},{3,2},{4,5},{5,4},{6,7},{7,6},{8,9},{9,8},{10,11... | collective-permute-start | bytes 393224 | tf_op jit(solution)/shard_map/ppermute | solution.py:142
  31.4 1.0 %collective-permute-done.7 = f32[2,16,1024]{2,1,0:T(8,128)S(1)} collective-permute-done((f32[2,16,1024]{2,1,0:T(8,128)S(1)}, f32[2,16,1024]{2,1,0:T(8,128)S(1)}, u32[]{:S(2)}, u32[]{:S(2)}) %collective-permute-start.7) | collective-permute-done | bytes 131104 | tf_op jit(solution)/shard_map/ppermute | solution.py:142
  32.4 1.5 %collective-permute-start.8 = (f32[16,1024]{1,0:T(8,128)S(1)}, f32[16,1024]{1,0:T(8,128)S(1)}, u32[]{:S(2)}, u32[]{:S(2)}) collective-permute-start(f32[16,1024]{1,0:T(8,128)S(1)} %slice_bitcast_fusion), channel_id=1, source_target_pairs={{0,2},{1,3},{2,0},{3,1},{4,6},{5,7},{6,4},{7,5},{8,10},{9,11},{10,... | collective-permute-start | bytes 196616 | tf_op jit(solution)/shard_map/ppermute | solution.py:142
  33.9 3.0 %collective-permute-done.8 = f32[16,1024]{1,0:T(8,128)S(1)} collective-permute-done((f32[16,1024]{1,0:T(8,128)S(1)}, f32[16,1024]{1,0:T(8,128)S(1)}, u32[]{:S(2)}, u32[]{:S(2)}) %collective-permute-start.8) | collective-permute-done | bytes 65568 | tf_op jit(solution)/shard_map/ppermute | solution.py:142
  36.9 0.6 %gather_fusion.1 = f32[8,16,128]{2,1,0:T(8,128)S(1)} fusion(f32[16,8,128]{2,0,1:T(8,128)S(1)} %bitcast.91, s32[1024]{0:T(1024)S(1)} %pad_clamp_fusion), kind=kCustom, calls=%fused_computation.1 | custom fusion | bytes 131104 | tf_op jit(solution)/shard_map/jit(_take)/gather | solution.py:216
  37.6 0.9 %fusion.4 = f32[8,2,8,128]{3,2,1,0:T(8,128)S(1)} fusion(f32[8,128,4,128]{3,2,1,0:T(4,128)S(1)} %bitcast.85, f32[16,8,1,128]{3,0,2,1:T(8,128)S(1)} %bitcast_select_fusion, f32[16,8,1,128]{3,0,2,1:T(8,128)S(1)} %get-tuple-element.29, f32[16,8,1,128]{3,0,2,1:T(8,128)S(1)} %get-tuple-element.28, f32[16,8,1,128]{3,0,2,1:T(8,128)S(1)} %copy.69), kind=kOutput, calls=%fused_computation.7 | convolution fusion | flops 50528256 | bytes 2424832 | tf_op jit(solution)/shard_map/xrkc,rikc->xri/dot_general | solution.py:218
  38.5 0.7 %copy.87 = f32[8,2,8,128]{3,2,0,1:T(8,128)} copy(f32[8,2,8,128]{3,2,1,0:T(8,128)S(1)} %fusion.4) | data formatting | bytes 131072 | tf_op jit(solution)/shard_map/reshape | solution.py:224
  (40 shorter events, 0.4 us)
Async XLA Ops:
  0.6 37.0 %copy-start = (f32[1024,4,128]{2,1,0:T(4,128)S(1)}, f32[1024,4,128]{2,1,0:T(4,128)}, u32[]{:S(2)}) copy-start(f32[1024,4,128]{2,1,0:T(4,128)} %param.26) | copy-start | bytes 6291460
  0.6 8.4 %copy-start.1 = (s32[2,4]{1,0:T(2,128)S(1)}, s32[2,4]{1,0:T(2,128)}, u32[]{:S(2)}) copy-start(s32[2,4]{1,0:T(2,128)} %param.25) | copy-start | bytes 100
  0.7 9.1 %copy-start.5 = (bf16[16,4,128]{2,1,0:T(4,128)(2,1)S(1)}, bf16[16,4,128]{2,1,0:T(4,128)(2,1)}, u32[]{:S(2)}) copy-start(bf16[16,4,128]{2,1,0:T(4,128)(2,1)} %param.24) | copy-start | bytes 49156
  0.7 12.5 %copy-start.6 = (s32[8,4]{0,1:T(4,128)S(1)}, s32[8,4]{0,1:T(4,128)}, u32[]{:S(2)}) copy-start(s32[8,4]{0,1:T(4,128)} %param.27) | copy-start | bytes 388
  5.3 8.7 %collective-permute-start = (f32[16,1024]{1,0:T(8,128)}, f32[16,1024]{1,0:T(8,128)S(1)}, u32[]{:S(2)}, u32[]{:S(2)}) collective-permute-start(f32[16,1024]{1,0:T(8,128)} %get-tuple-element.10.last_ref), channel_id=1, source_target_pairs={{0,1},{1,2},{2,3},{3,4},{4,5},{5,6},{6,7},{7,8},{8,9},{9,10},{10,1... | collective-permute-start | bytes 196616 | tf_op jit(solution)/shard_map/ppermute | solution.py:17
  7.6 6.4 %collective-permute-start.1 = (f32[2,16,1024]{2,1,0:T(8,128)}, f32[2,16,1024]{2,1,0:T(8,128)S(1)}, u32[]{:S(2)}, u32[]{:S(2)}) collective-permute-start(f32[2,16,1024]{2,1,0:T(8,128)} %get-tuple-element.11), channel_id=1, source_target_pairs={{1,0},{2,1},{3,2},{4,3},{5,4},{6,5},{7,6},{8,7},{9,8},{10,9},{11,1... | collective-permute-start | bytes 393224 | tf_op jit(solution)/shard_map/ppermute | solution.py:17
  9.9 4.1 %collective-permute-start.2 = (f32[16,256]{1,0:T(8,128)S(1)}, f32[16,256]{1,0:T(8,128)S(1)}, u32[]{:S(2)}, u32[]{:S(2)}) collective-permute-start(f32[16,256]{1,0:T(8,128)S(1)} %copy_bitcast_fusion.2), channel_id=1, source_target_pairs={{0,1},{1,0},{2,3},{3,2},{4,5},{5,4},{6,7},{7,6},{8,9},{9,8},{10,11... | collective-permute-start | bytes 49160 | tf_op jit(solution)/shard_map/ppermute | solution.py:142
  14.0 0.6 %copy-start.4 = (f32[16,1024]{1,0:T(8,128)}, f32[16,1024]{1,0:T(8,128)S(1)}, u32[]{:S(2)}) copy-start(f32[16,1024]{1,0:T(8,128)S(1)} %collective-permute-done.prev_ref) | copy-start | bytes 196612
  14.0 0.7 %copy-start.3 = (f32[2,16,1024]{2,1,0:T(8,128)}, f32[2,16,1024]{2,1,0:T(8,128)S(1)}, u32[]{:S(2)}) copy-start(f32[2,16,1024]{2,1,0:T(8,128)S(1)} %collective-permute-done.1.next_ref) | copy-start | bytes 393220
  16.4 14.2 %copy-start.2 = (f32[16,1024]{1,0:T(8,128)S(1)}, f32[16,1024]{1,0:T(8,128)}, u32[]{:S(2)}) copy-start(f32[16,1024]{1,0:T(8,128)} %shard_map.159) | copy-start | bytes 196612
  16.5 7.3 %collective-permute-start.3 = (f32[32,256]{0,1:T(8,128)S(1)}, f32[32,256]{0,1:T(8,128)S(1)}, u32[]{:S(2)}, u32[]{:S(2)}) collective-permute-start(f32[32,256]{0,1:T(8,128)S(1)} %copy.61), channel_id=1, source_target_pairs={{0,2},{1,3},{2,0},{3,1},{4,6},{5,7},{6,4},{7,5},{8,10},{9,11},{10,... | collective-permute-start | bytes 98312 | tf_op jit(solution)/shard_map/ppermute | solution.py:142
  19.4 4.6 %collective-permute-start.4 = (f32[1,16,1024]{2,1,0:T(8,128)}, f32[1,16,1024]{2,1,0:T(8,128)S(1)}, u32[]{:S(2)}, u32[]{:S(2)}) collective-permute-start(f32[1,16,1024]{2,1,0:T(8,128)} %bitcast.94), channel_id=1, source_target_pairs={{0,4},{1,5},{2,6},{3,7},{4,0},{5,1},{6,2},{7,3},{8,12},{9,13},{10,... | collective-permute-start | bytes 196616 | tf_op jit(solution)/shard_map/ppermute | solution.py:142
  21.0 6.4 %collective-permute-start.5 = (f32[1,16,1024]{2,1,0:T(8,128)}, f32[1,16,1024]{2,1,0:T(8,128)S(1)}, u32[]{:S(2)}, u32[]{:S(2)}) collective-permute-start(f32[1,16,1024]{2,1,0:T(8,128)} %bitcast.95), channel_id=1, source_target_pairs={{0,8},{1,9},{2,10},{3,11},{4,12},{5,13},{6,14},{7,15},{8,0},{9,1},... | collective-permute-start | bytes 196616 | tf_op jit(solution)/shard_map/ppermute | solution.py:142
  23.6 6.6 %collective-permute-start.6 = (f32[1,16,1024]{2,1,0:T(8,128)}, f32[1,16,1024]{2,1,0:T(8,128)S(1)}, u32[]{:S(2)}, u32[]{:S(2)}) collective-permute-start(f32[1,16,1024]{2,1,0:T(8,128)} %bitcast.96), channel_id=1, source_target_pairs={{0,12},{1,13},{2,14},{3,15},{4,8},{5,9},{6,10},{7,11},{8,4},{9,5},... | collective-permute-start | bytes 196616 | tf_op jit(solution)/shard_map/ppermute | solution.py:142
  30.9 1.4 %collective-permute-start.7 = (f32[2,16,1024]{2,1,0:T(8,128)S(1)}, f32[2,16,1024]{2,1,0:T(8,128)S(1)}, u32[]{:S(2)}, u32[]{:S(2)}) collective-permute-start(f32[2,16,1024]{2,1,0:T(8,128)S(1)} %slice.32), channel_id=1, source_target_pairs={{0,1},{1,0},{2,3},{3,2},{4,5},{5,4},{6,7},{7,6},{8,9},{9,8},{10,11... | collective-permute-start | bytes 393224 | tf_op jit(solution)/shard_map/ppermute | solution.py:142
  32.4 4.4 %collective-permute-start.8 = (f32[16,1024]{1,0:T(8,128)S(1)}, f32[16,1024]{1,0:T(8,128)S(1)}, u32[]{:S(2)}, u32[]{:S(2)}) collective-permute-start(f32[16,1024]{1,0:T(8,128)S(1)} %slice_bitcast_fusion), channel_id=1, source_target_pairs={{0,2},{1,3},{2,0},{3,1},{4,6},{5,7},{6,4},{7,5},{8,10},{9,11},{10,... | collective-permute-start | bytes 196616 | tf_op jit(solution)/shard_map/ppermute | solution.py:142

commit v18 on v17

--- a/solution.py
+++ b/solution.py
@@ -213,7 +213,8 @@
     col_block = (jnp.arange(nyb)[:, None] + offsets_y) % nyb
     blocks_y = mixed.reshape(rows, nyb, BLK)
     fixed = [blocks_y, jnp.roll(blocks_y, 1, axis=1), jnp.roll(blocks_y, -(nyb // 2), axis=1)]
-    rest = jnp.take(blocks_y, col_block[:, 3:], axis=1)
+    hit = col_block[:, 3:, None] == jnp.arange(nyb)[None, None, :]
+    rest = jnp.sum(jnp.where(hit[None, :, :, :, None], blocks_y[:, None, None, :, :], 0.0), axis=3)
     picked = jnp.concatenate([jnp.stack(fixed, axis=2), rest], axis=2)
     prior = jnp.einsum(
         "xrkc,rikc->xri",

time: 39.4 us -> 39.3 us (level)
  local copies, waits for them, and re-layouts: 2.91 us -> 2.4 us
  starting transfers between devices: 16 us -> 16.5 us
    ppermute x7, waiting for transfers between devices: 10.4 us -> 9 us  [swap(): return lax.ppermute(value, axis, [(i, i ^ mask) for i in range(count)])]
    ppermute x2, waiting for transfers between devices: 0.01 us -> 1.07 us  [passed_along(): lax.ppermute(value, axis, [(source, source + steps) for source in range(f...]
    ppermute x7, starting transfers between devices: 12.3 us -> 13.3 us  [swap(): return lax.ppermute(value, axis, [(i, i ^ mask) for i in range(count)])]
    gather x1 -> x0, local copies, waits for them, and re-layouts: 0.55 us -> none  [body(): rest = jnp.take(blocks_y, col_block[:, 3:], axis=1)]
    ppermute x2, starting transfers between devices: 3.65 us -> 3.21 us  [passed_along(): lax.ppermute(value, axis, [(source, source + steps) for source in range(f...]
where the time goes in v18:
time: 39.3 us; the launch traced here: 39.1 us
  starting transfers between devices  16.5 us (42%)
  waiting for transfers between devices  10.1 us (26%)
  Pallas kernels  6.29 us (16%)
  local copies, waits for them, and re-layouts  2.4 us (6%)
  matrix products  2.19 us (6%)
  between operations  0.98 us (2%)
  other arithmetic  0.67 us (2%)
    ppermute x7, starting transfers between devices, swap(): return lax.ppermute(value, axis, [(i, i ^ mask) for i in range(count)])  13.3 us
    ppermute x7, waiting for transfers between devices, swap(): return lax.ppermute(value, axis, [(i, i ^ mask) for i in range(count)])  9 us
    pallas_call x1, Pallas kernels, stencil(): pl.pallas_call(stencil_kernel, grid=(depth // zc,), in_specs=[pl.BlockSpe...  4.6 us
    ppermute x2, starting transfers between devices, passed_along(): lax.ppermute(value, axis, [(source, source + steps) for source in range(f...  3.21 us
    pallas_call x1, Pallas kernels, corrected(): pl.pallas_call(fix_kernel, in_specs=[pl.BlockSpec(memory_space=pltpu.SMEM...  1.69 us
    dot_general x4, matrix products, product(): jnp.dot(cols, piece.reshape(-1, piece.shape[-1]), precision=precise, pref...  1.27 us
    ppermute x2, waiting for transfers between devices, passed_along(): lax.ppermute(value, axis, [(source, source + steps) for source in range(f...  1.07 us
    dot_general x1, matrix products, body(): jnp.einsum('xrkc,rikc->xri', picked, cov_y.reshape(nyb, BLK, cov_y.shape[...  0.92 us
  transfers between devices with their start and end apart: 9, of which 5 were waited for; matrix products, arithmetic and copies ran while one was open for 5% of the time, Pallas kernels for 0%

profile of v18, /device:TPU:0, one launch (start us, length us, event | category | flops | bytes accessed | tf_op | source)
XLA Modules:
  0.0 39.1 jit_solution(13901143235628414051)
XLA Ops:
  0.7 4.6 %shard_map.158 = (f32[16,1024]{1,0:T(8,128)}, f32[2,16,1024]{2,1,0:T(8,128)}, f32[16,1024]{1,0:T(8,128)}, f32[16,1024]{1,0:T(8,128)}) custom-call(f32[16]{0:T(128)} %w_ref.3, f32[16,16,1024]{2,1,0:T(8,128)} %sprev_ref.1, f32[16,16,1024]{2,1,0:T(8,128)} %sprev_ref.1, s32[16,16,1024]{2,1,0:T(8,128)} %f_ref.1, f32[16,16,1024]{2,1,0:T(8,128)} %vx_ref.1, ...), custom_call_target="tpu_custom_call" | custom-call | tf_op jit(solution)/shard_map/pallas_call | solution.py:75
  5.3 1.3 %collective-permute-start.1 = (f32[2,16,1024]{2,1,0:T(8,128)}, f32[2,16,1024]{2,1,0:T(8,128)S(1)}, u32[]{:S(2)}, u32[]{:S(2)}) collective-permute-start(f32[2,16,1024]{2,1,0:T(8,128)} %get-tuple-element.11), channel_id=1, source_target_pairs={{1,0},{2,1},{3,2},{4,3},{5,4},{6,5},{7,6},{8,7},{9,8},{10,9},{11,1... | collective-permute-start | bytes 393224 | tf_op jit(solution)/shard_map/ppermute | solution.py:17
  6.6 0.6 %gather_fusion = s32[16,4]{1,0:T(8,128)S(1)} fusion(s32[2,4]{1,0:T(2,128)S(1)} %copy-done.1, s32[1024]{0:T(1024)S(1)} %pad_clamp_fusion), kind=kCustom, calls=%fused_computation | custom fusion | bytes 576 | tf_op jit(solution)/shard_map/gather | solution.py:149
  7.2 0.1 add_select_fusion
  7.3 0.1 copy.49
  7.4 0.1 select_reduce_fusion.1
  7.5 1.2 %collective-permute-start.2 = (f32[16,256]{1,0:T(8,128)S(1)}, f32[16,256]{1,0:T(8,128)S(1)}, u32[]{:S(2)}, u32[]{:S(2)}) collective-permute-start(f32[16,256]{1,0:T(8,128)S(1)} %copy_bitcast_fusion.2), channel_id=1, source_target_pairs={{0,1},{1,0},{2,3},{3,2},{4,5},{5,4},{6,7},{7,6},{8,9},{9,8},{10,11... | collective-permute-start | bytes 49160 | tf_op jit(solution)/shard_map/ppermute | solution.py:142
  8.7 1.9 %collective-permute-start = (f32[16,1024]{1,0:T(8,128)}, f32[16,1024]{1,0:T(8,128)S(1)}, u32[]{:S(2)}, u32[]{:S(2)}) collective-permute-start(f32[16,1024]{1,0:T(8,128)} %get-tuple-element.10.last_ref), channel_id=1, source_target_pairs={{0,1},{1,2},{2,3},{3,4},{4,5},{5,6},{6,7},{7,8},{8,9},{9,10},{10,1... | collective-permute-start | bytes 196616 | tf_op jit(solution)/shard_map/ppermute | solution.py:17
  10.6 1.1 %collective-permute-done.prev_ref = f32[16,1024]{1,0:T(8,128)S(1)} collective-permute-done((f32[16,1024]{1,0:T(8,128)}, f32[16,1024]{1,0:T(8,128)S(1)}, u32[]{:S(2)}, u32[]{:S(2)}) %collective-permute-start) | collective-permute-done | bytes 65568 | tf_op jit(solution)/shard_map/ppermute | solution.py:17
  11.7 0.6 %copy-done.4 = f32[16,1024]{1,0:T(8,128)} copy-done((f32[16,1024]{1,0:T(8,128)}, f32[16,1024]{1,0:T(8,128)S(1)}, u32[]{:S(2)}) %copy-start.4) | copy-done | bytes 65560
  12.4 1.7 %shard_map.159 = f32[16,1024]{1,0:T(8,128)} custom-call(f32[16]{0:T(128)} %w_ref.3, f32[16,1024]{1,0:T(8,128)} %get-tuple-element.8.partial_ref, f32[16,1024]{1,0:T(8,128)} %get-tuple-element.9.up_ref, f32[16,1024]{1,0:T(8,128)} %copy-done.4, f32[2,16,1024]{2,1,0:T(8,128)} %copy-done.3, f32[16,1024]{1,0:T(8,128)} %get-tuple-element.10.last_ref), custom_call_target="tpu_custom_call" | custom-call | tf_op jit(solution)/shard_map/pallas_call | solution.py:122
  14.1 0.1 copy.53
  14.2 5.8 %collective-permute-start.3 = (f32[32,256]{0,1:T(8,128)S(1)}, f32[32,256]{0,1:T(8,128)S(1)}, u32[]{:S(2)}, u32[]{:S(2)}) collective-permute-start(f32[32,256]{0,1:T(8,128)S(1)} %copy.53), channel_id=1, source_target_pairs={{0,2},{1,3},{2,0},{3,1},{4,6},{5,7},{6,4},{7,5},{8,10},{9,11},{10,... | collective-permute-start | bytes 98312 | tf_op jit(solution)/shard_map/ppermute | solution.py:142
  20.0 0.1 copy.65
  20.1 0.1 copy.66
  20.2 1.6 %collective-permute-start.4 = (f32[1,16,1024]{2,1,0:T(8,128)}, f32[1,16,1024]{2,1,0:T(8,128)S(1)}, u32[]{:S(2)}, u32[]{:S(2)}) collective-permute-start(f32[1,16,1024]{2,1,0:T(8,128)} %bitcast.90), channel_id=1, source_target_pairs={{0,4},{1,5},{2,6},{3,7},{4,0},{5,1},{6,2},{7,3},{8,12},{9,13},{10,... | collective-permute-start | bytes 196616 | tf_op jit(solution)/shard_map/ppermute | solution.py:142
  21.8 2.6 %collective-permute-start.5 = (f32[1,16,1024]{2,1,0:T(8,128)}, f32[1,16,1024]{2,1,0:T(8,128)S(1)}, u32[]{:S(2)}, u32[]{:S(2)}) collective-permute-start(f32[1,16,1024]{2,1,0:T(8,128)} %bitcast.91), channel_id=1, source_target_pairs={{0,8},{1,9},{2,10},{3,11},{4,12},{5,13},{6,14},{7,15},{8,0},{9,1},... | collective-permute-start | bytes 196616 | tf_op jit(solution)/shard_map/ppermute | solution.py:142
  24.4 0.2 collective-permute-start.6
  24.6 0.1 pad_maximum_fusion
  24.8 0.3 fusion.20
  25.1 3.8 %collective-permute-done.5 = f32[1,16,1024]{2,1,0:T(8,128)S(1)} collective-permute-done((f32[1,16,1024]{2,1,0:T(8,128)}, f32[1,16,1024]{2,1,0:T(8,128)S(1)}, u32[]{:S(2)}, u32[]{:S(2)}) %collective-permute-start.5) | collective-permute-done | bytes 65568 | tf_op jit(solution)/shard_map/ppermute | solution.py:142
  28.9 0.3 fusion.18
  29.2 1.4 %collective-permute-done.6 = f32[1,16,1024]{2,1,0:T(8,128)S(1)} collective-permute-done((f32[1,16,1024]{2,1,0:T(8,128)}, f32[1,16,1024]{2,1,0:T(8,128)S(1)}, u32[]{:S(2)}, u32[]{:S(2)}) %collective-permute-start.6) | collective-permute-done | bytes 65568 | tf_op jit(solution)/shard_map/ppermute | solution.py:142
  30.7 0.3 fusion.16
  31.0 0.3 fusion.3
  31.5 1.3 %collective-permute-done.7 = f32[2,16,1024]{2,1,0:T(8,128)S(1)} collective-permute-done((f32[2,16,1024]{2,1,0:T(8,128)S(1)}, f32[2,16,1024]{2,1,0:T(8,128)S(1)}, u32[]{:S(2)}, u32[]{:S(2)}) %collective-permute-start.7) | collective-permute-done | bytes 131104 | tf_op jit(solution)/shard_map/ppermute | solution.py:142
  32.8 1.8 %collective-permute-start.8 = (f32[16,1024]{1,0:T(8,128)S(1)}, f32[16,1024]{1,0:T(8,128)S(1)}, u32[]{:S(2)}, u32[]{:S(2)}) collective-permute-start(f32[16,1024]{1,0:T(8,128)S(1)} %slice_bitcast_fusion), channel_id=1, source_target_pairs={{0,2},{1,3},{2,0},{3,1},{4,6},{5,7},{6,4},{7,5},{8,10},{9,11},{10,... | collective-permute-start | bytes 196616 | tf_op jit(solution)/shard_map/ppermute | solution.py:142
  34.7 0.1 iota_compare_fusion
  34.7 2.4 %collective-permute-done.8 = f32[16,1024]{1,0:T(8,128)S(1)} collective-permute-done((f32[16,1024]{1,0:T(8,128)S(1)}, f32[16,1024]{1,0:T(8,128)S(1)}, u32[]{:S(2)}, u32[]{:S(2)}) %collective-permute-start.8) | collective-permute-done | bytes 65568 | tf_op jit(solution)/shard_map/ppermute | solution.py:142
  37.3 0.2 select_reduce_fusion
  37.6 0.9 %fusion.4 = f32[8,2,8,128]{3,2,1,0:T(8,128)S(1)} fusion(f32[8,128,4,128]{3,2,1,0:T(4,128)S(1)} %bitcast.79, f32[16,8,1,128]{3,0,2,1:T(8,128)S(1)} %bitcast.89, f32[16,8,1,128]{3,0,2,1:T(8,128)S(1)} %get-tuple-element.27, f32[16,8,1,128]{3,0,2,1:T(8,128)S(1)} %get-tuple-element.26, f32[16,8,1,128]{3,0,2,1:T(8,128)S(1)} %copy.61), kind=kOutput, calls=%fused_computation.6 | convolution fusion | flops 50528256 | bytes 2424832 | tf_op jit(solution)/shard_map/xrkc,rikc->xri/dot_general | solution.py:219
  38.5 0.7 %copy.83 = f32[8,2,8,128]{3,2,0,1:T(8,128)} copy(f32[8,2,8,128]{3,2,1,0:T(8,128)S(1)} %fusion.4) | data formatting | bytes 131072 | tf_op jit(solution)/shard_map/reshape | solution.py:225
  (40 shorter events, 0.4 us)
Async XLA Ops:
  0.6 36.9 %copy-start = (f32[1024,4,128]{2,1,0:T(4,128)S(1)}, f32[1024,4,128]{2,1,0:T(4,128)}, u32[]{:S(2)}) copy-start(f32[1024,4,128]{2,1,0:T(4,128)} %param.26) | copy-start | bytes 6291460
  0.6 6.0 %copy-start.1 = (s32[2,4]{1,0:T(2,128)S(1)}, s32[2,4]{1,0:T(2,128)}, u32[]{:S(2)}) copy-start(s32[2,4]{1,0:T(2,128)} %param.25) | copy-start | bytes 100
  0.7 6.7 %copy-start.5 = (bf16[16,4,128]{2,1,0:T(4,128)(2,1)S(1)}, bf16[16,4,128]{2,1,0:T(4,128)(2,1)}, u32[]{:S(2)}) copy-start(bf16[16,4,128]{2,1,0:T(4,128)(2,1)} %param.24) | copy-start | bytes 49156
  0.7 19.3 %copy-start.6 = (s32[8,4]{0,1:T(4,128)S(1)}, s32[8,4]{0,1:T(4,128)}, u32[]{:S(2)}) copy-start(s32[8,4]{0,1:T(4,128)} %param.27) | copy-start | bytes 388
  5.3 6.4 %collective-permute-start.1 = (f32[2,16,1024]{2,1,0:T(8,128)}, f32[2,16,1024]{2,1,0:T(8,128)S(1)}, u32[]{:S(2)}, u32[]{:S(2)}) collective-permute-start(f32[2,16,1024]{2,1,0:T(8,128)} %get-tuple-element.11), channel_id=1, source_target_pairs={{1,0},{2,1},{3,2},{4,3},{5,4},{6,5},{7,6},{8,7},{9,8},{10,9},{11,1... | collective-permute-start | bytes 393224 | tf_op jit(solution)/shard_map/ppermute | solution.py:17
  7.5 3.1 %collective-permute-start.2 = (f32[16,256]{1,0:T(8,128)S(1)}, f32[16,256]{1,0:T(8,128)S(1)}, u32[]{:S(2)}, u32[]{:S(2)}) collective-permute-start(f32[16,256]{1,0:T(8,128)S(1)} %copy_bitcast_fusion.2), channel_id=1, source_target_pairs={{0,1},{1,0},{2,3},{3,2},{4,5},{5,4},{6,7},{7,6},{8,9},{9,8},{10,11... | collective-permute-start | bytes 49160 | tf_op jit(solution)/shard_map/ppermute | solution.py:142
  8.7 3.0 %collective-permute-start = (f32[16,1024]{1,0:T(8,128)}, f32[16,1024]{1,0:T(8,128)S(1)}, u32[]{:S(2)}, u32[]{:S(2)}) collective-permute-start(f32[16,1024]{1,0:T(8,128)} %get-tuple-element.10.last_ref), channel_id=1, source_target_pairs={{0,1},{1,2},{2,3},{3,4},{4,5},{5,6},{6,7},{7,8},{8,9},{9,10},{10,1... | collective-permute-start | bytes 196616 | tf_op jit(solution)/shard_map/ppermute | solution.py:17
  11.7 0.6 %copy-start.4 = (f32[16,1024]{1,0:T(8,128)}, f32[16,1024]{1,0:T(8,128)S(1)}, u32[]{:S(2)}) copy-start(f32[16,1024]{1,0:T(8,128)S(1)} %collective-permute-done.prev_ref) | copy-start | bytes 196612
  11.7 0.7 %copy-start.3 = (f32[2,16,1024]{2,1,0:T(8,128)}, f32[2,16,1024]{2,1,0:T(8,128)S(1)}, u32[]{:S(2)}) copy-start(f32[2,16,1024]{2,1,0:T(8,128)S(1)} %collective-permute-done.1.next_ref) | copy-start | bytes 393220
  14.1 16.9 %copy-start.2 = (f32[16,1024]{1,0:T(8,128)S(1)}, f32[16,1024]{1,0:T(8,128)}, u32[]{:S(2)}) copy-start(f32[16,1024]{1,0:T(8,128)} %shard_map.159) | copy-start | bytes 196612
  14.2 10.5 %collective-permute-start.3 = (f32[32,256]{0,1:T(8,128)S(1)}, f32[32,256]{0,1:T(8,128)S(1)}, u32[]{:S(2)}, u32[]{:S(2)}) collective-permute-start(f32[32,256]{0,1:T(8,128)S(1)} %copy.53), channel_id=1, source_target_pairs={{0,2},{1,3},{2,0},{3,1},{4,6},{5,7},{6,4},{7,5},{8,10},{9,11},{10,... | collective-permute-start | bytes 98312 | tf_op jit(solution)/shard_map/ppermute | solution.py:142
  20.2 4.6 %collective-permute-start.4 = (f32[1,16,1024]{2,1,0:T(8,128)}, f32[1,16,1024]{2,1,0:T(8,128)S(1)}, u32[]{:S(2)}, u32[]{:S(2)}) collective-permute-start(f32[1,16,1024]{2,1,0:T(8,128)} %bitcast.90), channel_id=1, source_target_pairs={{0,4},{1,5},{2,6},{3,7},{4,0},{5,1},{6,2},{7,3},{8,12},{9,13},{10,... | collective-permute-start | bytes 196616 | tf_op jit(solution)/shard_map/ppermute | solution.py:142
  21.8 7.1 %collective-permute-start.5 = (f32[1,16,1024]{2,1,0:T(8,128)}, f32[1,16,1024]{2,1,0:T(8,128)S(1)}, u32[]{:S(2)}, u32[]{:S(2)}) collective-permute-start(f32[1,16,1024]{2,1,0:T(8,128)} %bitcast.91), channel_id=1, source_target_pairs={{0,8},{1,9},{2,10},{3,11},{4,12},{5,13},{6,14},{7,15},{8,0},{9,1},... | collective-permute-start | bytes 196616 | tf_op jit(solution)/shard_map/ppermute | solution.py:142
  24.4 6.3 %collective-permute-start.6 = (f32[1,16,1024]{2,1,0:T(8,128)}, f32[1,16,1024]{2,1,0:T(8,128)S(1)}, u32[]{:S(2)}, u32[]{:S(2)}) collective-permute-start(f32[1,16,1024]{2,1,0:T(8,128)} %bitcast.92), channel_id=1, source_target_pairs={{0,12},{1,13},{2,14},{3,15},{4,8},{5,9},{6,10},{7,11},{8,4},{9,5},... | collective-permute-start | bytes 196616 | tf_op jit(solution)/shard_map/ppermute | solution.py:142
  31.4 1.4 %collective-permute-start.7 = (f32[2,16,1024]{2,1,0:T(8,128)S(1)}, f32[2,16,1024]{2,1,0:T(8,128)S(1)}, u32[]{:S(2)}, u32[]{:S(2)}) collective-permute-start(f32[2,16,1024]{2,1,0:T(8,128)S(1)} %slice.32), channel_id=1, source_target_pairs={{0,1},{1,0},{2,3},{3,2},{4,5},{5,4},{6,7},{7,6},{8,9},{9,8},{10,11... | collective-permute-start | bytes 393224 | tf_op jit(solution)/shard_map/ppermute | solution.py:142
  32.8 4.3 %collective-permute-start.8 = (f32[16,1024]{1,0:T(8,128)S(1)}, f32[16,1024]{1,0:T(8,128)S(1)}, u32[]{:S(2)}, u32[]{:S(2)}) collective-permute-start(f32[16,1024]{1,0:T(8,128)S(1)} %slice_bitcast_fusion), channel_id=1, source_target_pairs={{0,2},{1,3},{2,0},{3,1},{4,6},{5,7},{6,4},{7,5},{8,10},{9,11},{10,... | collective-permute-start | bytes 196616 | tf_op jit(solution)/shard_map/ppermute | solution.py:142

commit v19 on v18

--- a/solution.py
+++ b/solution.py
@@ -160,7 +160,9 @@
     per_device = slab.reshape(slab.shape[0], count, rows)
 
     def product(piece, masks):
-        cols = jnp.take(per_device, me ^ jnp.array(masks, jnp.int32), axis=1).reshape(slab.shape[0], -1)
+        hit = (me ^ jnp.array(masks, jnp.int32))[:, None] == jnp.arange(count)[None, :]
+        picked = jnp.sum(jnp.where(hit[None, :, :, None], per_device[:, None, :, :], 0.0), axis=2)
+        cols = picked.reshape(slab.shape[0], -1)
         return jnp.dot(cols, piece.reshape(-1, piece.shape[-1]), precision=precise, preferred_element_type=jnp.float32)
 
     buf = local[None]

time: 39.3 us -> 42.2 us (1.074)
  waiting for transfers between devices: 10.1 us -> 13.6 us
  starting transfers between devices: 16.5 us -> 13.6 us
  local copies, waits for them, and re-layouts: 2.4 us -> 3.92 us
  matrix products: 2.19 us -> 3.01 us
    ppermute x2, waiting for transfers between devices: 1.07 us -> 4.15 us  [passed_along(): lax.ppermute(value, axis, [(source, source + steps) for source in range(f...]
    ppermute x7, starting transfers between devices: 13.3 us -> 10.4 us  [swap(): return lax.ppermute(value, axis, [(i, i ^ mask) for i in range(count)])]
    gather x1, local copies, waits for them, and re-layouts: 0.56 us -> 1.38 us  [cx_slab(): target = (row_block[:, None] + offsets[row_block]) % nxb]
    dot_general x4, matrix products: 1.27 us -> 2.09 us  [product(): jnp.dot(cols, piece.reshape(-1, piece.shape[-1]), precision=precise, pref...]
    convert_element_type x1, local copies, waits for them, and re-layouts: 0.01 us -> 0.72 us  [cx_slab(): cov_rows.astype(jnp.float32)[:, :, None, :]]
    ppermute x7, waiting for transfers between devices: 9 us -> 9.42 us  [swap(): return lax.ppermute(value, axis, [(i, i ^ mask) for i in range(count)])]
  transfers between devices with their start and end apart: 9 -> 9, of which waited for: 5 -> 5; matrix products, arithmetic and copies ran while one was open for 5% -> 3% of each run, Pallas kernels for 0% -> 11%
where the time goes in v19:
time: 42.2 us; the launch traced here: 42 us
  starting transfers between devices  13.6 us (32%)
  waiting for transfers between devices  13.6 us (32%)
  Pallas kernels  6.15 us (15%)
  local copies, waits for them, and re-layouts  3.92 us (9%)
  matrix products  3.01 us (7%)
  between operations  0.93 us (2%)
  other arithmetic  0.76 us (2%)
    ppermute x7, starting transfers between devices, swap(): return lax.ppermute(value, axis, [(i, i ^ mask) for i in range(count)])  10.4 us
    ppermute x7, waiting for transfers between devices, swap(): return lax.ppermute(value, axis, [(i, i ^ mask) for i in range(count)])  9.42 us
    pallas_call x1, Pallas kernels, stencil(): pl.pallas_call(stencil_kernel, grid=(depth // zc,), in_specs=[pl.BlockSpe...  4.45 us
    ppermute x2, waiting for transfers between devices, passed_along(): lax.ppermute(value, axis, [(source, source + steps) for source in range(f...  4.15 us
    ppermute x2, starting transfers between devices, passed_along(): lax.ppermute(value, axis, [(source, source + steps) for source in range(f...  3.26 us
    dot_general x4, matrix products, product(): jnp.dot(cols, piece.reshape(-1, piece.shape[-1]), precision=precise, pref...  2.09 us
    pallas_call x1, Pallas kernels, corrected(): pl.pallas_call(fix_kernel, in_specs=[pl.BlockSpec(memory_space=pltpu.SMEM...  1.69 us
    gather x1, local copies, waits for them, and re-layouts, cx_slab(): target = (row_block[:, None] + offsets[row_block]) % nxb  1.38 us
  transfers between devices with their start and end apart: 9, of which 5 were waited for; matrix products, arithmetic and copies ran while one was open for 3% of the time, Pallas kernels for 11%

profile of v19, /device:TPU:0, one launch (start us, length us, event | category | flops | bytes accessed | tf_op | source)
XLA Modules:
  0.0 42.0 jit_solution(8749355667572652481)
XLA Ops:
  0.7 1.4 %gather_fusion = s32[16,4]{1,0:T(8,128)S(1)} fusion(s32[2,4]{1,0:T(2,128)} %param.23, s32[1024]{0:T(1024)S(1)} %pad_clamp_fusion), kind=kCustom, calls=%fused_computation | custom fusion | bytes 576 | tf_op jit(solution)/shard_map/gather | solution.py:149
  2.2 0.1 copy.49
  2.3 0.7 %copy.50 = f32[16,4,128]{2,0,1:T(8,128)S(1)} copy(bf16[16,4,128]{2,1,0:T(4,128)(2,1)} %param.22) | data formatting | bytes 49152 | tf_op jit(solution)/shard_map/convert_element_type | solution.py:152
  3.0 0.1 select_reduce_fusion.5
  3.1 0.5 %collective-permute-start.2 = (f32[16,256]{1,0:T(8,128)S(1)}, f32[16,256]{1,0:T(8,128)S(1)}, u32[]{:S(2)}, u32[]{:S(2)}) collective-permute-start(f32[16,256]{1,0:T(8,128)S(1)} %copy_bitcast_fusion.2), channel_id=1, source_target_pairs={{0,1},{1,0},{2,3},{3,2},{4,5},{5,4},{6,7},{7,6},{8,9},{9,8},{10,11... | collective-permute-start | bytes 49160 | tf_op jit(solution)/shard_map/ppermute | solution.py:142
  3.6 4.5 %shard_map.158 = (f32[16,1024]{1,0:T(8,128)}, f32[2,16,1024]{2,1,0:T(8,128)}, f32[16,1024]{1,0:T(8,128)}, f32[16,1024]{1,0:T(8,128)}) custom-call(f32[16]{0:T(128)} %w_ref.3, f32[16,16,1024]{2,1,0:T(8,128)} %sprev_ref.1, f32[16,16,1024]{2,1,0:T(8,128)} %sprev_ref.1, s32[16,16,1024]{2,1,0:T(8,128)} %f_ref.1, f32[16,16,1024]{2,1,0:T(8,128)} %vx_ref.1, ...), custom_call_target="tpu_custom_call" | custom-call | tf_op jit(solution)/shard_map/pallas_call | solution.py:75
  8.1 2.0 %collective-permute-start = (f32[16,1024]{1,0:T(8,128)}, f32[16,1024]{1,0:T(8,128)S(1)}, u32[]{:S(2)}, u32[]{:S(2)}) collective-permute-start(f32[16,1024]{1,0:T(8,128)} %get-tuple-element.9.last_ref), channel_id=1, source_target_pairs={{0,1},{1,2},{2,3},{3,4},{4,5},{5,6},{6,7},{7,8},{8,9},{9,10},{10,1... | collective-permute-start | bytes 196616 | tf_op jit(solution)/shard_map/ppermute | solution.py:17
  10.0 1.3 %collective-permute-start.1 = (f32[2,16,1024]{2,1,0:T(8,128)}, f32[2,16,1024]{2,1,0:T(8,128)S(1)}, u32[]{:S(2)}, u32[]{:S(2)}) collective-permute-start(f32[2,16,1024]{2,1,0:T(8,128)} %get-tuple-element.10), channel_id=1, source_target_pairs={{1,0},{2,1},{3,2},{4,3},{5,4},{6,5},{7,6},{8,7},{9,8},{10,9},{11,1... | collective-permute-start | bytes 393224 | tf_op jit(solution)/shard_map/ppermute | solution.py:17
  11.4 4.2 %collective-permute-done.1.next_ref = f32[2,16,1024]{2,1,0:T(8,128)S(1)} collective-permute-done((f32[2,16,1024]{2,1,0:T(8,128)}, f32[2,16,1024]{2,1,0:T(8,128)S(1)}, u32[]{:S(2)}, u32[]{:S(2)}) %collective-permute-start.1) | collective-permute-done | bytes 131104 | tf_op jit(solution)/shard_map/ppermute | solution.py:17
  15.6 0.6 %copy-done.1 = f32[2,16,1024]{2,1,0:T(8,128)} copy-done((f32[2,16,1024]{2,1,0:T(8,128)}, f32[2,16,1024]{2,1,0:T(8,128)S(1)}, u32[]{:S(2)}) %copy-start.1) | copy-done | bytes 131096
  16.2 1.7 %shard_map.159 = f32[16,1024]{1,0:T(8,128)} custom-call(f32[16]{0:T(128)} %w_ref.3, f32[16,1024]{1,0:T(8,128)} %get-tuple-element.7.partial_ref, f32[16,1024]{1,0:T(8,128)} %get-tuple-element.8.up_ref, f32[16,1024]{1,0:T(8,128)} %copy-done.2, f32[2,16,1024]{2,1,0:T(8,128)} %copy-done.1, f32[16,1024]{1,0:T(8,128)} %get-tuple-element.9.last_ref), custom_call_target="tpu_custom_call" | custom-call | tf_op jit(solution)/shard_map/pallas_call | solution.py:122
  17.9 0.1 copy.53
  18.0 3.5 %collective-permute-start.3 = (f32[32,256]{0,1:T(8,128)S(1)}, f32[32,256]{0,1:T(8,128)S(1)}, u32[]{:S(2)}, u32[]{:S(2)}) collective-permute-start(f32[32,256]{0,1:T(8,128)S(1)} %copy.53), channel_id=1, source_target_pairs={{0,2},{1,3},{2,0},{3,1},{4,6},{5,7},{6,4},{7,5},{8,10},{9,11},{10,... | collective-permute-start | bytes 98312 | tf_op jit(solution)/shard_map/ppermute | solution.py:142
  21.5 0.1 copy.65
  21.6 0.1 copy.66
  21.7 1.6 %collective-permute-start.4 = (f32[1,16,1024]{2,1,0:T(8,128)}, f32[1,16,1024]{2,1,0:T(8,128)S(1)}, u32[]{:S(2)}, u32[]{:S(2)}) collective-permute-start(f32[1,16,1024]{2,1,0:T(8,128)} %bitcast.73), channel_id=1, source_target_pairs={{0,4},{1,5},{2,6},{3,7},{4,0},{5,1},{6,2},{7,3},{8,12},{9,13},{10,... | collective-permute-start | bytes 196616 | tf_op jit(solution)/shard_map/ppermute | solution.py:142
  23.3 2.6 %collective-permute-start.5 = (f32[1,16,1024]{2,1,0:T(8,128)}, f32[1,16,1024]{2,1,0:T(8,128)S(1)}, u32[]{:S(2)}, u32[]{:S(2)}) collective-permute-start(f32[1,16,1024]{2,1,0:T(8,128)} %bitcast.74), channel_id=1, source_target_pairs={{0,8},{1,9},{2,10},{3,11},{4,12},{5,13},{6,14},{7,15},{8,0},{9,1},... | collective-permute-start | bytes 196616 | tf_op jit(solution)/shard_map/ppermute | solution.py:142
  25.9 0.2 collective-permute-start.6
  26.2 0.2 select_reduce_fusion.4
  26.4 0.3 fusion.20
  26.7 3.1 %collective-permute-done.5 = f32[1,16,1024]{2,1,0:T(8,128)S(1)} collective-permute-done((f32[1,16,1024]{2,1,0:T(8,128)}, f32[1,16,1024]{2,1,0:T(8,128)S(1)}, u32[]{:S(2)}, u32[]{:S(2)}) %collective-permute-start.5) | collective-permute-done | bytes 65568 | tf_op jit(solution)/shard_map/ppermute | solution.py:142
  29.8 0.3 fusion.18
  30.1 2.5 %collective-permute-done.6 = f32[1,16,1024]{2,1,0:T(8,128)S(1)} collective-permute-done((f32[1,16,1024]{2,1,0:T(8,128)}, f32[1,16,1024]{2,1,0:T(8,128)S(1)}, u32[]{:S(2)}, u32[]{:S(2)}) %collective-permute-start.6) | collective-permute-done | bytes 65568 | tf_op jit(solution)/shard_map/ppermute | solution.py:142
  32.6 0.3 fusion.16
  32.9 1.2 %fusion.3 = f32[64,1024]{1,0:T(8,128)S(1)} fusion(f32[64,1024]{1,0:T(8,128)S(1)} %fusion.16, f32[64,1024]{1,0:T(8,128)S(1)} %fusion.18, f32[64,1024]{1,0:T(8,128)S(1)} %fusion.20, f32[64,16]{0,1:T(8,128)S(1)} %get-tuple-element.12, f32[16,1024]{1,0:T(8,128)} %shard_map.159), kind=kOutput, calls=%fused_computation.5 | convolution fusion | flops 6488064 | bytes 1118208 | tf_op jit(solution)/shard_map/dot_general | solution.py:166
  34.1 0.4 %collective-permute-start.7 = (f32[2,16,1024]{2,1,0:T(8,128)S(1)}, f32[2,16,1024]{2,1,0:T(8,128)S(1)}, u32[]{:S(2)}, u32[]{:S(2)}) collective-permute-start(f32[2,16,1024]{2,1,0:T(8,128)S(1)} %slice.32), channel_id=1, source_target_pairs={{0,1},{1,0},{2,3},{3,2},{4,5},{5,4},{6,7},{7,6},{8,9},{9,8},{10,11... | collective-permute-start | bytes 393224 | tf_op jit(solution)/shard_map/ppermute | solution.py:142
  34.5 1.0 %collective-permute-done.7 = f32[2,16,1024]{2,1,0:T(8,128)S(1)} collective-permute-done((f32[2,16,1024]{2,1,0:T(8,128)S(1)}, f32[2,16,1024]{2,1,0:T(8,128)S(1)}, u32[]{:S(2)}, u32[]{:S(2)}) %collective-permute-start.7) | collective-permute-done | bytes 131104 | tf_op jit(solution)/shard_map/ppermute | solution.py:142
  35.5 1.5 %collective-permute-start.8 = (f32[16,1024]{1,0:T(8,128)S(1)}, f32[16,1024]{1,0:T(8,128)S(1)}, u32[]{:S(2)}, u32[]{:S(2)}) collective-permute-start(f32[16,1024]{1,0:T(8,128)S(1)} %slice_bitcast_fusion), channel_id=1, source_target_pairs={{0,2},{1,3},{2,0},{3,1},{4,6},{5,7},{6,4},{7,5},{8,10},{9,11},{10,... | collective-permute-start | bytes 196616 | tf_op jit(solution)/shard_map/ppermute | solution.py:142
  37.1 2.9 %collective-permute-done.8 = f32[16,1024]{1,0:T(8,128)S(1)} collective-permute-done((f32[16,1024]{1,0:T(8,128)S(1)}, f32[16,1024]{1,0:T(8,128)S(1)}, u32[]{:S(2)}, u32[]{:S(2)}) %collective-permute-start.8) | collective-permute-done | bytes 65568 | tf_op jit(solution)/shard_map/ppermute | solution.py:142
  40.1 0.2 select_reduce_fusion
  40.4 0.9 %fusion.4 = f32[8,2,8,128]{3,2,1,0:T(8,128)S(1)} fusion(f32[8,128,4,128]{3,2,1,0:T(4,128)S(1)} %bitcast.62, f32[16,8,1,128]{3,0,2,1:T(8,128)S(1)} %bitcast.72, f32[16,8,1,128]{3,0,2,1:T(8,128)S(1)} %maximum_bitcast_fusion.1, f32[16,8,1,128]{3,0,2,1:T(8,128)S(1)} %maximum_bitcast_fusion, f32[16,8,1,128]{3,0,2,1:T(8,128)S(1)} %copy.61), kind=kOutput, calls=%fused_computation.6 | convolution fusion | flops 50528256 | bytes 2424832 | tf_op jit(solution)/shard_map/xrkc,rikc->xri/dot_general | solution.py:221
  41.3 0.7 %copy.83 = f32[8,2,8,128]{3,2,0,1:T(8,128)} copy(f32[8,2,8,128]{3,2,1,0:T(8,128)S(1)} %fusion.4) | data formatting | bytes 131072 | tf_op jit(solution)/shard_map/reshape | solution.py:227
  (37 shorter events, 0.4 us)
Async XLA Ops:
  0.6 39.7 %copy-start = (f32[1024,4,128]{2,1,0:T(4,128)S(1)}, f32[1024,4,128]{2,1,0:T(4,128)}, u32[]{:S(2)}) copy-start(f32[1024,4,128]{2,1,0:T(4,128)} %param.24) | copy-start | bytes 6291460
  3.1 8.3 %copy-start.3 = (s32[8,4]{0,1:T(4,128)S(1)}, s32[8,4]{0,1:T(4,128)}, u32[]{:S(2)}) copy-start(s32[8,4]{0,1:T(4,128)} %param.25) | copy-start | bytes 388
  3.1 8.3 %collective-permute-start.2 = (f32[16,256]{1,0:T(8,128)S(1)}, f32[16,256]{1,0:T(8,128)S(1)}, u32[]{:S(2)}, u32[]{:S(2)}) collective-permute-start(f32[16,256]{1,0:T(8,128)S(1)} %copy_bitcast_fusion.2), channel_id=1, source_target_pairs={{0,1},{1,0},{2,3},{3,2},{4,5},{5,4},{6,7},{7,6},{8,9},{9,8},{10,11... | collective-permute-start | bytes 49160 | tf_op jit(solution)/shard_map/ppermute | solution.py:142
  8.1 3.3 %collective-permute-start = (f32[16,1024]{1,0:T(8,128)}, f32[16,1024]{1,0:T(8,128)S(1)}, u32[]{:S(2)}, u32[]{:S(2)}) collective-permute-start(f32[16,1024]{1,0:T(8,128)} %get-tuple-element.9.last_ref), channel_id=1, source_target_pairs={{0,1},{1,2},{2,3},{3,4},{4,5},{5,6},{6,7},{7,8},{8,9},{9,10},{10,1... | collective-permute-start | bytes 196616 | tf_op jit(solution)/shard_map/ppermute | solution.py:17
  10.0 5.5 %collective-permute-start.1 = (f32[2,16,1024]{2,1,0:T(8,128)}, f32[2,16,1024]{2,1,0:T(8,128)S(1)}, u32[]{:S(2)}, u32[]{:S(2)}) collective-permute-start(f32[2,16,1024]{2,1,0:T(8,128)} %get-tuple-element.10), channel_id=1, source_target_pairs={{1,0},{2,1},{3,2},{4,3},{5,4},{6,5},{7,6},{8,7},{9,8},{10,9},{11,1... | collective-permute-start | bytes 393224 | tf_op jit(solution)/shard_map/ppermute | solution.py:17
  11.4 4.2 %copy-start.2 = (f32[16,1024]{1,0:T(8,128)}, f32[16,1024]{1,0:T(8,128)S(1)}, u32[]{:S(2)}) copy-start(f32[16,1024]{1,0:T(8,128)S(1)} %collective-permute-done.prev_ref) | copy-start | bytes 196612
  15.6 0.7 %copy-start.1 = (f32[2,16,1024]{2,1,0:T(8,128)}, f32[2,16,1024]{2,1,0:T(8,128)S(1)}, u32[]{:S(2)}) copy-start(f32[2,16,1024]{2,1,0:T(8,128)S(1)} %collective-permute-done.1.next_ref) | copy-start | bytes 393220
  18.0 8.1 %collective-permute-start.3 = (f32[32,256]{0,1:T(8,128)S(1)}, f32[32,256]{0,1:T(8,128)S(1)}, u32[]{:S(2)}, u32[]{:S(2)}) collective-permute-start(f32[32,256]{0,1:T(8,128)S(1)} %copy.53), channel_id=1, source_target_pairs={{0,2},{1,3},{2,0},{3,1},{4,6},{5,7},{6,4},{7,5},{8,10},{9,11},{10,... | collective-permute-start | bytes 98312 | tf_op jit(solution)/shard_map/ppermute | solution.py:142
  21.7 4.7 %collective-permute-start.4 = (f32[1,16,1024]{2,1,0:T(8,128)}, f32[1,16,1024]{2,1,0:T(8,128)S(1)}, u32[]{:S(2)}, u32[]{:S(2)}) collective-permute-start(f32[1,16,1024]{2,1,0:T(8,128)} %bitcast.73), channel_id=1, source_target_pairs={{0,4},{1,5},{2,6},{3,7},{4,0},{5,1},{6,2},{7,3},{8,12},{9,13},{10,... | collective-permute-start | bytes 196616 | tf_op jit(solution)/shard_map/ppermute | solution.py:142
  23.3 6.4 %collective-permute-start.5 = (f32[1,16,1024]{2,1,0:T(8,128)}, f32[1,16,1024]{2,1,0:T(8,128)S(1)}, u32[]{:S(2)}, u32[]{:S(2)}) collective-permute-start(f32[1,16,1024]{2,1,0:T(8,128)} %bitcast.74), channel_id=1, source_target_pairs={{0,8},{1,9},{2,10},{3,11},{4,12},{5,13},{6,14},{7,15},{8,0},{9,1},... | collective-permute-start | bytes 196616 | tf_op jit(solution)/shard_map/ppermute | solution.py:142
  25.9 6.6 %collective-permute-start.6 = (f32[1,16,1024]{2,1,0:T(8,128)}, f32[1,16,1024]{2,1,0:T(8,128)S(1)}, u32[]{:S(2)}, u32[]{:S(2)}) collective-permute-start(f32[1,16,1024]{2,1,0:T(8,128)} %bitcast.75), channel_id=1, source_target_pairs={{0,12},{1,13},{2,14},{3,15},{4,8},{5,9},{6,10},{7,11},{8,4},{9,5},... | collective-permute-start | bytes 196616 | tf_op jit(solution)/shard_map/ppermute | solution.py:142
  34.1 1.4 %collective-permute-start.7 = (f32[2,16,1024]{2,1,0:T(8,128)S(1)}, f32[2,16,1024]{2,1,0:T(8,128)S(1)}, u32[]{:S(2)}, u32[]{:S(2)}) collective-permute-start(f32[2,16,1024]{2,1,0:T(8,128)S(1)} %slice.32), channel_id=1, source_target_pairs={{0,1},{1,0},{2,3},{3,2},{4,5},{5,4},{6,7},{7,6},{8,9},{9,8},{10,11... | collective-permute-start | bytes 393224 | tf_op jit(solution)/shard_map/ppermute | solution.py:142
  35.5 4.4 %collective-permute-start.8 = (f32[16,1024]{1,0:T(8,128)S(1)}, f32[16,1024]{1,0:T(8,128)S(1)}, u32[]{:S(2)}, u32[]{:S(2)}) collective-permute-start(f32[16,1024]{1,0:T(8,128)S(1)} %slice_bitcast_fusion), channel_id=1, source_target_pairs={{0,2},{1,3},{2,0},{3,1},{4,6},{5,7},{6,4},{7,5},{8,10},{9,11},{10,... | collective-permute-start | bytes 196616 | tf_op jit(solution)/shard_map/ppermute | solution.py:142

commit v20 on v18

--- a/solution.py
+++ b/solution.py
@@ -165,7 +165,8 @@
 
     buf = local[None]
     entries = [0]
-    total = product(buf, entries)
+    own_cols = lax.dynamic_slice_in_dim(per_device, me, 1, axis=1).reshape(slab.shape[0], -1)
+    total = jnp.dot(own_cols, local, precision=precise, preferred_element_type=jnp.float32)
     for masks in gather_rounds(count):
         others = [swap(buf, axis, m) for m in masks]
         for m, other in zip(masks, others):

time: 39.3 us -> 39.3 us (level)
    dot_general x4 -> x3, matrix products: 1.27 us -> 0.94 us  [product(): jnp.dot(cols, piece.reshape(-1, piece.shape[-1]), precision=precise, pref...]
where the time goes in v20:
time: 39.3 us; the launch traced here: 39.1 us
  starting transfers between devices  16.5 us (42%)
  waiting for transfers between devices  10.1 us (26%)
  Pallas kernels  6.29 us (16%)
  local copies, waits for them, and re-layouts  2.4 us (6%)
  matrix products  2.2 us (6%)
  between operations  0.98 us (2%)
  other arithmetic  0.67 us (2%)
    ppermute x7, starting transfers between devices, swap(): return lax.ppermute(value, axis, [(i, i ^ mask) for i in range(count)])  13.3 us
    ppermute x7, waiting for transfers between devices, swap(): return lax.ppermute(value, axis, [(i, i ^ mask) for i in range(count)])  9.03 us
    pallas_call x1, Pallas kernels, stencil(): pl.pallas_call(stencil_kernel, grid=(depth // zc,), in_specs=[pl.BlockSpe...  4.6 us
    ppermute x2, starting transfers between devices, passed_along(): lax.ppermute(value, axis, [(source, source + steps) for source in range(f...  3.21 us
    pallas_call x1, Pallas kernels, corrected(): pl.pallas_call(fix_kernel, in_specs=[pl.BlockSpec(memory_space=pltpu.SMEM...  1.69 us
    ppermute x2, waiting for transfers between devices, passed_along(): lax.ppermute(value, axis, [(source, source + steps) for source in range(f...  1.07 us
    dot_general x3, matrix products, product(): jnp.dot(cols, piece.reshape(-1, piece.shape[-1]), precision=precise, pref...  0.94 us
    dot_general x1, matrix products, body(): jnp.einsum('xrkc,rikc->xri', picked, cov_y.reshape(nyb, BLK, cov_y.shape[...  0.92 us
  transfers between devices with their start and end apart: 9, of which 5 were waited for; matrix products, arithmetic and copies ran while one was open for 5% of the time, Pallas kernels for 0%

profile of v20, /device:TPU:0, one launch (start us, length us, event | category | flops | bytes accessed | tf_op | source)
XLA Modules:
  0.0 39.1 jit_solution(4922657590966188486)
XLA Ops:
  0.7 4.6 %shard_map.149 = (f32[16,1024]{1,0:T(8,128)}, f32[2,16,1024]{2,1,0:T(8,128)}, f32[16,1024]{1,0:T(8,128)}, f32[16,1024]{1,0:T(8,128)}) custom-call(f32[16]{0:T(128)} %w_ref.3, f32[16,16,1024]{2,1,0:T(8,128)} %sprev_ref.1, f32[16,16,1024]{2,1,0:T(8,128)} %sprev_ref.1, s32[16,16,1024]{2,1,0:T(8,128)} %f_ref.1, f32[16,16,1024]{2,1,0:T(8,128)} %vx_ref.1, ...), custom_call_target="tpu_custom_call" | custom-call | tf_op jit(solution)/shard_map/pallas_call | solution.py:75
  5.3 1.3 %collective-permute-start.1 = (f32[2,16,1024]{2,1,0:T(8,128)}, f32[2,16,1024]{2,1,0:T(8,128)S(1)}, u32[]{:S(2)}, u32[]{:S(2)}) collective-permute-start(f32[2,16,1024]{2,1,0:T(8,128)} %get-tuple-element.11), channel_id=1, source_target_pairs={{1,0},{2,1},{3,2},{4,3},{5,4},{6,5},{7,6},{8,7},{9,8},{10,9},{11,1... | collective-permute-start | bytes 393224 | tf_op jit(solution)/shard_map/ppermute | solution.py:17
  6.6 0.6 %gather_fusion = s32[16,4]{1,0:T(8,128)S(1)} fusion(s32[2,4]{1,0:T(2,128)S(1)} %copy-done.1, s32[1024]{0:T(1024)S(1)} %pad_clamp_fusion), kind=kCustom, calls=%fused_computation | custom fusion | bytes 576 | tf_op jit(solution)/shard_map/gather | solution.py:149
  7.2 0.1 add_select_fusion
  7.3 0.1 copy.48
  7.4 0.1 select_reduce_fusion.1
  7.5 1.2 %collective-permute-start.2 = (f32[16,256]{1,0:T(8,128)S(1)}, f32[16,256]{1,0:T(8,128)S(1)}, u32[]{:S(2)}, u32[]{:S(2)}) collective-permute-start(f32[16,256]{1,0:T(8,128)S(1)} %copy_bitcast_fusion.2), channel_id=1, source_target_pairs={{0,1},{1,0},{2,3},{3,2},{4,5},{5,4},{6,7},{7,6},{8,9},{9,8},{10,11... | collective-permute-start | bytes 49160 | tf_op jit(solution)/shard_map/ppermute | solution.py:142
  8.7 1.9 %collective-permute-start = (f32[16,1024]{1,0:T(8,128)}, f32[16,1024]{1,0:T(8,128)S(1)}, u32[]{:S(2)}, u32[]{:S(2)}) collective-permute-start(f32[16,1024]{1,0:T(8,128)} %get-tuple-element.10.last_ref), channel_id=1, source_target_pairs={{0,1},{1,2},{2,3},{3,4},{4,5},{5,6},{6,7},{7,8},{8,9},{9,10},{10,1... | collective-permute-start | bytes 196616 | tf_op jit(solution)/shard_map/ppermute | solution.py:17
  10.6 1.1 %collective-permute-done.prev_ref = f32[16,1024]{1,0:T(8,128)S(1)} collective-permute-done((f32[16,1024]{1,0:T(8,128)}, f32[16,1024]{1,0:T(8,128)S(1)}, u32[]{:S(2)}, u32[]{:S(2)}) %collective-permute-start) | collective-permute-done | bytes 65568 | tf_op jit(solution)/shard_map/ppermute | solution.py:17
  11.7 0.6 %copy-done.4 = f32[16,1024]{1,0:T(8,128)} copy-done((f32[16,1024]{1,0:T(8,128)}, f32[16,1024]{1,0:T(8,128)S(1)}, u32[]{:S(2)}) %copy-start.4) | copy-done | bytes 65560
  12.4 1.7 %shard_map.150 = f32[16,1024]{1,0:T(8,128)} custom-call(f32[16]{0:T(128)} %w_ref.3, f32[16,1024]{1,0:T(8,128)} %get-tuple-element.8.partial_ref, f32[16,1024]{1,0:T(8,128)} %get-tuple-element.9.up_ref, f32[16,1024]{1,0:T(8,128)} %copy-done.4, f32[2,16,1024]{2,1,0:T(8,128)} %copy-done.3, f32[16,1024]{1,0:T(8,128)} %get-tuple-element.10.last_ref), custom_call_target="tpu_custom_call" | custom-call | tf_op jit(solution)/shard_map/pallas_call | solution.py:122
  14.1 0.1 copy.52
  14.2 5.8 %collective-permute-start.3 = (f32[32,256]{0,1:T(8,128)S(1)}, f32[32,256]{0,1:T(8,128)S(1)}, u32[]{:S(2)}, u32[]{:S(2)}) collective-permute-start(f32[32,256]{0,1:T(8,128)S(1)} %copy.52), channel_id=1, source_target_pairs={{0,2},{1,3},{2,0},{3,1},{4,6},{5,7},{6,4},{7,5},{8,10},{9,11},{10,... | collective-permute-start | bytes 98312 | tf_op jit(solution)/shard_map/ppermute | solution.py:142
  20.0 0.1 copy.64
  20.1 0.1 copy.65
  20.2 1.6 %collective-permute-start.4 = (f32[1,16,1024]{2,1,0:T(8,128)}, f32[1,16,1024]{2,1,0:T(8,128)S(1)}, u32[]{:S(2)}, u32[]{:S(2)}) collective-permute-start(f32[1,16,1024]{2,1,0:T(8,128)} %bitcast.90), channel_id=1, source_target_pairs={{0,4},{1,5},{2,6},{3,7},{4,0},{5,1},{6,2},{7,3},{8,12},{9,13},{10,... | collective-permute-start | bytes 196616 | tf_op jit(solution)/shard_map/ppermute | solution.py:142
  21.8 2.6 %collective-permute-start.5 = (f32[1,16,1024]{2,1,0:T(8,128)}, f32[1,16,1024]{2,1,0:T(8,128)S(1)}, u32[]{:S(2)}, u32[]{:S(2)}) collective-permute-start(f32[1,16,1024]{2,1,0:T(8,128)} %bitcast.91), channel_id=1, source_target_pairs={{0,8},{1,9},{2,10},{3,11},{4,12},{5,13},{6,14},{7,15},{8,0},{9,1},... | collective-permute-start | bytes 196616 | tf_op jit(solution)/shard_map/ppermute | solution.py:142
  24.4 0.2 collective-permute-start.6
  24.6 0.1 pad_maximum_fusion
  24.8 0.3 fusion.20
  25.1 3.8 %collective-permute-done.5 = f32[1,16,1024]{2,1,0:T(8,128)S(1)} collective-permute-done((f32[1,16,1024]{2,1,0:T(8,128)}, f32[1,16,1024]{2,1,0:T(8,128)S(1)}, u32[]{:S(2)}, u32[]{:S(2)}) %collective-permute-start.5) | collective-permute-done | bytes 65568 | tf_op jit(solution)/shard_map/ppermute | solution.py:142
  28.9 0.3 fusion.18
  29.2 1.4 %collective-permute-done.6 = f32[1,16,1024]{2,1,0:T(8,128)S(1)} collective-permute-done((f32[1,16,1024]{2,1,0:T(8,128)}, f32[1,16,1024]{2,1,0:T(8,128)S(1)}, u32[]{:S(2)}, u32[]{:S(2)}) %collective-permute-start.6) | collective-permute-done | bytes 65568 | tf_op jit(solution)/shard_map/ppermute | solution.py:142
  30.7 0.3 fusion.16
  31.0 0.3 fusion.3
  31.5 1.3 %collective-permute-done.7 = f32[2,16,1024]{2,1,0:T(8,128)S(1)} collective-permute-done((f32[2,16,1024]{2,1,0:T(8,128)S(1)}, f32[2,16,1024]{2,1,0:T(8,128)S(1)}, u32[]{:S(2)}, u32[]{:S(2)}) %collective-permute-start.7) | collective-permute-done | bytes 131104 | tf_op jit(solution)/shard_map/ppermute | solution.py:142
  32.8 1.8 %collective-permute-start.8 = (f32[16,1024]{1,0:T(8,128)S(1)}, f32[16,1024]{1,0:T(8,128)S(1)}, u32[]{:S(2)}, u32[]{:S(2)}) collective-permute-start(f32[16,1024]{1,0:T(8,128)S(1)} %slice_bitcast_fusion), channel_id=1, source_target_pairs={{0,2},{1,3},{2,0},{3,1},{4,6},{5,7},{6,4},{7,5},{8,10},{9,11},{10,... | collective-permute-start | bytes 196616 | tf_op jit(solution)/shard_map/ppermute | solution.py:142
  34.7 0.1 iota_compare_fusion
  34.7 2.4 %collective-permute-done.8 = f32[16,1024]{1,0:T(8,128)S(1)} collective-permute-done((f32[16,1024]{1,0:T(8,128)S(1)}, f32[16,1024]{1,0:T(8,128)S(1)}, u32[]{:S(2)}, u32[]{:S(2)}) %collective-permute-start.8) | collective-permute-done | bytes 65568 | tf_op jit(solution)/shard_map/ppermute | solution.py:142
  37.3 0.2 select_reduce_fusion
  37.6 0.9 %fusion.4 = f32[8,2,8,128]{3,2,1,0:T(8,128)S(1)} fusion(f32[8,128,4,128]{3,2,1,0:T(4,128)S(1)} %bitcast.79, f32[16,8,1,128]{3,0,2,1:T(8,128)S(1)} %bitcast.89, f32[16,8,1,128]{3,0,2,1:T(8,128)S(1)} %get-tuple-element.27, f32[16,8,1,128]{3,0,2,1:T(8,128)S(1)} %get-tuple-element.26, f32[16,8,1,128]{3,0,2,1:T(8,128)S(1)} %copy.60), kind=kOutput, calls=%fused_computation.6 | convolution fusion | flops 50528256 | bytes 2424832 | tf_op jit(solution)/shard_map/xrkc,rikc->xri/dot_general | solution.py:220
  38.5 0.7 %copy.82 = f32[8,2,8,128]{3,2,0,1:T(8,128)} copy(f32[8,2,8,128]{3,2,1,0:T(8,128)S(1)} %fusion.4) | data formatting | bytes 131072 | tf_op jit(solution)/shard_map/reshape | solution.py:226
  (40 shorter events, 0.4 us)
Async XLA Ops:
  0.6 36.9 %copy-start = (f32[1024,4,128]{2,1,0:T(4,128)S(1)}, f32[1024,4,128]{2,1,0:T(4,128)}, u32[]{:S(2)}) copy-start(f32[1024,4,128]{2,1,0:T(4,128)} %param.25) | copy-start | bytes 6291460
  0.6 6.0 %copy-start.1 = (s32[2,4]{1,0:T(2,128)S(1)}, s32[2,4]{1,0:T(2,128)}, u32[]{:S(2)}) copy-start(s32[2,4]{1,0:T(2,128)} %param.24) | copy-start | bytes 100
  0.7 6.7 %copy-start.5 = (bf16[16,4,128]{2,1,0:T(4,128)(2,1)S(1)}, bf16[16,4,128]{2,1,0:T(4,128)(2,1)}, u32[]{:S(2)}) copy-start(bf16[16,4,128]{2,1,0:T(4,128)(2,1)} %param.23) | copy-start | bytes 49156
  0.7 19.3 %copy-start.6 = (s32[8,4]{0,1:T(4,128)S(1)}, s32[8,4]{0,1:T(4,128)}, u32[]{:S(2)}) copy-start(s32[8,4]{0,1:T(4,128)} %param.26) | copy-start | bytes 388
  5.3 6.4 %collective-permute-start.1 = (f32[2,16,1024]{2,1,0:T(8,128)}, f32[2,16,1024]{2,1,0:T(8,128)S(1)}, u32[]{:S(2)}, u32[]{:S(2)}) collective-permute-start(f32[2,16,1024]{2,1,0:T(8,128)} %get-tuple-element.11), channel_id=1, source_target_pairs={{1,0},{2,1},{3,2},{4,3},{5,4},{6,5},{7,6},{8,7},{9,8},{10,9},{11,1... | collective-permute-start | bytes 393224 | tf_op jit(solution)/shard_map/ppermute | solution.py:17
  7.5 3.1 %collective-permute-start.2 = (f32[16,256]{1,0:T(8,128)S(1)}, f32[16,256]{1,0:T(8,128)S(1)}, u32[]{:S(2)}, u32[]{:S(2)}) collective-permute-start(f32[16,256]{1,0:T(8,128)S(1)} %copy_bitcast_fusion.2), channel_id=1, source_target_pairs={{0,1},{1,0},{2,3},{3,2},{4,5},{5,4},{6,7},{7,6},{8,9},{9,8},{10,11... | collective-permute-start | bytes 49160 | tf_op jit(solution)/shard_map/ppermute | solution.py:142
  8.7 3.0 %collective-permute-start = (f32[16,1024]{1,0:T(8,128)}, f32[16,1024]{1,0:T(8,128)S(1)}, u32[]{:S(2)}, u32[]{:S(2)}) collective-permute-start(f32[16,1024]{1,0:T(8,128)} %get-tuple-element.10.last_ref), channel_id=1, source_target_pairs={{0,1},{1,2},{2,3},{3,4},{4,5},{5,6},{6,7},{7,8},{8,9},{9,10},{10,1... | collective-permute-start | bytes 196616 | tf_op jit(solution)/shard_map/ppermute | solution.py:17
  11.7 0.6 %copy-start.4 = (f32[16,1024]{1,0:T(8,128)}, f32[16,1024]{1,0:T(8,128)S(1)}, u32[]{:S(2)}) copy-start(f32[16,1024]{1,0:T(8,128)S(1)} %collective-permute-done.prev_ref) | copy-start | bytes 196612
  11.7 0.7 %copy-start.3 = (f32[2,16,1024]{2,1,0:T(8,128)}, f32[2,16,1024]{2,1,0:T(8,128)S(1)}, u32[]{:S(2)}) copy-start(f32[2,16,1024]{2,1,0:T(8,128)S(1)} %collective-permute-done.1.next_ref) | copy-start | bytes 393220
  14.1 16.9 %copy-start.2 = (f32[16,1024]{1,0:T(8,128)S(1)}, f32[16,1024]{1,0:T(8,128)}, u32[]{:S(2)}) copy-start(f32[16,1024]{1,0:T(8,128)} %shard_map.150) | copy-start | bytes 196612
  14.2 10.5 %collective-permute-start.3 = (f32[32,256]{0,1:T(8,128)S(1)}, f32[32,256]{0,1:T(8,128)S(1)}, u32[]{:S(2)}, u32[]{:S(2)}) collective-permute-start(f32[32,256]{0,1:T(8,128)S(1)} %copy.52), channel_id=1, source_target_pairs={{0,2},{1,3},{2,0},{3,1},{4,6},{5,7},{6,4},{7,5},{8,10},{9,11},{10,... | collective-permute-start | bytes 98312 | tf_op jit(solution)/shard_map/ppermute | solution.py:142
  20.2 4.6 %collective-permute-start.4 = (f32[1,16,1024]{2,1,0:T(8,128)}, f32[1,16,1024]{2,1,0:T(8,128)S(1)}, u32[]{:S(2)}, u32[]{:S(2)}) collective-permute-start(f32[1,16,1024]{2,1,0:T(8,128)} %bitcast.90), channel_id=1, source_target_pairs={{0,4},{1,5},{2,6},{3,7},{4,0},{5,1},{6,2},{7,3},{8,12},{9,13},{10,... | collective-permute-start | bytes 196616 | tf_op jit(solution)/shard_map/ppermute | solution.py:142
  21.8 7.1 %collective-permute-start.5 = (f32[1,16,1024]{2,1,0:T(8,128)}, f32[1,16,1024]{2,1,0:T(8,128)S(1)}, u32[]{:S(2)}, u32[]{:S(2)}) collective-permute-start(f32[1,16,1024]{2,1,0:T(8,128)} %bitcast.91), channel_id=1, source_target_pairs={{0,8},{1,9},{2,10},{3,11},{4,12},{5,13},{6,14},{7,15},{8,0},{9,1},... | collective-permute-start | bytes 196616 | tf_op jit(solution)/shard_map/ppermute | solution.py:142
  24.4 6.3 %collective-permute-start.6 = (f32[1,16,1024]{2,1,0:T(8,128)}, f32[1,16,1024]{2,1,0:T(8,128)S(1)}, u32[]{:S(2)}, u32[]{:S(2)}) collective-permute-start(f32[1,16,1024]{2,1,0:T(8,128)} %bitcast.92), channel_id=1, source_target_pairs={{0,12},{1,13},{2,14},{3,15},{4,8},{5,9},{6,10},{7,11},{8,4},{9,5},... | collective-permute-start | bytes 196616 | tf_op jit(solution)/shard_map/ppermute | solution.py:142
  31.4 1.4 %collective-permute-start.7 = (f32[2,16,1024]{2,1,0:T(8,128)S(1)}, f32[2,16,1024]{2,1,0:T(8,128)S(1)}, u32[]{:S(2)}, u32[]{:S(2)}) collective-permute-start(f32[2,16,1024]{2,1,0:T(8,128)S(1)} %slice.32), channel_id=1, source_target_pairs={{0,1},{1,0},{2,3},{3,2},{4,5},{5,4},{6,7},{7,6},{8,9},{9,8},{10,11... | collective-permute-start | bytes 393224 | tf_op jit(solution)/shard_map/ppermute | solution.py:142
  32.8 4.3 %collective-permute-start.8 = (f32[16,1024]{1,0:T(8,128)S(1)}, f32[16,1024]{1,0:T(8,128)S(1)}, u32[]{:S(2)}, u32[]{:S(2)}) collective-permute-start(f32[16,1024]{1,0:T(8,128)S(1)} %slice_bitcast_fusion), channel_id=1, source_target_pairs={{0,2},{1,3},{2,0},{3,1},{4,6},{5,7},{6,4},{7,5},{8,10},{9,11},{10,... | collective-permute-start | bytes 196616 | tf_op jit(solution)/shard_map/ppermute | solution.py:142
